TPU v7x, 32 devices: a whole 2x2x4 slice. The times are simulated.
32 devices in a mesh: grp: 2 (over x), blade: 8 (over z, y), dof: 2 (over core).
Axes of the slice: x: 2, y: 2, z: 4, core: 2. Of those that a mesh axis runs over, the one named last changes fastest.
Arguments:
- panel: bfloat16 [8192, 512], P(('grp', 'blade', 'dof')), parts along dimension 0, may hold values from -0.25 to 0.25
- stiffness: bfloat16 [96, 64, 128, 128], P(('grp', 'blade'), 'dof'), parts along dimension 0, may hold values from -0.5 to 0.5
- block_rows: int32 [96, 64], P(('grp', 'blade'), 'dof'), parts along dimension 0, may hold values from 0 to 31
- block_cols: int32 [96, 64], P(('grp', 'blade'), 'dof'), parts along dimension 0, may hold values from 0 to 31
Outputs:
- spectral: float32 [2, 96, 512, 512], P(None, ('grp', 'blade'), 'dof'), parts along dimension 1
There are 2 independent parts, one for each index of `grp`. A program takes and returns all parts, laid end to end along the dimension named above; each array names one. Nothing has to cross between parts.
Inputs may be any that keep to these rules, and one draw needn't show every extreme that they name: `block_rows`: row block index of each stiffness block; indices of one blade may repeat. `block_cols`: column block index of each stiffness block; indices of one blade may repeat.
All inputs are finite; a program needn't handle non-finite values.
Results may differ from a plain program's by a relative error of at most 0.0029.
Values may be sent and summed in bfloat16 or wider, within the bound.
No kernel may reach another device: no remote copies, remote signals or barrier semaphores. Data moves between devices by JAX's collectives and lax.ppermute only.
A program may use at most 128 MiB of HBM per device.

v0:
```python
import math

import jax
import jax.numpy as jnp
from jax import lax
from jax.sharding import PartitionSpec as P


def body(panel, stiffness, block_rows, block_cols):
    block_size = stiffness.shape[-1]
    modes = panel.shape[-1]
    whole = lax.all_gather(panel, ("blade", "dof"), axis=0, tiled=True)
    blocks = whole.reshape(-1, block_size, modes)

    def one_blade(items):
        mats, rows, cols = items
        chosen = jnp.take(blocks, cols, axis=0)
        image = jnp.einsum("nij,njm->nim", mats, chosen, preferred_element_type=jnp.float32)
        image = image.astype(jnp.bfloat16)
        left = jnp.take(blocks, rows, axis=0).reshape(-1, modes)
        return lax.dot_general(
            left,
            image.reshape(-1, modes),
            (((0,), (0,)), ((), ())),
            preferred_element_type=jnp.float32,
        )

    partial_proj = lax.map(one_blade, (stiffness, block_rows, block_cols))
    blade_count = stiffness.shape[0] * lax.axis_size("blade")
    index = jnp.arange(blade_count, dtype=jnp.int32)
    angle = (index[:, None] * index[None, :] % blade_count).astype(jnp.float32) * (
        2.0 * math.pi / blade_count
    )
    cosine = jnp.cos(angle)
    sine = jnp.sin(angle)
    stacked = lax.all_to_all(partial_proj, "blade", split_axis=1, concat_axis=0, tiled=True)
    real_part = jnp.einsum("hb,brc->hrc", cosine, stacked, precision=lax.Precision.HIGHEST)
    imag_part = -jnp.einsum("hb,brc->hrc", sine, stacked, precision=lax.Precision.HIGHEST)
    joined = jnp.stack([real_part, imag_part])
    full_spec = lax.all_to_all(joined, "blade", split_axis=1, concat_axis=2, tiled=True)
    result = lax.psum_scatter(full_spec, "dof", scatter_dimension=2, tiled=True)
    return result


def solution(mesh):
    placed = (
        P(("grp", "blade", "dof"), None),
        P(("grp", "blade"), "dof", None, None),
        P(("grp", "blade"), "dof"),
        P(("grp", "blade"), "dof"),
    )
    return jax.shard_map(
        body,
        mesh=mesh,
        in_specs=placed,
        out_specs=P(None, ("grp", "blade"), "dof", None),
        check_vma=False,
    )
```

profile of v0, /device:TPU:0, one launch (start us, length us, event | category | flops | bytes accessed | tf_op | source)
XLA Modules:
  0.0 863.4 jit_solution(7075036304253567163)
XLA Ops:
  6.5 0.0 all-gather.2.cloned.1.call-start
  6.5 0.7 all-gather.2.cloned.1.call-update
  7.3 0.0 reduce-scatter.2.cloned.1.call-start
  7.3 55.5 %all-gather.2.cloned.1.call-done = bf16[4096,512]{1,0:T(8,128)(2,1)} async-done(((bf16[256,512]{1,0:T(8,128)(2,1)}), bf16[4096,512]{1,0:T(8,128)(2,1)}) %all-gather.2.cloned.1.call-update) | async-done | bytes 4194320 | tf_op jit(solution)/shard_map/all_gather | solution.py:12
  62.8 244.8 %while.10 = (s32[]{:T(128)}, f32[6,512,512]{2,0,1:T(8,128)}, s32[6,32]{1,0:T(8,128)}, bf16[32,128,512]{2,1,0:T(8,128)(2,1)}, bf16[6,32,128,128]{3,2,1,0:T(8,128)...) while((s32[]{:T(128)}, f32[6,512,512]{2,0,1:T(8,128)}, s32[6,32]{1,0:T(8,128)}, ...), condition=%wide.region_1.3_spmd, body=%wide.region_0.2_spmd.sunk | while | flops 2690648576 | bytes 31466728 | solution.py:28
  62.8 0.7 compare_and_fusion.3
  63.5 4.9 gather_fusion.1
  68.5 5.0 gather_fusion
  73.5 7.2 fusion.71
  80.8 1.1 copy.41
  81.8 21.8 %dynamic_update_slice.5 = f32[6,512,512]{2,0,1:T(8,128)} dynamic-update-slice(f32[6,512,512]{2,0,1:T(8,128)} %get-tuple-element.111, f32[1,512,512]{2,0,1:T(1,128)S(1)} %copy.41, s32[]{:T(128)S(6)} %copy.45, s32[]{:T(128)} %constant.36.clone.1..sunk, s32[]{:T(128)} %constant.36.clone.1..sunk) | dynamic-update-slice | bytes 2097156 | tf_op jit(solution)/shard_map/while/body/jit(dynamic_update_index_in_dim)/dynamic_update_slice | solution.py:28
  103.6 0.7 compare_and_fusion.3
  104.3 4.9 gather_fusion.1
  109.3 5.0 gather_fusion
  114.3 7.2 fusion.71
  121.6 1.1 copy.41
  122.6 21.8 %dynamic_update_slice.5 = f32[6,512,512]{2,0,1:T(8,128)} dynamic-update-slice(f32[6,512,512]{2,0,1:T(8,128)} %get-tuple-element.111, f32[1,512,512]{2,0,1:T(1,128)S(1)} %copy.41, s32[]{:T(128)S(6)} %copy.45, s32[]{:T(128)} %constant.36.clone.1..sunk, s32[]{:T(128)} %constant.36.clone.1..sunk) | dynamic-update-slice | bytes 2097156 | tf_op jit(solution)/shard_map/while/body/jit(dynamic_update_index_in_dim)/dynamic_update_slice | solution.py:28
  144.4 0.7 compare_and_fusion.3
  145.1 4.9 gather_fusion.1
  150.1 5.0 gather_fusion
  155.1 7.2 fusion.71
  162.3 1.1 copy.41
  163.4 21.8 %dynamic_update_slice.5 = f32[6,512,512]{2,0,1:T(8,128)} dynamic-update-slice(f32[6,512,512]{2,0,1:T(8,128)} %get-tuple-element.111, f32[1,512,512]{2,0,1:T(1,128)S(1)} %copy.41, s32[]{:T(128)S(6)} %copy.45, s32[]{:T(128)} %constant.36.clone.1..sunk, s32[]{:T(128)} %constant.36.clone.1..sunk) | dynamic-update-slice | bytes 2097156 | tf_op jit(solution)/shard_map/while/body/jit(dynamic_update_index_in_dim)/dynamic_update_slice | solution.py:28
  185.2 0.7 compare_and_fusion.3
  185.9 4.9 gather_fusion.1
  190.9 5.0 gather_fusion
  195.9 7.2 fusion.71
  203.1 1.1 copy.41
  204.2 21.8 %dynamic_update_slice.5 = f32[6,512,512]{2,0,1:T(8,128)} dynamic-update-slice(f32[6,512,512]{2,0,1:T(8,128)} %get-tuple-element.111, f32[1,512,512]{2,0,1:T(1,128)S(1)} %copy.41, s32[]{:T(128)S(6)} %copy.45, s32[]{:T(128)} %constant.36.clone.1..sunk, s32[]{:T(128)} %constant.36.clone.1..sunk) | dynamic-update-slice | bytes 2097156 | tf_op jit(solution)/shard_map/while/body/jit(dynamic_update_index_in_dim)/dynamic_update_slice | solution.py:28
  226.0 0.7 compare_and_fusion.3
  226.7 4.9 gather_fusion.1
  231.7 5.0 gather_fusion
  236.7 7.2 fusion.71
  243.9 1.1 copy.41
  245.0 21.8 %dynamic_update_slice.5 = f32[6,512,512]{2,0,1:T(8,128)} dynamic-update-slice(f32[6,512,512]{2,0,1:T(8,128)} %get-tuple-element.111, f32[1,512,512]{2,0,1:T(1,128)S(1)} %copy.41, s32[]{:T(128)S(6)} %copy.45, s32[]{:T(128)} %constant.36.clone.1..sunk, s32[]{:T(128)} %constant.36.clone.1..sunk) | dynamic-update-slice | bytes 2097156 | tf_op jit(solution)/shard_map/while/body/jit(dynamic_update_index_in_dim)/dynamic_update_slice | solution.py:28
  266.8 0.7 compare_and_fusion.3
  267.5 4.9 gather_fusion.1
  272.5 5.0 gather_fusion
  277.5 7.2 fusion.71
  284.7 1.1 copy.41
  285.8 21.8 %dynamic_update_slice.5 = f32[6,512,512]{2,0,1:T(8,128)} dynamic-update-slice(f32[6,512,512]{2,0,1:T(8,128)} %get-tuple-element.111, f32[1,512,512]{2,0,1:T(1,128)S(1)} %copy.41, s32[]{:T(128)S(6)} %copy.45, s32[]{:T(128)} %constant.36.clone.1..sunk, s32[]{:T(128)} %constant.36.clone.1..sunk) | dynamic-update-slice | bytes 2097156 | tf_op jit(solution)/shard_map/while/body/jit(dynamic_update_index_in_dim)/dynamic_update_slice | solution.py:28
  307.6 187.5 %all_to_all.36 = f32[6,512,512]{2,0,1:T(8,128)S(1)} all-to-all(f32[6,512,512]{2,0,1:T(8,128)} %get-tuple-element.38), channel_id=1, replica_groups=mesh['grp'=2,'blade'=8,'dof'=2] {'blade'}, dimensions={1} | all-to-all | bytes 12582912 | tf_op jit(solution)/shard_map/all_to_all | solution.py:36
  495.1 3.6 copy.21
  498.6 9.7 %negate_bitcast_fusion = f32[1,48,64,512]{3,1,2,0:T(8,128)S(1)} fusion(f32[48,64,512]{2,1,0:T(8,128)S(1)} %bitcast.41), kind=kOutput, calls=%fused_computation.26 | convolution fusion | flops 907563264 | bytes 12582912 | tf_op jit(solution)/shard_map/hb,brc->hrc/dot_general | solution.py:38
  508.3 10.2 %fusion.34 = f32[1,48,64,512]{3,1,2,0:T(8,128)} fusion(f32[48,64,512]{2,1,0:T(8,128)S(1)} %bitcast.42), kind=kOutput, calls=%fused_computation.31 | convolution fusion | flops 905990400 | bytes 12582912 | tf_op jit(solution)/shard_map/hb,brc->hrc/dot_general | solution.py:37
  518.5 9.5 %pad_maximum_fusion = f32[2,48,64,512]{3,1,2,0:T(8,128)} fusion(f32[1,48,64,512]{3,1,2,0:T(8,128)S(1)} %negate_bitcast_fusion, f32[1,48,64,512]{3,1,2,0:T(8,128)} %fusion.34), kind=kLoop, calls=%fused_computation.25 | loop fusion | flops 3145728 | bytes 25165824 | tf_op jit(solution)/shard_map/stack | solution.py:39
  528.0 16.4 %copy.24 = f32[2,48,64,512]{3,2,0,1:T(8,128)} copy(f32[2,48,64,512]{3,1,2,0:T(8,128)} %pad_maximum_fusion) | data formatting | bytes 25165824 | tf_op jit(solution)/shard_map/stack | solution.py:39
  544.4 279.6 %all_to_all.37 = f32[2,48,64,512]{3,2,0,1:T(8,128)} all-to-all(f32[2,48,64,512]{3,2,0,1:T(8,128)} %copy.24), channel_id=1, replica_groups=mesh['grp'=2,'blade'=8,'dof'=2] {'blade'}, dimensions={1} | all-to-all | bytes 25165824 | tf_op jit(solution)/shard_map/all_to_all | solution.py:40
  823.9 12.0 %copy.26 = f32[2,6,8,64,512]{4,3,2,1,0:T(8,128)} copy(f32[2,6,8,64,512]{4,3,0,1,2:T(8,128)} %bitcast.44) | data formatting | bytes 25165824 | tf_op jit(solution)/shard_map/all_to_all | solution.py:40
  835.9 0.0 reduce-scatter.2.cloned.1.call-update
  835.9 20.6 %reduce-scatter.2.cloned.1.call-done = f32[2,6,256,512]{3,2,1,0:T(8,128)} async-done(((f32[2,6,512,512]{3,2,1,0:T(8,128)}), f32[2,6,256,512]{3,2,1,0:T(8,128)}) %reduce-scatter.2.cloned.1.call-update) | async-done | bytes 6291472 | tf_op jit(solution)/shard_map/reduce_scatter | solution.py:41
  (13 shorter events, 0.1 us)
Async XLA Ops:
  6.5 56.3 %all-gather.2.cloned.1.call-start = ((), (), s32[]{:S(2)}) async-start(), calls=%async_computation.3 | async-start | bytes 4456448 | tf_op jit(solution)/shard_map/all_gather | solution.py:12
  7.3 849.3 %reduce-scatter.2.cloned.1.call-start = ((), (), s32[]{:S(2)}) async-start(), calls=%async_computation.4 | async-start | bytes 18874368 | tf_op jit(solution)/shard_map/reduce_scatter | solution.py:41
Sparse Core Ops, SparseCore 0:
  9.5 53.2 all-gather.1
  836.0 20.4 reduce-scatter.1
where the time goes:
time: 868 us; the launch traced here: 863 us
  blocking collectives  467 us (54%)
  local copies, waits for them, and re-layouts  229 us (26%)
  waiting for transfers between devices  76.9 us (9%)
  matrix products  63.3 us (7%)
  other arithmetic  13.8 us (2%)
  between operations  13.4 us (2%)
    all_to_all x1, blocking collectives, body(): lax.all_to_all(joined, 'blade', split_axis=1, concat_axis=2, tiled=True)  280 us
    all_to_all x1, blocking collectives, body(): lax.all_to_all(partial_proj, 'blade', split_axis=1, concat_axis=0, tiled=...  187 us
    dynamic_update_slice x12, local copies, waits for them, and re-layouts, body(): partial_proj = lax.map(one_blade, (stiffness, block_rows, block_cols))  137 us
    all_gather x1, waiting for transfers between devices, body(): whole = lax.all_gather(panel, ('blade', 'dof'), axis=0, tiled=True)  55.5 us
    dot_general x6, matrix products, one_blade(): lax.dot_general(left, image.reshape(-1, modes), (((0,), (0,)), ((), ())),...  43.5 us
    gather x6, local copies, waits for them, and re-layouts, one_blade(): chosen = jnp.take(blocks, cols, axis=0)  30.1 us
    gather x6, local copies, waits for them, and re-layouts, one_blade(): left = jnp.take(blocks, rows, axis=0).reshape(-1, modes)  29.7 us
    reduce_scatter x1, waiting for transfers between devices, body(): result = lax.psum_scatter(full_spec, 'dof', scatter_dimension=2, tiled=True)  20.6 us
  transfers between devices with their start and end apart: 2, of which 2 were waited for; matrix products, arithmetic and copies ran while one was open for 0% of the time, Pallas kernels for 0%

commit v1 on v0

v1 whole, which is shorter than its diff:
```python
import math

import jax
import jax.numpy as jnp
from jax import lax
from jax.experimental import pallas as pl
from jax.experimental.pallas import tpu as pltpu
from jax.sharding import PartitionSpec as P


def _project_kernel(rows_ref, cols_ref, pb_ref, pt_ref, s_ref, o_ref, lt_ref, img_ref):
    b = pl.program_id(0)
    nblk = s_ref.shape[1]
    bs = s_ref.shape[2]
    last = pb_ref.shape[0] - 1
    for n in range(nblk):
        c = jnp.minimum(jnp.maximum(cols_ref[b * nblk + n], 0), last)
        r = jnp.minimum(jnp.maximum(rows_ref[b * nblk + n], 0), last)
        im = jnp.dot(s_ref[0, n], pb_ref[c], preferred_element_type=jnp.float32)
        img_ref[n * bs:(n + 1) * bs, :] = im.astype(jnp.bfloat16)
        lt_ref[:, n * bs:(n + 1) * bs] = pt_ref[r]
    o_ref[0] = jnp.dot(lt_ref[...], img_ref[...], preferred_element_type=jnp.float32)


def _project(pb, pt, stiffness, rows, cols):
    nbl, nblk, bs, _ = stiffness.shape
    nrb, _, modes = pb.shape
    grid_spec = pltpu.PrefetchScalarGridSpec(
        num_scalar_prefetch=2,
        grid=(nbl,),
        in_specs=[
            pl.BlockSpec((nrb, bs, modes), lambda b, rr, cc: (0, 0, 0)),
            pl.BlockSpec((nrb, modes, bs), lambda b, rr, cc: (0, 0, 0)),
            pl.BlockSpec((1, nblk, bs, bs), lambda b, rr, cc: (b, 0, 0, 0)),
        ],
        out_specs=pl.BlockSpec((1, modes, modes), lambda b, rr, cc: (b, 0, 0)),
        scratch_shapes=[
            pltpu.VMEM((modes, nblk * bs), jnp.bfloat16),
            pltpu.VMEM((nblk * bs, modes), jnp.bfloat16),
        ],
    )
    return pl.pallas_call(
        _project_kernel,
        grid_spec=grid_spec,
        out_shape=jax.ShapeDtypeStruct((nbl, modes, modes), jnp.float32),
        compiler_params=pltpu.CompilerParams(
            dimension_semantics=("arbitrary",),
            vmem_limit_bytes=56 * 1024 * 1024,
        ),
    )(rows, cols, pb, pt, stiffness)


def _trig(h, b, count):
    angle = ((h * b) % count).astype(jnp.float32) * (2.0 * math.pi / count)
    return jnp.cos(angle), -jnp.sin(angle)


def body(panel, stiffness, block_rows, block_cols):
    nbl, nblk, bs, _ = stiffness.shape
    modes = panel.shape[-1]
    whole = lax.all_gather(panel, ("blade", "dof"), axis=0, tiled=True)
    pb = whole.reshape(-1, bs, modes)
    pt = jnp.swapaxes(pb, 1, 2)
    proj = _project(pb, pt, stiffness, block_rows.reshape(-1), block_cols.reshape(-1))

    half = lax.psum_scatter(proj, "dof", scatter_dimension=1, tiled=True)
    nbd = lax.axis_size("blade")
    me = lax.axis_index("blade")
    rows_half = half.shape[1]
    r = rows_half // nbd
    chunks = half.reshape(nbl, nbd, r, modes)

    got = []
    for s in range(nbd):
        piece = lax.dynamic_index_in_dim(chunks, (me + s) % nbd, axis=1, keepdims=False)
        if s:
            piece = lax.ppermute(piece, "blade", [(j, (j + s) % nbd) for j in range(nbd)])
        got.append(piece)
    stacked = jnp.stack(got).reshape(nbd * nbl, r * modes)

    count = nbl * nbd
    src = (me - jnp.arange(nbd, dtype=jnp.int32)) % nbd
    blade = (nbl * src[:, None] + jnp.arange(nbl, dtype=jnp.int32)[None, :]).reshape(-1)
    dst = (me + jnp.arange(nbd, dtype=jnp.int32)) % nbd
    harm = (nbl * dst[:, None] + jnp.arange(nbl, dtype=jnp.int32)[None, :]).reshape(-1)
    cosine, sine = _trig(harm[:, None], blade[None, :], count)
    weights = jnp.concatenate([cosine, sine], axis=0)
    spec = jnp.dot(weights, stacked, precision=lax.Precision.HIGHEST)
    spec = spec.reshape(2, nbd, nbl, r, modes)

    out = jnp.zeros((2, nbl, rows_half, modes), jnp.float32)
    for t in range(nbd):
        piece = spec[:, t]
        if t:
            piece = lax.ppermute(piece, "blade", [(j, (j + t) % nbd) for j in range(nbd)])
        at = ((me - t) % nbd) * r
        out = lax.dynamic_update_slice(out, piece, (0, 0, at, 0))
    return out


def solution(mesh):
    placed = (
        P(("grp", "blade", "dof"), None),
        P(("grp", "blade"), "dof", None, None),
        P(("grp", "blade"), "dof"),
        P(("grp", "blade"), "dof"),
    )
    return jax.shard_map(
        body,
        mesh=mesh,
        in_specs=placed,
        out_specs=P(None, ("grp", "blade"), "dof", None),
        check_vma=False,
    )
```

time: 868 us -> 368 us (0.42)
  the two profiles are of different devices: /device:TPU:0 before, /device:TPU:28 now
where the time goes in v1:
time: 368 us
  waiting for transfers between devices  251 us (68%)
  local copies, waits for them, and re-layouts  55.9 us (15%)
  Pallas kernels  26.1 us (7%)
  between operations  13.7 us (4%)
  starting transfers between devices  12 us (3%)
  matrix products  8.15 us (2%)
    ppermute x7, waiting for transfers between devices, body(): lax.ppermute(piece, 'blade', [(j, (j + t) % nbd) for j in range(nbd)])  125 us
    ppermute x7, waiting for transfers between devices, body(): lax.ppermute(piece, 'blade', [(j, (j + s) % nbd) for j in range(nbd)])  61.3 us
    all_gather x1, waiting for transfers between devices, body(): whole = lax.all_gather(panel, ('blade', 'dof'), axis=0, tiled=True)  48.7 us
    pallas_call x1, Pallas kernels, _project(): pl.pallas_call(_project_kernel, grid_spec=grid_spec, out_shape=jax.ShapeD...  26.1 us
    slice x1, local copies, waits for them, and re-layouts, body(): piece = spec[:, t]  25 us
    reduce_scatter x1, waiting for transfers between devices, body(): half = lax.psum_scatter(proj, 'dof', scatter_dimension=1, tiled=True)  15.4 us
    unnamed x20, local copies, waits for them, and re-layouts  11.4 us
    dot_general x1, matrix products, body(): spec = jnp.dot(weights, stacked, precision=lax.Precision.HIGHEST)  8.15 us
  transfers between devices with their start and end apart: 16, of which 12 were waited for; matrix products, arithmetic and copies ran while one was open for 5% of the time, Pallas kernels for 0%

profile of v1, /device:TPU:28, one launch (start us, length us, event | category | flops | bytes accessed | tf_op | source)
XLA Modules:
  0.0 367.6 jit_solution(8472558283852909148)
XLA Ops:
  6.5 0.7 all-gather.2.cloned.1.call-update
  7.3 0.0 reduce-scatter.2.cloned.1.call-start
  7.3 1.3 reshape.81.rows_ref
  8.6 1.4 reshape.82.cols_ref
  9.9 48.7 %all-gather.2.cloned.1.call-done = bf16[4096,512]{1,0:T(8,128)(2,1)} async-done(((bf16[256,512]{1,0:T(8,128)(2,1)}), bf16[4096,512]{1,0:T(8,128)(2,1)}) %all-gather.2.cloned.1.call-update) | async-done | bytes 4194320 | tf_op jit(solution)/shard_map/all_gather | solution.py:61
  58.6 6.5 %copy.6 = bf16[32,128,512]{1,2,0:T(8,128)(2,1)} copy(bf16[32,128,512]{2,1,0:T(8,128)(2,1)} %bitcast.69) | data formatting | bytes 8388608 | tf_op jit(solution)/shard_map/reshape | solution.py:62
  65.1 26.1 %shard_map.46 = f32[6,512,512]{2,1,0:T(8,128)} custom-call(s32[192]{0:T(256)} %reshape.81.rows_ref, s32[192]{0:T(256)} %reshape.82.cols_ref, bf16[32,128,512]{2,1,0:T(8,128)(2,1)} %bitcast.70, bf16[32,512,128]{2,1,0:T(8,128)(2,1)} %bitcast.71, bf16[6,32,128,128]{3,2,1,0:T(8,128)(2,1)} %s_ref.1), custom_call_target="tpu_custom_call" | custom-call | tf_op jit(solution)/shard_map/pallas_call | solution.py:42
  91.3 0.0 reduce-scatter.2.cloned.1.call-update
  91.4 0.1 iota_add_fusion.1
  91.5 0.1 add.206
  91.6 0.1 iota_add_fusion
  91.6 0.1 add.211
  91.7 15.4 %reduce-scatter.2.cloned.1.call-done = f32[6,256,512]{2,1,0:T(8,128)} async-done(((f32[6,512,512]{2,1,0:T(8,128)}), f32[6,256,512]{2,1,0:T(8,128)}) %reduce-scatter.2.cloned.1.call-update) | async-done | bytes 3145744 | tf_op jit(solution)/shard_map/reduce_scatter | solution.py:66
  107.1 2.0 dynamic-slice_bitcast_fusion
  109.2 0.3 collective-permute-start
  109.5 0.2 fusion.7
  109.6 1.8 collective-permute-start.1
  111.4 0.6 pad_maximum_fusion
  112.1 1.4 dot_general.9
  113.5 1.5 collective-permute-start.2
  115.0 1.4 collective-permute-start.3
  116.4 1.5 collective-permute-start.4
  117.9 1.0 bitcast_dynamic-update-slice_fusion.8
  119.0 1.6 collective-permute-done
  120.6 0.5 collective-permute-start.5
  121.1 8.0 %collective-permute-done.1 = f32[6,32,512]{2,1,0:T(8,128)S(1)} collective-permute-done((f32[6,32,512]{2,1,0:T(8,128)S(1)}, f32[6,32,512]{2,1,0:T(8,128)S(1)}, u32[]{:S(2)}, u32[]{:S(2)}) %collective-permute-start.1) | collective-permute-done | bytes 393248 | tf_op jit(solution)/shard_map/ppermute | solution.py:77
  129.2 0.0 collective-permute-start.6
  129.2 6.7 %collective-permute-done.2 = f32[6,32,512]{2,1,0:T(8,128)S(1)} collective-permute-done((f32[6,32,512]{2,1,0:T(8,128)S(1)}, f32[6,32,512]{2,1,0:T(8,128)S(1)}, u32[]{:S(2)}, u32[]{:S(2)}) %collective-permute-start.2) | collective-permute-done | bytes 393248 | tf_op jit(solution)/shard_map/ppermute | solution.py:77
  135.9 43.6 %collective-permute-done.3 = f32[6,32,512]{2,1,0:T(8,128)S(1)} collective-permute-done((f32[6,32,512]{2,1,0:T(8,128)S(1)}, f32[6,32,512]{2,1,0:T(8,128)S(1)}, u32[]{:S(2)}, u32[]{:S(2)}) %collective-permute-start.3) | collective-permute-done | bytes 393248 | tf_op jit(solution)/shard_map/ppermute | solution.py:77
  179.5 1.4 collective-permute-done.4
  181.0 0.0 collective-permute-done.5
  181.0 0.0 collective-permute-done.6
  181.1 8.2 %fusion = f32[2,8,6,32,512]{4,1,3,2,0:T(8,128)} fusion(f32[32,512,48,1,1]{1,0,2,4,3:T(8,128)S(1)} %bitcast.72, f32[2,8,6,48,1]{3,2,1,0,4:T(8,128)S(1)} %bitcast.78), kind=kOutput, calls=%fused_computation | convolution fusion | flops 905969664 | bytes 9455616 | tf_op jit(solution)/shard_map/dot_general | solution.py:88
  189.2 25.0 %fusion.13 = (f32[2,1,6,32,512]{4,1,3,2,0:T(1,128)S(1)}, f32[2,1,6,32,512]{4,1,3,2,0:T(1,128)S(1)}, f32[2,1,6,32,512]{4,1,3,2,0:T(1,128)S(1)}, f32[2,1,6,32,512]...) fusion(f32[2,8,6,32,512]{4,1,3,2,0:T(8,128)} %fusion), kind=kLoop, calls=%fused_computation.55 | loop fusion | bytes 12582912 | tf_op jit(solution)/shard_map/slice | solution.py:93
  214.3 2.1 copy.43
  216.4 2.1 copy.42
  218.5 1.0 collective-permute-start.8
  219.5 2.1 copy.41
  221.5 1.8 collective-permute-start.9
  223.4 1.0 copy.40
  224.4 1.6 collective-permute-start.10
  225.9 0.1 copy.39
  226.0 0.5 collective-permute-start.11
  226.5 0.1 copy.38
  226.6 8.8 %collective-permute-done.7 = f32[2,6,32,512]{3,2,1,0:T(8,128)} collective-permute-done((f32[2,6,32,512]{3,2,1,0:T(8,128)}, f32[2,6,32,512]{3,2,1,0:T(8,128)}, u32[]{:S(2)}, u32[]{:S(2)}) %collective-permute-start.7) | collective-permute-done | bytes 786464 | tf_op jit(solution)/shard_map/ppermute | solution.py:95
  235.4 0.0 collective-permute-start.12
  235.4 0.8 broadcast_in_dim.2
  236.2 0.1 bitcast_dynamic-update-slice_fusion
  236.3 0.1 copy.37
  236.3 15.3 %collective-permute-done.8 = f32[2,6,32,512]{3,2,1,0:T(8,128)} collective-permute-done((f32[2,6,32,512]{3,2,1,0:T(8,128)}, f32[2,6,32,512]{3,2,1,0:T(8,128)}, u32[]{:S(2)}, u32[]{:S(2)}) %collective-permute-start.8) | collective-permute-done | bytes 786464 | tf_op jit(solution)/shard_map/ppermute | solution.py:95
  251.7 1.2 constant_dynamic-update-slice_fusion.6
  252.8 1.2 constant_dynamic-update-slice_fusion.5
  254.0 14.5 %collective-permute-done.9 = f32[2,6,32,512]{3,2,1,0:T(8,128)} collective-permute-done((f32[2,6,32,512]{3,2,1,0:T(8,128)}, f32[2,6,32,512]{3,2,1,0:T(8,128)}, u32[]{:S(2)}, u32[]{:S(2)}) %collective-permute-start.9) | collective-permute-done | bytes 786464 | tf_op jit(solution)/shard_map/ppermute | solution.py:95
  268.5 1.2 constant_dynamic-update-slice_fusion.4
  269.7 84.0 %collective-permute-done.10 = f32[2,6,32,512]{3,2,1,0:T(8,128)} collective-permute-done((f32[2,6,32,512]{3,2,1,0:T(8,128)}, f32[2,6,32,512]{3,2,1,0:T(8,128)}, u32[]{:S(2)}, u32[]{:S(2)}) %collective-permute-start.10) | collective-permute-done | bytes 786464 | tf_op jit(solution)/shard_map/ppermute | solution.py:95
  353.7 1.2 constant_dynamic-update-slice_fusion.3
  354.9 2.0 collective-permute-done.11
  356.9 0.1 constant_dynamic-update-slice_fusion.2
  357.0 0.0 collective-permute-done.12
  357.0 0.1 constant_dynamic-update-slice_fusion.1
  357.1 0.0 copy-start
  357.1 0.0 collective-permute-done.13
  357.1 2.7 copy-done
  359.8 1.0 constant_dynamic-update-slice_fusion
  (15 shorter events, 0.2 us)
Async XLA Ops:
  6.5 52.1 %all-gather.2.cloned.1.call-start = ((), (), s32[]{:S(2)}) async-start(), calls=%async_computation.1 | async-start | bytes 4456448 | tf_op jit(solution)/shard_map/all_gather | solution.py:61
  7.3 99.9 %reduce-scatter.2.cloned.1.call-start = ((), (), s32[]{:S(2)}) async-start(), calls=%async_computation.2 | async-start | bytes 9437184 | tf_op jit(solution)/shard_map/reduce_scatter | solution.py:66
  109.2 11.4 %collective-permute-start = (f32[6,32,512]{2,1,0:T(8,128)S(1)}, f32[6,32,512]{2,1,0:T(8,128)S(1)}, u32[]{:S(2)}, u32[]{:S(2)}) collective-permute-start(f32[6,32,512]{2,1,0:T(8,128)S(1)} %get-tuple-element.19), channel_id=1, source_target_pairs={{0,2},{2,4},{4,6},{6,8},{8,10},{10,12},{12,14},{14,0},{1,3},{3,5},... | collective-permute-start | bytes 1179656 | tf_op jit(solution)/shard_map/ppermute | solution.py:77
  109.6 19.5 %collective-permute-start.1 = (f32[6,32,512]{2,1,0:T(8,128)S(1)}, f32[6,32,512]{2,1,0:T(8,128)S(1)}, u32[]{:S(2)}, u32[]{:S(2)}) collective-permute-start(f32[6,32,512]{2,1,0:T(8,128)S(1)} %get-tuple-element.18), channel_id=1, source_target_pairs={{0,4},{2,6},{4,8},{6,10},{8,12},{10,14},{12,0},{14,2},{1,5},{3,7},... | collective-permute-start | bytes 1179656 | tf_op jit(solution)/shard_map/ppermute | solution.py:77
  113.5 67.6 %copy-start.2 = (f32[2,8,6,48]{3,2,1,0:T(8,128)S(1)}, f32[2,8,6,48]{3,2,1,0:T(8,128)}, u32[]{:S(2)}) copy-start(f32[2,8,6,48]{3,2,1,0:T(8,128)} %dot_general.9) | copy-start | bytes 55300
  113.5 22.4 %collective-permute-start.2 = (f32[6,32,512]{2,1,0:T(8,128)S(1)}, f32[6,32,512]{2,1,0:T(8,128)S(1)}, u32[]{:S(2)}, u32[]{:S(2)}) collective-permute-start(f32[6,32,512]{2,1,0:T(8,128)S(1)} %get-tuple-element.17), channel_id=1, source_target_pairs={{0,6},{2,8},{4,10},{6,12},{8,14},{10,0},{12,2},{14,4},{1,7},{3,9},... | collective-permute-start | bytes 1179656 | tf_op jit(solution)/shard_map/ppermute | solution.py:77
  115.0 64.5 %collective-permute-start.3 = (f32[6,32,512]{2,1,0:T(8,128)S(1)}, f32[6,32,512]{2,1,0:T(8,128)S(1)}, u32[]{:S(2)}, u32[]{:S(2)}) collective-permute-start(f32[6,32,512]{2,1,0:T(8,128)S(1)} %get-tuple-element.16), channel_id=1, source_target_pairs={{0,8},{2,10},{4,12},{6,14},{8,0},{10,2},{12,4},{14,6},{1,9},{3,11}... | collective-permute-start | bytes 1179656 | tf_op jit(solution)/shard_map/ppermute | solution.py:77
  116.4 64.5 %collective-permute-start.4 = (f32[6,32,512]{2,1,0:T(8,128)S(1)}, f32[6,32,512]{2,1,0:T(8,128)S(1)}, u32[]{:S(2)}, u32[]{:S(2)}) collective-permute-start(f32[6,32,512]{2,1,0:T(8,128)S(1)} %get-tuple-element.15), channel_id=1, source_target_pairs={{0,10},{2,12},{4,14},{6,0},{8,2},{10,4},{12,6},{14,8},{1,11},{3,13... | collective-permute-start | bytes 1179656 | tf_op jit(solution)/shard_map/ppermute | solution.py:77
  120.6 60.4 %collective-permute-start.5 = (f32[6,32,512]{2,1,0:T(8,128)S(1)}, f32[6,32,512]{2,1,0:T(8,128)S(1)}, u32[]{:S(2)}, u32[]{:S(2)}) collective-permute-start(f32[6,32,512]{2,1,0:T(8,128)S(1)} %get-tuple-element.14), channel_id=1, source_target_pairs={{0,12},{2,14},{4,0},{6,2},{8,4},{10,6},{12,8},{14,10},{1,13},{3,15... | collective-permute-start | bytes 1179656 | tf_op jit(solution)/shard_map/ppermute | solution.py:77
  129.2 51.9 %collective-permute-start.6 = (f32[6,32,512]{2,1,0:T(8,128)S(1)}, f32[6,32,512]{2,1,0:T(8,128)S(1)}, u32[]{:S(2)}, u32[]{:S(2)}) collective-permute-start(f32[6,32,512]{2,1,0:T(8,128)S(1)} %get-tuple-element.13), channel_id=1, source_target_pairs={{0,14},{2,0},{4,2},{6,4},{8,6},{10,8},{12,10},{14,12},{1,15},{3,1}... | collective-permute-start | bytes 1179656 | tf_op jit(solution)/shard_map/ppermute | solution.py:77
  214.2 9.1 %copy-start.1 = (f32[2,1,6,32,512]{4,1,3,2,0:T(1,128)S(1)}, f32[2,1,6,32,512]{4,1,3,2,0:T(1,128)}, u32[]{:S(2)}) copy-start(f32[2,1,6,32,512]{4,1,3,2,0:T(1,128)} %get-tuple-element.8) | copy-start | bytes 2359300
  216.4 19.0 %collective-permute-start.7 = (f32[2,6,32,512]{3,2,1,0:T(8,128)}, f32[2,6,32,512]{3,2,1,0:T(8,128)}, u32[]{:S(2)}, u32[]{:S(2)}) collective-permute-start(f32[2,6,32,512]{3,2,1,0:T(8,128)} %bitcast.68), channel_id=1, source_target_pairs={{0,2},{2,4},{4,6},{6,8},{8,10},{10,12},{12,14},{14,0},{1,3},{3,5},... | collective-permute-start | bytes 2359304 | tf_op jit(solution)/shard_map/ppermute | solution.py:95
  218.5 33.2 %collective-permute-start.8 = (f32[2,6,32,512]{3,2,1,0:T(8,128)}, f32[2,6,32,512]{3,2,1,0:T(8,128)}, u32[]{:S(2)}, u32[]{:S(2)}) collective-permute-start(f32[2,6,32,512]{3,2,1,0:T(8,128)} %bitcast.67), channel_id=1, source_target_pairs={{0,4},{2,6},{4,8},{6,10},{8,12},{10,14},{12,0},{14,2},{1,5},{3,7},... | collective-permute-start | bytes 2359304 | tf_op jit(solution)/shard_map/ppermute | solution.py:95
  221.5 47.0 %collective-permute-start.9 = (f32[2,6,32,512]{3,2,1,0:T(8,128)}, f32[2,6,32,512]{3,2,1,0:T(8,128)}, u32[]{:S(2)}, u32[]{:S(2)}) collective-permute-start(f32[2,6,32,512]{3,2,1,0:T(8,128)} %bitcast.66), channel_id=1, source_target_pairs={{0,6},{2,8},{4,10},{6,12},{8,14},{10,0},{12,2},{14,4},{1,7},{3,9},... | collective-permute-start | bytes 2359304 | tf_op jit(solution)/shard_map/ppermute | solution.py:95
  224.4 129.4 %collective-permute-start.10 = (f32[2,6,32,512]{3,2,1,0:T(8,128)}, f32[2,6,32,512]{3,2,1,0:T(8,128)}, u32[]{:S(2)}, u32[]{:S(2)}) collective-permute-start(f32[2,6,32,512]{3,2,1,0:T(8,128)} %bitcast.65), channel_id=1, source_target_pairs={{0,8},{2,10},{4,12},{6,14},{8,0},{10,2},{12,4},{14,6},{1,9},{3,11}... | collective-permute-start | bytes 2359304 | tf_op jit(solution)/shard_map/ppermute | solution.py:95
  226.0 130.9 %collective-permute-start.11 = (f32[2,6,32,512]{3,2,1,0:T(8,128)S(1)}, f32[2,6,32,512]{3,2,1,0:T(8,128)S(1)}, u32[]{:S(2)}, u32[]{:S(2)}) collective-permute-start(f32[2,6,32,512]{3,2,1,0:T(8,128)S(1)} %bitcast.76), channel_id=1, source_target_pairs={{0,10},{2,12},{4,14},{6,0},{8,2},{10,4},{12,6},{14,8},{1,11},{3,13... | collective-permute-start | bytes 2359304 | tf_op jit(solution)/shard_map/ppermute | solution.py:95
  235.4 121.6 %collective-permute-start.12 = (f32[2,6,32,512]{3,2,1,0:T(8,128)S(1)}, f32[2,6,32,512]{3,2,1,0:T(8,128)S(1)}, u32[]{:S(2)}, u32[]{:S(2)}) collective-permute-start(f32[2,6,32,512]{3,2,1,0:T(8,128)S(1)} %bitcast.75), channel_id=1, source_target_pairs={{0,12},{2,14},{4,0},{6,2},{8,4},{10,6},{12,8},{14,10},{1,13},{3,15... | collective-permute-start | bytes 2359304 | tf_op jit(solution)/shard_map/ppermute | solution.py:95
  251.6 105.4 %collective-permute-start.13 = (f32[2,6,32,512]{3,2,1,0:T(8,128)S(1)}, f32[2,6,32,512]{3,2,1,0:T(8,128)S(1)}, u32[]{:S(2)}, u32[]{:S(2)}) collective-permute-start(f32[2,6,32,512]{3,2,1,0:T(8,128)S(1)} %bitcast.77), channel_id=1, source_target_pairs={{0,14},{2,0},{4,2},{6,4},{8,6},{10,8},{12,10},{14,12},{1,15},{3,1}... | collective-permute-start | bytes 2359304 | tf_op jit(solution)/shard_map/ppermute | solution.py:95
  357.1 2.7 copy-start
Sparse Core Ops, SparseCore 0:
  9.5 49.0 all-gather.1
  91.4 15.6 reduce-scatter.1

commit v2 on v1

--- a/solution.py
+++ b/solution.py
@@ -50,6 +50,37 @@
     )(rows, cols, pb, pt, stiffness)
 
 
+def _dft_kernel(wh_ref, wl_ref, x_ref, o_ref):
+    x = x_ref[...]
+    xh = x.astype(jnp.bfloat16)
+    xl = (x - xh.astype(jnp.float32)).astype(jnp.bfloat16)
+    wh = wh_ref[...]
+    acc = jnp.dot(wh, xh, preferred_element_type=jnp.float32)
+    acc += jnp.dot(wh, xl, preferred_element_type=jnp.float32)
+    acc += jnp.dot(wl_ref[...], xh, preferred_element_type=jnp.float32)
+    o_ref[...] = acc
+
+
+def _dft(weights, x):
+    rows, k = weights.shape
+    n = x.shape[1]
+    wh = weights.astype(jnp.bfloat16)
+    wl = (weights - wh.astype(jnp.float32)).astype(jnp.bfloat16)
+    tn = 2048 if n % 2048 == 0 else n
+    return pl.pallas_call(
+        _dft_kernel,
+        grid=(n // tn,),
+        in_specs=[
+            pl.BlockSpec((rows, k), lambda i: (0, 0)),
+            pl.BlockSpec((rows, k), lambda i: (0, 0)),
+            pl.BlockSpec((k, tn), lambda i: (0, i)),
+        ],
+        out_specs=pl.BlockSpec((rows, tn), lambda i: (0, i)),
+        out_shape=jax.ShapeDtypeStruct((rows, n), jnp.float32),
+        compiler_params=pltpu.CompilerParams(dimension_semantics=("arbitrary",)),
+    )(wh, wl, x)
+
+
 def _trig(h, b, count):
     angle = ((h * b) % count).astype(jnp.float32) * (2.0 * math.pi / count)
     return jnp.cos(angle), -jnp.sin(angle)
@@ -58,13 +89,22 @@
 def body(panel, stiffness, block_rows, block_cols):
     nbl, nblk, bs, _ = stiffness.shape
     modes = panel.shape[-1]
-    whole = lax.all_gather(panel, ("blade", "dof"), axis=0, tiled=True)
+    nbd = lax.axis_size("blade")
+    nd = lax.axis_size("dof")
+    whole = lax.all_gather(panel, "blade", axis=0, tiled=True)
+    whole = lax.all_gather(whole, "dof", axis=0, tiled=True)
     pb = whole.reshape(-1, bs, modes)
     pt = jnp.swapaxes(pb, 1, 2)
-    proj = _project(pb, pt, stiffness, block_rows.reshape(-1), block_cols.reshape(-1))
+    bpd = panel.shape[0] // bs
+
+    def remap(j):
+        j = jnp.clip(j.reshape(-1), 0, pb.shape[0] - 1)
+        k = j // bpd
+        return ((k % nd) * nbd + k // nd) * bpd + j % bpd
+
+    proj = _project(pb, pt, stiffness, remap(block_rows), remap(block_cols))
 
     half = lax.psum_scatter(proj, "dof", scatter_dimension=1, tiled=True)
-    nbd = lax.axis_size("blade")
     me = lax.axis_index("blade")
     rows_half = half.shape[1]
     r = rows_half // nbd
@@ -84,13 +124,13 @@
     dst = (me + jnp.arange(nbd, dtype=jnp.int32)) % nbd
     harm = (nbl * dst[:, None] + jnp.arange(nbl, dtype=jnp.int32)[None, :]).reshape(-1)
     cosine, sine = _trig(harm[:, None], blade[None, :], count)
-    weights = jnp.concatenate([cosine, sine], axis=0)
-    spec = jnp.dot(weights, stacked, precision=lax.Precision.HIGHEST)
-    spec = spec.reshape(2, nbd, nbl, r, modes)
+    weights = jnp.stack([cosine.reshape(nbd, nbl, -1), sine.reshape(nbd, nbl, -1)], axis=1)
+    spec = _dft(weights.reshape(2 * count, count), stacked)
+    spec = spec.reshape(nbd, 2, nbl, r, modes)
 
     out = jnp.zeros((2, nbl, rows_half, modes), jnp.float32)
     for t in range(nbd):
-        piece = spec[:, t]
+        piece = spec[t]
         if t:
             piece = lax.ppermute(piece, "blade", [(j, (j + t) % nbd) for j in range(nbd)])
         at = ((me - t) % nbd) * r

time: 368 us -> 364 us (0.989)
  the two profiles are of different devices: /device:TPU:28 before, /device:TPU:15 now
where the time goes in v2:
time: 364 us
  waiting for transfers between devices  247 us (68%)
  local copies, waits for them, and re-layouts  37.2 us (10%)
  Pallas kernels  34.4 us (9%)
  starting transfers between devices  28.1 us (8%)
  between operations  13.4 us (4%)
  other arithmetic  3.78 us (1%)
    ppermute x7, waiting for transfers between devices, body(): lax.ppermute(piece, 'blade', [(j, (j + t) % nbd) for j in range(nbd)])  111 us
    ppermute x7, waiting for transfers between devices, body(): lax.ppermute(piece, 'blade', [(j, (j + s) % nbd) for j in range(nbd)])  54.3 us
    all_gather x1, waiting for transfers between devices, body(): whole = lax.all_gather(panel, 'blade', axis=0, tiled=True)  50.8 us
    pallas_call x1, Pallas kernels, _project(): pl.pallas_call(_project_kernel, grid_spec=grid_spec, out_shape=jax.ShapeD...  26.2 us
    ppermute x7, starting transfers between devices, body(): lax.ppermute(piece, 'blade', [(j, (j + t) % nbd) for j in range(nbd)])  17 us
    unnamed x26, local copies, waits for them, and re-layouts  15.4 us
    reduce_scatter x1, waiting for transfers between devices, body(): half = lax.psum_scatter(proj, 'dof', scatter_dimension=1, tiled=True)  15.3 us
    all_gather x1, waiting for transfers between devices, body(): whole = lax.all_gather(whole, 'dof', axis=0, tiled=True)  14.1 us
  transfers between devices with their start and end apart: 17, of which 13 were waited for; matrix products, arithmetic and copies ran while one was open for 6% of the time, Pallas kernels for 0%

profile of v2, /device:TPU:15, one launch (start us, length us, event | category | flops | bytes accessed | tf_op | source)
XLA Modules:
  0.0 363.6 jit_solution(4736734720545524746)
XLA Ops:
  6.5 0.7 all-gather.3.cloned.1.call-update
  7.3 50.8 %all-gather.3.cloned.1.call-done = bf16[2048,512]{1,0:T(8,128)(2,1)} async-done(((bf16[256,512]{1,0:T(8,128)(2,1)}), bf16[2048,512]{1,0:T(8,128)(2,1)}) %all-gather.3.cloned.1.call-update) | async-done | bytes 2097168 | tf_op jit(solution)/shard_map/all_gather | solution.py:94
  58.2 0.7 broadcast_clamp_fusion
  58.9 0.1 min.20
  59.1 0.6 fusion.11.cols_ref
  59.7 0.6 fusion.8.rows_ref
  60.3 14.1 %all-gather.5.cloned.1.call-done = bf16[4096,512]{1,0:T(8,128)(2,1)} async-done(((bf16[2048,512]{1,0:T(8,128)(2,1)}), bf16[4096,512]{1,0:T(8,128)(2,1)}) %all-gather.5.cloned.1.call-update) | async-done | bytes 4194320 | tf_op jit(solution)/shard_map/all_gather | solution.py:95
  74.4 6.5 %copy.6 = bf16[32,128,512]{1,2,0:T(8,128)(2,1)} copy(bf16[32,128,512]{2,1,0:T(8,128)(2,1)} %bitcast.68) | data formatting | bytes 8388608 | tf_op jit(solution)/shard_map/reshape | solution.py:96
  80.8 26.2 %shard_map.46 = f32[6,512,512]{2,1,0:T(8,128)} custom-call(s32[192]{0:T(256)} %fusion.8.rows_ref, s32[192]{0:T(256)} %fusion.11.cols_ref, bf16[32,128,512]{2,1,0:T(8,128)(2,1)} %bitcast.69, bf16[32,512,128]{2,1,0:T(8,128)(2,1)} %bitcast.70, bf16[6,32,128,128]{3,2,1,0:T(8,128)(2,1)} %s_ref.1), custom_call_target="tpu_custom_call" | custom-call | tf_op jit(solution)/shard_map/pallas_call | solution.py:42
  107.2 0.1 add.252
  107.3 0.2 fusion.4
  107.6 15.3 %reduce-scatter.2.cloned.1.call-done = f32[6,256,512]{2,1,0:T(8,128)} async-done(((f32[6,512,512]{2,1,0:T(8,128)}), f32[6,256,512]{2,1,0:T(8,128)}) %reduce-scatter.2.cloned.1.call-update) | async-done | bytes 3145744 | tf_op jit(solution)/shard_map/reduce_scatter | solution.py:107
  122.8 2.0 dynamic-slice_bitcast_fusion
  124.9 1.2 collective-permute-start
  126.1 0.6 reshape.157
  126.7 1.2 collective-permute-start.1
  127.9 1.5 subtract_convert_fusion
  129.4 0.3 collective-permute-start.6
  129.7 0.3 collective-permute-start.5
  130.0 2.9 collective-permute-start.4
  132.9 1.0 bitcast_dynamic-update-slice_fusion.7
  133.9 1.6 collective-permute-done
  135.5 3.0 collective-permute-start.2
  138.5 5.4 %collective-permute-done.1 = f32[6,32,512]{2,1,0:T(8,128)S(1)} collective-permute-done((f32[6,32,512]{2,1,0:T(8,128)S(1)}, f32[6,32,512]{2,1,0:T(8,128)S(1)}, u32[]{:S(2)}, u32[]{:S(2)}) %collective-permute-start.1) | collective-permute-done | bytes 393248 | tf_op jit(solution)/shard_map/ppermute | solution.py:117
  143.9 2.2 collective-permute-start.3
  146.1 38.9 %collective-permute-done.2 = f32[6,32,512]{2,1,0:T(8,128)S(1)} collective-permute-done((f32[6,32,512]{2,1,0:T(8,128)S(1)}, f32[6,32,512]{2,1,0:T(8,128)S(1)}, u32[]{:S(2)}, u32[]{:S(2)}) %collective-permute-start.2) | collective-permute-done | bytes 393248 | tf_op jit(solution)/shard_map/ppermute | solution.py:117
  185.1 8.4 %collective-permute-done.3 = f32[6,32,512]{2,1,0:T(8,128)S(1)} collective-permute-done((f32[6,32,512]{2,1,0:T(8,128)S(1)}, f32[6,32,512]{2,1,0:T(8,128)S(1)}, u32[]{:S(2)}, u32[]{:S(2)}) %collective-permute-start.3) | collective-permute-done | bytes 393248 | tf_op jit(solution)/shard_map/ppermute | solution.py:117
  193.6 3.4 copy.7
  197.1 8.2 %shard_map.47 = f32[96,16384]{1,0:T(8,128)} custom-call(bf16[96,48]{1,0:T(8,128)(2,1)} %get-tuple-element.6.wh_ref, bf16[96,48]{1,0:T(8,128)(2,1)} %get-tuple-element.5.wl_ref, f32[48,16384]{1,0:T(8,128)} %bitcast.71), custom_call_target="tpu_custom_call" | custom-call | tf_op jit(solution)/shard_map/pallas_call | solution.py:70
  205.3 4.6 %fusion.16 = (f32[12,16384]{1,0:T(8,128)S(1)}, f32[12,16384]{1,0:T(8,128)S(1)}, f32[12,16384]{1,0:T(8,128)S(1)}, f32[12,16384]{1,0:T(8,128)S(1)}, f32[12,16384]{...) fusion(f32[96,16384]{1,0:T(8,128)} %shard_map.47), kind=kLoop, calls=%fused_computation.74 | loop fusion | bytes 12582912 | tf_op jit(solution)/shard_map/slice | solution.py:133
  209.9 0.6 copy.10
  210.5 1.0 slice.50
  211.5 1.6 collective-permute-start.8
  213.1 0.6 copy.9
  213.7 0.9 slice.49
  214.6 3.3 collective-permute-start.7
  217.9 0.6 copy.11
  218.5 0.9 slice.51
  219.4 2.6 collective-permute-start.9
  222.0 0.6 copy.12
  222.6 1.0 slice.52
  223.6 0.6 copy.13
  224.2 1.0 slice.53
  225.1 2.4 collective-permute-start.11
  227.5 0.6 copy.15
  228.2 0.6 copy.14
  228.9 0.6 copy.8
  229.5 3.2 collective-permute-done.8
  232.8 3.0 collective-permute-start.12
  235.8 0.8 broadcast_in_dim.2
  236.6 0.1 constant_dynamic-update-slice_fusion.7
  236.7 10.0 %collective-permute-done.7 = f32[2,6,32,512]{3,2,1,0:T(8,128)} collective-permute-done((f32[2,6,32,512]{3,2,1,0:T(8,128)}, f32[2,6,32,512]{3,2,1,0:T(8,128)}, u32[]{:S(2)}, u32[]{:S(2)}) %collective-permute-start.7) | collective-permute-done | bytes 786464 | tf_op jit(solution)/shard_map/ppermute | solution.py:135
  246.6 4.2 %collective-permute-start.13 = (f32[2,6,32,512]{3,2,1,0:T(8,128)S(1)}, f32[2,6,32,512]{3,2,1,0:T(8,128)S(1)}, u32[]{:S(2)}, u32[]{:S(2)}) collective-permute-start(f32[2,6,32,512]{3,2,1,0:T(8,128)S(1)} %bitcast.92), channel_id=1, source_target_pairs={{0,14},{2,0},{4,2},{6,4},{8,6},{10,8},{12,10},{14,12},{1,15},{3,1}... | collective-permute-start | bytes 2359304 | tf_op jit(solution)/shard_map/ppermute | solution.py:135
  250.8 1.2 constant_dynamic-update-slice_fusion.6
  252.0 1.2 constant_dynamic-update-slice_fusion.5
  253.2 77.7 %collective-permute-done.9 = f32[2,6,32,512]{3,2,1,0:T(8,128)} collective-permute-done((f32[2,6,32,512]{3,2,1,0:T(8,128)}, f32[2,6,32,512]{3,2,1,0:T(8,128)}, u32[]{:S(2)}, u32[]{:S(2)}) %collective-permute-start.9) | collective-permute-done | bytes 786464 | tf_op jit(solution)/shard_map/ppermute | solution.py:135
  330.9 1.2 constant_dynamic-update-slice_fusion.4
  332.1 15.7 %collective-permute-done.10 = f32[2,6,32,512]{3,2,1,0:T(8,128)} collective-permute-done((f32[2,6,32,512]{3,2,1,0:T(8,128)}, f32[2,6,32,512]{3,2,1,0:T(8,128)}, u32[]{:S(2)}, u32[]{:S(2)}) %collective-permute-start.10) | collective-permute-done | bytes 786464 | tf_op jit(solution)/shard_map/ppermute | solution.py:135
  347.8 1.2 constant_dynamic-update-slice_fusion.3
  349.0 1.2 constant_dynamic-update-slice_fusion.2
  350.2 3.1 collective-permute-done.12
  353.4 1.7 collective-permute-done.13
  355.1 1.0 copy-done
  356.1 1.0 constant_dynamic-update-slice_fusion
  (27 shorter events, 0.8 us)
Async XLA Ops:
  6.5 51.6 %all-gather.3.cloned.1.call-start = ((), (), s32[]{:S(2)}) async-start(), calls=%async_computation.1 | async-start | bytes 2359296 | tf_op jit(solution)/shard_map/all_gather | solution.py:94
  7.3 67.1 %all-gather.5.cloned.1.call-start = ((), (), s32[]{:S(2)}) async-start(), calls=%async_computation.2 | async-start | bytes 6291456 | tf_op jit(solution)/shard_map/all_gather | solution.py:95
  58.1 64.7 %reduce-scatter.2.cloned.1.call-start = ((), (), s32[]{:S(2)}) async-start(), calls=%async_computation.3 | async-start | bytes 9437184 | tf_op jit(solution)/shard_map/reduce_scatter | solution.py:107
  124.9 10.7 %collective-permute-start = (f32[6,32,512]{2,1,0:T(8,128)S(1)}, f32[6,32,512]{2,1,0:T(8,128)S(1)}, u32[]{:S(2)}, u32[]{:S(2)}) collective-permute-start(f32[6,32,512]{2,1,0:T(8,128)S(1)} %get-tuple-element.21), channel_id=1, source_target_pairs={{0,2},{2,4},{4,6},{6,8},{8,10},{10,12},{12,14},{14,0},{1,3},{3,5},... | collective-permute-start | bytes 1179656 | tf_op jit(solution)/shard_map/ppermute | solution.py:117
  126.7 17.2 %collective-permute-start.1 = (f32[6,32,512]{2,1,0:T(8,128)S(1)}, f32[6,32,512]{2,1,0:T(8,128)S(1)}, u32[]{:S(2)}, u32[]{:S(2)}) collective-permute-start(f32[6,32,512]{2,1,0:T(8,128)S(1)} %get-tuple-element.20), channel_id=1, source_target_pairs={{0,4},{2,6},{4,8},{6,10},{8,12},{10,14},{12,0},{14,2},{1,5},{3,7},... | collective-permute-start | bytes 1179656 | tf_op jit(solution)/shard_map/ppermute | solution.py:117
  129.4 64.2 %collective-permute-start.6 = (f32[6,32,512]{2,1,0:T(8,128)S(1)}, f32[6,32,512]{2,1,0:T(8,128)S(1)}, u32[]{:S(2)}, u32[]{:S(2)}) collective-permute-start(f32[6,32,512]{2,1,0:T(8,128)S(1)} %get-tuple-element.15), channel_id=1, source_target_pairs={{0,14},{2,0},{4,2},{6,4},{8,6},{10,8},{12,10},{14,12},{1,15},{3,1}... | collective-permute-start | bytes 1179656 | tf_op jit(solution)/shard_map/ppermute | solution.py:117
  129.7 63.8 %collective-permute-start.5 = (f32[6,32,512]{2,1,0:T(8,128)S(1)}, f32[6,32,512]{2,1,0:T(8,128)S(1)}, u32[]{:S(2)}, u32[]{:S(2)}) collective-permute-start(f32[6,32,512]{2,1,0:T(8,128)S(1)} %get-tuple-element.16), channel_id=1, source_target_pairs={{0,12},{2,14},{4,0},{6,2},{8,4},{10,6},{12,8},{14,10},{1,13},{3,15... | collective-permute-start | bytes 1179656 | tf_op jit(solution)/shard_map/ppermute | solution.py:117
  130.0 63.5 %collective-permute-start.4 = (f32[6,32,512]{2,1,0:T(8,128)S(1)}, f32[6,32,512]{2,1,0:T(8,128)S(1)}, u32[]{:S(2)}, u32[]{:S(2)}) collective-permute-start(f32[6,32,512]{2,1,0:T(8,128)S(1)} %get-tuple-element.17), channel_id=1, source_target_pairs={{0,10},{2,12},{4,14},{6,0},{8,2},{10,4},{12,6},{14,8},{1,11},{3,13... | collective-permute-start | bytes 1179656 | tf_op jit(solution)/shard_map/ppermute | solution.py:117
  135.5 49.5 %collective-permute-start.2 = (f32[6,32,512]{2,1,0:T(8,128)S(1)}, f32[6,32,512]{2,1,0:T(8,128)S(1)}, u32[]{:S(2)}, u32[]{:S(2)}) collective-permute-start(f32[6,32,512]{2,1,0:T(8,128)S(1)} %get-tuple-element.19), channel_id=1, source_target_pairs={{0,6},{2,8},{4,10},{6,12},{8,14},{10,0},{12,2},{14,4},{1,7},{3,9},... | collective-permute-start | bytes 1179656 | tf_op jit(solution)/shard_map/ppermute | solution.py:117
  143.9 49.6 %collective-permute-start.3 = (f32[6,32,512]{2,1,0:T(8,128)S(1)}, f32[6,32,512]{2,1,0:T(8,128)S(1)}, u32[]{:S(2)}, u32[]{:S(2)}) collective-permute-start(f32[6,32,512]{2,1,0:T(8,128)S(1)} %get-tuple-element.18), channel_id=1, source_target_pairs={{0,8},{2,10},{4,12},{6,14},{8,0},{10,2},{12,4},{14,6},{1,9},{3,11}... | collective-permute-start | bytes 1179656 | tf_op jit(solution)/shard_map/ppermute | solution.py:117
  211.5 21.3 %collective-permute-start.8 = (f32[2,6,32,512]{3,2,1,0:T(8,128)}, f32[2,6,32,512]{3,2,1,0:T(8,128)}, u32[]{:S(2)}, u32[]{:S(2)}) collective-permute-start(f32[2,6,32,512]{3,2,1,0:T(8,128)} %bitcast.32), channel_id=1, source_target_pairs={{0,4},{2,6},{4,8},{6,10},{8,12},{10,14},{12,0},{14,2},{1,5},{3,7},... | collective-permute-start | bytes 2359304 | tf_op jit(solution)/shard_map/ppermute | solution.py:135
  214.6 32.0 %collective-permute-start.7 = (f32[2,6,32,512]{3,2,1,0:T(8,128)}, f32[2,6,32,512]{3,2,1,0:T(8,128)}, u32[]{:S(2)}, u32[]{:S(2)}) collective-permute-start(f32[2,6,32,512]{3,2,1,0:T(8,128)} %bitcast.28), channel_id=1, source_target_pairs={{0,2},{2,4},{4,6},{6,8},{8,10},{10,12},{12,14},{14,0},{1,3},{3,5},... | collective-permute-start | bytes 2359304 | tf_op jit(solution)/shard_map/ppermute | solution.py:135
  219.4 111.5 %collective-permute-start.9 = (f32[2,6,32,512]{3,2,1,0:T(8,128)}, f32[2,6,32,512]{3,2,1,0:T(8,128)}, u32[]{:S(2)}, u32[]{:S(2)}) collective-permute-start(f32[2,6,32,512]{3,2,1,0:T(8,128)} %bitcast.36), channel_id=1, source_target_pairs={{0,6},{2,8},{4,10},{6,12},{8,14},{10,0},{12,2},{14,4},{1,7},{3,9},... | collective-permute-start | bytes 2359304 | tf_op jit(solution)/shard_map/ppermute | solution.py:135
  223.6 124.2 %collective-permute-start.10 = (f32[2,6,32,512]{3,2,1,0:T(8,128)}, f32[2,6,32,512]{3,2,1,0:T(8,128)}, u32[]{:S(2)}, u32[]{:S(2)}) collective-permute-start(f32[2,6,32,512]{3,2,1,0:T(8,128)} %bitcast.40), channel_id=1, source_target_pairs={{0,8},{2,10},{4,12},{6,14},{8,0},{10,2},{12,4},{14,6},{1,9},{3,11}... | collective-permute-start | bytes 2359304 | tf_op jit(solution)/shard_map/ppermute | solution.py:135
  225.1 123.8 %collective-permute-start.11 = (f32[2,6,32,512]{3,2,1,0:T(8,128)}, f32[2,6,32,512]{3,2,1,0:T(8,128)}, u32[]{:S(2)}, u32[]{:S(2)}) collective-permute-start(f32[2,6,32,512]{3,2,1,0:T(8,128)} %bitcast.44), channel_id=1, source_target_pairs={{0,10},{2,12},{4,14},{6,0},{8,2},{10,4},{12,6},{14,8},{1,11},{3,13... | collective-permute-start | bytes 2359304 | tf_op jit(solution)/shard_map/ppermute | solution.py:135
  232.8 120.5 %collective-permute-start.12 = (f32[2,6,32,512]{3,2,1,0:T(8,128)S(1)}, f32[2,6,32,512]{3,2,1,0:T(8,128)S(1)}, u32[]{:S(2)}, u32[]{:S(2)}) collective-permute-start(f32[2,6,32,512]{3,2,1,0:T(8,128)S(1)} %bitcast.93), channel_id=1, source_target_pairs={{0,12},{2,14},{4,0},{6,2},{8,4},{10,6},{12,8},{14,10},{1,13},{3,15... | collective-permute-start | bytes 2359304 | tf_op jit(solution)/shard_map/ppermute | solution.py:135
  246.6 108.5 %collective-permute-start.13 = (f32[2,6,32,512]{3,2,1,0:T(8,128)S(1)}, f32[2,6,32,512]{3,2,1,0:T(8,128)S(1)}, u32[]{:S(2)}, u32[]{:S(2)}) collective-permute-start(f32[2,6,32,512]{3,2,1,0:T(8,128)S(1)} %bitcast.92), channel_id=1, source_target_pairs={{0,14},{2,0},{4,2},{6,4},{8,6},{10,8},{12,10},{14,12},{1,15},{3,1}... | collective-permute-start | bytes 2359304 | tf_op jit(solution)/shard_map/ppermute | solution.py:135
  353.4 2.7 copy-start
Sparse Core Ops, SparseCore 0:
  9.5 48.5 all-gather.2
  59.7 14.6 all-gather.4
  107.1 15.6 reduce-scatter.1

commit v3 on v2

--- a/solution.py
+++ b/solution.py
@@ -50,35 +50,34 @@
     )(rows, cols, pb, pt, stiffness)
 
 
-def _dft_kernel(wh_ref, wl_ref, x_ref, o_ref):
+def _dft_kernel(w_ref, x_ref, o_ref):
     x = x_ref[...]
     xh = x.astype(jnp.bfloat16)
     xl = (x - xh.astype(jnp.float32)).astype(jnp.bfloat16)
-    wh = wh_ref[...]
+    w = w_ref[...]
+    wh = w.astype(jnp.bfloat16)
+    wl = (w - wh.astype(jnp.float32)).astype(jnp.bfloat16)
     acc = jnp.dot(wh, xh, preferred_element_type=jnp.float32)
     acc += jnp.dot(wh, xl, preferred_element_type=jnp.float32)
-    acc += jnp.dot(wl_ref[...], xh, preferred_element_type=jnp.float32)
+    acc += jnp.dot(wl, xh, preferred_element_type=jnp.float32)
     o_ref[...] = acc
 
 
 def _dft(weights, x):
     rows, k = weights.shape
     n = x.shape[1]
-    wh = weights.astype(jnp.bfloat16)
-    wl = (weights - wh.astype(jnp.float32)).astype(jnp.bfloat16)
     tn = 2048 if n % 2048 == 0 else n
     return pl.pallas_call(
         _dft_kernel,
         grid=(n // tn,),
         in_specs=[
             pl.BlockSpec((rows, k), lambda i: (0, 0)),
-            pl.BlockSpec((rows, k), lambda i: (0, 0)),
             pl.BlockSpec((k, tn), lambda i: (0, i)),
         ],
         out_specs=pl.BlockSpec((rows, tn), lambda i: (0, i)),
         out_shape=jax.ShapeDtypeStruct((rows, n), jnp.float32),
         compiler_params=pltpu.CompilerParams(dimension_semantics=("arbitrary",)),
-    )(wh, wl, x)
+    )(weights, x)
 
 
 def _trig(h, b, count):
@@ -107,12 +106,14 @@
     half = lax.psum_scatter(proj, "dof", scatter_dimension=1, tiled=True)
     me = lax.axis_index("blade")
     rows_half = half.shape[1]
-    r = rows_half // nbd
-    chunks = half.reshape(nbl, nbd, r, modes)
+    groups = 2 if nbd % 2 == 0 and rows_half % (nbd // 2) == 0 else 1
+    per = nbd // groups
+    r = rows_half // per
+    chunks = half.reshape(nbl, per, r, modes)
 
     got = []
     for s in range(nbd):
-        piece = lax.dynamic_index_in_dim(chunks, (me + s) % nbd, axis=1, keepdims=False)
+        piece = lax.dynamic_index_in_dim(chunks, ((me + s) % nbd) % per, axis=1, keepdims=False)
         if s:
             piece = lax.ppermute(piece, "blade", [(j, (j + s) % nbd) for j in range(nbd)])
         got.append(piece)
@@ -121,19 +122,21 @@
     count = nbl * nbd
     src = (me - jnp.arange(nbd, dtype=jnp.int32)) % nbd
     blade = (nbl * src[:, None] + jnp.arange(nbl, dtype=jnp.int32)[None, :]).reshape(-1)
-    dst = (me + jnp.arange(nbd, dtype=jnp.int32)) % nbd
+    base = (me // per) * per
+    dst = base + (me % per + jnp.arange(per, dtype=jnp.int32)) % per
     harm = (nbl * dst[:, None] + jnp.arange(nbl, dtype=jnp.int32)[None, :]).reshape(-1)
     cosine, sine = _trig(harm[:, None], blade[None, :], count)
-    weights = jnp.stack([cosine.reshape(nbd, nbl, -1), sine.reshape(nbd, nbl, -1)], axis=1)
-    spec = _dft(weights.reshape(2 * count, count), stacked)
-    spec = spec.reshape(nbd, 2, nbl, r, modes)
+    weights = jnp.stack([cosine.reshape(per, nbl, -1), sine.reshape(per, nbl, -1)], axis=1)
+    spec = _dft(weights.reshape(2 * per * nbl, count), stacked)
+    spec = spec.reshape(per, 2, nbl, r, modes)
 
     out = jnp.zeros((2, nbl, rows_half, modes), jnp.float32)
-    for t in range(nbd):
-        piece = spec[t]
-        if t:
-            piece = lax.ppermute(piece, "blade", [(j, (j + t) % nbd) for j in range(nbd)])
-        at = ((me - t) % nbd) * r
+    for u in range(per):
+        piece = spec[u]
+        if u:
+            pairs = [(j, (j // per) * per + (j % per + u) % per) for j in range(nbd)]
+            piece = lax.ppermute(piece, "blade", pairs)
+        at = ((me % per - u) % per) * r
         out = lax.dynamic_update_slice(out, piece, (0, 0, at, 0))
     return out
 

time: 364 us -> 378 us (1.038)
  the two profiles are of different devices: /device:TPU:15 before, /device:TPU:0 now
where the time goes in v3:
time: 378 us; the launch traced here: 377 us
  waiting for transfers between devices  175 us (46%)
  starting transfers between devices  104 us (28%)
  local copies, waits for them, and re-layouts  42.9 us (11%)
  Pallas kernels  39.1 us (10%)
  between operations  13.5 us (4%)
    ppermute x7, starting transfers between devices, body(): lax.ppermute(piece, 'blade', [(j, (j + s) % nbd) for j in range(nbd)])  92.3 us
    ppermute x3, waiting for transfers between devices, body(): piece = lax.ppermute(piece, 'blade', pairs)  58.4 us
    all_gather x1, waiting for transfers between devices, body(): whole = lax.all_gather(panel, 'blade', axis=0, tiled=True)  54.2 us
    ppermute x7, waiting for transfers between devices, body(): lax.ppermute(piece, 'blade', [(j, (j + s) % nbd) for j in range(nbd)])  34.2 us
    pallas_call x1, Pallas kernels, _project(): pl.pallas_call(_project_kernel, grid_spec=grid_spec, out_shape=jax.ShapeD...  26.2 us
    unnamed x18, local copies, waits for them, and re-layouts  20.1 us
    reduce_scatter x1, waiting for transfers between devices, body(): half = lax.psum_scatter(proj, 'dof', scatter_dimension=1, tiled=True)  15.5 us
    pallas_call x1, Pallas kernels, _dft(): pl.pallas_call(_dft_kernel, grid=(n // tn,), in_specs=[pl.BlockSpec((rows...  13 us
  transfers between devices with their start and end apart: 13, of which 9 were waited for; matrix products, arithmetic and copies ran while one was open for 5% of the time, Pallas kernels for 0%

profile of v3, /device:TPU:0, one launch (start us, length us, event | category | flops | bytes accessed | tf_op | source)
XLA Modules:
  0.0 376.8 jit_solution(10310715217148443574)
XLA Ops:
  6.5 0.7 all-gather.3.cloned.1.call-update
  7.3 0.0 all-gather.5.cloned.1.call-start
  7.3 54.2 %all-gather.3.cloned.1.call-done = bf16[2048,512]{1,0:T(8,128)(2,1)} async-done(((bf16[256,512]{1,0:T(8,128)(2,1)}), bf16[2048,512]{1,0:T(8,128)(2,1)}) %all-gather.3.cloned.1.call-update) | async-done | bytes 2097168 | tf_op jit(solution)/shard_map/all_gather | solution.py:93
  61.5 0.0 all-gather.5.cloned.1.call-update
  61.5 0.0 reduce-scatter.2.cloned.1.call-start
  61.6 0.7 broadcast_clamp_fusion
  62.3 0.1 min.20
  62.4 0.1 min.18
  62.4 0.6 fusion.11.cols_ref
  63.0 0.6 fusion.8.rows_ref
  63.7 11.6 %all-gather.5.cloned.1.call-done = bf16[4096,512]{1,0:T(8,128)(2,1)} async-done(((bf16[2048,512]{1,0:T(8,128)(2,1)}), bf16[4096,512]{1,0:T(8,128)(2,1)}) %all-gather.5.cloned.1.call-update) | async-done | bytes 4194320 | tf_op jit(solution)/shard_map/all_gather | solution.py:94
  75.2 6.4 %copy.6 = bf16[32,128,512]{1,2,0:T(8,128)(2,1)} copy(bf16[32,128,512]{2,1,0:T(8,128)(2,1)} %bitcast.53) | data formatting | bytes 8388608 | tf_op jit(solution)/shard_map/reshape | solution.py:95
  81.7 26.2 %shard_map.46 = f32[6,512,512]{2,1,0:T(8,128)} custom-call(s32[192]{0:T(256)} %fusion.8.rows_ref, s32[192]{0:T(256)} %fusion.11.cols_ref, bf16[32,128,512]{2,1,0:T(8,128)(2,1)} %bitcast.54, bf16[32,512,128]{2,1,0:T(8,128)(2,1)} %bitcast.55, bf16[6,32,128,128]{3,2,1,0:T(8,128)(2,1)} %s_ref.1), custom_call_target="tpu_custom_call" | custom-call | tf_op jit(solution)/shard_map/pallas_call | solution.py:42
  107.8 0.0 reduce-scatter.2.cloned.1.call-update
  108.1 0.1 iota_add_fusion
  108.2 15.5 %reduce-scatter.2.cloned.1.call-done = f32[6,256,512]{2,1,0:T(8,128)} async-done(((f32[6,512,512]{2,1,0:T(8,128)}), f32[6,256,512]{2,1,0:T(8,128)}) %reduce-scatter.2.cloned.1.call-update) | async-done | bytes 3145744 | tf_op jit(solution)/shard_map/reduce_scatter | solution.py:106
  123.7 4.5 %dynamic-slice_bitcast_fusion = (f32[6,64,512]{2,1,0:T(8,128)S(1)}, f32[6,64,512]{2,1,0:T(8,128)S(1)}, f32[6,64,512]{2,1,0:T(8,128)S(1)}, f32[6,64,512]{2,1,0:T(...) fusion(f32[6,4,64,512]{3,2,1,0:T(8,128)} %bitcast.56, s32[]{:T(128)S(6)} %select_n.241, ...), kind=kLoop, calls=%fused_computation.8 | loop fusion | bytes 11010076 | tf_op jit(solution)/shard_map/jit(dynamic_index_in_dim)/squeeze | solution.py:116
  128.2 1.7 collective-permute-start
  129.9 1.5 collective-permute-start.1
  131.5 0.1 iota_add_fusion.1
  131.5 0.1 add.273
  131.6 2.4 collective-permute-start.2
  134.0 0.2 fusion.4
  134.2 0.6 reshape.150.w_ref
  134.8 2.3 collective-permute-start.6
  137.2 0.5 collective-permute-start.5
  137.7 1.2 bitcast_dynamic-update-slice_fusion.7
  138.9 12.9 %collective-permute-done = f32[6,64,512]{2,1,0:T(8,128)} collective-permute-done((f32[6,64,512]{2,1,0:T(8,128)}, f32[6,64,512]{2,1,0:T(8,128)}, u32[]{:S(2)}, u32[]{:S(2)}) %collective-permute-start) | collective-permute-done | bytes 786464 | tf_op jit(solution)/shard_map/ppermute | solution.py:118
  151.8 0.7 collective-permute-start.3
  152.5 1.2 bitcast_dynamic-update-slice_fusion.6
  153.6 0.0 collective-permute-done.1
  153.7 83.1 %collective-permute-start.4 = (f32[6,64,512]{2,1,0:T(8,128)S(1)}, f32[6,64,512]{2,1,0:T(8,128)S(1)}, u32[]{:S(2)}, u32[]{:S(2)}) collective-permute-start(f32[6,64,512]{2,1,0:T(8,128)S(1)} %get-tuple-element.11), channel_id=1, source_target_pairs={{0,10},{2,12},{4,14},{6,0},{8,2},{10,4},{12,6},{14,8},{1,11},{3,13... | collective-permute-start | bytes 2359304 | tf_op jit(solution)/shard_map/ppermute | solution.py:118
  236.7 1.2 bitcast_dynamic-update-slice_fusion.5
  237.9 0.0 collective-permute-done.2
  237.9 1.2 bitcast_dynamic-update-slice_fusion.4
  239.1 13.6 %collective-permute-done.3 = f32[6,64,512]{2,1,0:T(8,128)S(1)} collective-permute-done((f32[6,64,512]{2,1,0:T(8,128)S(1)}, f32[6,64,512]{2,1,0:T(8,128)S(1)}, u32[]{:S(2)}, u32[]{:S(2)}) %collective-permute-start.3) | collective-permute-done | bytes 786464 | tf_op jit(solution)/shard_map/ppermute | solution.py:118
  252.7 0.1 bitcast_dynamic-update-slice_fusion.3
  252.8 7.8 %collective-permute-done.4 = f32[6,64,512]{2,1,0:T(8,128)S(1)} collective-permute-done((f32[6,64,512]{2,1,0:T(8,128)S(1)}, f32[6,64,512]{2,1,0:T(8,128)S(1)}, u32[]{:S(2)}, u32[]{:S(2)}) %collective-permute-start.4) | collective-permute-done | bytes 786464 | tf_op jit(solution)/shard_map/ppermute | solution.py:118
  260.5 0.1 bitcast_dynamic-update-slice_fusion.2
  260.6 0.0 collective-permute-done.5
  260.6 0.1 bitcast_dynamic-update-slice_fusion.1
  260.7 0.1 bitcast_dynamic-update-slice_fusion
  260.8 6.3 %copy.7 = f32[6,8,64,512]{3,1,2,0:T(8,128)} copy(f32[6,8,64,512]{3,2,1,0:T(8,128)S(1)} %bitcast.62) | data formatting | bytes 12582912
  267.1 13.0 %shard_map.47 = f32[48,32768]{1,0:T(8,128)} custom-call(f32[48,48]{1,0:T(8,128)} %reshape.150.w_ref, f32[48,32768]{1,0:T(8,128)} %bitcast.52), custom_call_target="tpu_custom_call" | custom-call | tf_op jit(solution)/shard_map/pallas_call | solution.py:70
  280.1 4.3 %fusion.17 = (f32[12,32768]{1,0:T(8,128)S(1)}, f32[12,32768]{1,0:T(8,128)S(1)}, f32[12,32768]{1,0:T(8,128)S(1)}, f32[12,32768]{1,0:T(8,128)S(1)}) fusion(f32[48,32768]{1,0:T(8,128)} %shard_map.47), kind=kLoop, calls=%fused_computation.70 | loop fusion | bytes 12582912 | tf_op jit(solution)/shard_map/slice | solution.py:135
  284.4 1.2 copy.9
  285.6 1.3 slice.25
  286.9 10.4 %collective-permute-start.7 = (f32[2,6,64,512]{3,2,1,0:T(8,128)}, f32[2,6,64,512]{3,2,1,0:T(8,128)}, u32[]{:S(2)}, u32[]{:S(2)}) collective-permute-start(f32[2,6,64,512]{3,2,1,0:T(8,128)} %bitcast.28), channel_id=1, source_target_pairs={{0,2},{2,4},{4,6},{6,0},{8,10},{10,12},{12,14},{14,8},{1,3},{3,5},... | collective-permute-start | bytes 4718600 | tf_op jit(solution)/shard_map/ppermute | solution.py:138
  297.3 1.2 copy.10
  298.5 1.3 slice.26
  299.7 1.2 copy.11
  301.0 1.3 slice.27
  302.3 1.6 collective-permute-start.9
  303.9 1.2 copy.8
  305.1 0.1 slice.24
  305.2 0.8 broadcast_in_dim.2
  306.0 0.1 constant_dynamic-update-slice_fusion.3
  306.2 25.2 %collective-permute-done.7 = f32[2,6,64,512]{3,2,1,0:T(8,128)} collective-permute-done((f32[2,6,64,512]{3,2,1,0:T(8,128)}, f32[2,6,64,512]{3,2,1,0:T(8,128)}, u32[]{:S(2)}, u32[]{:S(2)}) %collective-permute-start.7) | collective-permute-done | bytes 1572896 | tf_op jit(solution)/shard_map/ppermute | solution.py:138
  331.4 1.5 constant_dynamic-update-slice_fusion.2
  332.9 4.4 %collective-permute-done.8 = f32[2,6,64,512]{3,2,1,0:T(8,128)} collective-permute-done((f32[2,6,64,512]{3,2,1,0:T(8,128)}, f32[2,6,64,512]{3,2,1,0:T(8,128)}, u32[]{:S(2)}, u32[]{:S(2)}) %collective-permute-start.8) | collective-permute-done | bytes 1572896 | tf_op jit(solution)/shard_map/ppermute | solution.py:138
  337.3 1.5 constant_dynamic-update-slice_fusion.1
  338.9 0.0 copy-start
  338.9 28.7 %collective-permute-done.9 = f32[2,6,64,512]{3,2,1,0:T(8,128)} collective-permute-done((f32[2,6,64,512]{3,2,1,0:T(8,128)}, f32[2,6,64,512]{3,2,1,0:T(8,128)}, u32[]{:S(2)}, u32[]{:S(2)}) %collective-permute-start.9) | collective-permute-done | bytes 1572896 | tf_op jit(solution)/shard_map/ppermute | solution.py:138
  367.6 2.7 constant_dynamic-update-slice_fusion
  (7 shorter events, 0.0 us)
Async XLA Ops:
  6.5 55.0 %all-gather.3.cloned.1.call-start = ((), (), s32[]{:S(2)}) async-start(), calls=%async_computation.1 | async-start | bytes 2359296 | tf_op jit(solution)/shard_map/all_gather | solution.py:93
  7.3 68.0 %all-gather.5.cloned.1.call-start = ((), (), s32[]{:S(2)}) async-start(), calls=%async_computation.2 | async-start | bytes 6291456 | tf_op jit(solution)/shard_map/all_gather | solution.py:94
  61.5 62.1 %reduce-scatter.2.cloned.1.call-start = ((), (), s32[]{:S(2)}) async-start(), calls=%async_computation.3 | async-start | bytes 9437184 | tf_op jit(solution)/shard_map/reduce_scatter | solution.py:106
  128.2 23.6 %collective-permute-start = (f32[6,64,512]{2,1,0:T(8,128)}, f32[6,64,512]{2,1,0:T(8,128)}, u32[]{:S(2)}, u32[]{:S(2)}) collective-permute-start(f32[6,64,512]{2,1,0:T(8,128)} %get-tuple-element.15), channel_id=1, source_target_pairs={{0,2},{2,4},{4,6},{6,8},{8,10},{10,12},{12,14},{14,0},{1,3},{3,5},... | collective-permute-start | bytes 2359304 | tf_op jit(solution)/shard_map/ppermute | solution.py:118
  129.9 23.7 %collective-permute-start.1 = (f32[6,64,512]{2,1,0:T(8,128)}, f32[6,64,512]{2,1,0:T(8,128)}, u32[]{:S(2)}, u32[]{:S(2)}) collective-permute-start(f32[6,64,512]{2,1,0:T(8,128)} %get-tuple-element.14), channel_id=1, source_target_pairs={{0,4},{2,6},{4,8},{6,10},{8,12},{10,14},{12,0},{14,2},{1,5},{3,7},... | collective-permute-start | bytes 2359304 | tf_op jit(solution)/shard_map/ppermute | solution.py:118
  131.6 106.3 %collective-permute-start.2 = (f32[6,64,512]{2,1,0:T(8,128)}, f32[6,64,512]{2,1,0:T(8,128)}, u32[]{:S(2)}, u32[]{:S(2)}) collective-permute-start(f32[6,64,512]{2,1,0:T(8,128)} %get-tuple-element.13), channel_id=1, source_target_pairs={{0,6},{2,8},{4,10},{6,12},{8,14},{10,0},{12,2},{14,4},{1,7},{3,9},... | collective-permute-start | bytes 2359304 | tf_op jit(solution)/shard_map/ppermute | solution.py:118
  134.8 125.9 %collective-permute-start.6 = (f32[6,64,512]{2,1,0:T(8,128)S(1)}, f32[6,64,512]{2,1,0:T(8,128)S(1)}, u32[]{:S(2)}, u32[]{:S(2)}) collective-permute-start(f32[6,64,512]{2,1,0:T(8,128)S(1)} %get-tuple-element.9), channel_id=1, source_target_pairs={{0,14},{2,0},{4,2},{6,4},{8,6},{10,8},{12,10},{14,12},{1,15},{3,1}... | collective-permute-start | bytes 2359304 | tf_op jit(solution)/shard_map/ppermute | solution.py:118
  137.2 123.5 %collective-permute-start.5 = (f32[6,64,512]{2,1,0:T(8,128)S(1)}, f32[6,64,512]{2,1,0:T(8,128)S(1)}, u32[]{:S(2)}, u32[]{:S(2)}) collective-permute-start(f32[6,64,512]{2,1,0:T(8,128)S(1)} %get-tuple-element.10), channel_id=1, source_target_pairs={{0,12},{2,14},{4,0},{6,2},{8,4},{10,6},{12,8},{14,10},{1,13},{3,15... | collective-permute-start | bytes 2359304 | tf_op jit(solution)/shard_map/ppermute | solution.py:118
  151.8 100.9 %collective-permute-start.3 = (f32[6,64,512]{2,1,0:T(8,128)S(1)}, f32[6,64,512]{2,1,0:T(8,128)S(1)}, u32[]{:S(2)}, u32[]{:S(2)}) collective-permute-start(f32[6,64,512]{2,1,0:T(8,128)S(1)} %get-tuple-element.12), channel_id=1, source_target_pairs={{0,8},{2,10},{4,12},{6,14},{8,0},{10,2},{12,4},{14,6},{1,9},{3,11}... | collective-permute-start | bytes 2359304 | tf_op jit(solution)/shard_map/ppermute | solution.py:118
  153.7 106.9 %collective-permute-start.4 = (f32[6,64,512]{2,1,0:T(8,128)S(1)}, f32[6,64,512]{2,1,0:T(8,128)S(1)}, u32[]{:S(2)}, u32[]{:S(2)}) collective-permute-start(f32[6,64,512]{2,1,0:T(8,128)S(1)} %get-tuple-element.11), channel_id=1, source_target_pairs={{0,10},{2,12},{4,14},{6,0},{8,2},{10,4},{12,6},{14,8},{1,11},{3,13... | collective-permute-start | bytes 2359304 | tf_op jit(solution)/shard_map/ppermute | solution.py:118
  286.9 44.5 %collective-permute-start.7 = (f32[2,6,64,512]{3,2,1,0:T(8,128)}, f32[2,6,64,512]{3,2,1,0:T(8,128)}, u32[]{:S(2)}, u32[]{:S(2)}) collective-permute-start(f32[2,6,64,512]{3,2,1,0:T(8,128)} %bitcast.28), channel_id=1, source_target_pairs={{0,2},{2,4},{4,6},{6,0},{8,10},{10,12},{12,14},{14,8},{1,3},{3,5},... | collective-permute-start | bytes 4718600 | tf_op jit(solution)/shard_map/ppermute | solution.py:138
  299.7 37.6 %collective-permute-start.8 = (f32[2,6,64,512]{3,2,1,0:T(8,128)}, f32[2,6,64,512]{3,2,1,0:T(8,128)}, u32[]{:S(2)}, u32[]{:S(2)}) collective-permute-start(f32[2,6,64,512]{3,2,1,0:T(8,128)} %bitcast.32), channel_id=1, source_target_pairs={{0,4},{2,6},{4,0},{6,2},{8,12},{10,14},{12,8},{14,10},{1,5},{3,7},... | collective-permute-start | bytes 4718600 | tf_op jit(solution)/shard_map/ppermute | solution.py:138
  302.3 65.3 %collective-permute-start.9 = (f32[2,6,64,512]{3,2,1,0:T(8,128)}, f32[2,6,64,512]{3,2,1,0:T(8,128)}, u32[]{:S(2)}, u32[]{:S(2)}) collective-permute-start(f32[2,6,64,512]{3,2,1,0:T(8,128)} %bitcast.36), channel_id=1, source_target_pairs={{0,6},{2,0},{4,2},{6,4},{8,14},{10,8},{12,10},{14,12},{1,7},{3,1},... | collective-permute-start | bytes 4718600 | tf_op jit(solution)/shard_map/ppermute | solution.py:138
  338.9 28.7 %copy-start = (f32[2,6,256,512]{3,2,1,0:T(8,128)}, f32[2,6,256,512]{3,2,1,0:T(8,128)S(1)}, u32[]{:S(2)}) copy-start(f32[2,6,256,512]{3,2,1,0:T(8,128)S(1)} %constant_dynamic-update-slice_fusion.1) | copy-start | bytes 18874372
Sparse Core Ops, SparseCore 0:
  9.5 51.9 all-gather.2
  63.0 12.1 all-gather.4
  108.0 15.6 reduce-scatter.1

commit v4 on v2

--- a/solution.py
+++ b/solution.py
@@ -50,35 +50,34 @@
     )(rows, cols, pb, pt, stiffness)
 
 
-def _dft_kernel(wh_ref, wl_ref, x_ref, o_ref):
+def _dft_kernel(w_ref, x_ref, o_ref):
     x = x_ref[...]
     xh = x.astype(jnp.bfloat16)
     xl = (x - xh.astype(jnp.float32)).astype(jnp.bfloat16)
-    wh = wh_ref[...]
+    w = w_ref[...]
+    wh = w.astype(jnp.bfloat16)
+    wl = (w - wh.astype(jnp.float32)).astype(jnp.bfloat16)
     acc = jnp.dot(wh, xh, preferred_element_type=jnp.float32)
     acc += jnp.dot(wh, xl, preferred_element_type=jnp.float32)
-    acc += jnp.dot(wl_ref[...], xh, preferred_element_type=jnp.float32)
+    acc += jnp.dot(wl, xh, preferred_element_type=jnp.float32)
     o_ref[...] = acc
 
 
 def _dft(weights, x):
     rows, k = weights.shape
     n = x.shape[1]
-    wh = weights.astype(jnp.bfloat16)
-    wl = (weights - wh.astype(jnp.float32)).astype(jnp.bfloat16)
     tn = 2048 if n % 2048 == 0 else n
     return pl.pallas_call(
         _dft_kernel,
         grid=(n // tn,),
         in_specs=[
             pl.BlockSpec((rows, k), lambda i: (0, 0)),
-            pl.BlockSpec((rows, k), lambda i: (0, 0)),
             pl.BlockSpec((k, tn), lambda i: (0, i)),
         ],
         out_specs=pl.BlockSpec((rows, tn), lambda i: (0, i)),
         out_shape=jax.ShapeDtypeStruct((rows, n), jnp.float32),
         compiler_params=pltpu.CompilerParams(dimension_semantics=("arbitrary",)),
-    )(wh, wl, x)
+    )(weights, x)
 
 
 def _trig(h, b, count):
@@ -90,19 +89,10 @@
     nbl, nblk, bs, _ = stiffness.shape
     modes = panel.shape[-1]
     nbd = lax.axis_size("blade")
-    nd = lax.axis_size("dof")
-    whole = lax.all_gather(panel, "blade", axis=0, tiled=True)
-    whole = lax.all_gather(whole, "dof", axis=0, tiled=True)
+    whole = lax.all_gather(panel, ("blade", "dof"), axis=0, tiled=True)
     pb = whole.reshape(-1, bs, modes)
     pt = jnp.swapaxes(pb, 1, 2)
-    bpd = panel.shape[0] // bs
-
-    def remap(j):
-        j = jnp.clip(j.reshape(-1), 0, pb.shape[0] - 1)
-        k = j // bpd
-        return ((k % nd) * nbd + k // nd) * bpd + j % bpd
-
-    proj = _project(pb, pt, stiffness, remap(block_rows), remap(block_cols))
+    proj = _project(pb, pt, stiffness, block_rows.reshape(-1), block_cols.reshape(-1))
 
     half = lax.psum_scatter(proj, "dof", scatter_dimension=1, tiled=True)
     me = lax.axis_index("blade")

time: 364 us -> 350 us (0.962)
  waiting for transfers between devices: 247 us -> 231 us
  local copies, waits for them, and re-layouts: 37.2 us -> 40.9 us
    all_gather x2 -> x1, waiting for transfers between devices: 64.9 us -> 50.8 us  [body(): whole = lax.all_gather(panel, ('blade', 'dof'), axis=0, tiled=True)]
  transfers between devices with their start and end apart: 17 -> 16, of which waited for: 13 -> 12; matrix products, arithmetic and copies ran while one was open for 6% -> 6% of each run, Pallas kernels for 0% -> 0%
where the time goes in v4:
time: 350 us; the launch traced here: 349 us
  waiting for transfers between devices  231 us (66%)
  local copies, waits for them, and re-layouts  40.9 us (12%)
  Pallas kernels  34.3 us (10%)
  starting transfers between devices  27.6 us (8%)
  between operations  13.7 us (4%)
    ppermute x7, waiting for transfers between devices, body(): lax.ppermute(piece, 'blade', [(j, (j + t) % nbd) for j in range(nbd)])  111 us
    ppermute x7, waiting for transfers between devices, body(): lax.ppermute(piece, 'blade', [(j, (j + s) % nbd) for j in range(nbd)])  54.2 us
    all_gather x1, waiting for transfers between devices, body(): whole = lax.all_gather(panel, ('blade', 'dof'), axis=0, tiled=True)  50.8 us
    pallas_call x1, Pallas kernels, _project(): pl.pallas_call(_project_kernel, grid_spec=grid_spec, out_shape=jax.ShapeD...  26.2 us
    ppermute x7, starting transfers between devices, body(): lax.ppermute(piece, 'blade', [(j, (j + t) % nbd) for j in range(nbd)])  16.6 us
    unnamed x26, local copies, waits for them, and re-layouts  15.7 us
    reduce_scatter x1, waiting for transfers between devices, body(): half = lax.psum_scatter(proj, 'dof', scatter_dimension=1, tiled=True)  14 us
    ppermute x7, starting transfers between devices, body(): lax.ppermute(piece, 'blade', [(j, (j + s) % nbd) for j in range(nbd)])  11 us
  transfers between devices with their start and end apart: 16, of which 12 were waited for; matrix products, arithmetic and copies ran while one was open for 6% of the time, Pallas kernels for 0%

profile of v4, /device:TPU:15, one launch (start us, length us, event | category | flops | bytes accessed | tf_op | source)
XLA Modules:
  0.0 348.8 jit_solution(1749773823770402436)
XLA Ops:
  6.5 0.7 all-gather.2.cloned.1.call-update
  7.3 1.3 reshape.156.rows_ref
  8.6 1.3 reshape.157.cols_ref
  9.9 50.8 %all-gather.2.cloned.1.call-done = bf16[4096,512]{1,0:T(8,128)(2,1)} async-done(((bf16[256,512]{1,0:T(8,128)(2,1)}), bf16[4096,512]{1,0:T(8,128)(2,1)}) %all-gather.2.cloned.1.call-update) | async-done | bytes 4194320 | tf_op jit(solution)/shard_map/all_gather | solution.py:92
  60.7 6.5 %copy.6 = bf16[32,128,512]{1,2,0:T(8,128)(2,1)} copy(bf16[32,128,512]{2,1,0:T(8,128)(2,1)} %bitcast.68) | data formatting | bytes 8388608 | tf_op jit(solution)/shard_map/reshape | solution.py:93
  67.2 26.2 %shard_map.46 = f32[6,512,512]{2,1,0:T(8,128)} custom-call(s32[192]{0:T(256)} %reshape.156.rows_ref, s32[192]{0:T(256)} %reshape.157.cols_ref, bf16[32,128,512]{2,1,0:T(8,128)(2,1)} %bitcast.69, bf16[32,512,128]{2,1,0:T(8,128)(2,1)} %bitcast.70, bf16[6,32,128,128]{3,2,1,0:T(8,128)(2,1)} %s_ref.1), custom_call_target="tpu_custom_call" | custom-call | tf_op jit(solution)/shard_map/pallas_call | solution.py:42
  93.5 0.1 iota_add_fusion
  93.6 0.1 add.218
  93.7 0.1 iota_add_fusion.1
  93.7 14.0 %reduce-scatter.2.cloned.1.call-done = f32[6,256,512]{2,1,0:T(8,128)} async-done(((f32[6,512,512]{2,1,0:T(8,128)}), f32[6,256,512]{2,1,0:T(8,128)}) %reduce-scatter.2.cloned.1.call-update) | async-done | bytes 3145744 | tf_op jit(solution)/shard_map/reduce_scatter | solution.py:97
  107.8 2.0 dynamic-slice_bitcast_fusion
  109.8 1.2 collective-permute-start
  111.0 0.2 fusion.4
  111.3 1.3 collective-permute-start.1
  112.5 0.6 pad_maximum_fusion
  113.2 1.5 reshape.155.w_ref
  114.6 0.3 collective-permute-start.6
  114.9 0.3 collective-permute-start.5
  115.2 2.9 collective-permute-start.4
  118.1 1.0 bitcast_dynamic-update-slice_fusion.7
  119.1 1.4 collective-permute-done
  120.5 2.9 collective-permute-start.2
  123.5 5.4 %collective-permute-done.1 = f32[6,32,512]{2,1,0:T(8,128)S(1)} collective-permute-done((f32[6,32,512]{2,1,0:T(8,128)S(1)}, f32[6,32,512]{2,1,0:T(8,128)S(1)}, u32[]{:S(2)}, u32[]{:S(2)}) %collective-permute-start.1) | collective-permute-done | bytes 393248 | tf_op jit(solution)/shard_map/ppermute | solution.py:107
  128.9 2.1 collective-permute-start.3
  131.0 39.0 %collective-permute-done.2 = f32[6,32,512]{2,1,0:T(8,128)S(1)} collective-permute-done((f32[6,32,512]{2,1,0:T(8,128)S(1)}, f32[6,32,512]{2,1,0:T(8,128)S(1)}, u32[]{:S(2)}, u32[]{:S(2)}) %collective-permute-start.2) | collective-permute-done | bytes 393248 | tf_op jit(solution)/shard_map/ppermute | solution.py:107
  170.0 8.4 %collective-permute-done.3 = f32[6,32,512]{2,1,0:T(8,128)S(1)} collective-permute-done((f32[6,32,512]{2,1,0:T(8,128)S(1)}, f32[6,32,512]{2,1,0:T(8,128)S(1)}, u32[]{:S(2)}, u32[]{:S(2)}) %collective-permute-start.3) | collective-permute-done | bytes 393248 | tf_op jit(solution)/shard_map/ppermute | solution.py:107
  178.6 3.4 copy.7
  182.0 8.2 %shard_map.47 = f32[96,16384]{1,0:T(8,128)} custom-call(f32[96,48]{1,0:T(8,128)} %reshape.155.w_ref, f32[48,16384]{1,0:T(8,128)} %bitcast.71), custom_call_target="tpu_custom_call" | custom-call | tf_op jit(solution)/shard_map/pallas_call | solution.py:70
  190.2 4.6 %fusion.10 = (f32[12,16384]{1,0:T(8,128)S(1)}, f32[12,16384]{1,0:T(8,128)S(1)}, f32[12,16384]{1,0:T(8,128)S(1)}, f32[12,16384]{1,0:T(8,128)S(1)}, f32[12,16384]{...) fusion(f32[96,16384]{1,0:T(8,128)} %shard_map.47), kind=kLoop, calls=%fused_computation.45 | loop fusion | bytes 12582912 | tf_op jit(solution)/shard_map/slice | solution.py:123
  194.8 0.6 copy.10
  195.4 1.0 slice.50
  196.4 1.6 collective-permute-start.8
  198.0 0.6 copy.9
  198.6 0.9 slice.49
  199.5 2.9 collective-permute-start.7
  202.4 0.6 copy.11
  203.1 0.9 slice.51
  204.0 2.5 collective-permute-start.9
  206.5 0.6 copy.12
  207.1 1.0 slice.52
  208.1 0.6 copy.13
  208.7 0.9 slice.53
  209.7 2.4 collective-permute-start.11
  212.0 0.6 copy.15
  212.7 0.6 copy.14
  213.4 0.6 copy.8
  214.1 3.6 %collective-permute-done.8 = f32[2,6,32,512]{3,2,1,0:T(8,128)} collective-permute-done((f32[2,6,32,512]{3,2,1,0:T(8,128)}, f32[2,6,32,512]{3,2,1,0:T(8,128)}, u32[]{:S(2)}, u32[]{:S(2)}) %collective-permute-start.8) | collective-permute-done | bytes 786464 | tf_op jit(solution)/shard_map/ppermute | solution.py:125
  217.7 3.0 collective-permute-start.12
  220.7 0.8 broadcast_in_dim.2
  221.5 0.1 constant_dynamic-update-slice_fusion.7
  221.6 10.0 %collective-permute-done.7 = f32[2,6,32,512]{3,2,1,0:T(8,128)} collective-permute-done((f32[2,6,32,512]{3,2,1,0:T(8,128)}, f32[2,6,32,512]{3,2,1,0:T(8,128)}, u32[]{:S(2)}, u32[]{:S(2)}) %collective-permute-start.7) | collective-permute-done | bytes 786464 | tf_op jit(solution)/shard_map/ppermute | solution.py:125
  231.5 4.2 %collective-permute-start.13 = (f32[2,6,32,512]{3,2,1,0:T(8,128)S(1)}, f32[2,6,32,512]{3,2,1,0:T(8,128)S(1)}, u32[]{:S(2)}, u32[]{:S(2)}) collective-permute-start(f32[2,6,32,512]{3,2,1,0:T(8,128)S(1)} %bitcast.92), channel_id=1, source_target_pairs={{0,14},{2,0},{4,2},{6,4},{8,6},{10,8},{12,10},{14,12},{1,15},{3,1}... | collective-permute-start | bytes 2359304 | tf_op jit(solution)/shard_map/ppermute | solution.py:125
  235.7 1.2 constant_dynamic-update-slice_fusion.6
  236.9 1.2 constant_dynamic-update-slice_fusion.5
  238.1 77.7 %collective-permute-done.9 = f32[2,6,32,512]{3,2,1,0:T(8,128)} collective-permute-done((f32[2,6,32,512]{3,2,1,0:T(8,128)}, f32[2,6,32,512]{3,2,1,0:T(8,128)}, u32[]{:S(2)}, u32[]{:S(2)}) %collective-permute-start.9) | collective-permute-done | bytes 786464 | tf_op jit(solution)/shard_map/ppermute | solution.py:125
  315.8 1.2 constant_dynamic-update-slice_fusion.4
  317.0 15.7 %collective-permute-done.10 = f32[2,6,32,512]{3,2,1,0:T(8,128)} collective-permute-done((f32[2,6,32,512]{3,2,1,0:T(8,128)}, f32[2,6,32,512]{3,2,1,0:T(8,128)}, u32[]{:S(2)}, u32[]{:S(2)}) %collective-permute-start.10) | collective-permute-done | bytes 786464 | tf_op jit(solution)/shard_map/ppermute | solution.py:125
  332.7 1.2 constant_dynamic-update-slice_fusion.3
  333.9 1.2 constant_dynamic-update-slice_fusion.2
  335.1 3.1 collective-permute-done.12
  338.2 0.1 constant_dynamic-update-slice_fusion.1
  338.3 1.4 collective-permute-done.13
  339.7 1.3 copy-done
  341.0 1.0 constant_dynamic-update-slice_fusion
  (20 shorter events, 0.4 us)
Async XLA Ops:
  6.5 54.2 %all-gather.2.cloned.1.call-start = ((), (), s32[]{:S(2)}) async-start(), calls=%async_computation.1 | async-start | bytes 4456448 | tf_op jit(solution)/shard_map/all_gather | solution.py:92
  7.3 100.5 %reduce-scatter.2.cloned.1.call-start = ((), (), s32[]{:S(2)}) async-start(), calls=%async_computation.2 | async-start | bytes 9437184 | tf_op jit(solution)/shard_map/reduce_scatter | solution.py:97
  109.8 10.7 %collective-permute-start = (f32[6,32,512]{2,1,0:T(8,128)S(1)}, f32[6,32,512]{2,1,0:T(8,128)S(1)}, u32[]{:S(2)}, u32[]{:S(2)}) collective-permute-start(f32[6,32,512]{2,1,0:T(8,128)S(1)} %get-tuple-element.19), channel_id=1, source_target_pairs={{0,2},{2,4},{4,6},{6,8},{8,10},{10,12},{12,14},{14,0},{1,3},{3,5},... | collective-permute-start | bytes 1179656 | tf_op jit(solution)/shard_map/ppermute | solution.py:107
  111.3 17.6 %collective-permute-start.1 = (f32[6,32,512]{2,1,0:T(8,128)S(1)}, f32[6,32,512]{2,1,0:T(8,128)S(1)}, u32[]{:S(2)}, u32[]{:S(2)}) collective-permute-start(f32[6,32,512]{2,1,0:T(8,128)S(1)} %get-tuple-element.18), channel_id=1, source_target_pairs={{0,4},{2,6},{4,8},{6,10},{8,12},{10,14},{12,0},{14,2},{1,5},{3,7},... | collective-permute-start | bytes 1179656 | tf_op jit(solution)/shard_map/ppermute | solution.py:107
  114.6 63.9 %collective-permute-start.6 = (f32[6,32,512]{2,1,0:T(8,128)S(1)}, f32[6,32,512]{2,1,0:T(8,128)S(1)}, u32[]{:S(2)}, u32[]{:S(2)}) collective-permute-start(f32[6,32,512]{2,1,0:T(8,128)S(1)} %get-tuple-element.13), channel_id=1, source_target_pairs={{0,14},{2,0},{4,2},{6,4},{8,6},{10,8},{12,10},{14,12},{1,15},{3,1}... | collective-permute-start | bytes 1179656 | tf_op jit(solution)/shard_map/ppermute | solution.py:107
  114.9 63.6 %collective-permute-start.5 = (f32[6,32,512]{2,1,0:T(8,128)S(1)}, f32[6,32,512]{2,1,0:T(8,128)S(1)}, u32[]{:S(2)}, u32[]{:S(2)}) collective-permute-start(f32[6,32,512]{2,1,0:T(8,128)S(1)} %get-tuple-element.14), channel_id=1, source_target_pairs={{0,12},{2,14},{4,0},{6,2},{8,4},{10,6},{12,8},{14,10},{1,13},{3,15... | collective-permute-start | bytes 1179656 | tf_op jit(solution)/shard_map/ppermute | solution.py:107
  115.2 63.3 %collective-permute-start.4 = (f32[6,32,512]{2,1,0:T(8,128)S(1)}, f32[6,32,512]{2,1,0:T(8,128)S(1)}, u32[]{:S(2)}, u32[]{:S(2)}) collective-permute-start(f32[6,32,512]{2,1,0:T(8,128)S(1)} %get-tuple-element.15), channel_id=1, source_target_pairs={{0,10},{2,12},{4,14},{6,0},{8,2},{10,4},{12,6},{14,8},{1,11},{3,13... | collective-permute-start | bytes 1179656 | tf_op jit(solution)/shard_map/ppermute | solution.py:107
  120.5 49.5 %collective-permute-start.2 = (f32[6,32,512]{2,1,0:T(8,128)S(1)}, f32[6,32,512]{2,1,0:T(8,128)S(1)}, u32[]{:S(2)}, u32[]{:S(2)}) collective-permute-start(f32[6,32,512]{2,1,0:T(8,128)S(1)} %get-tuple-element.17), channel_id=1, source_target_pairs={{0,6},{2,8},{4,10},{6,12},{8,14},{10,0},{12,2},{14,4},{1,7},{3,9},... | collective-permute-start | bytes 1179656 | tf_op jit(solution)/shard_map/ppermute | solution.py:107
  128.9 49.6 %collective-permute-start.3 = (f32[6,32,512]{2,1,0:T(8,128)S(1)}, f32[6,32,512]{2,1,0:T(8,128)S(1)}, u32[]{:S(2)}, u32[]{:S(2)}) collective-permute-start(f32[6,32,512]{2,1,0:T(8,128)S(1)} %get-tuple-element.16), channel_id=1, source_target_pairs={{0,8},{2,10},{4,12},{6,14},{8,0},{10,2},{12,4},{14,6},{1,9},{3,11}... | collective-permute-start | bytes 1179656 | tf_op jit(solution)/shard_map/ppermute | solution.py:107
  196.4 21.3 %collective-permute-start.8 = (f32[2,6,32,512]{3,2,1,0:T(8,128)}, f32[2,6,32,512]{3,2,1,0:T(8,128)}, u32[]{:S(2)}, u32[]{:S(2)}) collective-permute-start(f32[2,6,32,512]{3,2,1,0:T(8,128)} %bitcast.32), channel_id=1, source_target_pairs={{0,4},{2,6},{4,8},{6,10},{8,12},{10,14},{12,0},{14,2},{1,5},{3,7},... | collective-permute-start | bytes 2359304 | tf_op jit(solution)/shard_map/ppermute | solution.py:125
  199.5 32.0 %collective-permute-start.7 = (f32[2,6,32,512]{3,2,1,0:T(8,128)}, f32[2,6,32,512]{3,2,1,0:T(8,128)}, u32[]{:S(2)}, u32[]{:S(2)}) collective-permute-start(f32[2,6,32,512]{3,2,1,0:T(8,128)} %bitcast.28), channel_id=1, source_target_pairs={{0,2},{2,4},{4,6},{6,8},{8,10},{10,12},{12,14},{14,0},{1,3},{3,5},... | collective-permute-start | bytes 2359304 | tf_op jit(solution)/shard_map/ppermute | solution.py:125
  204.0 111.8 %collective-permute-start.9 = (f32[2,6,32,512]{3,2,1,0:T(8,128)}, f32[2,6,32,512]{3,2,1,0:T(8,128)}, u32[]{:S(2)}, u32[]{:S(2)}) collective-permute-start(f32[2,6,32,512]{3,2,1,0:T(8,128)} %bitcast.36), channel_id=1, source_target_pairs={{0,6},{2,8},{4,10},{6,12},{8,14},{10,0},{12,2},{14,4},{1,7},{3,9},... | collective-permute-start | bytes 2359304 | tf_op jit(solution)/shard_map/ppermute | solution.py:125
  208.1 124.6 %collective-permute-start.10 = (f32[2,6,32,512]{3,2,1,0:T(8,128)}, f32[2,6,32,512]{3,2,1,0:T(8,128)}, u32[]{:S(2)}, u32[]{:S(2)}) collective-permute-start(f32[2,6,32,512]{3,2,1,0:T(8,128)} %bitcast.40), channel_id=1, source_target_pairs={{0,8},{2,10},{4,12},{6,14},{8,0},{10,2},{12,4},{14,6},{1,9},{3,11}... | collective-permute-start | bytes 2359304 | tf_op jit(solution)/shard_map/ppermute | solution.py:125
  209.7 124.2 %collective-permute-start.11 = (f32[2,6,32,512]{3,2,1,0:T(8,128)}, f32[2,6,32,512]{3,2,1,0:T(8,128)}, u32[]{:S(2)}, u32[]{:S(2)}) collective-permute-start(f32[2,6,32,512]{3,2,1,0:T(8,128)} %bitcast.44), channel_id=1, source_target_pairs={{0,10},{2,12},{4,14},{6,0},{8,2},{10,4},{12,6},{14,8},{1,11},{3,13... | collective-permute-start | bytes 2359304 | tf_op jit(solution)/shard_map/ppermute | solution.py:125
  217.7 120.5 %collective-permute-start.12 = (f32[2,6,32,512]{3,2,1,0:T(8,128)S(1)}, f32[2,6,32,512]{3,2,1,0:T(8,128)S(1)}, u32[]{:S(2)}, u32[]{:S(2)}) collective-permute-start(f32[2,6,32,512]{3,2,1,0:T(8,128)S(1)} %bitcast.93), channel_id=1, source_target_pairs={{0,12},{2,14},{4,0},{6,2},{8,4},{10,6},{12,8},{14,10},{1,13},{3,15... | collective-permute-start | bytes 2359304 | tf_op jit(solution)/shard_map/ppermute | solution.py:125
  231.5 108.1 %collective-permute-start.13 = (f32[2,6,32,512]{3,2,1,0:T(8,128)S(1)}, f32[2,6,32,512]{3,2,1,0:T(8,128)S(1)}, u32[]{:S(2)}, u32[]{:S(2)}) collective-permute-start(f32[2,6,32,512]{3,2,1,0:T(8,128)S(1)} %bitcast.92), channel_id=1, source_target_pairs={{0,14},{2,0},{4,2},{6,4},{8,6},{10,8},{12,10},{14,12},{1,15},{3,1}... | collective-permute-start | bytes 2359304 | tf_op jit(solution)/shard_map/ppermute | solution.py:125
  338.3 2.7 copy-start
Sparse Core Ops, SparseCore 0:
  9.5 51.1 all-gather.1
  93.5 14.2 reduce-scatter.1

commit v5 on v4

--- a/solution.py
+++ b/solution.py
@@ -22,16 +22,18 @@
     o_ref[0] = jnp.dot(lt_ref[...], img_ref[...], preferred_element_type=jnp.float32)
 
 
-def _project(pb, pt, stiffness, rows, cols):
-    nbl, nblk, bs, _ = stiffness.shape
+def _project(pb, pt, stiffness, rows, cols, start, nbl):
+    _, nblk, bs, _ = stiffness.shape
     nrb, _, modes = pb.shape
+    rows = rows[start * nblk:(start + nbl) * nblk]
+    cols = cols[start * nblk:(start + nbl) * nblk]
     grid_spec = pltpu.PrefetchScalarGridSpec(
         num_scalar_prefetch=2,
         grid=(nbl,),
         in_specs=[
             pl.BlockSpec((nrb, bs, modes), lambda b, rr, cc: (0, 0, 0)),
             pl.BlockSpec((nrb, modes, bs), lambda b, rr, cc: (0, 0, 0)),
-            pl.BlockSpec((1, nblk, bs, bs), lambda b, rr, cc: (b, 0, 0, 0)),
+            pl.BlockSpec((1, nblk, bs, bs), lambda b, rr, cc: (b + start, 0, 0, 0)),
         ],
         out_specs=pl.BlockSpec((1, modes, modes), lambda b, rr, cc: (b, 0, 0)),
         scratch_shapes=[
@@ -92,20 +94,25 @@
     whole = lax.all_gather(panel, ("blade", "dof"), axis=0, tiled=True)
     pb = whole.reshape(-1, bs, modes)
     pt = jnp.swapaxes(pb, 1, 2)
-    proj = _project(pb, pt, stiffness, block_rows.reshape(-1), block_cols.reshape(-1))
+    rows_all = block_rows.reshape(-1)
+    cols_all = block_cols.reshape(-1)
+    me = lax.axis_index("blade")
+    rows_half = modes // lax.axis_size("dof")
+    r = rows_half // nbd
 
-    half = lax.psum_scatter(proj, "dof", scatter_dimension=1, tiled=True)
-    me = lax.axis_index("blade")
-    rows_half = half.shape[1]
-    r = rows_half // nbd
-    chunks = half.reshape(nbl, nbd, r, modes)
-
-    got = []
-    for s in range(nbd):
-        piece = lax.dynamic_index_in_dim(chunks, (me + s) % nbd, axis=1, keepdims=False)
-        if s:
-            piece = lax.ppermute(piece, "blade", [(j, (j + s) % nbd) for j in range(nbd)])
-        got.append(piece)
+    groups = 2 if nbl % 2 == 0 else 1
+    size = nbl // groups
+    parts = [[] for _ in range(nbd)]
+    for g in range(groups):
+        proj = _project(pb, pt, stiffness, rows_all, cols_all, g * size, size)
+        half = lax.psum_scatter(proj, "dof", scatter_dimension=1, tiled=True)
+        chunks = half.reshape(size, nbd, r, modes)
+        for s in range(nbd):
+            piece = lax.dynamic_index_in_dim(chunks, (me + s) % nbd, axis=1, keepdims=False)
+            if s:
+                piece = lax.ppermute(piece, "blade", [(j, (j + s) % nbd) for j in range(nbd)])
+            parts[s].append(piece)
+    got = [jnp.concatenate(p, axis=0) if len(p) > 1 else p[0] for p in parts]
     stacked = jnp.stack(got).reshape(nbd * nbl, r * modes)
 
     count = nbl * nbd

time: 350 us -> 356 us (1.017)
  the two profiles are of different devices: /device:TPU:15 before, /device:TPU:28 now
where the time goes in v5:
time: 356 us; the launch traced here: 355 us
  waiting for transfers between devices  221 us (62%)
  local copies, waits for them, and re-layouts  42.8 us (12%)
  Pallas kernels  39.7 us (11%)
  starting transfers between devices  36.7 us (10%)
  between operations  13.5 us (4%)
    ppermute x7, waiting for transfers between devices, body(): lax.ppermute(piece, 'blade', [(j, (j + t) % nbd) for j in range(nbd)])  118 us
    all_gather x1, waiting for transfers between devices, body(): whole = lax.all_gather(panel, ('blade', 'dof'), axis=0, tiled=True)  48.6 us
    ppermute x14, waiting for transfers between devices, body(): lax.ppermute(piece, 'blade', [(j, (j + s) % nbd) for j in range(nbd)])  43.1 us
    pallas_call x2, Pallas kernels, _project(): pl.pallas_call(_project_kernel, grid_spec=grid_spec, out_shape=jax.ShapeD...  31.5 us
    ppermute x14, starting transfers between devices, body(): lax.ppermute(piece, 'blade', [(j, (j + s) % nbd) for j in range(nbd)])  30.5 us
    unnamed x19, local copies, waits for them, and re-layouts  16 us
    reduce_scatter x2, waiting for transfers between devices, body(): half = lax.psum_scatter(proj, 'dof', scatter_dimension=1, tiled=True)  10.5 us
    pallas_call x1, Pallas kernels, _dft(): pl.pallas_call(_dft_kernel, grid=(n // tn,), in_specs=[pl.BlockSpec((rows...  8.2 us
  transfers between devices with their start and end apart: 24, of which 15 were waited for; matrix products, arithmetic and copies ran while one was open for 6% of the time, Pallas kernels for 4%

profile of v5, /device:TPU:28, one launch (start us, length us, event | category | flops | bytes accessed | tf_op | source)
XLA Modules:
  0.0 354.8 jit_solution(2396103219033648847)
XLA Ops:
  6.5 0.7 all-gather.2.cloned.1.call-update
  7.3 0.8 fusion.20
  8.1 0.6 slice.57.rows_ref
  8.7 0.8 fusion.19
  9.4 0.6 slice.59.cols_ref
  10.0 48.6 %all-gather.2.cloned.1.call-done = bf16[4096,512]{1,0:T(8,128)(2,1)} async-done(((bf16[256,512]{1,0:T(8,128)(2,1)}), bf16[4096,512]{1,0:T(8,128)(2,1)}) %all-gather.2.cloned.1.call-update) | async-done | bytes 4194320 | tf_op jit(solution)/shard_map/all_gather | solution.py:94
  58.6 6.4 %copy.7 = bf16[32,128,512]{1,2,0:T(8,128)(2,1)} copy(bf16[32,128,512]{2,1,0:T(8,128)(2,1)} %bitcast.103) | data formatting | bytes 8388608 | tf_op jit(solution)/shard_map/reshape | solution.py:95
  65.0 15.8 %shard_map.46 = f32[3,512,512]{2,1,0:T(8,128)} custom-call(s32[96]{0:T(128)} %slice.57.rows_ref, s32[96]{0:T(128)} %slice.59.cols_ref, bf16[32,128,512]{2,1,0:T(8,128)(2,1)} %bitcast.104, bf16[32,512,128]{2,1,0:T(8,128)(2,1)} %bitcast.106, bf16[6,32,128,128]{3,2,1,0:T(8,128)(2,1)} %s_ref.3), custom_call_target="tpu_custom_call" | custom-call | tf_op jit(solution)/shard_map/pallas_call | solution.py:44
  80.8 0.7 slice.61.rows_ref
  81.5 0.7 slice.63.cols_ref
  82.2 15.8 %shard_map.47 = f32[3,512,512]{2,1,0:T(8,128)} custom-call(s32[96]{0:T(128)} %slice.61.rows_ref, s32[96]{0:T(128)} %slice.63.cols_ref, bf16[32,128,512]{2,1,0:T(8,128)(2,1)} %bitcast.105, bf16[32,512,128]{2,1,0:T(8,128)(2,1)} %bitcast.107, bf16[6,32,128,128]{3,2,1,0:T(8,128)(2,1)} %s_ref.3), custom_call_target="tpu_custom_call" | custom-call | tf_op jit(solution)/shard_map/pallas_call | solution.py:44
  98.6 1.6 dynamic-slice_bitcast_fusion.1
  100.2 10.5 %reduce-scatter.5.cloned.1.call-done = f32[3,256,512]{2,1,0:T(8,128)} async-done(((f32[3,512,512]{2,1,0:T(8,128)}), f32[3,256,512]{2,1,0:T(8,128)}) %reduce-scatter.5.cloned.1.call-update) | async-done | bytes 1572880 | tf_op jit(solution)/shard_map/reduce_scatter | solution.py:108
  110.8 1.6 dynamic-slice_bitcast_fusion
  112.4 0.3 collective-permute-start.1
  112.7 1.7 collective-permute-start
  114.4 0.6 reshape.157.w_ref
  115.0 0.3 collective-permute-start.13
  115.3 1.7 collective-permute-start.3
  117.1 1.5 collective-permute-start.2
  118.6 1.6 collective-permute-done.1
  120.2 3.5 collective-permute-start.5
  123.7 4.3 %collective-permute-done = f32[3,32,512]{2,1,0:T(8,128)} collective-permute-done((f32[3,32,512]{2,1,0:T(8,128)S(1)}, f32[3,32,512]{2,1,0:T(8,128)}, u32[]{:S(2)}, u32[]{:S(2)}) %collective-permute-start) | collective-permute-done | bytes 196640 | tf_op jit(solution)/shard_map/ppermute | solution.py:113
  128.1 1.0 fusion.1
  129.0 1.9 collective-permute-start.7
  130.9 1.5 collective-permute-done.2
  132.5 14.5 %collective-permute-start.6 = (f32[3,32,512]{2,1,0:T(8,128)S(1)}, f32[3,32,512]{2,1,0:T(8,128)S(1)}, u32[]{:S(2)}, u32[]{:S(2)}) collective-permute-start(f32[3,32,512]{2,1,0:T(8,128)S(1)} %get-tuple-element.16), channel_id=1, source_target_pairs={{0,8},{2,10},{4,12},{6,14},{8,0},{10,2},{12,4},{14,6},{1,9},{3,11}... | collective-permute-start | bytes 589832 | tf_op jit(solution)/shard_map/ppermute | solution.py:113
  147.1 5.0 %collective-permute-start.8 = (f32[3,32,512]{2,1,0:T(8,128)S(1)}, f32[3,32,512]{2,1,0:T(8,128)S(1)}, u32[]{:S(2)}, u32[]{:S(2)}) collective-permute-start(f32[3,32,512]{2,1,0:T(8,128)S(1)} %get-tuple-element.15), channel_id=1, source_target_pairs={{0,10},{2,12},{4,14},{6,0},{8,2},{10,4},{12,6},{14,8},{1,11},{3,13... | collective-permute-start | bytes 589832 | tf_op jit(solution)/shard_map/ppermute | solution.py:113
  152.1 14.4 %collective-permute-done.7 = f32[3,32,512]{2,1,0:T(8,128)S(1)} collective-permute-done((f32[3,32,512]{2,1,0:T(8,128)S(1)}, f32[3,32,512]{2,1,0:T(8,128)S(1)}, u32[]{:S(2)}, u32[]{:S(2)}) %collective-permute-start.7) | collective-permute-done | bytes 196640 | tf_op jit(solution)/shard_map/ppermute | solution.py:113
  166.5 12.0 %collective-permute-done.6 = f32[3,32,512]{2,1,0:T(8,128)S(1)} collective-permute-done((f32[3,32,512]{2,1,0:T(8,128)S(1)}, f32[3,32,512]{2,1,0:T(8,128)S(1)}, u32[]{:S(2)}, u32[]{:S(2)}) %collective-permute-start.6) | collective-permute-done | bytes 196640 | tf_op jit(solution)/shard_map/ppermute | solution.py:113
  178.6 0.6 collective-permute-done.9
  179.2 3.5 collective-permute-done.8
  182.8 3.9 %collective-permute-done.10 = f32[3,32,512]{2,1,0:T(8,128)S(1)} collective-permute-done((f32[3,32,512]{2,1,0:T(8,128)S(1)}, f32[3,32,512]{2,1,0:T(8,128)S(1)}, u32[]{:S(2)}, u32[]{:S(2)}) %collective-permute-start.10) | collective-permute-done | bytes 196640 | tf_op jit(solution)/shard_map/ppermute | solution.py:113
  186.7 1.1 collective-permute-done.12
  187.9 3.4 copy.8
  191.3 8.2 %shard_map.48 = f32[96,16384]{1,0:T(8,128)} custom-call(f32[96,48]{1,0:T(8,128)} %reshape.157.w_ref, f32[48,16384]{1,0:T(8,128)} %bitcast.108), custom_call_target="tpu_custom_call" | custom-call | tf_op jit(solution)/shard_map/pallas_call | solution.py:72
  199.5 4.6 %fusion.18 = (f32[12,16384]{1,0:T(8,128)S(1)}, f32[12,16384]{1,0:T(8,128)S(1)}, f32[12,16384]{1,0:T(8,128)S(1)}, f32[12,16384]{1,0:T(8,128)S(1)}, f32[12,16384]{...) fusion(f32[96,16384]{1,0:T(8,128)} %shard_map.48), kind=kLoop, calls=%fused_computation.62 | loop fusion | bytes 12582912 | tf_op jit(solution)/shard_map/slice | solution.py:130
  204.1 0.6 copy.11
  204.7 1.0 slice.82
  205.7 1.7 collective-permute-start.15
  207.4 0.6 copy.10
  208.0 0.9 slice.81
  209.0 0.6 copy.12
  209.6 1.0 slice.83
  210.7 0.6 copy.13
  211.3 0.9 slice.84
  212.3 4.2 %collective-permute-start.17 = (f32[2,6,32,512]{3,2,1,0:T(8,128)}, f32[2,6,32,512]{3,2,1,0:T(8,128)}, u32[]{:S(2)}, u32[]{:S(2)}) collective-permute-start(f32[2,6,32,512]{3,2,1,0:T(8,128)} %bitcast.50), channel_id=1, source_target_pairs={{0,8},{2,10},{4,12},{6,14},{8,0},{10,2},{12,4},{14,6},{1,9},{3,11}... | collective-permute-start | bytes 2359304 | tf_op jit(solution)/shard_map/ppermute | solution.py:132
  216.5 0.6 copy.14
  217.1 1.0 slice.85
  218.1 0.6 copy.16
  218.7 0.6 copy.15
  219.4 0.6 copy.9
  220.1 6.4 %collective-permute-done.15 = f32[2,6,32,512]{3,2,1,0:T(8,128)} collective-permute-done((f32[2,6,32,512]{3,2,1,0:T(8,128)}, f32[2,6,32,512]{3,2,1,0:T(8,128)}, u32[]{:S(2)}, u32[]{:S(2)}) %collective-permute-start.15) | collective-permute-done | bytes 786464 | tf_op jit(solution)/shard_map/ppermute | solution.py:132
  226.5 0.8 broadcast_in_dim.2
  227.4 16.2 %collective-permute-done.14 = f32[2,6,32,512]{3,2,1,0:T(8,128)} collective-permute-done((f32[2,6,32,512]{3,2,1,0:T(8,128)}, f32[2,6,32,512]{3,2,1,0:T(8,128)}, u32[]{:S(2)}, u32[]{:S(2)}) %collective-permute-start.14) | collective-permute-done | bytes 786464 | tf_op jit(solution)/shard_map/ppermute | solution.py:132
  243.6 1.2 constant_dynamic-update-slice_fusion.6
  244.8 1.2 constant_dynamic-update-slice_fusion.5
  246.0 13.6 %collective-permute-done.16 = f32[2,6,32,512]{3,2,1,0:T(8,128)} collective-permute-done((f32[2,6,32,512]{3,2,1,0:T(8,128)}, f32[2,6,32,512]{3,2,1,0:T(8,128)}, u32[]{:S(2)}, u32[]{:S(2)}) %collective-permute-start.16) | collective-permute-done | bytes 786464 | tf_op jit(solution)/shard_map/ppermute | solution.py:132
  259.6 1.2 constant_dynamic-update-slice_fusion.4
  260.8 81.3 %collective-permute-done.17 = f32[2,6,32,512]{3,2,1,0:T(8,128)} collective-permute-done((f32[2,6,32,512]{3,2,1,0:T(8,128)}, f32[2,6,32,512]{3,2,1,0:T(8,128)}, u32[]{:S(2)}, u32[]{:S(2)}) %collective-permute-start.17) | collective-permute-done | bytes 786464 | tf_op jit(solution)/shard_map/ppermute | solution.py:132
  342.1 1.2 constant_dynamic-update-slice_fusion.3
  343.3 1.2 constant_dynamic-update-slice_fusion.2
  344.6 2.7 copy-done
  347.3 0.9 constant_dynamic-update-slice_fusion
  (43 shorter events, 1.4 us)
Async XLA Ops:
  6.5 52.1 %all-gather.2.cloned.1.call-start = ((), (), s32[]{:S(2)}) async-start(), calls=%async_computation.2 | async-start | bytes 4456448 | tf_op jit(solution)/shard_map/all_gather | solution.py:94
  7.3 91.3 %reduce-scatter.3.cloned.1.call-start = ((), (), s32[]{:S(2)}) async-start(), calls=%async_computation.3 | async-start | bytes 4718592 | tf_op jit(solution)/shard_map/reduce_scatter | solution.py:108
  80.8 30.0 %reduce-scatter.5.cloned.1.call-start = ((), (), s32[]{:S(2)}) async-start(), calls=%async_computation.4 | async-start | bytes 4718592 | tf_op jit(solution)/shard_map/reduce_scatter | solution.py:108
  112.4 7.8 %collective-permute-start.1 = (f32[3,32,512]{2,1,0:T(8,128)S(1)}, f32[3,32,512]{2,1,0:T(8,128)S(1)}, u32[]{:S(2)}, u32[]{:S(2)}) collective-permute-start(f32[3,32,512]{2,1,0:T(8,128)S(1)} %get-tuple-element.27), channel_id=1, source_target_pairs={{0,2},{2,4},{4,6},{6,8},{8,10},{10,12},{12,14},{14,0},{1,3},{3,5},... | collective-permute-start | bytes 589832 | tf_op jit(solution)/shard_map/ppermute | solution.py:113
  112.7 15.4 %collective-permute-start = (f32[3,32,512]{2,1,0:T(8,128)S(1)}, f32[3,32,512]{2,1,0:T(8,128)}, u32[]{:S(2)}, u32[]{:S(2)}) collective-permute-start(f32[3,32,512]{2,1,0:T(8,128)S(1)} %get-tuple-element.19), channel_id=1, source_target_pairs={{0,2},{2,4},{4,6},{6,8},{8,10},{10,12},{12,14},{14,0},{1,3},{3,5},... | collective-permute-start | bytes 589832 | tf_op jit(solution)/shard_map/ppermute | solution.py:113
  115.0 71.6 %collective-permute-start.13 = (f32[3,32,512]{2,1,0:T(8,128)S(1)}, f32[3,32,512]{2,1,0:T(8,128)S(1)}, u32[]{:S(2)}, u32[]{:S(2)}) collective-permute-start(f32[3,32,512]{2,1,0:T(8,128)S(1)} %get-tuple-element.21), channel_id=1, source_target_pairs={{0,14},{2,0},{4,2},{6,4},{8,6},{10,8},{12,10},{14,12},{1,15},{3,1}... | collective-permute-start | bytes 589832 | tf_op jit(solution)/shard_map/ppermute | solution.py:113
  115.3 13.7 %collective-permute-start.3 = (f32[3,32,512]{2,1,0:T(8,128)S(1)}, f32[3,32,512]{2,1,0:T(8,128)S(1)}, u32[]{:S(2)}, u32[]{:S(2)}) collective-permute-start(f32[3,32,512]{2,1,0:T(8,128)S(1)} %get-tuple-element.26), channel_id=1, source_target_pairs={{0,4},{2,6},{4,8},{6,10},{8,12},{10,14},{12,0},{14,2},{1,5},{3,7},... | collective-permute-start | bytes 589832 | tf_op jit(solution)/shard_map/ppermute | solution.py:113
  117.1 15.4 %collective-permute-start.2 = (f32[3,32,512]{2,1,0:T(8,128)S(1)}, f32[3,32,512]{2,1,0:T(8,128)S(1)}, u32[]{:S(2)}, u32[]{:S(2)}) collective-permute-start(f32[3,32,512]{2,1,0:T(8,128)S(1)} %get-tuple-element.18), channel_id=1, source_target_pairs={{0,4},{2,6},{4,8},{6,10},{8,12},{10,14},{12,0},{14,2},{1,5},{3,7},... | collective-permute-start | bytes 589832 | tf_op jit(solution)/shard_map/ppermute | solution.py:113
  120.2 26.8 %collective-permute-start.5 = (f32[3,32,512]{2,1,0:T(8,128)S(1)}, f32[3,32,512]{2,1,0:T(8,128)S(1)}, u32[]{:S(2)}, u32[]{:S(2)}) collective-permute-start(f32[3,32,512]{2,1,0:T(8,128)S(1)} %get-tuple-element.25), channel_id=1, source_target_pairs={{0,6},{2,8},{4,10},{6,12},{8,14},{10,0},{12,2},{14,4},{1,7},{3,9},... | collective-permute-start | bytes 589832 | tf_op jit(solution)/shard_map/ppermute | solution.py:113
  128.1 19.0 %collective-permute-start.4 = (f32[3,32,512]{2,1,0:T(8,128)S(1)}, f32[3,32,512]{2,1,0:T(8,128)S(1)}, u32[]{:S(2)}, u32[]{:S(2)}) collective-permute-start(f32[3,32,512]{2,1,0:T(8,128)S(1)} %get-tuple-element.17), channel_id=1, source_target_pairs={{0,6},{2,8},{4,10},{6,12},{8,14},{10,0},{12,2},{14,4},{1,7},{3,9},... | collective-permute-start | bytes 589832 | tf_op jit(solution)/shard_map/ppermute | solution.py:113
  129.0 37.5 %collective-permute-start.7 = (f32[3,32,512]{2,1,0:T(8,128)S(1)}, f32[3,32,512]{2,1,0:T(8,128)S(1)}, u32[]{:S(2)}, u32[]{:S(2)}) collective-permute-start(f32[3,32,512]{2,1,0:T(8,128)S(1)} %get-tuple-element.24), channel_id=1, source_target_pairs={{0,8},{2,10},{4,12},{6,14},{8,0},{10,2},{12,4},{14,6},{1,9},{3,11}... | collective-permute-start | bytes 589832 | tf_op jit(solution)/shard_map/ppermute | solution.py:113
  132.5 46.1 %collective-permute-start.6 = (f32[3,32,512]{2,1,0:T(8,128)S(1)}, f32[3,32,512]{2,1,0:T(8,128)S(1)}, u32[]{:S(2)}, u32[]{:S(2)}) collective-permute-start(f32[3,32,512]{2,1,0:T(8,128)S(1)} %get-tuple-element.16), channel_id=1, source_target_pairs={{0,8},{2,10},{4,12},{6,14},{8,0},{10,2},{12,4},{14,6},{1,9},{3,11}... | collective-permute-start | bytes 589832 | tf_op jit(solution)/shard_map/ppermute | solution.py:113
  147.0 32.2 %collective-permute-start.9 = (f32[3,32,512]{2,1,0:T(8,128)S(1)}, f32[3,32,512]{2,1,0:T(8,128)S(1)}, u32[]{:S(2)}, u32[]{:S(2)}) collective-permute-start(f32[3,32,512]{2,1,0:T(8,128)S(1)} %get-tuple-element.23), channel_id=1, source_target_pairs={{0,10},{2,12},{4,14},{6,0},{8,2},{10,4},{12,6},{14,8},{1,11},{3,13... | collective-permute-start | bytes 589832 | tf_op jit(solution)/shard_map/ppermute | solution.py:113
  147.1 35.6 %collective-permute-start.8 = (f32[3,32,512]{2,1,0:T(8,128)S(1)}, f32[3,32,512]{2,1,0:T(8,128)S(1)}, u32[]{:S(2)}, u32[]{:S(2)}) collective-permute-start(f32[3,32,512]{2,1,0:T(8,128)S(1)} %get-tuple-element.15), channel_id=1, source_target_pairs={{0,10},{2,12},{4,14},{6,0},{8,2},{10,4},{12,6},{14,8},{1,11},{3,13... | collective-permute-start | bytes 589832 | tf_op jit(solution)/shard_map/ppermute | solution.py:113
  166.5 16.2 %collective-permute-start.11 = (f32[3,32,512]{2,1,0:T(8,128)S(1)}, f32[3,32,512]{2,1,0:T(8,128)S(1)}, u32[]{:S(2)}, u32[]{:S(2)}) collective-permute-start(f32[3,32,512]{2,1,0:T(8,128)S(1)} %get-tuple-element.22), channel_id=1, source_target_pairs={{0,12},{2,14},{4,0},{6,2},{8,4},{10,6},{12,8},{14,10},{1,13},{3,15... | collective-permute-start | bytes 589832 | tf_op jit(solution)/shard_map/ppermute | solution.py:113
  178.5 8.1 %collective-permute-start.10 = (f32[3,32,512]{2,1,0:T(8,128)S(1)}, f32[3,32,512]{2,1,0:T(8,128)S(1)}, u32[]{:S(2)}, u32[]{:S(2)}) collective-permute-start(f32[3,32,512]{2,1,0:T(8,128)S(1)} %get-tuple-element.14), channel_id=1, source_target_pairs={{0,12},{2,14},{4,0},{6,2},{8,4},{10,6},{12,8},{14,10},{1,13},{3,15... | collective-permute-start | bytes 589832 | tf_op jit(solution)/shard_map/ppermute | solution.py:113
  179.2 8.6 %collective-permute-start.12 = (f32[3,32,512]{2,1,0:T(8,128)S(1)}, f32[3,32,512]{2,1,0:T(8,128)S(1)}, u32[]{:S(2)}, u32[]{:S(2)}) collective-permute-start(f32[3,32,512]{2,1,0:T(8,128)S(1)} %get-tuple-element.13), channel_id=1, source_target_pairs={{0,14},{2,0},{4,2},{6,4},{8,6},{10,8},{12,10},{14,12},{1,15},{3,1}... | collective-permute-start | bytes 589832 | tf_op jit(solution)/shard_map/ppermute | solution.py:113
  205.7 20.8 %collective-permute-start.15 = (f32[2,6,32,512]{3,2,1,0:T(8,128)}, f32[2,6,32,512]{3,2,1,0:T(8,128)}, u32[]{:S(2)}, u32[]{:S(2)}) collective-permute-start(f32[2,6,32,512]{3,2,1,0:T(8,128)} %bitcast.42), channel_id=1, source_target_pairs={{0,4},{2,6},{4,8},{6,10},{8,12},{10,14},{12,0},{14,2},{1,5},{3,7},... | collective-permute-start | bytes 2359304 | tf_op jit(solution)/shard_map/ppermute | solution.py:132
  209.0 34.6 %collective-permute-start.14 = (f32[2,6,32,512]{3,2,1,0:T(8,128)}, f32[2,6,32,512]{3,2,1,0:T(8,128)}, u32[]{:S(2)}, u32[]{:S(2)}) collective-permute-start(f32[2,6,32,512]{3,2,1,0:T(8,128)} %bitcast.38), channel_id=1, source_target_pairs={{0,2},{2,4},{4,6},{6,8},{8,10},{10,12},{12,14},{14,0},{1,3},{3,5},... | collective-permute-start | bytes 2359304 | tf_op jit(solution)/shard_map/ppermute | solution.py:132
  210.6 49.0 %collective-permute-start.16 = (f32[2,6,32,512]{3,2,1,0:T(8,128)}, f32[2,6,32,512]{3,2,1,0:T(8,128)}, u32[]{:S(2)}, u32[]{:S(2)}) collective-permute-start(f32[2,6,32,512]{3,2,1,0:T(8,128)} %bitcast.46), channel_id=1, source_target_pairs={{0,6},{2,8},{4,10},{6,12},{8,14},{10,0},{12,2},{14,4},{1,7},{3,9},... | collective-permute-start | bytes 2359304 | tf_op jit(solution)/shard_map/ppermute | solution.py:132
  212.3 129.8 %collective-permute-start.17 = (f32[2,6,32,512]{3,2,1,0:T(8,128)}, f32[2,6,32,512]{3,2,1,0:T(8,128)}, u32[]{:S(2)}, u32[]{:S(2)}) collective-permute-start(f32[2,6,32,512]{3,2,1,0:T(8,128)} %bitcast.50), channel_id=1, source_target_pairs={{0,8},{2,10},{4,12},{6,14},{8,0},{10,2},{12,4},{14,6},{1,9},{3,11}... | collective-permute-start | bytes 2359304 | tf_op jit(solution)/shard_map/ppermute | solution.py:132
  218.1 125.2 %collective-permute-start.18 = (f32[2,6,32,512]{3,2,1,0:T(8,128)}, f32[2,6,32,512]{3,2,1,0:T(8,128)}, u32[]{:S(2)}, u32[]{:S(2)}) collective-permute-start(f32[2,6,32,512]{3,2,1,0:T(8,128)} %bitcast.54), channel_id=1, source_target_pairs={{0,10},{2,12},{4,14},{6,0},{8,2},{10,4},{12,6},{14,8},{1,11},{3,13... | collective-permute-start | bytes 2359304 | tf_op jit(solution)/shard_map/ppermute | solution.py:132
  226.5 118.0 %collective-permute-start.19 = (f32[2,6,32,512]{3,2,1,0:T(8,128)S(1)}, f32[2,6,32,512]{3,2,1,0:T(8,128)S(1)}, u32[]{:S(2)}, u32[]{:S(2)}) collective-permute-start(f32[2,6,32,512]{3,2,1,0:T(8,128)S(1)} %bitcast.130), channel_id=1, source_target_pairs={{0,12},{2,14},{4,0},{6,2},{8,4},{10,6},{12,8},{14,10},{1,13},{3,15... | collective-permute-start | bytes 2359304 | tf_op jit(solution)/shard_map/ppermute | solution.py:132
  243.6 101.0 %collective-permute-start.20 = (f32[2,6,32,512]{3,2,1,0:T(8,128)S(1)}, f32[2,6,32,512]{3,2,1,0:T(8,128)S(1)}, u32[]{:S(2)}, u32[]{:S(2)}) collective-permute-start(f32[2,6,32,512]{3,2,1,0:T(8,128)S(1)} %bitcast.129), channel_id=1, source_target_pairs={{0,14},{2,0},{4,2},{6,4},{8,6},{10,8},{12,10},{14,12},{1,15},{3,1}... | collective-permute-start | bytes 2359304 | tf_op jit(solution)/shard_map/ppermute | solution.py:132
  344.6 2.7 copy-start
Sparse Core Ops, SparseCore 0:
  9.5 49.0 all-gather.1
  80.9 12.0 reduce-scatter.2
  98.1 12.6 reduce-scatter.4

commit v6 on v4

--- a/solution.py
+++ b/solution.py
@@ -85,14 +85,51 @@
     return jnp.cos(angle), -jnp.sin(angle)
 
 
+def _ring_gather(x, nbd):
+    me = lax.axis_index("blade")
+    if nbd % 2 == 0:
+        cycle = [2 * z for z in range(nbd // 2)] + [2 * z + 1 for z in reversed(range(nbd // 2))]
+    else:
+        cycle = list(range(nbd))
+    place = [0] * nbd
+    for q, j in enumerate(cycle):
+        place[j] = q
+    at = jnp.array(place, jnp.int32)[me]
+    order = jnp.array(cycle, jnp.int32)
+    fwd = [(cycle[q], cycle[(q + 1) % nbd]) for q in range(nbd)]
+    bwd = [(cycle[q], cycle[(q - 1) % nbd]) for q in range(nbd)]
+    buf = jnp.zeros((nbd,) + x.shape, x.dtype)
+    buf = lax.dynamic_update_slice(buf, x[None], (me, 0, 0))
+    ahead = nbd // 2
+    behind = nbd - 1 - ahead
+    a = x
+    b = x
+    for k in range(1, ahead + 1):
+        a = lax.ppermute(a, "blade", fwd)
+        buf = lax.dynamic_update_slice(buf, a[None], (order[(at - k) % nbd], 0, 0))
+        if k <= behind:
+            b = lax.ppermute(b, "blade", bwd)
+            buf = lax.dynamic_update_slice(buf, b[None], (order[(at + k) % nbd], 0, 0))
+    return buf
+
+
 def body(panel, stiffness, block_rows, block_cols):
     nbl, nblk, bs, _ = stiffness.shape
     modes = panel.shape[-1]
     nbd = lax.axis_size("blade")
-    whole = lax.all_gather(panel, ("blade", "dof"), axis=0, tiled=True)
+    nd = lax.axis_size("dof")
+    whole = _ring_gather(panel, nbd)
+    whole = lax.all_gather(whole, "dof", axis=0, tiled=True)
     pb = whole.reshape(-1, bs, modes)
     pt = jnp.swapaxes(pb, 1, 2)
-    proj = _project(pb, pt, stiffness, block_rows.reshape(-1), block_cols.reshape(-1))
+    bpd = panel.shape[0] // bs
+
+    def remap(j):
+        j = jnp.clip(j.reshape(-1), 0, pb.shape[0] - 1)
+        k = j // bpd
+        return ((k % nd) * nbd + k // nd) * bpd + j % bpd
+
+    proj = _project(pb, pt, stiffness, remap(block_rows), remap(block_cols))
 
     half = lax.psum_scatter(proj, "dof", scatter_dimension=1, tiled=True)
     me = lax.axis_index("blade")

time: 350 us -> 359 us (1.026)
  waiting for transfers between devices: 231 us -> 213 us
  between operations: 13.7 us -> 31.6 us
  starting transfers between devices: 27.6 us -> 32.5 us
    all_gather x1, waiting for transfers between devices: 50.8 us -> 16.9 us  [body(): whole = lax.all_gather(whole, 'dof', axis=0, tiled=True)]
    ppermute x0 -> x7, waiting for transfers between devices: none -> 15.5 us  [the longest x4 10.5 us: _ring_gather(): a = lax.ppermute(a, 'blade', fwd)]
    ppermute x0 -> x7, starting transfers between devices: none -> 4.62 us  [the longest x3 3.94 us: _ring_gather(): b = lax.ppermute(b, 'blade', bwd)]
    unnamed x26 -> x32, local copies, waits for them, and re-layouts: 15.7 us -> 17.1 us
  transfers between devices with their start and end apart: 16 -> 23, of which waited for: 12 -> 15; matrix products, arithmetic and copies ran while one was open for 6% -> 7% of each run, Pallas kernels for 0% -> 0%
where the time goes in v6:
time: 359 us; the launch traced here: 358 us
  waiting for transfers between devices  213 us (59%)
  local copies, waits for them, and re-layouts  43.9 us (12%)
  Pallas kernels  34.4 us (10%)
  starting transfers between devices  32.5 us (9%)
  between operations  31.6 us (9%)
    ppermute x7, waiting for transfers between devices, body(): lax.ppermute(piece, 'blade', [(j, (j + t) % nbd) for j in range(nbd)])  111 us
    ppermute x7, waiting for transfers between devices, body(): lax.ppermute(piece, 'blade', [(j, (j + s) % nbd) for j in range(nbd)])  54 us
    pallas_call x1, Pallas kernels, _project(): pl.pallas_call(_project_kernel, grid_spec=grid_spec, out_shape=jax.ShapeD...  26.2 us
    unnamed x32, local copies, waits for them, and re-layouts  17.1 us
    all_gather x1, waiting for transfers between devices, body(): whole = lax.all_gather(whole, 'dof', axis=0, tiled=True)  16.9 us
    ppermute x7, starting transfers between devices, body(): lax.ppermute(piece, 'blade', [(j, (j + t) % nbd) for j in range(nbd)])  16.6 us
    reduce_scatter x1, waiting for transfers between devices, body(): half = lax.psum_scatter(proj, 'dof', scatter_dimension=1, tiled=True)  15.5 us
    ppermute x7, starting transfers between devices, body(): lax.ppermute(piece, 'blade', [(j, (j + s) % nbd) for j in range(nbd)])  11.2 us
  transfers between devices with their start and end apart: 23, of which 15 were waited for; matrix products, arithmetic and copies ran while one was open for 7% of the time, Pallas kernels for 0%

profile of v6, /device:TPU:15, one launch (start us, length us, event | category | flops | bytes accessed | tf_op | source)
XLA Modules:
  0.0 357.9 jit_solution(3356127301305012721)
XLA Ops:
  6.5 1.3 collective-permute-start.1
  8.0 1.2 dynamic_slice.49
  13.9 1.6 fusion.17
  28.8 1.0 bitcast_dynamic-update-slice_fusion.15
  29.8 1.3 collective-permute-start.3
  31.3 5.0 %collective-permute-done.3 = bf16[256,512]{1,0:T(8,128)(2,1)S(1)} collective-permute-done((bf16[256,512]{1,0:T(8,128)(2,1)S(1)}, bf16[256,512]{1,0:T(8,128)(2,1)S(1)}, u32[]{:S(2)}, u32[]{:S(2)}) %collective-permute-start.3) | collective-permute-done | bytes 262176 | tf_op jit(solution)/shard_map/ppermute | solution.py:111
  36.4 1.3 collective-permute-start.5
  37.9 5.3 %collective-permute-done.4 = bf16[256,512]{1,0:T(8,128)(2,1)S(1)} collective-permute-done((bf16[256,512]{1,0:T(8,128)(2,1)S(1)}, bf16[256,512]{1,0:T(8,128)(2,1)S(1)}, u32[]{:S(2)}, u32[]{:S(2)}) %collective-permute-start.4) | collective-permute-done | bytes 262176 | tf_op jit(solution)/shard_map/ppermute | solution.py:108
  43.4 5.2 %collective-permute-done.6 = bf16[256,512]{1,0:T(8,128)(2,1)S(1)} collective-permute-done((bf16[256,512]{1,0:T(8,128)(2,1)S(1)}, bf16[256,512]{1,0:T(8,128)(2,1)S(1)}, u32[]{:S(2)}, u32[]{:S(2)}) %collective-permute-start.6) | collective-permute-done | bytes 262176 | tf_op jit(solution)/shard_map/ppermute | solution.py:108
  48.6 1.3 copy-done
  50.8 0.6 fusion.8.rows_ref
  51.4 16.9 %all-gather.2.cloned.1.call-done = bf16[16,256,512]{2,1,0:T(8,128)(2,1)} async-done(((bf16[8,256,512]{2,1,0:T(8,128)(2,1)}), bf16[16,256,512]{2,1,0:T(8,128)(2,1)}) %all-gather.2.cloned.1.call-update) | async-done | bytes 4194320 | tf_op jit(solution)/shard_map/all_gather | solution.py:122
  68.3 6.5 %copy.9 = bf16[32,128,512]{1,2,0:T(8,128)(2,1)} copy(bf16[32,128,512]{2,1,0:T(8,128)(2,1)} %bitcast.98) | data formatting | bytes 8388608 | tf_op jit(solution)/shard_map/reshape | solution.py:123
  74.8 26.2 %shard_map.64 = f32[6,512,512]{2,1,0:T(8,128)} custom-call(s32[192]{0:T(256)} %fusion.8.rows_ref, s32[192]{0:T(256)} %fusion.11.cols_ref, bf16[32,128,512]{2,1,0:T(8,128)(2,1)} %bitcast.99, bf16[32,512,128]{2,1,0:T(8,128)(2,1)} %bitcast.100, bf16[6,32,128,128]{3,2,1,0:T(8,128)(2,1)} %s_ref.1), custom_call_target="tpu_custom_call" | custom-call | tf_op jit(solution)/shard_map/pallas_call | solution.py:42
  101.3 15.5 %reduce-scatter.2.cloned.1.call-done = f32[6,256,512]{2,1,0:T(8,128)} async-done(((f32[6,512,512]{2,1,0:T(8,128)}), f32[6,256,512]{2,1,0:T(8,128)}) %reduce-scatter.2.cloned.1.call-update) | async-done | bytes 3145744 | tf_op jit(solution)/shard_map/reduce_scatter | solution.py:134
  116.8 2.0 dynamic-slice_bitcast_fusion
  118.8 1.3 collective-permute-start.7
  120.3 1.3 collective-permute-start.8
  121.6 0.6 pad_maximum_fusion
  122.2 1.5 reshape.171.w_ref
  124.2 3.0 collective-permute-start.11
  127.2 1.0 bitcast_dynamic-update-slice_fusion.7
  128.2 1.3 collective-permute-done.7
  129.5 3.0 collective-permute-start.9
  132.5 5.4 %collective-permute-done.8 = f32[6,32,512]{2,1,0:T(8,128)S(1)} collective-permute-done((f32[6,32,512]{2,1,0:T(8,128)S(1)}, f32[6,32,512]{2,1,0:T(8,128)S(1)}, u32[]{:S(2)}, u32[]{:S(2)}) %collective-permute-start.8) | collective-permute-done | bytes 393248 | tf_op jit(solution)/shard_map/ppermute | solution.py:144
  137.9 2.2 collective-permute-start.10
  140.1 38.9 %collective-permute-done.9 = f32[6,32,512]{2,1,0:T(8,128)S(1)} collective-permute-done((f32[6,32,512]{2,1,0:T(8,128)S(1)}, f32[6,32,512]{2,1,0:T(8,128)S(1)}, u32[]{:S(2)}, u32[]{:S(2)}) %collective-permute-start.9) | collective-permute-done | bytes 393248 | tf_op jit(solution)/shard_map/ppermute | solution.py:144
  179.1 8.4 %collective-permute-done.10 = f32[6,32,512]{2,1,0:T(8,128)S(1)} collective-permute-done((f32[6,32,512]{2,1,0:T(8,128)S(1)}, f32[6,32,512]{2,1,0:T(8,128)S(1)}, u32[]{:S(2)}, u32[]{:S(2)}) %collective-permute-start.10) | collective-permute-done | bytes 393248 | tf_op jit(solution)/shard_map/ppermute | solution.py:144
  187.6 3.4 copy.10
  191.1 8.2 %shard_map.65 = f32[96,16384]{1,0:T(8,128)} custom-call(f32[96,48]{1,0:T(8,128)} %reshape.171.w_ref, f32[48,16384]{1,0:T(8,128)} %bitcast.101), custom_call_target="tpu_custom_call" | custom-call | tf_op jit(solution)/shard_map/pallas_call | solution.py:70
  199.3 4.6 %fusion.16 = (f32[12,16384]{1,0:T(8,128)S(1)}, f32[12,16384]{1,0:T(8,128)S(1)}, f32[12,16384]{1,0:T(8,128)S(1)}, f32[12,16384]{1,0:T(8,128)S(1)}, f32[12,16384]{...) fusion(f32[96,16384]{1,0:T(8,128)} %shard_map.65), kind=kLoop, calls=%fused_computation.81 | loop fusion | bytes 12582912 | tf_op jit(solution)/shard_map/slice | solution.py:160
  203.9 0.6 copy.13
  204.5 1.0 slice.50
  205.4 1.6 collective-permute-start.15
  207.0 0.6 copy.12
  207.7 0.9 slice.49
  208.6 2.9 collective-permute-start.14
  211.5 0.6 copy.14
  212.1 1.0 slice.51
  213.1 2.6 collective-permute-start.16
  215.6 0.6 copy.15
  216.2 0.9 slice.52
  217.2 0.6 copy.16
  217.8 1.0 slice.53
  218.8 2.4 collective-permute-start.18
  221.1 0.6 copy.18
  221.8 0.6 copy.17
  222.5 0.6 copy.11
  223.2 3.6 %collective-permute-done.15 = f32[2,6,32,512]{3,2,1,0:T(8,128)} collective-permute-done((f32[2,6,32,512]{3,2,1,0:T(8,128)}, f32[2,6,32,512]{3,2,1,0:T(8,128)}, u32[]{:S(2)}, u32[]{:S(2)}) %collective-permute-start.15) | collective-permute-done | bytes 786464 | tf_op jit(solution)/shard_map/ppermute | solution.py:162
  226.7 3.0 collective-permute-start.19
  229.8 0.8 broadcast_in_dim.34
  230.7 10.0 %collective-permute-done.14 = f32[2,6,32,512]{3,2,1,0:T(8,128)} collective-permute-done((f32[2,6,32,512]{3,2,1,0:T(8,128)}, f32[2,6,32,512]{3,2,1,0:T(8,128)}, u32[]{:S(2)}, u32[]{:S(2)}) %collective-permute-start.14) | collective-permute-done | bytes 786464 | tf_op jit(solution)/shard_map/ppermute | solution.py:162
  240.6 4.1 %collective-permute-start.20 = (f32[2,6,32,512]{3,2,1,0:T(8,128)S(1)}, f32[2,6,32,512]{3,2,1,0:T(8,128)S(1)}, u32[]{:S(2)}, u32[]{:S(2)}) collective-permute-start(f32[2,6,32,512]{3,2,1,0:T(8,128)S(1)} %bitcast.122), channel_id=1, source_target_pairs={{0,14},{2,0},{4,2},{6,4},{8,6},{10,8},{12,10},{14,12},{1,15},{3,1}... | collective-permute-start | bytes 2359304 | tf_op jit(solution)/shard_map/ppermute | solution.py:162
  244.8 1.2 constant_dynamic-update-slice_fusion.6
  246.0 1.2 constant_dynamic-update-slice_fusion.5
  247.2 77.7 %collective-permute-done.16 = f32[2,6,32,512]{3,2,1,0:T(8,128)} collective-permute-done((f32[2,6,32,512]{3,2,1,0:T(8,128)}, f32[2,6,32,512]{3,2,1,0:T(8,128)}, u32[]{:S(2)}, u32[]{:S(2)}) %collective-permute-start.16) | collective-permute-done | bytes 786464 | tf_op jit(solution)/shard_map/ppermute | solution.py:162
  324.9 1.2 constant_dynamic-update-slice_fusion.4
  326.1 15.7 %collective-permute-done.17 = f32[2,6,32,512]{3,2,1,0:T(8,128)} collective-permute-done((f32[2,6,32,512]{3,2,1,0:T(8,128)}, f32[2,6,32,512]{3,2,1,0:T(8,128)}, u32[]{:S(2)}, u32[]{:S(2)}) %collective-permute-start.17) | collective-permute-done | bytes 786464 | tf_op jit(solution)/shard_map/ppermute | solution.py:162
  341.8 1.2 constant_dynamic-update-slice_fusion.3
  343.0 1.2 constant_dynamic-update-slice_fusion.2
  344.1 3.1 collective-permute-done.19
  347.4 1.4 collective-permute-done.20
  348.7 1.3 copy-done.1
  350.1 1.0 constant_dynamic-update-slice_fusion
  (54 shorter events, 3.3 us)
Async XLA Ops:
  6.5 61.8 %all-gather.2.cloned.1.call-start = ((), (), s32[]{:S(2)}) async-start(), calls=%async_computation.1 | async-start | bytes 6291456 | tf_op jit(solution)/shard_map/all_gather | solution.py:122
  6.5 23.2 %collective-permute-start.1 = (bf16[256,512]{1,0:T(8,128)(2,1)}, bf16[256,512]{1,0:T(8,128)(2,1)S(1)}, u32[]{:S(2)}, u32[]{:S(2)}) collective-permute-start(bf16[256,512]{1,0:T(8,128)(2,1)} %param.6), channel_id=1, source_target_pairs={{0,2},{4,0},{8,4},{12,8},{14,12},{10,14},{6,10},{2,6},{1,3},{5,1},... | collective-permute-start | bytes 786440 | tf_op jit(solution)/shard_map/ppermute | solution.py:111
  7.8 23.3 %collective-permute-start = (bf16[256,512]{1,0:T(8,128)(2,1)}, bf16[256,512]{1,0:T(8,128)(2,1)S(1)}, u32[]{:S(2)}, u32[]{:S(2)}) collective-permute-start(bf16[256,512]{1,0:T(8,128)(2,1)} %param.6), channel_id=1, source_target_pairs={{0,4},{4,8},{8,12},{12,14},{14,10},{10,6},{6,2},{2,0},{1,5},{5,9},... | collective-permute-start | bytes 786440 | tf_op jit(solution)/shard_map/ppermute | solution.py:108
  28.7 21.3 %copy-start.2 = (s32[6,32]{1,0:T(8,128)S(1)}, s32[6,32]{1,0:T(8,128)}, u32[]{:S(2)}) copy-start(s32[6,32]{1,0:T(8,128)} %param.9) | copy-start | bytes 2308
  28.8 21.3 %copy-start.3 = (s32[6,32]{1,0:T(8,128)S(1)}, s32[6,32]{1,0:T(8,128)}, u32[]{:S(2)}) copy-start(s32[6,32]{1,0:T(8,128)} %param.8) | copy-start | bytes 2308
  29.8 6.6 %collective-permute-start.3 = (bf16[256,512]{1,0:T(8,128)(2,1)S(1)}, bf16[256,512]{1,0:T(8,128)(2,1)S(1)}, u32[]{:S(2)}, u32[]{:S(2)}) collective-permute-start(bf16[256,512]{1,0:T(8,128)(2,1)S(1)} %collective-permute-done.1), channel_id=1, source_target_pairs={{0,2},{4,0},{8,4},{12,8},{14,12},{10,14},{6,10},{2,6},{1,3},{5,1},... | collective-permute-start | bytes 786440 | tf_op jit(solution)/shard_map/ppermute | solution.py:111
  31.1 6.6 %collective-permute-start.2 = (bf16[256,512]{1,0:T(8,128)(2,1)S(1)}, bf16[256,512]{1,0:T(8,128)(2,1)S(1)}, u32[]{:S(2)}, u32[]{:S(2)}) collective-permute-start(bf16[256,512]{1,0:T(8,128)(2,1)S(1)} %collective-permute-done), channel_id=1, source_target_pairs={{0,4},{4,8},{8,12},{12,14},{14,10},{10,6},{6,2},{2,0},{1,5},{5,9},... | collective-permute-start | bytes 786440 | tf_op jit(solution)/shard_map/ppermute | solution.py:108
  36.4 7.0 %collective-permute-start.5 = (bf16[256,512]{1,0:T(8,128)(2,1)S(1)}, bf16[256,512]{1,0:T(8,128)(2,1)S(1)}, u32[]{:S(2)}, u32[]{:S(2)}) collective-permute-start(bf16[256,512]{1,0:T(8,128)(2,1)S(1)} %collective-permute-done.3), channel_id=1, source_target_pairs={{0,2},{4,0},{8,4},{12,8},{14,12},{10,14},{6,10},{2,6},{1,3},{5,1},... | collective-permute-start | bytes 786440 | tf_op jit(solution)/shard_map/ppermute | solution.py:111
  37.7 5.5 %collective-permute-start.4 = (bf16[256,512]{1,0:T(8,128)(2,1)S(1)}, bf16[256,512]{1,0:T(8,128)(2,1)S(1)}, u32[]{:S(2)}, u32[]{:S(2)}) collective-permute-start(bf16[256,512]{1,0:T(8,128)(2,1)S(1)} %collective-permute-done.2), channel_id=1, source_target_pairs={{0,4},{4,8},{8,12},{12,14},{14,10},{10,6},{6,2},{2,0},{1,5},{5,9},... | collective-permute-start | bytes 786440 | tf_op jit(solution)/shard_map/ppermute | solution.py:108
  43.2 5.4 %collective-permute-start.6 = (bf16[256,512]{1,0:T(8,128)(2,1)S(1)}, bf16[256,512]{1,0:T(8,128)(2,1)S(1)}, u32[]{:S(2)}, u32[]{:S(2)}) collective-permute-start(bf16[256,512]{1,0:T(8,128)(2,1)S(1)} %collective-permute-done.4), channel_id=1, source_target_pairs={{0,4},{4,8},{8,12},{12,14},{14,10},{10,6},{6,2},{2,0},{1,5},{5,9},... | collective-permute-start | bytes 786440 | tf_op jit(solution)/shard_map/ppermute | solution.py:108
  48.6 1.3 copy-start
  50.0 66.8 %reduce-scatter.2.cloned.1.call-start = ((), (), s32[]{:S(2)}) async-start(), calls=%async_computation.2 | async-start | bytes 9437184 | tf_op jit(solution)/shard_map/reduce_scatter | solution.py:134
  118.8 10.7 %collective-permute-start.7 = (f32[6,32,512]{2,1,0:T(8,128)S(1)}, f32[6,32,512]{2,1,0:T(8,128)S(1)}, u32[]{:S(2)}, u32[]{:S(2)}) collective-permute-start(f32[6,32,512]{2,1,0:T(8,128)S(1)} %get-tuple-element.19), channel_id=1, source_target_pairs={{0,2},{2,4},{4,6},{6,8},{8,10},{10,12},{12,14},{14,0},{1,3},{3,5},... | collective-permute-start | bytes 1179656 | tf_op jit(solution)/shard_map/ppermute | solution.py:144
  120.3 17.6 %collective-permute-start.8 = (f32[6,32,512]{2,1,0:T(8,128)S(1)}, f32[6,32,512]{2,1,0:T(8,128)S(1)}, u32[]{:S(2)}, u32[]{:S(2)}) collective-permute-start(f32[6,32,512]{2,1,0:T(8,128)S(1)} %get-tuple-element.18), channel_id=1, source_target_pairs={{0,4},{2,6},{4,8},{6,10},{8,12},{10,14},{12,0},{14,2},{1,5},{3,7},... | collective-permute-start | bytes 1179656 | tf_op jit(solution)/shard_map/ppermute | solution.py:144
  123.7 63.9 %collective-permute-start.13 = (f32[6,32,512]{2,1,0:T(8,128)S(1)}, f32[6,32,512]{2,1,0:T(8,128)S(1)}, u32[]{:S(2)}, u32[]{:S(2)}) collective-permute-start(f32[6,32,512]{2,1,0:T(8,128)S(1)} %get-tuple-element.13), channel_id=1, source_target_pairs={{0,14},{2,0},{4,2},{6,4},{8,6},{10,8},{12,10},{14,12},{1,15},{3,1}... | collective-permute-start | bytes 1179656 | tf_op jit(solution)/shard_map/ppermute | solution.py:144
  123.9 63.6 %collective-permute-start.12 = (f32[6,32,512]{2,1,0:T(8,128)S(1)}, f32[6,32,512]{2,1,0:T(8,128)S(1)}, u32[]{:S(2)}, u32[]{:S(2)}) collective-permute-start(f32[6,32,512]{2,1,0:T(8,128)S(1)} %get-tuple-element.14), channel_id=1, source_target_pairs={{0,12},{2,14},{4,0},{6,2},{8,4},{10,6},{12,8},{14,10},{1,13},{3,15... | collective-permute-start | bytes 1179656 | tf_op jit(solution)/shard_map/ppermute | solution.py:144
  124.2 63.3 %collective-permute-start.11 = (f32[6,32,512]{2,1,0:T(8,128)S(1)}, f32[6,32,512]{2,1,0:T(8,128)S(1)}, u32[]{:S(2)}, u32[]{:S(2)}) collective-permute-start(f32[6,32,512]{2,1,0:T(8,128)S(1)} %get-tuple-element.15), channel_id=1, source_target_pairs={{0,10},{2,12},{4,14},{6,0},{8,2},{10,4},{12,6},{14,8},{1,11},{3,13... | collective-permute-start | bytes 1179656 | tf_op jit(solution)/shard_map/ppermute | solution.py:144
  129.5 49.5 %collective-permute-start.9 = (f32[6,32,512]{2,1,0:T(8,128)S(1)}, f32[6,32,512]{2,1,0:T(8,128)S(1)}, u32[]{:S(2)}, u32[]{:S(2)}) collective-permute-start(f32[6,32,512]{2,1,0:T(8,128)S(1)} %get-tuple-element.17), channel_id=1, source_target_pairs={{0,6},{2,8},{4,10},{6,12},{8,14},{10,0},{12,2},{14,4},{1,7},{3,9},... | collective-permute-start | bytes 1179656 | tf_op jit(solution)/shard_map/ppermute | solution.py:144
  137.9 49.6 %collective-permute-start.10 = (f32[6,32,512]{2,1,0:T(8,128)S(1)}, f32[6,32,512]{2,1,0:T(8,128)S(1)}, u32[]{:S(2)}, u32[]{:S(2)}) collective-permute-start(f32[6,32,512]{2,1,0:T(8,128)S(1)} %get-tuple-element.16), channel_id=1, source_target_pairs={{0,8},{2,10},{4,12},{6,14},{8,0},{10,2},{12,4},{14,6},{1,9},{3,11}... | collective-permute-start | bytes 1179656 | tf_op jit(solution)/shard_map/ppermute | solution.py:144
  205.4 21.3 %collective-permute-start.15 = (f32[2,6,32,512]{3,2,1,0:T(8,128)}, f32[2,6,32,512]{3,2,1,0:T(8,128)}, u32[]{:S(2)}, u32[]{:S(2)}) collective-permute-start(f32[2,6,32,512]{3,2,1,0:T(8,128)} %bitcast.54), channel_id=1, source_target_pairs={{0,4},{2,6},{4,8},{6,10},{8,12},{10,14},{12,0},{14,2},{1,5},{3,7},... | collective-permute-start | bytes 2359304 | tf_op jit(solution)/shard_map/ppermute | solution.py:162
  208.6 32.0 %collective-permute-start.14 = (f32[2,6,32,512]{3,2,1,0:T(8,128)}, f32[2,6,32,512]{3,2,1,0:T(8,128)}, u32[]{:S(2)}, u32[]{:S(2)}) collective-permute-start(f32[2,6,32,512]{3,2,1,0:T(8,128)} %bitcast.50), channel_id=1, source_target_pairs={{0,2},{2,4},{4,6},{6,8},{8,10},{10,12},{12,14},{14,0},{1,3},{3,5},... | collective-permute-start | bytes 2359304 | tf_op jit(solution)/shard_map/ppermute | solution.py:162
  213.1 111.8 %collective-permute-start.16 = (f32[2,6,32,512]{3,2,1,0:T(8,128)}, f32[2,6,32,512]{3,2,1,0:T(8,128)}, u32[]{:S(2)}, u32[]{:S(2)}) collective-permute-start(f32[2,6,32,512]{3,2,1,0:T(8,128)} %bitcast.58), channel_id=1, source_target_pairs={{0,6},{2,8},{4,10},{6,12},{8,14},{10,0},{12,2},{14,4},{1,7},{3,9},... | collective-permute-start | bytes 2359304 | tf_op jit(solution)/shard_map/ppermute | solution.py:162
  217.2 124.6 %collective-permute-start.17 = (f32[2,6,32,512]{3,2,1,0:T(8,128)}, f32[2,6,32,512]{3,2,1,0:T(8,128)}, u32[]{:S(2)}, u32[]{:S(2)}) collective-permute-start(f32[2,6,32,512]{3,2,1,0:T(8,128)} %bitcast.62), channel_id=1, source_target_pairs={{0,8},{2,10},{4,12},{6,14},{8,0},{10,2},{12,4},{14,6},{1,9},{3,11}... | collective-permute-start | bytes 2359304 | tf_op jit(solution)/shard_map/ppermute | solution.py:162
  218.8 124.2 %collective-permute-start.18 = (f32[2,6,32,512]{3,2,1,0:T(8,128)}, f32[2,6,32,512]{3,2,1,0:T(8,128)}, u32[]{:S(2)}, u32[]{:S(2)}) collective-permute-start(f32[2,6,32,512]{3,2,1,0:T(8,128)} %bitcast.66), channel_id=1, source_target_pairs={{0,10},{2,12},{4,14},{6,0},{8,2},{10,4},{12,6},{14,8},{1,11},{3,13... | collective-permute-start | bytes 2359304 | tf_op jit(solution)/shard_map/ppermute | solution.py:162
  226.7 120.5 %collective-permute-start.19 = (f32[2,6,32,512]{3,2,1,0:T(8,128)S(1)}, f32[2,6,32,512]{3,2,1,0:T(8,128)S(1)}, u32[]{:S(2)}, u32[]{:S(2)}) collective-permute-start(f32[2,6,32,512]{3,2,1,0:T(8,128)S(1)} %bitcast.123), channel_id=1, source_target_pairs={{0,12},{2,14},{4,0},{6,2},{8,4},{10,6},{12,8},{14,10},{1,13},{3,15... | collective-permute-start | bytes 2359304 | tf_op jit(solution)/shard_map/ppermute | solution.py:162
  240.6 108.1 %collective-permute-start.20 = (f32[2,6,32,512]{3,2,1,0:T(8,128)S(1)}, f32[2,6,32,512]{3,2,1,0:T(8,128)S(1)}, u32[]{:S(2)}, u32[]{:S(2)}) collective-permute-start(f32[2,6,32,512]{3,2,1,0:T(8,128)S(1)} %bitcast.122), channel_id=1, source_target_pairs={{0,14},{2,0},{4,2},{6,4},{8,6},{10,8},{12,10},{14,12},{1,15},{3,1}... | collective-permute-start | bytes 2359304 | tf_op jit(solution)/shard_map/ppermute | solution.py:162
  347.3 2.7 copy-start.1
Sparse Core Ops, SparseCore 0:
  50.1 18.1 all-gather.1
  101.1 15.6 reduce-scatter.1

commit v7 on v4

--- a/solution.py
+++ b/solution.py
@@ -51,33 +51,33 @@
 
 
 def _dft_kernel(w_ref, x_ref, o_ref):
-    x = x_ref[...]
-    xh = x.astype(jnp.bfloat16)
-    xl = (x - xh.astype(jnp.float32)).astype(jnp.bfloat16)
+    r = x_ref.shape[1]
     w = w_ref[...]
     wh = w.astype(jnp.bfloat16)
     wl = (w - wh.astype(jnp.float32)).astype(jnp.bfloat16)
-    acc = jnp.dot(wh, xh, preferred_element_type=jnp.float32)
-    acc += jnp.dot(wh, xl, preferred_element_type=jnp.float32)
-    acc += jnp.dot(wl, xh, preferred_element_type=jnp.float32)
-    o_ref[...] = acc
+
+    def step(i, carry):
+        x = x_ref[:, i, :]
+        xh = x.astype(jnp.bfloat16)
+        xl = (x - xh.astype(jnp.float32)).astype(jnp.bfloat16)
+        acc = jnp.dot(wh, xh, preferred_element_type=jnp.float32)
+        acc += jnp.dot(wh, xl, preferred_element_type=jnp.float32)
+        acc += jnp.dot(wl, xh, preferred_element_type=jnp.float32)
+        o_ref[:, i, :] = acc
+        return carry
+
+    lax.fori_loop(0, r, step, 0)
 
 
 def _dft(weights, x):
     rows, k = weights.shape
-    n = x.shape[1]
-    tn = 2048 if n % 2048 == 0 else n
-    return pl.pallas_call(
+    _, r, n = x.shape
+    out = pl.pallas_call(
         _dft_kernel,
-        grid=(n // tn,),
-        in_specs=[
-            pl.BlockSpec((rows, k), lambda i: (0, 0)),
-            pl.BlockSpec((k, tn), lambda i: (0, i)),
-        ],
-        out_specs=pl.BlockSpec((rows, tn), lambda i: (0, i)),
-        out_shape=jax.ShapeDtypeStruct((rows, n), jnp.float32),
-        compiler_params=pltpu.CompilerParams(dimension_semantics=("arbitrary",)),
+        out_shape=jax.ShapeDtypeStruct((rows, r, n), jnp.float32),
+        compiler_params=pltpu.CompilerParams(vmem_limit_bytes=56 * 1024 * 1024),
     )(weights, x)
+    return out
 
 
 def _trig(h, b, count):
@@ -106,7 +106,7 @@
         if s:
             piece = lax.ppermute(piece, "blade", [(j, (j + s) % nbd) for j in range(nbd)])
         got.append(piece)
-    stacked = jnp.stack(got).reshape(nbd * nbl, r * modes)
+    stacked = jnp.stack(got).reshape(nbd * nbl, r, modes)
 
     count = nbl * nbd
     src = (me - jnp.arange(nbd, dtype=jnp.int32)) % nbd

time: 350 us -> 361 us (1.031)
  the two profiles are of different devices: /device:TPU:15 before, /device:TPU:28 now
where the time goes in v7:
time: 361 us; the launch traced here: 360 us
  waiting for transfers between devices  254 us (70%)
  Pallas kernels  48 us (13%)
  local copies, waits for them, and re-layouts  31 us (9%)
  between operations  13.7 us (4%)
  starting transfers between devices  12 us (3%)
    ppermute x7, waiting for transfers between devices, body(): lax.ppermute(piece, 'blade', [(j, (j + t) % nbd) for j in range(nbd)])  128 us
    ppermute x7, waiting for transfers between devices, body(): lax.ppermute(piece, 'blade', [(j, (j + s) % nbd) for j in range(nbd)])  61.3 us
    all_gather x1, waiting for transfers between devices, body(): whole = lax.all_gather(panel, ('blade', 'dof'), axis=0, tiled=True)  48.7 us
    pallas_call x1, Pallas kernels, _project(): pl.pallas_call(_project_kernel, grid_spec=grid_spec, out_shape=jax.ShapeD...  26.1 us
    pallas_call x1, Pallas kernels, _dft(): pl.pallas_call(_dft_kernel, out_shape=jax.ShapeDtypeStruct((rows, r, n),...  21.8 us
    reduce_scatter x1, waiting for transfers between devices, body(): half = lax.psum_scatter(proj, 'dof', scatter_dimension=1, tiled=True)  15.5 us
  transfers between devices with their start and end apart: 16, of which 11 were waited for; matrix products, arithmetic and copies ran while one was open for 4% of the time, Pallas kernels for 0%

profile of v7, /device:TPU:28, one launch (start us, length us, event | category | flops | bytes accessed | tf_op | source)
XLA Modules:
  0.0 360.0 jit_solution(2488245499919918651)
XLA Ops:
  6.5 0.0 all-gather.2.cloned.1.call-start
  6.5 0.7 all-gather.2.cloned.1.call-update
  7.3 0.0 reduce-scatter.2.cloned.1.call-start
  7.3 1.3 reshape.156.rows_ref
  8.6 1.3 reshape.157.cols_ref
  9.9 48.7 %all-gather.2.cloned.1.call-done = bf16[4096,512]{1,0:T(8,128)(2,1)} async-done(((bf16[256,512]{1,0:T(8,128)(2,1)}), bf16[4096,512]{1,0:T(8,128)(2,1)}) %all-gather.2.cloned.1.call-update) | async-done | bytes 4194320 | tf_op jit(solution)/shard_map/all_gather | solution.py:92
  58.6 6.5 %copy.6 = bf16[32,128,512]{1,2,0:T(8,128)(2,1)} copy(bf16[32,128,512]{2,1,0:T(8,128)(2,1)} %bitcast.42) | data formatting | bytes 8388608 | tf_op jit(solution)/shard_map/reshape | solution.py:93
  65.1 26.1 %shard_map.46 = f32[6,512,512]{2,1,0:T(8,128)} custom-call(s32[192]{0:T(256)} %reshape.156.rows_ref, s32[192]{0:T(256)} %reshape.157.cols_ref, bf16[32,128,512]{2,1,0:T(8,128)(2,1)} %bitcast.43, bf16[32,512,128]{2,1,0:T(8,128)(2,1)} %bitcast.44, bf16[6,32,128,128]{3,2,1,0:T(8,128)(2,1)} %s_ref.1), custom_call_target="tpu_custom_call" | custom-call | tf_op jit(solution)/shard_map/pallas_call | solution.py:42
  91.2 0.0 reduce-scatter.2.cloned.1.call-update
  91.4 0.1 iota_add_fusion
  91.4 0.1 add.218
  91.5 0.1 iota_add_fusion.1
  91.6 15.5 %reduce-scatter.2.cloned.1.call-done = f32[6,256,512]{2,1,0:T(8,128)} async-done(((f32[6,512,512]{2,1,0:T(8,128)}), f32[6,256,512]{2,1,0:T(8,128)}) %reduce-scatter.2.cloned.1.call-update) | async-done | bytes 3145744 | tf_op jit(solution)/shard_map/reduce_scatter | solution.py:97
  107.1 2.0 dynamic-slice_bitcast_fusion
  109.1 0.3 collective-permute-start
  109.4 0.2 fusion.4
  109.6 1.8 collective-permute-start.1
  111.4 0.6 pad_maximum_fusion
  112.0 1.5 reshape.155.w_ref
  113.5 1.5 collective-permute-start.2
  115.0 1.4 collective-permute-start.3
  116.4 1.5 collective-permute-start.4
  117.9 1.0 bitcast_dynamic-update-slice_fusion.7
  118.9 1.5 collective-permute-done
  120.5 0.5 collective-permute-start.5
  121.0 8.1 %collective-permute-done.1 = f32[6,32,512]{2,1,0:T(8,128)S(1)} collective-permute-done((f32[6,32,512]{2,1,0:T(8,128)S(1)}, f32[6,32,512]{2,1,0:T(8,128)S(1)}, u32[]{:S(2)}, u32[]{:S(2)}) %collective-permute-start.1) | collective-permute-done | bytes 393248 | tf_op jit(solution)/shard_map/ppermute | solution.py:107
  129.1 0.0 collective-permute-start.6
  129.2 6.7 %collective-permute-done.2 = f32[6,32,512]{2,1,0:T(8,128)S(1)} collective-permute-done((f32[6,32,512]{2,1,0:T(8,128)S(1)}, f32[6,32,512]{2,1,0:T(8,128)S(1)}, u32[]{:S(2)}, u32[]{:S(2)}) %collective-permute-start.2) | collective-permute-done | bytes 393248 | tf_op jit(solution)/shard_map/ppermute | solution.py:107
  135.9 43.6 %collective-permute-done.3 = f32[6,32,512]{2,1,0:T(8,128)S(1)} collective-permute-done((f32[6,32,512]{2,1,0:T(8,128)S(1)}, f32[6,32,512]{2,1,0:T(8,128)S(1)}, u32[]{:S(2)}, u32[]{:S(2)}) %collective-permute-start.3) | collective-permute-done | bytes 393248 | tf_op jit(solution)/shard_map/ppermute | solution.py:107
  179.5 1.4 collective-permute-done.4
  180.9 0.0 collective-permute-done.5
  181.0 0.0 collective-permute-done.6
  181.0 0.0 copy-start.1
  181.0 1.6 copy-done.1
  182.7 21.8 %shard_map.47 = f32[96,32,512]{2,1,0:T(8,128)} custom-call(f32[96,48]{1,0:T(8,128)} %reshape.155.w_ref, f32[48,32,512]{2,1,0:T(8,128)} %bitcast.45), custom_call_target="tpu_custom_call" | custom-call | tf_op jit(solution)/shard_map/pallas_call | solution.py:75
  204.5 5.1 %fusion.10 = (f32[12,32,512]{2,1,0:T(8,128)S(1)}, f32[12,32,512]{2,1,0:T(8,128)S(1)}, f32[12,32,512]{2,1,0:T(8,128)S(1)}, f32[12,32,512]{2,1,0:T(8,128)}, f32[12...) fusion(f32[96,32,512]{2,1,0:T(8,128)} %shard_map.47), kind=kLoop, calls=%fused_computation.45 | loop fusion | bytes 12582912 | tf_op jit(solution)/shard_map/slice | solution.py:123
  209.6 0.0 collective-permute-start.7
  209.6 1.0 collective-permute-start.8
  210.6 1.8 collective-permute-start.9
  212.4 1.5 collective-permute-start.10
  214.0 0.5 collective-permute-start.11
  214.4 15.0 %collective-permute-done.7 = f32[2,6,32,512]{3,2,1,0:T(8,128)} collective-permute-done((f32[2,6,32,512]{3,2,1,0:T(8,128)}, f32[2,6,32,512]{3,2,1,0:T(8,128)}, u32[]{:S(2)}, u32[]{:S(2)}) %collective-permute-start.7) | collective-permute-done | bytes 786464 | tf_op jit(solution)/shard_map/ppermute | solution.py:125
  229.5 0.0 collective-permute-start.12
  229.5 0.8 broadcast_in_dim.2
  230.3 0.1 constant_dynamic-update-slice_fusion.7
  230.3 14.5 %collective-permute-done.8 = f32[2,6,32,512]{3,2,1,0:T(8,128)} collective-permute-done((f32[2,6,32,512]{3,2,1,0:T(8,128)}, f32[2,6,32,512]{3,2,1,0:T(8,128)}, u32[]{:S(2)}, u32[]{:S(2)}) %collective-permute-start.8) | collective-permute-done | bytes 786464 | tf_op jit(solution)/shard_map/ppermute | solution.py:125
  244.8 0.0 collective-permute-start.13
  244.8 1.2 constant_dynamic-update-slice_fusion.6
  246.0 1.2 constant_dynamic-update-slice_fusion.5
  247.2 14.5 %collective-permute-done.9 = f32[2,6,32,512]{3,2,1,0:T(8,128)} collective-permute-done((f32[2,6,32,512]{3,2,1,0:T(8,128)}, f32[2,6,32,512]{3,2,1,0:T(8,128)}, u32[]{:S(2)}, u32[]{:S(2)}) %collective-permute-start.9) | collective-permute-done | bytes 786464 | tf_op jit(solution)/shard_map/ppermute | solution.py:125
  261.7 1.2 constant_dynamic-update-slice_fusion.4
  262.9 84.1 %collective-permute-done.10 = f32[2,6,32,512]{3,2,1,0:T(8,128)} collective-permute-done((f32[2,6,32,512]{3,2,1,0:T(8,128)}, f32[2,6,32,512]{3,2,1,0:T(8,128)}, u32[]{:S(2)}, u32[]{:S(2)}) %collective-permute-start.10) | collective-permute-done | bytes 786464 | tf_op jit(solution)/shard_map/ppermute | solution.py:125
  347.0 1.2 constant_dynamic-update-slice_fusion.3
  348.1 0.0 collective-permute-done.11
  348.1 1.2 constant_dynamic-update-slice_fusion.2
  349.3 0.0 collective-permute-done.12
  349.4 0.1 constant_dynamic-update-slice_fusion.1
  349.4 0.0 copy-start
  349.5 0.0 collective-permute-done.13
  349.5 2.7 copy-done
  352.1 1.0 constant_dynamic-update-slice_fusion
  (8 shorter events, 0.2 us)
Async XLA Ops:
  6.5 52.1 %all-gather.2.cloned.1.call-start = ((), (), s32[]{:S(2)}) async-start(), calls=%async_computation.1 | async-start | bytes 4456448 | tf_op jit(solution)/shard_map/all_gather | solution.py:92
  7.3 99.8 %reduce-scatter.2.cloned.1.call-start = ((), (), s32[]{:S(2)}) async-start(), calls=%async_computation.2 | async-start | bytes 9437184 | tf_op jit(solution)/shard_map/reduce_scatter | solution.py:97
  109.1 11.4 %collective-permute-start = (f32[6,32,512]{2,1,0:T(8,128)S(1)}, f32[6,32,512]{2,1,0:T(8,128)S(1)}, u32[]{:S(2)}, u32[]{:S(2)}) collective-permute-start(f32[6,32,512]{2,1,0:T(8,128)S(1)} %get-tuple-element.19), channel_id=1, source_target_pairs={{0,2},{2,4},{4,6},{6,8},{8,10},{10,12},{12,14},{14,0},{1,3},{3,5},... | collective-permute-start | bytes 1179656 | tf_op jit(solution)/shard_map/ppermute | solution.py:107
  109.6 19.5 %collective-permute-start.1 = (f32[6,32,512]{2,1,0:T(8,128)S(1)}, f32[6,32,512]{2,1,0:T(8,128)S(1)}, u32[]{:S(2)}, u32[]{:S(2)}) collective-permute-start(f32[6,32,512]{2,1,0:T(8,128)S(1)} %get-tuple-element.18), channel_id=1, source_target_pairs={{0,4},{2,6},{4,8},{6,10},{8,12},{10,14},{12,0},{14,2},{1,5},{3,7},... | collective-permute-start | bytes 1179656 | tf_op jit(solution)/shard_map/ppermute | solution.py:107
  113.5 22.4 %collective-permute-start.2 = (f32[6,32,512]{2,1,0:T(8,128)S(1)}, f32[6,32,512]{2,1,0:T(8,128)S(1)}, u32[]{:S(2)}, u32[]{:S(2)}) collective-permute-start(f32[6,32,512]{2,1,0:T(8,128)S(1)} %get-tuple-element.17), channel_id=1, source_target_pairs={{0,6},{2,8},{4,10},{6,12},{8,14},{10,0},{12,2},{14,4},{1,7},{3,9},... | collective-permute-start | bytes 1179656 | tf_op jit(solution)/shard_map/ppermute | solution.py:107
  115.0 64.4 %collective-permute-start.3 = (f32[6,32,512]{2,1,0:T(8,128)S(1)}, f32[6,32,512]{2,1,0:T(8,128)S(1)}, u32[]{:S(2)}, u32[]{:S(2)}) collective-permute-start(f32[6,32,512]{2,1,0:T(8,128)S(1)} %get-tuple-element.16), channel_id=1, source_target_pairs={{0,8},{2,10},{4,12},{6,14},{8,0},{10,2},{12,4},{14,6},{1,9},{3,11}... | collective-permute-start | bytes 1179656 | tf_op jit(solution)/shard_map/ppermute | solution.py:107
  116.4 64.5 %collective-permute-start.4 = (f32[6,32,512]{2,1,0:T(8,128)S(1)}, f32[6,32,512]{2,1,0:T(8,128)S(1)}, u32[]{:S(2)}, u32[]{:S(2)}) collective-permute-start(f32[6,32,512]{2,1,0:T(8,128)S(1)} %get-tuple-element.15), channel_id=1, source_target_pairs={{0,10},{2,12},{4,14},{6,0},{8,2},{10,4},{12,6},{14,8},{1,11},{3,13... | collective-permute-start | bytes 1179656 | tf_op jit(solution)/shard_map/ppermute | solution.py:107
  120.5 60.4 %collective-permute-start.5 = (f32[6,32,512]{2,1,0:T(8,128)S(1)}, f32[6,32,512]{2,1,0:T(8,128)S(1)}, u32[]{:S(2)}, u32[]{:S(2)}) collective-permute-start(f32[6,32,512]{2,1,0:T(8,128)S(1)} %get-tuple-element.14), channel_id=1, source_target_pairs={{0,12},{2,14},{4,0},{6,2},{8,4},{10,6},{12,8},{14,10},{1,13},{3,15... | collective-permute-start | bytes 1179656 | tf_op jit(solution)/shard_map/ppermute | solution.py:107
  129.1 51.9 %collective-permute-start.6 = (f32[6,32,512]{2,1,0:T(8,128)S(1)}, f32[6,32,512]{2,1,0:T(8,128)S(1)}, u32[]{:S(2)}, u32[]{:S(2)}) collective-permute-start(f32[6,32,512]{2,1,0:T(8,128)S(1)} %get-tuple-element.13), channel_id=1, source_target_pairs={{0,14},{2,0},{4,2},{6,4},{8,6},{10,8},{12,10},{14,12},{1,15},{3,1}... | collective-permute-start | bytes 1179656 | tf_op jit(solution)/shard_map/ppermute | solution.py:107
  181.0 1.6 copy-start.1
  209.6 19.9 %collective-permute-start.7 = (f32[2,6,32,512]{3,2,1,0:T(8,128)}, f32[2,6,32,512]{3,2,1,0:T(8,128)}, u32[]{:S(2)}, u32[]{:S(2)}) collective-permute-start(f32[2,6,32,512]{3,2,1,0:T(8,128)} %bitcast.20), channel_id=1, source_target_pairs={{0,2},{2,4},{4,6},{6,8},{8,10},{10,12},{12,14},{14,0},{1,3},{3,5},... | collective-permute-start | bytes 2359304 | tf_op jit(solution)/shard_map/ppermute | solution.py:125
  209.6 35.3 %collective-permute-start.8 = (f32[2,6,32,512]{3,2,1,0:T(8,128)}, f32[2,6,32,512]{3,2,1,0:T(8,128)}, u32[]{:S(2)}, u32[]{:S(2)}) collective-permute-start(f32[2,6,32,512]{3,2,1,0:T(8,128)} %bitcast.21), channel_id=1, source_target_pairs={{0,4},{2,6},{4,8},{6,10},{8,12},{10,14},{12,0},{14,2},{1,5},{3,7},... | collective-permute-start | bytes 2359304 | tf_op jit(solution)/shard_map/ppermute | solution.py:125
  210.6 51.1 %collective-permute-start.9 = (f32[2,6,32,512]{3,2,1,0:T(8,128)}, f32[2,6,32,512]{3,2,1,0:T(8,128)}, u32[]{:S(2)}, u32[]{:S(2)}) collective-permute-start(f32[2,6,32,512]{3,2,1,0:T(8,128)} %bitcast.22), channel_id=1, source_target_pairs={{0,6},{2,8},{4,10},{6,12},{8,14},{10,0},{12,2},{14,4},{1,7},{3,9},... | collective-permute-start | bytes 2359304 | tf_op jit(solution)/shard_map/ppermute | solution.py:125
  212.4 134.5 %collective-permute-start.10 = (f32[2,6,32,512]{3,2,1,0:T(8,128)}, f32[2,6,32,512]{3,2,1,0:T(8,128)}, u32[]{:S(2)}, u32[]{:S(2)}) collective-permute-start(f32[2,6,32,512]{3,2,1,0:T(8,128)} %bitcast.23), channel_id=1, source_target_pairs={{0,8},{2,10},{4,12},{6,14},{8,0},{10,2},{12,4},{14,6},{1,9},{3,11}... | collective-permute-start | bytes 2359304 | tf_op jit(solution)/shard_map/ppermute | solution.py:125
  214.0 134.2 %collective-permute-start.11 = (f32[2,6,32,512]{3,2,1,0:T(8,128)S(1)}, f32[2,6,32,512]{3,2,1,0:T(8,128)}, u32[]{:S(2)}, u32[]{:S(2)}) collective-permute-start(f32[2,6,32,512]{3,2,1,0:T(8,128)S(1)} %bitcast.51), channel_id=1, source_target_pairs={{0,10},{2,12},{4,14},{6,0},{8,2},{10,4},{12,6},{14,8},{1,11},{3,13... | collective-permute-start | bytes 2359304 | tf_op jit(solution)/shard_map/ppermute | solution.py:125
  229.5 119.9 %collective-permute-start.12 = (f32[2,6,32,512]{3,2,1,0:T(8,128)S(1)}, f32[2,6,32,512]{3,2,1,0:T(8,128)S(1)}, u32[]{:S(2)}, u32[]{:S(2)}) collective-permute-start(f32[2,6,32,512]{3,2,1,0:T(8,128)S(1)} %bitcast.50), channel_id=1, source_target_pairs={{0,12},{2,14},{4,0},{6,2},{8,4},{10,6},{12,8},{14,10},{1,13},{3,15... | collective-permute-start | bytes 2359304 | tf_op jit(solution)/shard_map/ppermute | solution.py:125
  244.8 104.6 %collective-permute-start.13 = (f32[2,6,32,512]{3,2,1,0:T(8,128)S(1)}, f32[2,6,32,512]{3,2,1,0:T(8,128)S(1)}, u32[]{:S(2)}, u32[]{:S(2)}) collective-permute-start(f32[2,6,32,512]{3,2,1,0:T(8,128)S(1)} %bitcast.49), channel_id=1, source_target_pairs={{0,14},{2,0},{4,2},{6,4},{8,6},{10,8},{12,10},{14,12},{1,15},{3,1}... | collective-permute-start | bytes 2359304 | tf_op jit(solution)/shard_map/ppermute | solution.py:125
  349.4 2.7 copy-start
Sparse Core Ops, SparseCore 0:
  9.5 49.0 all-gather.1
  91.4 15.6 reduce-scatter.1

commit v8 on v4

--- a/solution.py
+++ b/solution.py
@@ -122,7 +122,9 @@
     for t in range(nbd):
         piece = spec[t]
         if t:
+            piece = piece.astype(jnp.bfloat16)
             piece = lax.ppermute(piece, "blade", [(j, (j + t) % nbd) for j in range(nbd)])
+            piece = piece.astype(jnp.float32)
         at = ((me - t) % nbd) * r
         out = lax.dynamic_update_slice(out, piece, (0, 0, at, 0))
     return out

time: 350 us -> 286 us (0.82)
  the two profiles are of different devices: /device:TPU:15 before, /device:TPU:0 now
where the time goes in v8:
time: 286 us; the launch traced here: 285 us
  waiting for transfers between devices  162 us (57%)
  starting transfers between devices  40.4 us (14%)
  Pallas kernels  34.4 us (12%)
  local copies, waits for them, and re-layouts  26.7 us (9%)
  between operations  13.8 us (5%)
  other arithmetic  7.6 us (3%)
    ppermute x7, waiting for transfers between devices, body(): lax.ppermute(piece, 'blade', [(j, (j + t) % nbd) for j in range(nbd)])  58.8 us
    all_gather x1, waiting for transfers between devices, body(): whole = lax.all_gather(panel, ('blade', 'dof'), axis=0, tiled=True)  52.8 us
    ppermute x7, waiting for transfers between devices, body(): lax.ppermute(piece, 'blade', [(j, (j + s) % nbd) for j in range(nbd)])  36.9 us
    ppermute x7, starting transfers between devices, body(): lax.ppermute(piece, 'blade', [(j, (j + s) % nbd) for j in range(nbd)])  33.6 us
    pallas_call x1, Pallas kernels, _project(): pl.pallas_call(_project_kernel, grid_spec=grid_spec, out_shape=jax.ShapeD...  26.2 us
    reduce_scatter x1, waiting for transfers between devices, body(): half = lax.psum_scatter(proj, 'dof', scatter_dimension=1, tiled=True)  12.8 us
    unnamed x28, local copies, waits for them, and re-layouts  11.5 us
    pallas_call x1, Pallas kernels, _dft(): pl.pallas_call(_dft_kernel, grid=(n // tn,), in_specs=[pl.BlockSpec((rows...  8.2 us
  transfers between devices with their start and end apart: 16, of which 10 were waited for; matrix products, arithmetic and copies ran while one was open for 5% of the time, Pallas kernels for 0%

profile of v8, /device:TPU:0, one launch (start us, length us, event | category | flops | bytes accessed | tf_op | source)
XLA Modules:
  0.0 285.0 jit_solution(12226242579826764177)
XLA Ops:
  6.5 0.7 all-gather.2.cloned.1.call-update
  7.3 0.0 reduce-scatter.2.cloned.1.call-start
  7.3 1.4 reshape.163.rows_ref
  8.7 1.4 reshape.164.cols_ref
  10.0 52.8 %all-gather.2.cloned.1.call-done = bf16[4096,512]{1,0:T(8,128)(2,1)} async-done(((bf16[256,512]{1,0:T(8,128)(2,1)}), bf16[4096,512]{1,0:T(8,128)(2,1)}) %all-gather.2.cloned.1.call-update) | async-done | bytes 4194320 | tf_op jit(solution)/shard_map/all_gather | solution.py:92
  62.8 6.5 %copy.6 = bf16[32,128,512]{1,2,0:T(8,128)(2,1)} copy(bf16[32,128,512]{2,1,0:T(8,128)(2,1)} %bitcast.69) | data formatting | bytes 8388608 | tf_op jit(solution)/shard_map/reshape | solution.py:93
  69.3 26.2 %shard_map.46 = f32[6,512,512]{2,1,0:T(8,128)} custom-call(s32[192]{0:T(256)} %reshape.163.rows_ref, s32[192]{0:T(256)} %reshape.164.cols_ref, bf16[32,128,512]{2,1,0:T(8,128)(2,1)} %bitcast.70, bf16[32,512,128]{2,1,0:T(8,128)(2,1)} %bitcast.71, bf16[6,32,128,128]{3,2,1,0:T(8,128)(2,1)} %s_ref.1), custom_call_target="tpu_custom_call" | custom-call | tf_op jit(solution)/shard_map/pallas_call | solution.py:42
  95.4 0.0 reduce-scatter.2.cloned.1.call-update
  95.6 0.1 iota_add_fusion
  95.6 0.1 add.218
  95.7 0.1 iota_add_fusion.1
  95.8 12.8 %reduce-scatter.2.cloned.1.call-done = f32[6,256,512]{2,1,0:T(8,128)} async-done(((f32[6,512,512]{2,1,0:T(8,128)}), f32[6,256,512]{2,1,0:T(8,128)}) %reduce-scatter.2.cloned.1.call-update) | async-done | bytes 3145744 | tf_op jit(solution)/shard_map/reduce_scatter | solution.py:97
  108.6 2.0 dynamic-slice_bitcast_fusion
  110.6 1.8 collective-permute-start
  112.4 0.2 fusion.4
  112.6 1.5 collective-permute-start.1
  114.2 0.6 pad_maximum_fusion
  114.8 1.5 reshape.162.w_ref
  116.3 3.3 %collective-permute-start.6 = (f32[6,32,512]{2,1,0:T(8,128)S(1)}, f32[6,32,512]{2,1,0:T(8,128)S(1)}, u32[]{:S(2)}, u32[]{:S(2)}) collective-permute-start(f32[6,32,512]{2,1,0:T(8,128)S(1)} %get-tuple-element.12), channel_id=1, source_target_pairs={{0,14},{2,0},{4,2},{6,4},{8,6},{10,8},{12,10},{14,12},{1,15},{3,1}... | collective-permute-start | bytes 1179656 | tf_op jit(solution)/shard_map/ppermute | solution.py:107
  119.5 0.3 collective-permute-start.5
  119.8 0.9 collective-permute-start.4
  120.7 1.0 bitcast_dynamic-update-slice_fusion.7
  121.7 3.8 %collective-permute-done = f32[6,32,512]{2,1,0:T(8,128)S(1)} collective-permute-done((f32[6,32,512]{2,1,0:T(8,128)S(1)}, f32[6,32,512]{2,1,0:T(8,128)S(1)}, u32[]{:S(2)}, u32[]{:S(2)}) %collective-permute-start) | collective-permute-done | bytes 393248 | tf_op jit(solution)/shard_map/ppermute | solution.py:107
  125.5 1.0 collective-permute-done.1
  126.5 25.8 %collective-permute-start.3 = (f32[6,32,512]{2,1,0:T(8,128)S(1)}, f32[6,32,512]{2,1,0:T(8,128)S(1)}, u32[]{:S(2)}, u32[]{:S(2)}) collective-permute-start(f32[6,32,512]{2,1,0:T(8,128)S(1)} %get-tuple-element.15), channel_id=1, source_target_pairs={{0,8},{2,10},{4,12},{6,14},{8,0},{10,2},{12,4},{14,6},{1,9},{3,11}... | collective-permute-start | bytes 1179656 | tf_op jit(solution)/shard_map/ppermute | solution.py:107
  152.4 23.1 %collective-permute-done.2 = f32[6,32,512]{2,1,0:T(8,128)S(1)} collective-permute-done((f32[6,32,512]{2,1,0:T(8,128)S(1)}, f32[6,32,512]{2,1,0:T(8,128)S(1)}, u32[]{:S(2)}, u32[]{:S(2)}) %collective-permute-start.2) | collective-permute-done | bytes 393248 | tf_op jit(solution)/shard_map/ppermute | solution.py:107
  175.5 9.0 %collective-permute-done.3 = f32[6,32,512]{2,1,0:T(8,128)S(1)} collective-permute-done((f32[6,32,512]{2,1,0:T(8,128)S(1)}, f32[6,32,512]{2,1,0:T(8,128)S(1)}, u32[]{:S(2)}, u32[]{:S(2)}) %collective-permute-start.3) | collective-permute-done | bytes 393248 | tf_op jit(solution)/shard_map/ppermute | solution.py:107
  184.6 0.0 collective-permute-done.5
  184.6 0.0 collective-permute-done.6
  184.7 3.4 %copy.7 = f32[6,8,32,512]{3,1,2,0:T(8,128)} copy(f32[6,8,32,512]{3,2,1,0:T(8,128)S(1)} %bitcast.73) | data formatting | bytes 6291456
  188.1 8.2 %shard_map.47 = f32[96,16384]{1,0:T(8,128)} custom-call(f32[96,48]{1,0:T(8,128)} %reshape.162.w_ref, f32[48,16384]{1,0:T(8,128)} %bitcast.72), custom_call_target="tpu_custom_call" | custom-call | tf_op jit(solution)/shard_map/pallas_call | solution.py:70
  196.3 3.1 %convert.9 = bf16[96,16384]{1,0:T(8,128)(2,1)S(1)} convert(f32[96,16384]{1,0:T(8,128)} %shard_map.47) | non-fusion elementwise | flops 1572864 | bytes 9437184 | tf_op jit(solution)/shard_map/convert.6
  199.5 1.6 fusion.10
  201.1 0.2 copy.9
  201.3 0.1 collective-permute-start.7
  201.4 1.2 copy.10
  202.6 0.8 slice.57
  203.4 0.6 copy.8
  204.0 0.1 slice.55
  204.1 0.4 copy-done.1
  204.4 0.2 copy.15
  204.6 0.2 copy.14
  204.8 3.9 %collective-permute-start.12 = (bf16[2,6,32,512]{3,2,1,0:T(8,128)(2,1)S(1)}, bf16[2,6,32,512]{3,2,1,0:T(8,128)(2,1)S(1)}, u32[]{:S(2)}, u32[]{:S(2)}) collective-permute-start(bf16[2,6,32,512]{3,2,1,0:T(8,128)(2,1)S(1)} %bitcast.94), channel_id=1, source_target_pairs={{0,12},{2,14},{4,0},{6,2},{8,4},{10,6},{12,8},{14,10},{1,13},{3,15... | collective-permute-start | bytes 1179656 | tf_op jit(solution)/shard_map/ppermute | solution.py:126
  208.7 2.9 %collective-permute-start.13 = (bf16[2,6,32,512]{3,2,1,0:T(8,128)(2,1)S(1)}, bf16[2,6,32,512]{3,2,1,0:T(8,128)(2,1)S(1)}, u32[]{:S(2)}, u32[]{:S(2)}) collective-permute-start(bf16[2,6,32,512]{3,2,1,0:T(8,128)(2,1)S(1)} %bitcast.93), channel_id=1, source_target_pairs={{0,14},{2,0},{4,2},{6,4},{8,6},{10,8},{12,10},{14,12},{1,15},{3,1}... | collective-permute-start | bytes 1179656 | tf_op jit(solution)/shard_map/ppermute | solution.py:126
  211.6 0.2 copy.13
  211.8 0.1 collective-permute-start.11
  211.8 0.2 copy.12
  212.0 0.2 copy.11
  212.2 0.8 broadcast_in_dim.2
  213.0 0.1 constant_dynamic-update-slice_fusion
  213.1 3.2 %collective-permute-done.7 = bf16[2,6,32,512]{3,2,1,0:T(8,128)(2,1)} collective-permute-done((bf16[2,6,32,512]{3,2,1,0:T(8,128)(2,1)S(1)}, bf16[2,6,32,512]{3,2,1,0:T(8,128)(2,1)}, u32[]{:S(2)}, u32[]{:S(2)}) %collective-permute-start.7) | collective-permute-done | bytes 393248 | tf_op jit(solution)/shard_map/ppermute | solution.py:126
  216.3 1.1 convert_dynamic-update-slice_fusion.6
  217.4 0.1 collective-permute-done.8
  217.5 0.0 collective-permute-start.10
  217.5 1.1 convert_dynamic-update-slice_fusion.5
  218.6 47.1 %collective-permute-done.9 = bf16[2,6,32,512]{3,2,1,0:T(8,128)(2,1)S(1)} collective-permute-done((bf16[2,6,32,512]{3,2,1,0:T(8,128)(2,1)S(1)}, bf16[2,6,32,512]{3,2,1,0:T(8,128)(2,1)S(1)}, u32[]{:S(2)}, u32[]{:S(2)}) %collective-permute-start.9) | collective-permute-done | bytes 393248 | tf_op jit(solution)/shard_map/ppermute | solution.py:126
  265.8 0.1 convert_dynamic-update-slice_fusion.4
  265.8 8.3 %collective-permute-done.10 = bf16[2,6,32,512]{3,2,1,0:T(8,128)(2,1)S(1)} collective-permute-done((bf16[2,6,32,512]{3,2,1,0:T(8,128)(2,1)S(1)}, bf16[2,6,32,512]{3,2,1,0:T(8,128)(2,1)S(1)}, u32[]{:S(2)}, u32[]{:S(2)}) %collective-permute-start.10) | collective-permute-done | bytes 393248 | tf_op jit(solution)/shard_map/ppermute | solution.py:126
  274.2 0.1 convert_dynamic-update-slice_fusion.3
  274.3 0.1 convert_dynamic-update-slice_fusion.2
  274.4 0.1 convert_dynamic-update-slice_fusion.1
  274.5 0.0 copy-start
  274.5 2.7 copy-done
  277.2 1.0 convert_dynamic-update-slice_fusion
  (25 shorter events, 0.4 us)
Async XLA Ops:
  6.5 56.3 %all-gather.2.cloned.1.call-start = ((), (), s32[]{:S(2)}) async-start(), calls=%async_computation.1 | async-start | bytes 4456448 | tf_op jit(solution)/shard_map/all_gather | solution.py:92
  7.3 101.4 %reduce-scatter.2.cloned.1.call-start = ((), (), s32[]{:S(2)}) async-start(), calls=%async_computation.2 | async-start | bytes 9437184 | tf_op jit(solution)/shard_map/reduce_scatter | solution.py:97
  110.6 14.8 %collective-permute-start = (f32[6,32,512]{2,1,0:T(8,128)S(1)}, f32[6,32,512]{2,1,0:T(8,128)S(1)}, u32[]{:S(2)}, u32[]{:S(2)}) collective-permute-start(f32[6,32,512]{2,1,0:T(8,128)S(1)} %get-tuple-element.18), channel_id=1, source_target_pairs={{0,2},{2,4},{4,6},{6,8},{8,10},{10,12},{12,14},{14,0},{1,3},{3,5},... | collective-permute-start | bytes 1179656 | tf_op jit(solution)/shard_map/ppermute | solution.py:107
  112.6 13.9 %collective-permute-start.1 = (f32[6,32,512]{2,1,0:T(8,128)S(1)}, f32[6,32,512]{2,1,0:T(8,128)S(1)}, u32[]{:S(2)}, u32[]{:S(2)}) collective-permute-start(f32[6,32,512]{2,1,0:T(8,128)S(1)} %get-tuple-element.17), channel_id=1, source_target_pairs={{0,4},{2,6},{4,8},{6,10},{8,12},{10,14},{12,0},{14,2},{1,5},{3,7},... | collective-permute-start | bytes 1179656 | tf_op jit(solution)/shard_map/ppermute | solution.py:107
  116.3 68.4 %collective-permute-start.6 = (f32[6,32,512]{2,1,0:T(8,128)S(1)}, f32[6,32,512]{2,1,0:T(8,128)S(1)}, u32[]{:S(2)}, u32[]{:S(2)}) collective-permute-start(f32[6,32,512]{2,1,0:T(8,128)S(1)} %get-tuple-element.12), channel_id=1, source_target_pairs={{0,14},{2,0},{4,2},{6,4},{8,6},{10,8},{12,10},{14,12},{1,15},{3,1}... | collective-permute-start | bytes 1179656 | tf_op jit(solution)/shard_map/ppermute | solution.py:107
  119.5 65.1 %collective-permute-start.5 = (f32[6,32,512]{2,1,0:T(8,128)S(1)}, f32[6,32,512]{2,1,0:T(8,128)S(1)}, u32[]{:S(2)}, u32[]{:S(2)}) collective-permute-start(f32[6,32,512]{2,1,0:T(8,128)S(1)} %get-tuple-element.13), channel_id=1, source_target_pairs={{0,12},{2,14},{4,0},{6,2},{8,4},{10,6},{12,8},{14,10},{1,13},{3,15... | collective-permute-start | bytes 1179656 | tf_op jit(solution)/shard_map/ppermute | solution.py:107
  119.8 64.7 %collective-permute-start.4 = (f32[6,32,512]{2,1,0:T(8,128)S(1)}, f32[6,32,512]{2,1,0:T(8,128)S(1)}, u32[]{:S(2)}, u32[]{:S(2)}) collective-permute-start(f32[6,32,512]{2,1,0:T(8,128)S(1)} %get-tuple-element.14), channel_id=1, source_target_pairs={{0,10},{2,12},{4,14},{6,0},{8,2},{10,4},{12,6},{14,8},{1,11},{3,13... | collective-permute-start | bytes 1179656 | tf_op jit(solution)/shard_map/ppermute | solution.py:107
  125.5 50.0 %collective-permute-start.2 = (f32[6,32,512]{2,1,0:T(8,128)S(1)}, f32[6,32,512]{2,1,0:T(8,128)S(1)}, u32[]{:S(2)}, u32[]{:S(2)}) collective-permute-start(f32[6,32,512]{2,1,0:T(8,128)S(1)} %get-tuple-element.16), channel_id=1, source_target_pairs={{0,6},{2,8},{4,10},{6,12},{8,14},{10,0},{12,2},{14,4},{1,7},{3,9},... | collective-permute-start | bytes 1179656 | tf_op jit(solution)/shard_map/ppermute | solution.py:107
  126.5 58.0 %collective-permute-start.3 = (f32[6,32,512]{2,1,0:T(8,128)S(1)}, f32[6,32,512]{2,1,0:T(8,128)S(1)}, u32[]{:S(2)}, u32[]{:S(2)}) collective-permute-start(f32[6,32,512]{2,1,0:T(8,128)S(1)} %get-tuple-element.15), channel_id=1, source_target_pairs={{0,8},{2,10},{4,12},{6,14},{8,0},{10,2},{12,4},{14,6},{1,9},{3,11}... | collective-permute-start | bytes 1179656 | tf_op jit(solution)/shard_map/ppermute | solution.py:107
  201.1 2.3 slice-start
  201.3 15.0 %collective-permute-start.7 = (bf16[2,6,32,512]{3,2,1,0:T(8,128)(2,1)S(1)}, bf16[2,6,32,512]{3,2,1,0:T(8,128)(2,1)}, u32[]{:S(2)}, u32[]{:S(2)}) collective-permute-start(bf16[2,6,32,512]{3,2,1,0:T(8,128)(2,1)S(1)} %bitcast.92), channel_id=1, source_target_pairs={{0,2},{2,4},{4,6},{6,8},{8,10},{10,12},{12,14},{14,0},{1,3},{3,5},... | collective-permute-start | bytes 1179656 | tf_op jit(solution)/shard_map/ppermute | solution.py:126
  203.4 14.1 %collective-permute-start.8 = (bf16[2,6,32,512]{3,2,1,0:T(8,128)(2,1)}, bf16[2,6,32,512]{3,2,1,0:T(8,128)(2,1)}, u32[]{:S(2)}, u32[]{:S(2)}) collective-permute-start(bf16[2,6,32,512]{3,2,1,0:T(8,128)(2,1)} %bitcast.32), channel_id=1, source_target_pairs={{0,4},{2,6},{4,8},{6,10},{8,12},{10,14},{12,0},{14,2},{1,5},{3,7},... | collective-permute-start | bytes 1179656 | tf_op jit(solution)/shard_map/ppermute | solution.py:126
  203.4 1.0 copy-start.1
  204.8 69.5 %collective-permute-start.12 = (bf16[2,6,32,512]{3,2,1,0:T(8,128)(2,1)S(1)}, bf16[2,6,32,512]{3,2,1,0:T(8,128)(2,1)S(1)}, u32[]{:S(2)}, u32[]{:S(2)}) collective-permute-start(bf16[2,6,32,512]{3,2,1,0:T(8,128)(2,1)S(1)} %bitcast.94), channel_id=1, source_target_pairs={{0,12},{2,14},{4,0},{6,2},{8,4},{10,6},{12,8},{14,10},{1,13},{3,15... | collective-permute-start | bytes 1179656 | tf_op jit(solution)/shard_map/ppermute | solution.py:126
  208.7 65.8 %collective-permute-start.13 = (bf16[2,6,32,512]{3,2,1,0:T(8,128)(2,1)S(1)}, bf16[2,6,32,512]{3,2,1,0:T(8,128)(2,1)S(1)}, u32[]{:S(2)}, u32[]{:S(2)}) collective-permute-start(bf16[2,6,32,512]{3,2,1,0:T(8,128)(2,1)S(1)} %bitcast.93), channel_id=1, source_target_pairs={{0,14},{2,0},{4,2},{6,4},{8,6},{10,8},{12,10},{14,12},{1,15},{3,1}... | collective-permute-start | bytes 1179656 | tf_op jit(solution)/shard_map/ppermute | solution.py:126
  211.8 62.5 %collective-permute-start.11 = (bf16[2,6,32,512]{3,2,1,0:T(8,128)(2,1)S(1)}, bf16[2,6,32,512]{3,2,1,0:T(8,128)(2,1)S(1)}, u32[]{:S(2)}, u32[]{:S(2)}) collective-permute-start(bf16[2,6,32,512]{3,2,1,0:T(8,128)(2,1)S(1)} %bitcast.95), channel_id=1, source_target_pairs={{0,10},{2,12},{4,14},{6,0},{8,2},{10,4},{12,6},{14,8},{1,11},{3,13... | collective-permute-start | bytes 1179656 | tf_op jit(solution)/shard_map/ppermute | solution.py:126
  216.3 49.5 %collective-permute-start.9 = (bf16[2,6,32,512]{3,2,1,0:T(8,128)(2,1)S(1)}, bf16[2,6,32,512]{3,2,1,0:T(8,128)(2,1)S(1)}, u32[]{:S(2)}, u32[]{:S(2)}) collective-permute-start(bf16[2,6,32,512]{3,2,1,0:T(8,128)(2,1)S(1)} %bitcast.97), channel_id=1, source_target_pairs={{0,6},{2,8},{4,10},{6,12},{8,14},{10,0},{12,2},{14,4},{1,7},{3,9},... | collective-permute-start | bytes 1179656 | tf_op jit(solution)/shard_map/ppermute | solution.py:126
  217.5 56.6 %collective-permute-start.10 = (bf16[2,6,32,512]{3,2,1,0:T(8,128)(2,1)S(1)}, bf16[2,6,32,512]{3,2,1,0:T(8,128)(2,1)S(1)}, u32[]{:S(2)}, u32[]{:S(2)}) collective-permute-start(bf16[2,6,32,512]{3,2,1,0:T(8,128)(2,1)S(1)} %bitcast.96), channel_id=1, source_target_pairs={{0,8},{2,10},{4,12},{6,14},{8,0},{10,2},{12,4},{14,6},{1,9},{3,11}... | collective-permute-start | bytes 1179656 | tf_op jit(solution)/shard_map/ppermute | solution.py:126
  274.5 2.7 copy-start
Sparse Core Ops, SparseCore 0:
  9.5 53.2 all-gather.1
  95.6 12.9 reduce-scatter.1

commit v9 on v8

--- a/solution.py
+++ b/solution.py
@@ -89,7 +89,10 @@
     nbl, nblk, bs, _ = stiffness.shape
     modes = panel.shape[-1]
     nbd = lax.axis_size("blade")
-    whole = lax.all_gather(panel, ("blade", "dof"), axis=0, tiled=True)
+    nd = lax.axis_size("dof")
+    at = (lax.axis_index("blade") * nd + lax.axis_index("dof")) * panel.shape[0]
+    whole = jnp.zeros((nbd * nd * panel.shape[0], modes), panel.dtype)
+    whole = lax.psum(lax.dynamic_update_slice(whole, panel, (at, 0)), ("blade", "dof"))
     pb = whole.reshape(-1, bs, modes)
     pt = jnp.swapaxes(pb, 1, 2)
     proj = _project(pb, pt, stiffness, block_rows.reshape(-1), block_cols.reshape(-1))

time: 286 us -> 354 us (1.24)
  waiting for transfers between devices: 162 us -> 221 us
  local copies, waits for them, and re-layouts: 26.7 us -> 35.5 us
    psum x0 -> x1, waiting for transfers between devices: none -> 112 us  [body(): lax.psum(lax.dynamic_update_slice(whole, panel, (at, 0)), ('blade', 'dof'))]
    all_gather x1 -> x0, waiting for transfers between devices: 52.8 us -> none  [body(): whole = lax.all_gather(panel, ('blade', 'dof'), axis=0, tiled=True)]
    psum x0 -> x1, local copies, waits for them, and re-layouts: none -> 6.51 us  [body(): lax.psum(lax.dynamic_update_slice(whole, panel, (at, 0)), ('blade', 'dof'))]
    unnamed x28 -> x34, local copies, waits for them, and re-layouts: 11.5 us -> 12.1 us
  transfers between devices with their start and end apart: 16 -> 16, of which waited for: 10 -> 10; matrix products, arithmetic and copies ran while one was open for 5% -> 3% of each run, Pallas kernels for 0% -> 0%
where the time goes in v9:
time: 354 us; the launch traced here: 353 us
  waiting for transfers between devices  221 us (62%)
  starting transfers between devices  40.4 us (11%)
  local copies, waits for them, and re-layouts  35.5 us (10%)
  Pallas kernels  34.4 us (10%)
  between operations  13.8 us (4%)
  other arithmetic  7.6 us (2%)
    psum x1, waiting for transfers between devices, body(): lax.psum(lax.dynamic_update_slice(whole, panel, (at, 0)), ('blade', 'dof'))  112 us
    ppermute x7, waiting for transfers between devices, body(): lax.ppermute(piece, 'blade', [(j, (j + t) % nbd) for j in range(nbd)])  58.8 us
    ppermute x7, waiting for transfers between devices, body(): lax.ppermute(piece, 'blade', [(j, (j + s) % nbd) for j in range(nbd)])  36.9 us
    ppermute x7, starting transfers between devices, body(): lax.ppermute(piece, 'blade', [(j, (j + s) % nbd) for j in range(nbd)])  33.5 us
    pallas_call x1, Pallas kernels, _project(): pl.pallas_call(_project_kernel, grid_spec=grid_spec, out_shape=jax.ShapeD...  26.2 us
    reduce_scatter x1, waiting for transfers between devices, body(): half = lax.psum_scatter(proj, 'dof', scatter_dimension=1, tiled=True)  13.2 us
    unnamed x34, local copies, waits for them, and re-layouts  12.1 us
    pallas_call x1, Pallas kernels, _dft(): pl.pallas_call(_dft_kernel, grid=(n // tn,), in_specs=[pl.BlockSpec((rows...  8.2 us
  transfers between devices with their start and end apart: 16, of which 10 were waited for; matrix products, arithmetic and copies ran while one was open for 3% of the time, Pallas kernels for 0%

profile of v9, /device:TPU:0, one launch (start us, length us, event | category | flops | bytes accessed | tf_op | source)
XLA Modules:
  0.0 353.0 jit_solution(16964447700493124532)
XLA Ops:
  6.5 2.3 broadcast_in_dim.5
  8.8 0.7 constant_dynamic-update-slice_fusion.1
  9.5 6.5 %copy.6 = bf16[32,128,512]{1,2,0:T(8,128)(2,1)} copy(bf16[32,128,512]{2,1,0:T(8,128)(2,1)} %bitcast) | data formatting | bytes 8388608 | tf_op jit(solution)/shard_map/reshape | solution.py:96
  16.0 0.0 all-reduce.2.cloned.1.call-update
  16.0 0.0 reduce-scatter.2.cloned.1.call-start
  16.1 0.6 copy-done.3
  16.7 0.7 reshape.163.rows_ref
  17.4 0.7 reshape.164.cols_ref
  18.0 112.3 %all-reduce.2.cloned.1.call-done = bf16[32,128,512]{1,2,0:T(8,128)(2,1)} async-done(((bf16[32,128,512]{1,2,0:T(8,128)(2,1)}), bf16[32,128,512]{1,2,0:T(8,128)(2,1)}) %all-reduce.2.cloned.1.call-update) | async-done | bytes 4194320 | tf_op jit(solution)/shard_map/psum | solution.py:95
  130.3 6.5 %copy.7.pb_ref = bf16[32,128,512]{2,1,0:T(8,128)(2,1)} copy(bf16[32,128,512]{1,2,0:T(8,128)(2,1)} %all-reduce.2.cloned.1.call-done) | data formatting | bytes 8388608 | tf_op jit(solution)/shard_map/psum | solution.py:95
  136.8 26.2 %shard_map.46 = f32[6,512,512]{2,1,0:T(8,128)} custom-call(s32[192]{0:T(256)} %reshape.163.rows_ref, s32[192]{0:T(256)} %reshape.164.cols_ref, bf16[32,128,512]{2,1,0:T(8,128)(2,1)} %copy.7.pb_ref, bf16[32,512,128]{2,1,0:T(8,128)(2,1)} %bitcast.69, bf16[6,32,128,128]{3,2,1,0:T(8,128)(2,1)} %s_ref.1), custom_call_target="tpu_custom_call" | custom-call | tf_op jit(solution)/shard_map/pallas_call | solution.py:42
  163.0 0.0 reduce-scatter.2.cloned.1.call-update
  163.1 0.1 iota_add_fusion
  163.2 0.1 add.226
  163.3 0.1 iota_add_fusion.1
  163.3 13.2 %reduce-scatter.2.cloned.1.call-done = f32[6,256,512]{2,1,0:T(8,128)} async-done(((f32[6,512,512]{2,1,0:T(8,128)}), f32[6,256,512]{2,1,0:T(8,128)}) %reduce-scatter.2.cloned.1.call-update) | async-done | bytes 3145744 | tf_op jit(solution)/shard_map/reduce_scatter | solution.py:100
  176.6 2.0 dynamic-slice_bitcast_fusion
  178.6 1.8 collective-permute-start
  180.4 0.2 fusion.4
  180.6 1.5 collective-permute-start.1
  182.2 0.6 pad_maximum_fusion
  182.8 1.5 reshape.162.w_ref
  184.3 3.2 collective-permute-start.6
  187.5 0.3 collective-permute-start.5
  187.8 0.9 collective-permute-start.4
  188.7 1.0 bitcast_dynamic-update-slice_fusion.7
  189.7 3.8 %collective-permute-done = f32[6,32,512]{2,1,0:T(8,128)S(1)} collective-permute-done((f32[6,32,512]{2,1,0:T(8,128)S(1)}, f32[6,32,512]{2,1,0:T(8,128)S(1)}, u32[]{:S(2)}, u32[]{:S(2)}) %collective-permute-start) | collective-permute-done | bytes 393248 | tf_op jit(solution)/shard_map/ppermute | solution.py:110
  193.5 1.0 collective-permute-done.1
  194.5 25.8 %collective-permute-start.3 = (f32[6,32,512]{2,1,0:T(8,128)S(1)}, f32[6,32,512]{2,1,0:T(8,128)S(1)}, u32[]{:S(2)}, u32[]{:S(2)}) collective-permute-start(f32[6,32,512]{2,1,0:T(8,128)S(1)} %get-tuple-element.15), channel_id=1, source_target_pairs={{0,8},{2,10},{4,12},{6,14},{8,0},{10,2},{12,4},{14,6},{1,9},{3,11}... | collective-permute-start | bytes 1179656 | tf_op jit(solution)/shard_map/ppermute | solution.py:110
  220.3 23.1 %collective-permute-done.2 = f32[6,32,512]{2,1,0:T(8,128)S(1)} collective-permute-done((f32[6,32,512]{2,1,0:T(8,128)S(1)}, f32[6,32,512]{2,1,0:T(8,128)S(1)}, u32[]{:S(2)}, u32[]{:S(2)}) %collective-permute-start.2) | collective-permute-done | bytes 393248 | tf_op jit(solution)/shard_map/ppermute | solution.py:110
  243.4 9.1 %collective-permute-done.3 = f32[6,32,512]{2,1,0:T(8,128)S(1)} collective-permute-done((f32[6,32,512]{2,1,0:T(8,128)S(1)}, f32[6,32,512]{2,1,0:T(8,128)S(1)}, u32[]{:S(2)}, u32[]{:S(2)}) %collective-permute-start.3) | collective-permute-done | bytes 393248 | tf_op jit(solution)/shard_map/ppermute | solution.py:110
  252.7 3.4 copy.8
  256.1 8.2 %shard_map.47 = f32[96,16384]{1,0:T(8,128)} custom-call(f32[96,48]{1,0:T(8,128)} %reshape.162.w_ref, f32[48,16384]{1,0:T(8,128)} %bitcast.70), custom_call_target="tpu_custom_call" | custom-call | tf_op jit(solution)/shard_map/pallas_call | solution.py:70
  264.3 3.1 convert.9
  267.4 1.6 fusion.10
  269.1 0.2 copy.10
  269.3 0.1 collective-permute-start.7
  269.3 1.2 copy.11
  270.6 0.8 slice.57
  271.4 0.6 copy.9
  272.0 0.1 slice.55
  272.1 0.4 copy-done.1
  272.4 0.2 copy.16
  272.6 0.2 copy.15
  272.8 3.9 %collective-permute-start.12 = (bf16[2,6,32,512]{3,2,1,0:T(8,128)(2,1)S(1)}, bf16[2,6,32,512]{3,2,1,0:T(8,128)(2,1)S(1)}, u32[]{:S(2)}, u32[]{:S(2)}) collective-permute-start(bf16[2,6,32,512]{3,2,1,0:T(8,128)(2,1)S(1)} %bitcast.92), channel_id=1, source_target_pairs={{0,12},{2,14},{4,0},{6,2},{8,4},{10,6},{12,8},{14,10},{1,13},{3,15... | collective-permute-start | bytes 1179656 | tf_op jit(solution)/shard_map/ppermute | solution.py:129
  276.7 2.9 collective-permute-start.13
  279.5 0.2 copy.14
  279.7 0.1 collective-permute-start.11
  279.8 0.2 copy.13
  280.0 0.2 copy.12
  280.2 0.8 broadcast_in_dim.4
  281.0 0.1 constant_dynamic-update-slice_fusion
  281.1 3.2 collective-permute-done.7
  284.3 1.1 convert_dynamic-update-slice_fusion.6
  285.4 0.1 collective-permute-done.8
  285.5 1.1 convert_dynamic-update-slice_fusion.5
  286.6 47.1 %collective-permute-done.9 = bf16[2,6,32,512]{3,2,1,0:T(8,128)(2,1)S(1)} collective-permute-done((bf16[2,6,32,512]{3,2,1,0:T(8,128)(2,1)S(1)}, bf16[2,6,32,512]{3,2,1,0:T(8,128)(2,1)S(1)}, u32[]{:S(2)}, u32[]{:S(2)}) %collective-permute-start.9) | collective-permute-done | bytes 393248 | tf_op jit(solution)/shard_map/ppermute | solution.py:129
  333.7 0.1 convert_dynamic-update-slice_fusion.4
  333.8 8.3 %collective-permute-done.10 = bf16[2,6,32,512]{3,2,1,0:T(8,128)(2,1)S(1)} collective-permute-done((bf16[2,6,32,512]{3,2,1,0:T(8,128)(2,1)S(1)}, bf16[2,6,32,512]{3,2,1,0:T(8,128)(2,1)S(1)}, u32[]{:S(2)}, u32[]{:S(2)}) %collective-permute-start.10) | collective-permute-done | bytes 393248 | tf_op jit(solution)/shard_map/ppermute | solution.py:129
  342.2 0.1 convert_dynamic-update-slice_fusion.3
  342.3 0.1 convert_dynamic-update-slice_fusion.2
  342.4 0.1 convert_dynamic-update-slice_fusion.1
  342.5 2.7 copy-done
  345.2 1.0 convert_dynamic-update-slice_fusion
  (34 shorter events, 0.4 us)
Async XLA Ops:
  6.5 2.3 copy-start.2
  6.5 123.8 %all-reduce.2.cloned.1.call-start = ((), (), s32[]{:S(2)}) async-start(), calls=%async_computation.1 | async-start | bytes 8388608 | tf_op jit(solution)/shard_map/psum | solution.py:95
  16.0 0.7 copy-start.3
  16.0 1.4 copy-start.4
  16.0 160.5 %reduce-scatter.2.cloned.1.call-start = ((), (), s32[]{:S(2)}) async-start(), calls=%async_computation.2 | async-start | bytes 9437184 | tf_op jit(solution)/shard_map/reduce_scatter | solution.py:100
  178.6 14.8 %collective-permute-start = (f32[6,32,512]{2,1,0:T(8,128)S(1)}, f32[6,32,512]{2,1,0:T(8,128)S(1)}, u32[]{:S(2)}, u32[]{:S(2)}) collective-permute-start(f32[6,32,512]{2,1,0:T(8,128)S(1)} %get-tuple-element.18), channel_id=1, source_target_pairs={{0,2},{2,4},{4,6},{6,8},{8,10},{10,12},{12,14},{14,0},{1,3},{3,5},... | collective-permute-start | bytes 1179656 | tf_op jit(solution)/shard_map/ppermute | solution.py:110
  180.6 13.9 %collective-permute-start.1 = (f32[6,32,512]{2,1,0:T(8,128)S(1)}, f32[6,32,512]{2,1,0:T(8,128)S(1)}, u32[]{:S(2)}, u32[]{:S(2)}) collective-permute-start(f32[6,32,512]{2,1,0:T(8,128)S(1)} %get-tuple-element.17), channel_id=1, source_target_pairs={{0,4},{2,6},{4,8},{6,10},{8,12},{10,14},{12,0},{14,2},{1,5},{3,7},... | collective-permute-start | bytes 1179656 | tf_op jit(solution)/shard_map/ppermute | solution.py:110
  184.3 68.4 %collective-permute-start.6 = (f32[6,32,512]{2,1,0:T(8,128)S(1)}, f32[6,32,512]{2,1,0:T(8,128)S(1)}, u32[]{:S(2)}, u32[]{:S(2)}) collective-permute-start(f32[6,32,512]{2,1,0:T(8,128)S(1)} %get-tuple-element.12), channel_id=1, source_target_pairs={{0,14},{2,0},{4,2},{6,4},{8,6},{10,8},{12,10},{14,12},{1,15},{3,1}... | collective-permute-start | bytes 1179656 | tf_op jit(solution)/shard_map/ppermute | solution.py:110
  187.5 65.1 %collective-permute-start.5 = (f32[6,32,512]{2,1,0:T(8,128)S(1)}, f32[6,32,512]{2,1,0:T(8,128)S(1)}, u32[]{:S(2)}, u32[]{:S(2)}) collective-permute-start(f32[6,32,512]{2,1,0:T(8,128)S(1)} %get-tuple-element.13), channel_id=1, source_target_pairs={{0,12},{2,14},{4,0},{6,2},{8,4},{10,6},{12,8},{14,10},{1,13},{3,15... | collective-permute-start | bytes 1179656 | tf_op jit(solution)/shard_map/ppermute | solution.py:110
  187.8 64.7 %collective-permute-start.4 = (f32[6,32,512]{2,1,0:T(8,128)S(1)}, f32[6,32,512]{2,1,0:T(8,128)S(1)}, u32[]{:S(2)}, u32[]{:S(2)}) collective-permute-start(f32[6,32,512]{2,1,0:T(8,128)S(1)} %get-tuple-element.14), channel_id=1, source_target_pairs={{0,10},{2,12},{4,14},{6,0},{8,2},{10,4},{12,6},{14,8},{1,11},{3,13... | collective-permute-start | bytes 1179656 | tf_op jit(solution)/shard_map/ppermute | solution.py:110
  193.4 50.0 %collective-permute-start.2 = (f32[6,32,512]{2,1,0:T(8,128)S(1)}, f32[6,32,512]{2,1,0:T(8,128)S(1)}, u32[]{:S(2)}, u32[]{:S(2)}) collective-permute-start(f32[6,32,512]{2,1,0:T(8,128)S(1)} %get-tuple-element.16), channel_id=1, source_target_pairs={{0,6},{2,8},{4,10},{6,12},{8,14},{10,0},{12,2},{14,4},{1,7},{3,9},... | collective-permute-start | bytes 1179656 | tf_op jit(solution)/shard_map/ppermute | solution.py:110
  194.5 58.0 %collective-permute-start.3 = (f32[6,32,512]{2,1,0:T(8,128)S(1)}, f32[6,32,512]{2,1,0:T(8,128)S(1)}, u32[]{:S(2)}, u32[]{:S(2)}) collective-permute-start(f32[6,32,512]{2,1,0:T(8,128)S(1)} %get-tuple-element.15), channel_id=1, source_target_pairs={{0,8},{2,10},{4,12},{6,14},{8,0},{10,2},{12,4},{14,6},{1,9},{3,11}... | collective-permute-start | bytes 1179656 | tf_op jit(solution)/shard_map/ppermute | solution.py:110
  269.1 2.3 slice-start
  269.3 15.0 %collective-permute-start.7 = (bf16[2,6,32,512]{3,2,1,0:T(8,128)(2,1)S(1)}, bf16[2,6,32,512]{3,2,1,0:T(8,128)(2,1)}, u32[]{:S(2)}, u32[]{:S(2)}) collective-permute-start(bf16[2,6,32,512]{3,2,1,0:T(8,128)(2,1)S(1)} %bitcast.90), channel_id=1, source_target_pairs={{0,2},{2,4},{4,6},{6,8},{8,10},{10,12},{12,14},{14,0},{1,3},{3,5},... | collective-permute-start | bytes 1179656 | tf_op jit(solution)/shard_map/ppermute | solution.py:129
  271.4 14.1 %collective-permute-start.8 = (bf16[2,6,32,512]{3,2,1,0:T(8,128)(2,1)}, bf16[2,6,32,512]{3,2,1,0:T(8,128)(2,1)}, u32[]{:S(2)}, u32[]{:S(2)}) collective-permute-start(bf16[2,6,32,512]{3,2,1,0:T(8,128)(2,1)} %bitcast.32), channel_id=1, source_target_pairs={{0,4},{2,6},{4,8},{6,10},{8,12},{10,14},{12,0},{14,2},{1,5},{3,7},... | collective-permute-start | bytes 1179656 | tf_op jit(solution)/shard_map/ppermute | solution.py:129
  271.4 1.0 copy-start.1
  272.8 69.5 %collective-permute-start.12 = (bf16[2,6,32,512]{3,2,1,0:T(8,128)(2,1)S(1)}, bf16[2,6,32,512]{3,2,1,0:T(8,128)(2,1)S(1)}, u32[]{:S(2)}, u32[]{:S(2)}) collective-permute-start(bf16[2,6,32,512]{3,2,1,0:T(8,128)(2,1)S(1)} %bitcast.92), channel_id=1, source_target_pairs={{0,12},{2,14},{4,0},{6,2},{8,4},{10,6},{12,8},{14,10},{1,13},{3,15... | collective-permute-start | bytes 1179656 | tf_op jit(solution)/shard_map/ppermute | solution.py:129
  276.7 65.8 %collective-permute-start.13 = (bf16[2,6,32,512]{3,2,1,0:T(8,128)(2,1)S(1)}, bf16[2,6,32,512]{3,2,1,0:T(8,128)(2,1)S(1)}, u32[]{:S(2)}, u32[]{:S(2)}) collective-permute-start(bf16[2,6,32,512]{3,2,1,0:T(8,128)(2,1)S(1)} %bitcast.91), channel_id=1, source_target_pairs={{0,14},{2,0},{4,2},{6,4},{8,6},{10,8},{12,10},{14,12},{1,15},{3,1}... | collective-permute-start | bytes 1179656 | tf_op jit(solution)/shard_map/ppermute | solution.py:129
  279.7 62.5 %collective-permute-start.11 = (bf16[2,6,32,512]{3,2,1,0:T(8,128)(2,1)S(1)}, bf16[2,6,32,512]{3,2,1,0:T(8,128)(2,1)S(1)}, u32[]{:S(2)}, u32[]{:S(2)}) collective-permute-start(bf16[2,6,32,512]{3,2,1,0:T(8,128)(2,1)S(1)} %bitcast.93), channel_id=1, source_target_pairs={{0,10},{2,12},{4,14},{6,0},{8,2},{10,4},{12,6},{14,8},{1,11},{3,13... | collective-permute-start | bytes 1179656 | tf_op jit(solution)/shard_map/ppermute | solution.py:129
  284.3 49.5 %collective-permute-start.9 = (bf16[2,6,32,512]{3,2,1,0:T(8,128)(2,1)S(1)}, bf16[2,6,32,512]{3,2,1,0:T(8,128)(2,1)S(1)}, u32[]{:S(2)}, u32[]{:S(2)}) collective-permute-start(bf16[2,6,32,512]{3,2,1,0:T(8,128)(2,1)S(1)} %bitcast.95), channel_id=1, source_target_pairs={{0,6},{2,8},{4,10},{6,12},{8,14},{10,0},{12,2},{14,4},{1,7},{3,9},... | collective-permute-start | bytes 1179656 | tf_op jit(solution)/shard_map/ppermute | solution.py:129
  285.5 56.6 %collective-permute-start.10 = (bf16[2,6,32,512]{3,2,1,0:T(8,128)(2,1)S(1)}, bf16[2,6,32,512]{3,2,1,0:T(8,128)(2,1)S(1)}, u32[]{:S(2)}, u32[]{:S(2)}) collective-permute-start(bf16[2,6,32,512]{3,2,1,0:T(8,128)(2,1)S(1)} %bitcast.94), channel_id=1, source_target_pairs={{0,8},{2,10},{4,12},{6,14},{8,0},{10,2},{12,4},{14,6},{1,9},{3,11}... | collective-permute-start | bytes 1179656 | tf_op jit(solution)/shard_map/ppermute | solution.py:129
  342.5 2.7 copy-start
Sparse Core Ops, SparseCore 0:
  16.2 114.1 all-reduce.1
  163.1 13.3 reduce-scatter.1

commit v10 on v8

--- a/solution.py
+++ b/solution.py
@@ -8,35 +8,37 @@
 from jax.sharding import PartitionSpec as P
 
 
-def _project_kernel(rows_ref, cols_ref, pb_ref, pt_ref, s_ref, o_ref, lt_ref, img_ref):
+_NT = (((1,), (1,)), ((), ()))
+
+
+def _project_kernel(rows_ref, cols_ref, pt_ref, s_ref, o_ref, lt_ref, it_ref):
     b = pl.program_id(0)
     nblk = s_ref.shape[1]
     bs = s_ref.shape[2]
-    last = pb_ref.shape[0] - 1
+    last = pt_ref.shape[0] - 1
     for n in range(nblk):
         c = jnp.minimum(jnp.maximum(cols_ref[b * nblk + n], 0), last)
         r = jnp.minimum(jnp.maximum(rows_ref[b * nblk + n], 0), last)
-        im = jnp.dot(s_ref[0, n], pb_ref[c], preferred_element_type=jnp.float32)
-        img_ref[n * bs:(n + 1) * bs, :] = im.astype(jnp.bfloat16)
+        im = lax.dot_general(pt_ref[c], s_ref[0, n], _NT, preferred_element_type=jnp.float32)
+        it_ref[:, n * bs:(n + 1) * bs] = im.astype(jnp.bfloat16)
         lt_ref[:, n * bs:(n + 1) * bs] = pt_ref[r]
-    o_ref[0] = jnp.dot(lt_ref[...], img_ref[...], preferred_element_type=jnp.float32)
+    o_ref[0] = lax.dot_general(lt_ref[...], it_ref[...], _NT, preferred_element_type=jnp.float32)
 
 
-def _project(pb, pt, stiffness, rows, cols):
+def _project(pt, stiffness, rows, cols):
     nbl, nblk, bs, _ = stiffness.shape
-    nrb, _, modes = pb.shape
+    nrb, modes, _ = pt.shape
     grid_spec = pltpu.PrefetchScalarGridSpec(
         num_scalar_prefetch=2,
         grid=(nbl,),
         in_specs=[
-            pl.BlockSpec((nrb, bs, modes), lambda b, rr, cc: (0, 0, 0)),
             pl.BlockSpec((nrb, modes, bs), lambda b, rr, cc: (0, 0, 0)),
             pl.BlockSpec((1, nblk, bs, bs), lambda b, rr, cc: (b, 0, 0, 0)),
         ],
         out_specs=pl.BlockSpec((1, modes, modes), lambda b, rr, cc: (b, 0, 0)),
         scratch_shapes=[
             pltpu.VMEM((modes, nblk * bs), jnp.bfloat16),
-            pltpu.VMEM((nblk * bs, modes), jnp.bfloat16),
+            pltpu.VMEM((modes, nblk * bs), jnp.bfloat16),
         ],
     )
     return pl.pallas_call(
@@ -47,7 +49,7 @@
             dimension_semantics=("arbitrary",),
             vmem_limit_bytes=56 * 1024 * 1024,
         ),
-    )(rows, cols, pb, pt, stiffness)
+    )(rows, cols, pt, stiffness)
 
 
 def _dft_kernel(w_ref, x_ref, o_ref):
@@ -89,10 +91,9 @@
     nbl, nblk, bs, _ = stiffness.shape
     modes = panel.shape[-1]
     nbd = lax.axis_size("blade")
-    whole = lax.all_gather(panel, ("blade", "dof"), axis=0, tiled=True)
-    pb = whole.reshape(-1, bs, modes)
-    pt = jnp.swapaxes(pb, 1, 2)
-    proj = _project(pb, pt, stiffness, block_rows.reshape(-1), block_cols.reshape(-1))
+    mine = jnp.swapaxes(panel.reshape(-1, bs, modes), 1, 2)
+    pt = lax.all_gather(mine, ("blade", "dof"), axis=0, tiled=True)
+    proj = _project(pt, stiffness, block_rows.reshape(-1), block_cols.reshape(-1))
 
     half = lax.psum_scatter(proj, "dof", scatter_dimension=1, tiled=True)
     me = lax.axis_index("blade")

time: 286 us -> 278 us (0.972)
  local copies, waits for them, and re-layouts: 26.7 us -> 22 us
    reshape x1 -> x0, local copies, waits for them, and re-layouts: 6.47 us -> none  [body(): pb = whole.reshape(-1, bs, modes)]
where the time goes in v10:
time: 278 us; the launch traced here: 277 us
  waiting for transfers between devices  160 us (58%)
  starting transfers between devices  40.4 us (15%)
  Pallas kernels  33.3 us (12%)
  local copies, waits for them, and re-layouts  22 us (8%)
  between operations  13.8 us (5%)
  other arithmetic  7.6 us (3%)
    ppermute x7, waiting for transfers between devices, body(): lax.ppermute(piece, 'blade', [(j, (j + t) % nbd) for j in range(nbd)])  58.8 us
    all_gather x1, waiting for transfers between devices, body(): pt = lax.all_gather(mine, ('blade', 'dof'), axis=0, tiled=True)  51.7 us
    ppermute x7, waiting for transfers between devices, body(): lax.ppermute(piece, 'blade', [(j, (j + s) % nbd) for j in range(nbd)])  36.9 us
    ppermute x7, starting transfers between devices, body(): lax.ppermute(piece, 'blade', [(j, (j + s) % nbd) for j in range(nbd)])  33.5 us
    pallas_call x1, Pallas kernels, _project(): pl.pallas_call(_project_kernel, grid_spec=grid_spec, out_shape=jax.ShapeD...  25.1 us
    reduce_scatter x1, waiting for transfers between devices, body(): half = lax.psum_scatter(proj, 'dof', scatter_dimension=1, tiled=True)  12.8 us
    unnamed x28, local copies, waits for them, and re-layouts  11.5 us
    pallas_call x1, Pallas kernels, _dft(): pl.pallas_call(_dft_kernel, grid=(n // tn,), in_specs=[pl.BlockSpec((rows...  8.2 us
  transfers between devices with their start and end apart: 16, of which 10 were waited for; matrix products, arithmetic and copies ran while one was open for 5% of the time, Pallas kernels for 0%

profile of v10, /device:TPU:0, one launch (start us, length us, event | category | flops | bytes accessed | tf_op | source)
XLA Modules:
  0.0 277.5 jit_solution(3340440854341859074)
XLA Ops:
  6.5 1.8 copy.6
  8.3 0.0 all-gather.2.cloned.1.call-update
  8.4 0.0 reduce-scatter.2.cloned.1.call-start
  8.4 1.3 reshape.163.rows_ref
  9.7 1.3 reshape.164.cols_ref
  11.1 51.7 %all-gather.2.cloned.1.call-done.pt_ref = bf16[32,512,128]{2,1,0:T(8,128)(2,1)} async-done(((bf16[2,512,128]{2,1,0:T(8,128)(2,1)}), bf16[32,512,128]{2,1,0:T(8,128)(2,1)}) %all-gather.2.cloned.1.call-update) | async-done | bytes 4194320 | tf_op jit(solution)/shard_map/all_gather | solution.py:95
  62.8 25.1 %shard_map.46 = f32[6,512,512]{2,1,0:T(8,128)} custom-call(s32[192]{0:T(256)} %reshape.163.rows_ref, s32[192]{0:T(256)} %reshape.164.cols_ref, bf16[32,512,128]{2,1,0:T(8,128)(2,1)} %all-gather.2.cloned.1.call-done.pt_ref, bf16[6,32,128,128]{3,2,1,0:T(8,128)(2,1)} %s_ref.1), custom_call_target="tpu_custom_call" | custom-call | tf_op jit(solution)/shard_map/pallas_call | solution.py:44
  87.9 0.0 reduce-scatter.2.cloned.1.call-update
  88.1 0.1 iota_add_fusion
  88.1 0.1 add.218
  88.2 0.1 iota_add_fusion.1
  88.3 12.8 %reduce-scatter.2.cloned.1.call-done = f32[6,256,512]{2,1,0:T(8,128)} async-done(((f32[6,512,512]{2,1,0:T(8,128)}), f32[6,256,512]{2,1,0:T(8,128)}) %reduce-scatter.2.cloned.1.call-update) | async-done | bytes 3145744 | tf_op jit(solution)/shard_map/reduce_scatter | solution.py:98
  101.1 2.0 dynamic-slice_bitcast_fusion
  103.1 1.8 collective-permute-start
  104.9 0.2 fusion.4
  105.1 1.5 collective-permute-start.1
  106.6 0.6 pad_maximum_fusion
  107.3 1.5 reshape.162.w_ref
  108.7 3.2 %collective-permute-start.6 = (f32[6,32,512]{2,1,0:T(8,128)S(1)}, f32[6,32,512]{2,1,0:T(8,128)S(1)}, u32[]{:S(2)}, u32[]{:S(2)}) collective-permute-start(f32[6,32,512]{2,1,0:T(8,128)S(1)} %get-tuple-element.12), channel_id=1, source_target_pairs={{0,14},{2,0},{4,2},{6,4},{8,6},{10,8},{12,10},{14,12},{1,15},{3,1}... | collective-permute-start | bytes 1179656 | tf_op jit(solution)/shard_map/ppermute | solution.py:108
  112.0 0.3 collective-permute-start.5
  112.3 0.9 collective-permute-start.4
  113.2 1.0 bitcast_dynamic-update-slice_fusion.7
  114.2 3.8 %collective-permute-done = f32[6,32,512]{2,1,0:T(8,128)S(1)} collective-permute-done((f32[6,32,512]{2,1,0:T(8,128)S(1)}, f32[6,32,512]{2,1,0:T(8,128)S(1)}, u32[]{:S(2)}, u32[]{:S(2)}) %collective-permute-start) | collective-permute-done | bytes 393248 | tf_op jit(solution)/shard_map/ppermute | solution.py:108
  118.0 0.0 collective-permute-start.2
  118.0 1.0 collective-permute-done.1
  119.0 25.8 %collective-permute-start.3 = (f32[6,32,512]{2,1,0:T(8,128)S(1)}, f32[6,32,512]{2,1,0:T(8,128)S(1)}, u32[]{:S(2)}, u32[]{:S(2)}) collective-permute-start(f32[6,32,512]{2,1,0:T(8,128)S(1)} %get-tuple-element.15), channel_id=1, source_target_pairs={{0,8},{2,10},{4,12},{6,14},{8,0},{10,2},{12,4},{14,6},{1,9},{3,11}... | collective-permute-start | bytes 1179656 | tf_op jit(solution)/shard_map/ppermute | solution.py:108
  144.8 23.1 %collective-permute-done.2 = f32[6,32,512]{2,1,0:T(8,128)S(1)} collective-permute-done((f32[6,32,512]{2,1,0:T(8,128)S(1)}, f32[6,32,512]{2,1,0:T(8,128)S(1)}, u32[]{:S(2)}, u32[]{:S(2)}) %collective-permute-start.2) | collective-permute-done | bytes 393248 | tf_op jit(solution)/shard_map/ppermute | solution.py:108
  168.0 9.1 %collective-permute-done.3 = f32[6,32,512]{2,1,0:T(8,128)S(1)} collective-permute-done((f32[6,32,512]{2,1,0:T(8,128)S(1)}, f32[6,32,512]{2,1,0:T(8,128)S(1)}, u32[]{:S(2)}, u32[]{:S(2)}) %collective-permute-start.3) | collective-permute-done | bytes 393248 | tf_op jit(solution)/shard_map/ppermute | solution.py:108
  177.0 0.0 collective-permute-done.4
  177.1 0.0 collective-permute-done.6
  177.2 3.4 %copy.7 = f32[6,8,32,512]{3,1,2,0:T(8,128)} copy(f32[6,8,32,512]{3,2,1,0:T(8,128)S(1)} %bitcast.71) | data formatting | bytes 6291456
  180.6 8.2 %shard_map.47 = f32[96,16384]{1,0:T(8,128)} custom-call(f32[96,48]{1,0:T(8,128)} %reshape.162.w_ref, f32[48,16384]{1,0:T(8,128)} %bitcast.70), custom_call_target="tpu_custom_call" | custom-call | tf_op jit(solution)/shard_map/pallas_call | solution.py:72
  188.8 3.1 %convert.9 = bf16[96,16384]{1,0:T(8,128)(2,1)S(1)} convert(f32[96,16384]{1,0:T(8,128)} %shard_map.47) | non-fusion elementwise | flops 1572864 | bytes 9437184 | tf_op jit(solution)/shard_map/convert.6
  191.9 1.6 fusion.10
  193.6 0.2 copy.9
  193.8 0.1 collective-permute-start.7
  193.9 1.2 copy.10
  195.1 0.8 slice.57
  195.9 0.6 copy.8
  196.5 0.1 slice.55
  196.6 0.4 copy-done.1
  196.9 0.2 copy.15
  197.1 0.2 copy.14
  197.3 3.9 %collective-permute-start.12 = (bf16[2,6,32,512]{3,2,1,0:T(8,128)(2,1)S(1)}, bf16[2,6,32,512]{3,2,1,0:T(8,128)(2,1)S(1)}, u32[]{:S(2)}, u32[]{:S(2)}) collective-permute-start(bf16[2,6,32,512]{3,2,1,0:T(8,128)(2,1)S(1)} %bitcast.92), channel_id=1, source_target_pairs={{0,12},{2,14},{4,0},{6,2},{8,4},{10,6},{12,8},{14,10},{1,13},{3,15... | collective-permute-start | bytes 1179656 | tf_op jit(solution)/shard_map/ppermute | solution.py:127
  201.2 2.9 %collective-permute-start.13 = (bf16[2,6,32,512]{3,2,1,0:T(8,128)(2,1)S(1)}, bf16[2,6,32,512]{3,2,1,0:T(8,128)(2,1)S(1)}, u32[]{:S(2)}, u32[]{:S(2)}) collective-permute-start(bf16[2,6,32,512]{3,2,1,0:T(8,128)(2,1)S(1)} %bitcast.91), channel_id=1, source_target_pairs={{0,14},{2,0},{4,2},{6,4},{8,6},{10,8},{12,10},{14,12},{1,15},{3,1}... | collective-permute-start | bytes 1179656 | tf_op jit(solution)/shard_map/ppermute | solution.py:127
  204.0 0.2 copy.13
  204.2 0.1 collective-permute-start.11
  204.3 0.2 copy.12
  204.5 0.2 copy.11
  204.7 0.8 broadcast_in_dim.2
  205.5 0.1 constant_dynamic-update-slice_fusion
  205.6 3.2 %collective-permute-done.7 = bf16[2,6,32,512]{3,2,1,0:T(8,128)(2,1)} collective-permute-done((bf16[2,6,32,512]{3,2,1,0:T(8,128)(2,1)S(1)}, bf16[2,6,32,512]{3,2,1,0:T(8,128)(2,1)}, u32[]{:S(2)}, u32[]{:S(2)}) %collective-permute-start.7) | collective-permute-done | bytes 393248 | tf_op jit(solution)/shard_map/ppermute | solution.py:127
  208.8 1.1 convert_dynamic-update-slice_fusion.6
  209.9 0.1 collective-permute-done.8
  210.0 1.1 convert_dynamic-update-slice_fusion.5
  211.1 47.1 %collective-permute-done.9 = bf16[2,6,32,512]{3,2,1,0:T(8,128)(2,1)S(1)} collective-permute-done((bf16[2,6,32,512]{3,2,1,0:T(8,128)(2,1)S(1)}, bf16[2,6,32,512]{3,2,1,0:T(8,128)(2,1)S(1)}, u32[]{:S(2)}, u32[]{:S(2)}) %collective-permute-start.9) | collective-permute-done | bytes 393248 | tf_op jit(solution)/shard_map/ppermute | solution.py:127
  258.2 0.1 convert_dynamic-update-slice_fusion.4
  258.3 8.3 %collective-permute-done.10 = bf16[2,6,32,512]{3,2,1,0:T(8,128)(2,1)S(1)} collective-permute-done((bf16[2,6,32,512]{3,2,1,0:T(8,128)(2,1)S(1)}, bf16[2,6,32,512]{3,2,1,0:T(8,128)(2,1)S(1)}, u32[]{:S(2)}, u32[]{:S(2)}) %collective-permute-start.10) | collective-permute-done | bytes 393248 | tf_op jit(solution)/shard_map/ppermute | solution.py:127
  266.7 0.1 convert_dynamic-update-slice_fusion.3
  266.8 0.1 convert_dynamic-update-slice_fusion.2
  266.9 0.1 convert_dynamic-update-slice_fusion.1
  267.0 0.0 copy-start
  267.0 2.7 copy-done
  269.7 1.0 convert_dynamic-update-slice_fusion
  (25 shorter events, 0.4 us)
Async XLA Ops:
  6.5 56.3 %all-gather.2.cloned.1.call-start = ((), (), s32[]{:S(2)}) async-start(), calls=%async_computation.1 | async-start | bytes 4456448 | tf_op jit(solution)/shard_map/all_gather | solution.py:95
  8.4 92.7 %reduce-scatter.2.cloned.1.call-start = ((), (), s32[]{:S(2)}) async-start(), calls=%async_computation.2 | async-start | bytes 9437184 | tf_op jit(solution)/shard_map/reduce_scatter | solution.py:98
  103.1 14.8 %collective-permute-start = (f32[6,32,512]{2,1,0:T(8,128)S(1)}, f32[6,32,512]{2,1,0:T(8,128)S(1)}, u32[]{:S(2)}, u32[]{:S(2)}) collective-permute-start(f32[6,32,512]{2,1,0:T(8,128)S(1)} %get-tuple-element.18), channel_id=1, source_target_pairs={{0,2},{2,4},{4,6},{6,8},{8,10},{10,12},{12,14},{14,0},{1,3},{3,5},... | collective-permute-start | bytes 1179656 | tf_op jit(solution)/shard_map/ppermute | solution.py:108
  105.1 13.9 %collective-permute-start.1 = (f32[6,32,512]{2,1,0:T(8,128)S(1)}, f32[6,32,512]{2,1,0:T(8,128)S(1)}, u32[]{:S(2)}, u32[]{:S(2)}) collective-permute-start(f32[6,32,512]{2,1,0:T(8,128)S(1)} %get-tuple-element.17), channel_id=1, source_target_pairs={{0,4},{2,6},{4,8},{6,10},{8,12},{10,14},{12,0},{14,2},{1,5},{3,7},... | collective-permute-start | bytes 1179656 | tf_op jit(solution)/shard_map/ppermute | solution.py:108
  108.7 68.4 %collective-permute-start.6 = (f32[6,32,512]{2,1,0:T(8,128)S(1)}, f32[6,32,512]{2,1,0:T(8,128)S(1)}, u32[]{:S(2)}, u32[]{:S(2)}) collective-permute-start(f32[6,32,512]{2,1,0:T(8,128)S(1)} %get-tuple-element.12), channel_id=1, source_target_pairs={{0,14},{2,0},{4,2},{6,4},{8,6},{10,8},{12,10},{14,12},{1,15},{3,1}... | collective-permute-start | bytes 1179656 | tf_op jit(solution)/shard_map/ppermute | solution.py:108
  112.0 65.1 %collective-permute-start.5 = (f32[6,32,512]{2,1,0:T(8,128)S(1)}, f32[6,32,512]{2,1,0:T(8,128)S(1)}, u32[]{:S(2)}, u32[]{:S(2)}) collective-permute-start(f32[6,32,512]{2,1,0:T(8,128)S(1)} %get-tuple-element.13), channel_id=1, source_target_pairs={{0,12},{2,14},{4,0},{6,2},{8,4},{10,6},{12,8},{14,10},{1,13},{3,15... | collective-permute-start | bytes 1179656 | tf_op jit(solution)/shard_map/ppermute | solution.py:108
  112.3 64.7 %collective-permute-start.4 = (f32[6,32,512]{2,1,0:T(8,128)S(1)}, f32[6,32,512]{2,1,0:T(8,128)S(1)}, u32[]{:S(2)}, u32[]{:S(2)}) collective-permute-start(f32[6,32,512]{2,1,0:T(8,128)S(1)} %get-tuple-element.14), channel_id=1, source_target_pairs={{0,10},{2,12},{4,14},{6,0},{8,2},{10,4},{12,6},{14,8},{1,11},{3,13... | collective-permute-start | bytes 1179656 | tf_op jit(solution)/shard_map/ppermute | solution.py:108
  118.0 50.0 %collective-permute-start.2 = (f32[6,32,512]{2,1,0:T(8,128)S(1)}, f32[6,32,512]{2,1,0:T(8,128)S(1)}, u32[]{:S(2)}, u32[]{:S(2)}) collective-permute-start(f32[6,32,512]{2,1,0:T(8,128)S(1)} %get-tuple-element.16), channel_id=1, source_target_pairs={{0,6},{2,8},{4,10},{6,12},{8,14},{10,0},{12,2},{14,4},{1,7},{3,9},... | collective-permute-start | bytes 1179656 | tf_op jit(solution)/shard_map/ppermute | solution.py:108
  119.0 58.0 %collective-permute-start.3 = (f32[6,32,512]{2,1,0:T(8,128)S(1)}, f32[6,32,512]{2,1,0:T(8,128)S(1)}, u32[]{:S(2)}, u32[]{:S(2)}) collective-permute-start(f32[6,32,512]{2,1,0:T(8,128)S(1)} %get-tuple-element.15), channel_id=1, source_target_pairs={{0,8},{2,10},{4,12},{6,14},{8,0},{10,2},{12,4},{14,6},{1,9},{3,11}... | collective-permute-start | bytes 1179656 | tf_op jit(solution)/shard_map/ppermute | solution.py:108
  193.6 2.3 slice-start
  193.8 15.0 %collective-permute-start.7 = (bf16[2,6,32,512]{3,2,1,0:T(8,128)(2,1)S(1)}, bf16[2,6,32,512]{3,2,1,0:T(8,128)(2,1)}, u32[]{:S(2)}, u32[]{:S(2)}) collective-permute-start(bf16[2,6,32,512]{3,2,1,0:T(8,128)(2,1)S(1)} %bitcast.90), channel_id=1, source_target_pairs={{0,2},{2,4},{4,6},{6,8},{8,10},{10,12},{12,14},{14,0},{1,3},{3,5},... | collective-permute-start | bytes 1179656 | tf_op jit(solution)/shard_map/ppermute | solution.py:127
  195.9 14.1 %collective-permute-start.8 = (bf16[2,6,32,512]{3,2,1,0:T(8,128)(2,1)}, bf16[2,6,32,512]{3,2,1,0:T(8,128)(2,1)}, u32[]{:S(2)}, u32[]{:S(2)}) collective-permute-start(bf16[2,6,32,512]{3,2,1,0:T(8,128)(2,1)} %bitcast.33), channel_id=1, source_target_pairs={{0,4},{2,6},{4,8},{6,10},{8,12},{10,14},{12,0},{14,2},{1,5},{3,7},... | collective-permute-start | bytes 1179656 | tf_op jit(solution)/shard_map/ppermute | solution.py:127
  195.9 1.0 copy-start.1
  197.3 69.5 %collective-permute-start.12 = (bf16[2,6,32,512]{3,2,1,0:T(8,128)(2,1)S(1)}, bf16[2,6,32,512]{3,2,1,0:T(8,128)(2,1)S(1)}, u32[]{:S(2)}, u32[]{:S(2)}) collective-permute-start(bf16[2,6,32,512]{3,2,1,0:T(8,128)(2,1)S(1)} %bitcast.92), channel_id=1, source_target_pairs={{0,12},{2,14},{4,0},{6,2},{8,4},{10,6},{12,8},{14,10},{1,13},{3,15... | collective-permute-start | bytes 1179656 | tf_op jit(solution)/shard_map/ppermute | solution.py:127
  201.2 65.8 %collective-permute-start.13 = (bf16[2,6,32,512]{3,2,1,0:T(8,128)(2,1)S(1)}, bf16[2,6,32,512]{3,2,1,0:T(8,128)(2,1)S(1)}, u32[]{:S(2)}, u32[]{:S(2)}) collective-permute-start(bf16[2,6,32,512]{3,2,1,0:T(8,128)(2,1)S(1)} %bitcast.91), channel_id=1, source_target_pairs={{0,14},{2,0},{4,2},{6,4},{8,6},{10,8},{12,10},{14,12},{1,15},{3,1}... | collective-permute-start | bytes 1179656 | tf_op jit(solution)/shard_map/ppermute | solution.py:127
  204.2 62.5 %collective-permute-start.11 = (bf16[2,6,32,512]{3,2,1,0:T(8,128)(2,1)S(1)}, bf16[2,6,32,512]{3,2,1,0:T(8,128)(2,1)S(1)}, u32[]{:S(2)}, u32[]{:S(2)}) collective-permute-start(bf16[2,6,32,512]{3,2,1,0:T(8,128)(2,1)S(1)} %bitcast.93), channel_id=1, source_target_pairs={{0,10},{2,12},{4,14},{6,0},{8,2},{10,4},{12,6},{14,8},{1,11},{3,13... | collective-permute-start | bytes 1179656 | tf_op jit(solution)/shard_map/ppermute | solution.py:127
  208.8 49.5 %collective-permute-start.9 = (bf16[2,6,32,512]{3,2,1,0:T(8,128)(2,1)S(1)}, bf16[2,6,32,512]{3,2,1,0:T(8,128)(2,1)S(1)}, u32[]{:S(2)}, u32[]{:S(2)}) collective-permute-start(bf16[2,6,32,512]{3,2,1,0:T(8,128)(2,1)S(1)} %bitcast.95), channel_id=1, source_target_pairs={{0,6},{2,8},{4,10},{6,12},{8,14},{10,0},{12,2},{14,4},{1,7},{3,9},... | collective-permute-start | bytes 1179656 | tf_op jit(solution)/shard_map/ppermute | solution.py:127
  210.0 56.6 %collective-permute-start.10 = (bf16[2,6,32,512]{3,2,1,0:T(8,128)(2,1)S(1)}, bf16[2,6,32,512]{3,2,1,0:T(8,128)(2,1)S(1)}, u32[]{:S(2)}, u32[]{:S(2)}) collective-permute-start(bf16[2,6,32,512]{3,2,1,0:T(8,128)(2,1)S(1)} %bitcast.94), channel_id=1, source_target_pairs={{0,8},{2,10},{4,12},{6,14},{8,0},{10,2},{12,4},{14,6},{1,9},{3,11}... | collective-permute-start | bytes 1179656 | tf_op jit(solution)/shard_map/ppermute | solution.py:127
  267.0 2.7 copy-start
Sparse Core Ops, SparseCore 0:
  9.5 53.2 all-gather.1
  88.1 12.9 reduce-scatter.1

commit v11 on v10

--- a/solution.py
+++ b/solution.py
@@ -62,7 +62,7 @@
     acc = jnp.dot(wh, xh, preferred_element_type=jnp.float32)
     acc += jnp.dot(wh, xl, preferred_element_type=jnp.float32)
     acc += jnp.dot(wl, xh, preferred_element_type=jnp.float32)
-    o_ref[...] = acc
+    o_ref[...] = acc.astype(o_ref.dtype)
 
 
 def _dft(weights, x):
@@ -77,7 +77,7 @@
             pl.BlockSpec((k, tn), lambda i: (0, i)),
         ],
         out_specs=pl.BlockSpec((rows, tn), lambda i: (0, i)),
-        out_shape=jax.ShapeDtypeStruct((rows, n), jnp.float32),
+        out_shape=jax.ShapeDtypeStruct((rows, n), jnp.bfloat16),
         compiler_params=pltpu.CompilerParams(dimension_semantics=("arbitrary",)),
     )(weights, x)
 
@@ -123,9 +123,8 @@
     for t in range(nbd):
         piece = spec[t]
         if t:
-            piece = piece.astype(jnp.bfloat16)
             piece = lax.ppermute(piece, "blade", [(j, (j + t) % nbd) for j in range(nbd)])
-            piece = piece.astype(jnp.float32)
+        piece = piece.astype(jnp.float32)
         at = ((me - t) % nbd) * r
         out = lax.dynamic_update_slice(out, piece, (0, 0, at, 0))
     return out

time: 278 us -> 277 us (level)
  waiting for transfers between devices: 160 us -> 145 us
  starting transfers between devices: 40.4 us -> 54.5 us
    ppermute x7, waiting for transfers between devices: 58.8 us -> 44 us  [body(): lax.ppermute(piece, 'blade', [(j, (j + t) % nbd) for j in range(nbd)])]
    ppermute x7, starting transfers between devices: 6.85 us -> 21 us  [body(): lax.ppermute(piece, 'blade', [(j, (j + t) % nbd) for j in range(nbd)])]
    slice x0 -> x1, other arithmetic: none -> 3.86 us  [body(): piece = spec[t]]
    another operation x1 -> x0, other arithmetic: 3.13 us -> none
    unnamed x28 -> x26, local copies, waits for them, and re-layouts: 11.5 us -> 12.1 us
  transfers between devices with their start and end apart: 16 -> 16, of which waited for: 10 -> 9; matrix products, arithmetic and copies ran while one was open for 5% -> 5% of each run, Pallas kernels for 0% -> 0%
where the time goes in v11:
time: 277 us; the launch traced here: 276 us
  waiting for transfers between devices  145 us (52%)
  starting transfers between devices  54.5 us (20%)
  Pallas kernels  32.9 us (12%)
  local copies, waits for them, and re-layouts  21.1 us (8%)
  between operations  13.8 us (5%)
  other arithmetic  8.33 us (3%)
    all_gather x1, waiting for transfers between devices, body(): pt = lax.all_gather(mine, ('blade', 'dof'), axis=0, tiled=True)  51.7 us
    ppermute x7, waiting for transfers between devices, body(): lax.ppermute(piece, 'blade', [(j, (j + t) % nbd) for j in range(nbd)])  44 us
    ppermute x7, waiting for transfers between devices, body(): lax.ppermute(piece, 'blade', [(j, (j + s) % nbd) for j in range(nbd)])  36.9 us
    ppermute x7, starting transfers between devices, body(): lax.ppermute(piece, 'blade', [(j, (j + s) % nbd) for j in range(nbd)])  33.5 us
    pallas_call x1, Pallas kernels, _project(): pl.pallas_call(_project_kernel, grid_spec=grid_spec, out_shape=jax.ShapeD...  25.1 us
    ppermute x7, starting transfers between devices, body(): lax.ppermute(piece, 'blade', [(j, (j + t) % nbd) for j in range(nbd)])  21 us
    reduce_scatter x1, waiting for transfers between devices, body(): half = lax.psum_scatter(proj, 'dof', scatter_dimension=1, tiled=True)  12.8 us
    unnamed x26, local copies, waits for them, and re-layouts  12.1 us
  transfers between devices with their start and end apart: 16, of which 9 were waited for; matrix products, arithmetic and copies ran while one was open for 5% of the time, Pallas kernels for 0%

profile of v11, /device:TPU:0, one launch (start us, length us, event | category | flops | bytes accessed | tf_op | source)
XLA Modules:
  0.0 276.2 jit_solution(170513198328514762)
XLA Ops:
  6.5 1.8 copy.6
  8.3 0.0 all-gather.2.cloned.1.call-update
  8.4 0.0 reduce-scatter.2.cloned.1.call-start
  8.4 1.4 reshape.158.rows_ref
  9.8 1.4 reshape.159.cols_ref
  11.1 51.7 %all-gather.2.cloned.1.call-done.pt_ref = bf16[32,512,128]{2,1,0:T(8,128)(2,1)} async-done(((bf16[2,512,128]{2,1,0:T(8,128)(2,1)}), bf16[32,512,128]{2,1,0:T(8,128)(2,1)}) %all-gather.2.cloned.1.call-update) | async-done | bytes 4194320 | tf_op jit(solution)/shard_map/all_gather | solution.py:95
  62.8 25.1 %shard_map.46 = f32[6,512,512]{2,1,0:T(8,128)} custom-call(s32[192]{0:T(256)} %reshape.158.rows_ref, s32[192]{0:T(256)} %reshape.159.cols_ref, bf16[32,512,128]{2,1,0:T(8,128)(2,1)} %all-gather.2.cloned.1.call-done.pt_ref, bf16[6,32,128,128]{3,2,1,0:T(8,128)(2,1)} %s_ref.1), custom_call_target="tpu_custom_call" | custom-call | tf_op jit(solution)/shard_map/pallas_call | solution.py:44
  87.9 0.0 reduce-scatter.2.cloned.1.call-update
  88.1 0.1 iota_add_fusion
  88.1 0.1 add.218
  88.2 0.1 iota_add_fusion.1
  88.3 12.8 %reduce-scatter.2.cloned.1.call-done = f32[6,256,512]{2,1,0:T(8,128)} async-done(((f32[6,512,512]{2,1,0:T(8,128)}), f32[6,256,512]{2,1,0:T(8,128)}) %reduce-scatter.2.cloned.1.call-update) | async-done | bytes 3145744 | tf_op jit(solution)/shard_map/reduce_scatter | solution.py:98
  101.1 2.0 dynamic-slice_bitcast_fusion
  103.1 1.8 collective-permute-start
  104.9 0.2 fusion.4
  105.1 1.5 collective-permute-start.1
  106.6 0.6 pad_maximum_fusion
  107.3 1.5 reshape.157.w_ref
  108.7 3.2 %collective-permute-start.6 = (f32[6,32,512]{2,1,0:T(8,128)S(1)}, f32[6,32,512]{2,1,0:T(8,128)S(1)}, u32[]{:S(2)}, u32[]{:S(2)}) collective-permute-start(f32[6,32,512]{2,1,0:T(8,128)S(1)} %get-tuple-element.13), channel_id=1, source_target_pairs={{0,14},{2,0},{4,2},{6,4},{8,6},{10,8},{12,10},{14,12},{1,15},{3,1}... | collective-permute-start | bytes 1179656 | tf_op jit(solution)/shard_map/ppermute | solution.py:108
  112.0 0.3 collective-permute-start.5
  112.3 0.9 collective-permute-start.4
  113.2 1.0 bitcast_dynamic-update-slice_fusion.7
  114.2 3.8 %collective-permute-done = f32[6,32,512]{2,1,0:T(8,128)S(1)} collective-permute-done((f32[6,32,512]{2,1,0:T(8,128)S(1)}, f32[6,32,512]{2,1,0:T(8,128)S(1)}, u32[]{:S(2)}, u32[]{:S(2)}) %collective-permute-start) | collective-permute-done | bytes 393248 | tf_op jit(solution)/shard_map/ppermute | solution.py:108
  118.0 0.0 collective-permute-start.2
  118.0 1.0 collective-permute-done.1
  119.0 25.8 %collective-permute-start.3 = (f32[6,32,512]{2,1,0:T(8,128)S(1)}, f32[6,32,512]{2,1,0:T(8,128)S(1)}, u32[]{:S(2)}, u32[]{:S(2)}) collective-permute-start(f32[6,32,512]{2,1,0:T(8,128)S(1)} %get-tuple-element.16), channel_id=1, source_target_pairs={{0,8},{2,10},{4,12},{6,14},{8,0},{10,2},{12,4},{14,6},{1,9},{3,11}... | collective-permute-start | bytes 1179656 | tf_op jit(solution)/shard_map/ppermute | solution.py:108
  144.8 23.1 %collective-permute-done.2 = f32[6,32,512]{2,1,0:T(8,128)S(1)} collective-permute-done((f32[6,32,512]{2,1,0:T(8,128)S(1)}, f32[6,32,512]{2,1,0:T(8,128)S(1)}, u32[]{:S(2)}, u32[]{:S(2)}) %collective-permute-start.2) | collective-permute-done | bytes 393248 | tf_op jit(solution)/shard_map/ppermute | solution.py:108
  168.0 9.1 %collective-permute-done.3 = f32[6,32,512]{2,1,0:T(8,128)S(1)} collective-permute-done((f32[6,32,512]{2,1,0:T(8,128)S(1)}, f32[6,32,512]{2,1,0:T(8,128)S(1)}, u32[]{:S(2)}, u32[]{:S(2)}) %collective-permute-start.3) | collective-permute-done | bytes 393248 | tf_op jit(solution)/shard_map/ppermute | solution.py:108
  177.0 0.0 collective-permute-done.4
  177.1 0.0 collective-permute-done.6
  177.2 3.5 %copy.7 = f32[6,8,32,512]{3,1,2,0:T(8,128)} copy(f32[6,8,32,512]{3,2,1,0:T(8,128)S(1)} %bitcast.71) | data formatting | bytes 6291456
  180.6 7.7 %shard_map.47 = bf16[96,16384]{1,0:T(8,128)(2,1)} custom-call(f32[96,48]{1,0:T(8,128)} %reshape.157.w_ref, f32[48,16384]{1,0:T(8,128)} %bitcast.69), custom_call_target="tpu_custom_call" | custom-call | tf_op jit(solution)/shard_map/pallas_call | solution.py:72
  188.4 3.9 %fusion.10 = (bf16[12,16384]{1,0:T(8,128)(2,1)}, bf16[12,16384]{1,0:T(8,128)(2,1)S(1)}, bf16[12,16384]{1,0:T(8,128)(2,1)S(1)}, bf16[12,16384]{1,0:T(8,128)(2,1)S...) fusion(bf16[96,16384]{1,0:T(8,128)(2,1)} %shard_map.47), kind=kLoop, calls=%fused_computation.46 | loop fusion | flops 196608 | bytes 6684672 | tf_op jit(solution)/shard_map/slice | solution.py:124
  192.3 0.2 copy.9
  192.5 0.1 collective-permute-start.7
  192.5 1.2 copy.10
  193.7 0.8 slice.50
  194.5 0.0 collective-permute-start.8
  194.5 1.2 copy.15
  195.8 0.2 copy.14
  196.0 3.9 %collective-permute-start.12 = (bf16[2,6,32,512]{3,2,1,0:T(8,128)(2,1)S(1)}, bf16[2,6,32,512]{3,2,1,0:T(8,128)(2,1)S(1)}, u32[]{:S(2)}, u32[]{:S(2)}) collective-permute-start(bf16[2,6,32,512]{3,2,1,0:T(8,128)(2,1)S(1)} %bitcast.92), channel_id=1, source_target_pairs={{0,12},{2,14},{4,0},{6,2},{8,4},{10,6},{12,8},{14,10},{1,13},{3,15... | collective-permute-start | bytes 1179656 | tf_op jit(solution)/shard_map/ppermute | solution.py:126
  199.8 2.9 %collective-permute-start.13 = (bf16[2,6,32,512]{3,2,1,0:T(8,128)(2,1)S(1)}, bf16[2,6,32,512]{3,2,1,0:T(8,128)(2,1)S(1)}, u32[]{:S(2)}, u32[]{:S(2)}) collective-permute-start(bf16[2,6,32,512]{3,2,1,0:T(8,128)(2,1)S(1)} %bitcast.91), channel_id=1, source_target_pairs={{0,14},{2,0},{4,2},{6,4},{8,6},{10,8},{12,10},{14,12},{1,15},{3,1}... | collective-permute-start | bytes 1179656 | tf_op jit(solution)/shard_map/ppermute | solution.py:126
  202.7 0.2 copy.13
  202.9 0.1 collective-permute-start.11
  203.0 0.2 copy.12
  203.2 0.2 copy.11
  203.4 0.6 copy.8
  204.0 0.1 slice.48
  204.1 0.8 broadcast_in_dim.2
  204.9 0.1 constant_dynamic-update-slice_fusion
  204.9 2.5 collective-permute-done.7
  207.5 0.4 collective-permute-start.9
  207.9 1.1 convert_dynamic-update-slice_fusion.6
  209.0 13.7 %collective-permute-start.10 = (bf16[2,6,32,512]{3,2,1,0:T(8,128)(2,1)S(1)}, bf16[2,6,32,512]{3,2,1,0:T(8,128)(2,1)S(1)}, u32[]{:S(2)}, u32[]{:S(2)}) collective-permute-start(bf16[2,6,32,512]{3,2,1,0:T(8,128)(2,1)S(1)} %bitcast.94), channel_id=1, source_target_pairs={{0,8},{2,10},{4,12},{6,14},{8,0},{10,2},{12,4},{14,6},{1,9},{3,11}... | collective-permute-start | bytes 1179656 | tf_op jit(solution)/shard_map/ppermute | solution.py:126
  222.7 1.1 convert_dynamic-update-slice_fusion.5
  223.8 33.2 %collective-permute-done.9 = bf16[2,6,32,512]{3,2,1,0:T(8,128)(2,1)S(1)} collective-permute-done((bf16[2,6,32,512]{3,2,1,0:T(8,128)(2,1)S(1)}, bf16[2,6,32,512]{3,2,1,0:T(8,128)(2,1)S(1)}, u32[]{:S(2)}, u32[]{:S(2)}) %collective-permute-start.9) | collective-permute-done | bytes 393248 | tf_op jit(solution)/shard_map/ppermute | solution.py:126
  256.9 0.1 convert_dynamic-update-slice_fusion.4
  257.0 8.3 %collective-permute-done.10 = bf16[2,6,32,512]{3,2,1,0:T(8,128)(2,1)S(1)} collective-permute-done((bf16[2,6,32,512]{3,2,1,0:T(8,128)(2,1)S(1)}, bf16[2,6,32,512]{3,2,1,0:T(8,128)(2,1)S(1)}, u32[]{:S(2)}, u32[]{:S(2)}) %collective-permute-start.10) | collective-permute-done | bytes 393248 | tf_op jit(solution)/shard_map/ppermute | solution.py:126
  265.3 0.1 convert_dynamic-update-slice_fusion.3
  265.4 0.1 convert_dynamic-update-slice_fusion.2
  265.5 0.1 convert_dynamic-update-slice_fusion.1
  265.6 0.0 copy-start
  265.7 2.7 copy-done
  268.3 1.0 convert_dynamic-update-slice_fusion
  (20 shorter events, 0.4 us)
Async XLA Ops:
  6.5 56.3 %all-gather.2.cloned.1.call-start = ((), (), s32[]{:S(2)}) async-start(), calls=%async_computation.1 | async-start | bytes 4456448 | tf_op jit(solution)/shard_map/all_gather | solution.py:95
  8.4 92.7 %reduce-scatter.2.cloned.1.call-start = ((), (), s32[]{:S(2)}) async-start(), calls=%async_computation.2 | async-start | bytes 9437184 | tf_op jit(solution)/shard_map/reduce_scatter | solution.py:98
  103.1 14.8 %collective-permute-start = (f32[6,32,512]{2,1,0:T(8,128)S(1)}, f32[6,32,512]{2,1,0:T(8,128)S(1)}, u32[]{:S(2)}, u32[]{:S(2)}) collective-permute-start(f32[6,32,512]{2,1,0:T(8,128)S(1)} %get-tuple-element.19), channel_id=1, source_target_pairs={{0,2},{2,4},{4,6},{6,8},{8,10},{10,12},{12,14},{14,0},{1,3},{3,5},... | collective-permute-start | bytes 1179656 | tf_op jit(solution)/shard_map/ppermute | solution.py:108
  105.1 13.9 %collective-permute-start.1 = (f32[6,32,512]{2,1,0:T(8,128)S(1)}, f32[6,32,512]{2,1,0:T(8,128)S(1)}, u32[]{:S(2)}, u32[]{:S(2)}) collective-permute-start(f32[6,32,512]{2,1,0:T(8,128)S(1)} %get-tuple-element.18), channel_id=1, source_target_pairs={{0,4},{2,6},{4,8},{6,10},{8,12},{10,14},{12,0},{14,2},{1,5},{3,7},... | collective-permute-start | bytes 1179656 | tf_op jit(solution)/shard_map/ppermute | solution.py:108
  108.7 68.4 %collective-permute-start.6 = (f32[6,32,512]{2,1,0:T(8,128)S(1)}, f32[6,32,512]{2,1,0:T(8,128)S(1)}, u32[]{:S(2)}, u32[]{:S(2)}) collective-permute-start(f32[6,32,512]{2,1,0:T(8,128)S(1)} %get-tuple-element.13), channel_id=1, source_target_pairs={{0,14},{2,0},{4,2},{6,4},{8,6},{10,8},{12,10},{14,12},{1,15},{3,1}... | collective-permute-start | bytes 1179656 | tf_op jit(solution)/shard_map/ppermute | solution.py:108
  112.0 65.1 %collective-permute-start.5 = (f32[6,32,512]{2,1,0:T(8,128)S(1)}, f32[6,32,512]{2,1,0:T(8,128)S(1)}, u32[]{:S(2)}, u32[]{:S(2)}) collective-permute-start(f32[6,32,512]{2,1,0:T(8,128)S(1)} %get-tuple-element.14), channel_id=1, source_target_pairs={{0,12},{2,14},{4,0},{6,2},{8,4},{10,6},{12,8},{14,10},{1,13},{3,15... | collective-permute-start | bytes 1179656 | tf_op jit(solution)/shard_map/ppermute | solution.py:108
  112.3 64.7 %collective-permute-start.4 = (f32[6,32,512]{2,1,0:T(8,128)S(1)}, f32[6,32,512]{2,1,0:T(8,128)S(1)}, u32[]{:S(2)}, u32[]{:S(2)}) collective-permute-start(f32[6,32,512]{2,1,0:T(8,128)S(1)} %get-tuple-element.15), channel_id=1, source_target_pairs={{0,10},{2,12},{4,14},{6,0},{8,2},{10,4},{12,6},{14,8},{1,11},{3,13... | collective-permute-start | bytes 1179656 | tf_op jit(solution)/shard_map/ppermute | solution.py:108
  118.0 50.0 %collective-permute-start.2 = (f32[6,32,512]{2,1,0:T(8,128)S(1)}, f32[6,32,512]{2,1,0:T(8,128)S(1)}, u32[]{:S(2)}, u32[]{:S(2)}) collective-permute-start(f32[6,32,512]{2,1,0:T(8,128)S(1)} %get-tuple-element.17), channel_id=1, source_target_pairs={{0,6},{2,8},{4,10},{6,12},{8,14},{10,0},{12,2},{14,4},{1,7},{3,9},... | collective-permute-start | bytes 1179656 | tf_op jit(solution)/shard_map/ppermute | solution.py:108
  119.0 58.0 %collective-permute-start.3 = (f32[6,32,512]{2,1,0:T(8,128)S(1)}, f32[6,32,512]{2,1,0:T(8,128)S(1)}, u32[]{:S(2)}, u32[]{:S(2)}) collective-permute-start(f32[6,32,512]{2,1,0:T(8,128)S(1)} %get-tuple-element.16), channel_id=1, source_target_pairs={{0,8},{2,10},{4,12},{6,14},{8,0},{10,2},{12,4},{14,6},{1,9},{3,11}... | collective-permute-start | bytes 1179656 | tf_op jit(solution)/shard_map/ppermute | solution.py:108
  192.5 15.0 %collective-permute-start.7 = (bf16[2,6,32,512]{3,2,1,0:T(8,128)(2,1)S(1)}, bf16[2,6,32,512]{3,2,1,0:T(8,128)(2,1)}, u32[]{:S(2)}, u32[]{:S(2)}) collective-permute-start(bf16[2,6,32,512]{3,2,1,0:T(8,128)(2,1)S(1)} %bitcast.90), channel_id=1, source_target_pairs={{0,2},{2,4},{4,6},{6,8},{8,10},{10,12},{12,14},{14,0},{1,3},{3,5},... | collective-permute-start | bytes 1179656 | tf_op jit(solution)/shard_map/ppermute | solution.py:126
  194.5 14.5 %collective-permute-start.8 = (bf16[2,6,32,512]{3,2,1,0:T(8,128)(2,1)}, bf16[2,6,32,512]{3,2,1,0:T(8,128)(2,1)}, u32[]{:S(2)}, u32[]{:S(2)}) collective-permute-start(bf16[2,6,32,512]{3,2,1,0:T(8,128)(2,1)} %bitcast.33), channel_id=1, source_target_pairs={{0,4},{2,6},{4,8},{6,10},{8,12},{10,14},{12,0},{14,2},{1,5},{3,7},... | collective-permute-start | bytes 1179656 | tf_op jit(solution)/shard_map/ppermute | solution.py:126
  196.0 69.6 %collective-permute-start.12 = (bf16[2,6,32,512]{3,2,1,0:T(8,128)(2,1)S(1)}, bf16[2,6,32,512]{3,2,1,0:T(8,128)(2,1)S(1)}, u32[]{:S(2)}, u32[]{:S(2)}) collective-permute-start(bf16[2,6,32,512]{3,2,1,0:T(8,128)(2,1)S(1)} %bitcast.92), channel_id=1, source_target_pairs={{0,12},{2,14},{4,0},{6,2},{8,4},{10,6},{12,8},{14,10},{1,13},{3,15... | collective-permute-start | bytes 1179656 | tf_op jit(solution)/shard_map/ppermute | solution.py:126
  199.8 65.8 %collective-permute-start.13 = (bf16[2,6,32,512]{3,2,1,0:T(8,128)(2,1)S(1)}, bf16[2,6,32,512]{3,2,1,0:T(8,128)(2,1)S(1)}, u32[]{:S(2)}, u32[]{:S(2)}) collective-permute-start(bf16[2,6,32,512]{3,2,1,0:T(8,128)(2,1)S(1)} %bitcast.91), channel_id=1, source_target_pairs={{0,14},{2,0},{4,2},{6,4},{8,6},{10,8},{12,10},{14,12},{1,15},{3,1}... | collective-permute-start | bytes 1179656 | tf_op jit(solution)/shard_map/ppermute | solution.py:126
  202.9 62.5 %collective-permute-start.11 = (bf16[2,6,32,512]{3,2,1,0:T(8,128)(2,1)S(1)}, bf16[2,6,32,512]{3,2,1,0:T(8,128)(2,1)S(1)}, u32[]{:S(2)}, u32[]{:S(2)}) collective-permute-start(bf16[2,6,32,512]{3,2,1,0:T(8,128)(2,1)S(1)} %bitcast.93), channel_id=1, source_target_pairs={{0,10},{2,12},{4,14},{6,0},{8,2},{10,4},{12,6},{14,8},{1,11},{3,13... | collective-permute-start | bytes 1179656 | tf_op jit(solution)/shard_map/ppermute | solution.py:126
  207.5 49.5 %collective-permute-start.9 = (bf16[2,6,32,512]{3,2,1,0:T(8,128)(2,1)S(1)}, bf16[2,6,32,512]{3,2,1,0:T(8,128)(2,1)S(1)}, u32[]{:S(2)}, u32[]{:S(2)}) collective-permute-start(bf16[2,6,32,512]{3,2,1,0:T(8,128)(2,1)S(1)} %bitcast.95), channel_id=1, source_target_pairs={{0,6},{2,8},{4,10},{6,12},{8,14},{10,0},{12,2},{14,4},{1,7},{3,9},... | collective-permute-start | bytes 1179656 | tf_op jit(solution)/shard_map/ppermute | solution.py:126
  209.0 56.3 %collective-permute-start.10 = (bf16[2,6,32,512]{3,2,1,0:T(8,128)(2,1)S(1)}, bf16[2,6,32,512]{3,2,1,0:T(8,128)(2,1)S(1)}, u32[]{:S(2)}, u32[]{:S(2)}) collective-permute-start(bf16[2,6,32,512]{3,2,1,0:T(8,128)(2,1)S(1)} %bitcast.94), channel_id=1, source_target_pairs={{0,8},{2,10},{4,12},{6,14},{8,0},{10,2},{12,4},{14,6},{1,9},{3,11}... | collective-permute-start | bytes 1179656 | tf_op jit(solution)/shard_map/ppermute | solution.py:126
  265.6 2.7 copy-start
Sparse Core Ops, SparseCore 0:
  9.5 53.2 all-gather.1
  88.1 12.9 reduce-scatter.1

commit v12 on v10

--- a/solution.py
+++ b/solution.py
@@ -95,7 +95,14 @@
     pt = lax.all_gather(mine, ("blade", "dof"), axis=0, tiled=True)
     proj = _project(pt, stiffness, block_rows.reshape(-1), block_cols.reshape(-1))
 
-    half = lax.psum_scatter(proj, "dof", scatter_dimension=1, tiled=True)
+    if lax.axis_size("dof") == 2:
+        rows_half = modes // 2
+        d = lax.axis_index("dof")
+        mine = lax.dynamic_slice_in_dim(proj, d * rows_half, rows_half, axis=1)
+        other = lax.dynamic_slice_in_dim(proj, (1 - d) * rows_half, rows_half, axis=1)
+        half = mine + lax.ppermute(other, "dof", [(0, 1), (1, 0)])
+    else:
+        half = lax.psum_scatter(proj, "dof", scatter_dimension=1, tiled=True)
     me = lax.axis_index("blade")
     rows_half = half.shape[1]
     r = rows_half // nbd

time: 278 us -> 276 us (level)
  waiting for transfers between devices: 160 us -> 155 us
  other arithmetic: 7.6 us -> 11.2 us
  starting transfers between devices: 40.4 us -> 37.5 us
    reduce_scatter x1 -> x0, waiting for transfers between devices: 12.8 us -> none  [body(): half = lax.psum_scatter(proj, 'dof', scatter_dimension=1, tiled=True)]
    ppermute x0 -> x1, waiting for transfers between devices: none -> 5.3 us  [body(): half = mine + lax.ppermute(other, 'dof', [(0, 1), (1, 0)])]
    add x0 -> x1, other arithmetic: none -> 3.59 us  [body(): half = mine + lax.ppermute(other, 'dof', [(0, 1), (1, 0)])]
    ppermute x7, starting transfers between devices: 33.5 us -> 30.2 us  [body(): lax.ppermute(piece, 'blade', [(j, (j + s) % nbd) for j in range(nbd)])]
  transfers between devices with their start and end apart: 16 -> 16, of which waited for: 10 -> 9; matrix products, arithmetic and copies ran while one was open for 5% -> 5% of each run, Pallas kernels for 0% -> 0%
where the time goes in v12:
time: 276 us; the launch traced here: 275 us
  waiting for transfers between devices  155 us (56%)
  starting transfers between devices  37.5 us (14%)
  Pallas kernels  33.3 us (12%)
  local copies, waits for them, and re-layouts  24.6 us (9%)
  between operations  13.7 us (5%)
  other arithmetic  11.2 us (4%)
    ppermute x7, waiting for transfers between devices, body(): lax.ppermute(piece, 'blade', [(j, (j + t) % nbd) for j in range(nbd)])  59.5 us
    all_gather x1, waiting for transfers between devices, body(): pt = lax.all_gather(mine, ('blade', 'dof'), axis=0, tiled=True)  51.8 us
    ppermute x7, waiting for transfers between devices, body(): lax.ppermute(piece, 'blade', [(j, (j + s) % nbd) for j in range(nbd)])  38.1 us
    ppermute x7, starting transfers between devices, body(): lax.ppermute(piece, 'blade', [(j, (j + s) % nbd) for j in range(nbd)])  30.2 us
    pallas_call x1, Pallas kernels, _project(): pl.pallas_call(_project_kernel, grid_spec=grid_spec, out_shape=jax.ShapeD...  25.1 us
    unnamed x28, local copies, waits for them, and re-layouts  12.4 us
    pallas_call x1, Pallas kernels, _dft(): pl.pallas_call(_dft_kernel, grid=(n // tn,), in_specs=[pl.BlockSpec((rows...  8.2 us
    ppermute x7, starting transfers between devices, body(): lax.ppermute(piece, 'blade', [(j, (j + t) % nbd) for j in range(nbd)])  6.92 us
  transfers between devices with their start and end apart: 16, of which 9 were waited for; matrix products, arithmetic and copies ran while one was open for 5% of the time, Pallas kernels for 0%

profile of v12, /device:TPU:0, one launch (start us, length us, event | category | flops | bytes accessed | tf_op | source)
XLA Modules:
  0.0 275.0 jit_solution(1286034983820418660)
XLA Ops:
  6.5 1.8 copy.6
  8.3 0.0 all-gather.2.cloned.1.call-update
  8.4 1.3 reshape.163.rows_ref
  9.7 1.3 reshape.164.cols_ref
  11.0 51.8 %all-gather.2.cloned.1.call-done.pt_ref = bf16[32,512,128]{2,1,0:T(8,128)(2,1)} async-done(((bf16[2,512,128]{2,1,0:T(8,128)(2,1)}), bf16[32,512,128]{2,1,0:T(8,128)(2,1)}) %all-gather.2.cloned.1.call-update) | async-done | bytes 4194320 | tf_op jit(solution)/shard_map/all_gather | solution.py:95
  62.8 25.1 %shard_map.46 = f32[6,512,512]{2,1,0:T(8,128)} custom-call(s32[192]{0:T(256)} %reshape.163.rows_ref, s32[192]{0:T(256)} %reshape.164.cols_ref, bf16[32,512,128]{2,1,0:T(8,128)(2,1)} %all-gather.2.cloned.1.call-done.pt_ref, bf16[6,32,128,128]{3,2,1,0:T(8,128)(2,1)} %s_ref.1), custom_call_target="tpu_custom_call" | custom-call | tf_op jit(solution)/shard_map/pallas_call | solution.py:44
  87.9 2.2 constant_dynamic-slice_fusion
  90.1 0.3 collective-permute-start
  90.5 0.1 iota_add_fusion
  90.5 0.1 add.225
  90.6 0.1 iota_add_fusion.1
  90.7 5.3 %collective-permute-done = f32[6,256,512]{2,1,0:T(8,128)} collective-permute-done((f32[6,256,512]{2,1,0:T(8,128)S(1)}, f32[6,256,512]{2,1,0:T(8,128)}, u32[]{:S(2)}, u32[]{:S(2)}) %collective-permute-start) | collective-permute-done | bytes 3145760 | tf_op jit(solution)/shard_map/ppermute | solution.py:103
  96.0 3.6 %dynamic-slice_add_fusion = f32[6,256,512]{2,1,0:T(8,128)S(1)} fusion(f32[6,256,512]{2,1,0:T(8,128)} %collective-permute-done, f32[6,512,512]{2,1,0:T(8,128)} %shard_map.46, s32[]{:T(128)S(6)} %select_n.158), kind=kLoop, calls=%fused_computation | loop fusion | flops 786432 | bytes 9437188 | tf_op jit(solution)/shard_map/add | solution.py:103
  99.6 1.5 dynamic-slice_bitcast_fusion
  101.0 0.6 collective-permute-start.1
  101.6 0.2 fusion.4
  101.8 1.5 collective-permute-start.2
  103.4 0.6 pad_maximum_fusion
  104.0 1.5 reshape.162.w_ref
  105.5 4.2 %collective-permute-start.7 = (f32[6,32,512]{2,1,0:T(8,128)S(1)}, f32[6,32,512]{2,1,0:T(8,128)S(1)}, u32[]{:S(2)}, u32[]{:S(2)}) collective-permute-start(f32[6,32,512]{2,1,0:T(8,128)S(1)} %get-tuple-element.12), channel_id=1, source_target_pairs={{0,14},{2,0},{4,2},{6,4},{8,6},{10,8},{12,10},{14,12},{1,15},{3,1}... | collective-permute-start | bytes 1179656 | tf_op jit(solution)/shard_map/ppermute | solution.py:115
  109.6 0.5 collective-permute-start.6
  110.2 6.0 %collective-permute-done.1 = f32[6,32,512]{2,1,0:T(8,128)} collective-permute-done((f32[6,32,512]{2,1,0:T(8,128)}, f32[6,32,512]{2,1,0:T(8,128)}, u32[]{:S(2)}, u32[]{:S(2)}) %collective-permute-start.1) | collective-permute-done | bytes 393248 | tf_op jit(solution)/shard_map/ppermute | solution.py:115
  116.2 0.0 collective-permute-start.3
  116.2 1.0 bitcast_dynamic-update-slice_fusion.6
  117.2 23.4 %collective-permute-start.4 = (f32[6,32,512]{2,1,0:T(8,128)}, f32[6,32,512]{2,1,0:T(8,128)S(1)}, u32[]{:S(2)}, u32[]{:S(2)}) collective-permute-start(f32[6,32,512]{2,1,0:T(8,128)} %get-tuple-element.15), channel_id=1, source_target_pairs={{0,8},{2,10},{4,12},{6,14},{8,0},{10,2},{12,4},{14,6},{1,9},{3,11}... | collective-permute-start | bytes 1179656 | tf_op jit(solution)/shard_map/ppermute | solution.py:115
  140.6 1.0 bitcast_dynamic-update-slice_fusion.5
  141.7 24.2 %collective-permute-done.3 = f32[6,32,512]{2,1,0:T(8,128)S(1)} collective-permute-done((f32[6,32,512]{2,1,0:T(8,128)}, f32[6,32,512]{2,1,0:T(8,128)S(1)}, u32[]{:S(2)}, u32[]{:S(2)}) %collective-permute-start.3) | collective-permute-done | bytes 393248 | tf_op jit(solution)/shard_map/ppermute | solution.py:115
  165.9 7.9 %collective-permute-done.4 = f32[6,32,512]{2,1,0:T(8,128)S(1)} collective-permute-done((f32[6,32,512]{2,1,0:T(8,128)}, f32[6,32,512]{2,1,0:T(8,128)S(1)}, u32[]{:S(2)}, u32[]{:S(2)}) %collective-permute-start.4) | collective-permute-done | bytes 393248 | tf_op jit(solution)/shard_map/ppermute | solution.py:115
  173.9 0.0 collective-permute-done.5
  174.0 0.0 collective-permute-done.7
  174.0 3.4 %copy.7 = f32[6,8,32,512]{3,1,2,0:T(8,128)} copy(f32[6,8,32,512]{3,2,1,0:T(8,128)S(1)} %bitcast.73) | data formatting | bytes 6291456
  177.5 8.2 %shard_map.47 = f32[96,16384]{1,0:T(8,128)} custom-call(f32[96,48]{1,0:T(8,128)} %reshape.162.w_ref, f32[48,16384]{1,0:T(8,128)} %bitcast.72), custom_call_target="tpu_custom_call" | custom-call | tf_op jit(solution)/shard_map/pallas_call | solution.py:72
  185.7 3.1 %convert.9 = bf16[96,16384]{1,0:T(8,128)(2,1)S(1)} convert(f32[96,16384]{1,0:T(8,128)} %shard_map.47) | non-fusion elementwise | flops 1572864 | bytes 9437184 | tf_op jit(solution)/shard_map/convert.6
  188.8 1.6 fusion.10
  190.4 0.2 copy.9
  190.6 1.0 collective-permute-start.8
  191.6 1.2 copy.10
  192.8 0.8 slice.57
  193.6 0.6 copy.8
  194.2 0.1 slice.55
  194.3 0.4 copy-done.1
  194.6 0.2 copy.15
  194.8 0.2 copy.14
  195.0 3.9 %collective-permute-start.13 = (bf16[2,6,32,512]{3,2,1,0:T(8,128)(2,1)S(1)}, bf16[2,6,32,512]{3,2,1,0:T(8,128)(2,1)S(1)}, u32[]{:S(2)}, u32[]{:S(2)}) collective-permute-start(bf16[2,6,32,512]{3,2,1,0:T(8,128)(2,1)S(1)} %bitcast.92), channel_id=1, source_target_pairs={{0,12},{2,14},{4,0},{6,2},{8,4},{10,6},{12,8},{14,10},{1,13},{3,15... | collective-permute-start | bytes 1179656 | tf_op jit(solution)/shard_map/ppermute | solution.py:134
  198.9 2.0 collective-permute-start.14
  200.9 0.2 copy.13
  201.1 0.1 collective-permute-start.12
  201.2 0.2 copy.12
  201.4 0.2 copy.11
  201.6 0.8 broadcast_in_dim.2
  202.4 0.1 constant_dynamic-update-slice_fusion
  202.5 3.2 %collective-permute-done.8 = bf16[2,6,32,512]{3,2,1,0:T(8,128)(2,1)} collective-permute-done((bf16[2,6,32,512]{3,2,1,0:T(8,128)(2,1)S(1)}, bf16[2,6,32,512]{3,2,1,0:T(8,128)(2,1)}, u32[]{:S(2)}, u32[]{:S(2)}) %collective-permute-start.8) | collective-permute-done | bytes 393248 | tf_op jit(solution)/shard_map/ppermute | solution.py:134
  205.7 1.1 convert_dynamic-update-slice_fusion.6
  206.8 1.0 collective-permute-done.9
  207.7 1.1 convert_dynamic-update-slice_fusion.5
  208.8 46.3 %collective-permute-done.10 = bf16[2,6,32,512]{3,2,1,0:T(8,128)(2,1)S(1)} collective-permute-done((bf16[2,6,32,512]{3,2,1,0:T(8,128)(2,1)S(1)}, bf16[2,6,32,512]{3,2,1,0:T(8,128)(2,1)S(1)}, u32[]{:S(2)}, u32[]{:S(2)}) %collective-permute-start.10) | collective-permute-done | bytes 393248 | tf_op jit(solution)/shard_map/ppermute | solution.py:134
  255.1 0.1 convert_dynamic-update-slice_fusion.4
  255.2 9.0 %collective-permute-done.11 = bf16[2,6,32,512]{3,2,1,0:T(8,128)(2,1)S(1)} collective-permute-done((bf16[2,6,32,512]{3,2,1,0:T(8,128)(2,1)S(1)}, bf16[2,6,32,512]{3,2,1,0:T(8,128)(2,1)S(1)}, u32[]{:S(2)}, u32[]{:S(2)}) %collective-permute-start.11) | collective-permute-done | bytes 393248 | tf_op jit(solution)/shard_map/ppermute | solution.py:134
  264.2 0.1 convert_dynamic-update-slice_fusion.3
  264.3 0.1 convert_dynamic-update-slice_fusion.2
  264.4 0.1 convert_dynamic-update-slice_fusion.1
  264.5 0.0 copy-start
  264.5 2.7 copy-done
  267.2 1.0 convert_dynamic-update-slice_fusion
  (26 shorter events, 0.4 us)
Async XLA Ops:
  6.5 56.3 %all-gather.2.cloned.1.call-start = ((), (), s32[]{:S(2)}) async-start(), calls=%async_computation | async-start | bytes 4456448 | tf_op jit(solution)/shard_map/all_gather | solution.py:95
  90.1 5.9 %collective-permute-start = (f32[6,256,512]{2,1,0:T(8,128)S(1)}, f32[6,256,512]{2,1,0:T(8,128)}, u32[]{:S(2)}, u32[]{:S(2)}) collective-permute-start(f32[6,256,512]{2,1,0:T(8,128)S(1)} %constant_dynamic-slice_fusion), channel_id=1, source_target_pairs={{0,1},{1,0},{2,3},{3,2},{4,5},{5,4},{6,7},{7,6},{8,9},{9,8},{10,11... | collective-permute-start | bytes 9437192 | tf_op jit(solution)/shard_map/ppermute | solution.py:103
  101.0 15.1 %collective-permute-start.1 = (f32[6,32,512]{2,1,0:T(8,128)}, f32[6,32,512]{2,1,0:T(8,128)}, u32[]{:S(2)}, u32[]{:S(2)}) collective-permute-start(f32[6,32,512]{2,1,0:T(8,128)} %get-tuple-element.18), channel_id=1, source_target_pairs={{0,2},{2,4},{4,6},{6,8},{8,10},{10,12},{12,14},{14,0},{1,3},{3,5},... | collective-permute-start | bytes 1179656 | tf_op jit(solution)/shard_map/ppermute | solution.py:115
  101.8 15.4 %collective-permute-start.2 = (f32[6,32,512]{2,1,0:T(8,128)}, f32[6,32,512]{2,1,0:T(8,128)}, u32[]{:S(2)}, u32[]{:S(2)}) collective-permute-start(f32[6,32,512]{2,1,0:T(8,128)} %get-tuple-element.17), channel_id=1, source_target_pairs={{0,4},{2,6},{4,8},{6,10},{8,12},{10,14},{12,0},{14,2},{1,5},{3,7},... | collective-permute-start | bytes 1179656 | tf_op jit(solution)/shard_map/ppermute | solution.py:115
  105.5 68.5 %collective-permute-start.7 = (f32[6,32,512]{2,1,0:T(8,128)S(1)}, f32[6,32,512]{2,1,0:T(8,128)S(1)}, u32[]{:S(2)}, u32[]{:S(2)}) collective-permute-start(f32[6,32,512]{2,1,0:T(8,128)S(1)} %get-tuple-element.12), channel_id=1, source_target_pairs={{0,14},{2,0},{4,2},{6,4},{8,6},{10,8},{12,10},{14,12},{1,15},{3,1}... | collective-permute-start | bytes 1179656 | tf_op jit(solution)/shard_map/ppermute | solution.py:115
  109.6 64.3 %collective-permute-start.6 = (f32[6,32,512]{2,1,0:T(8,128)}, f32[6,32,512]{2,1,0:T(8,128)S(1)}, u32[]{:S(2)}, u32[]{:S(2)}) collective-permute-start(f32[6,32,512]{2,1,0:T(8,128)} %get-tuple-element.13), channel_id=1, source_target_pairs={{0,12},{2,14},{4,0},{6,2},{8,4},{10,6},{12,8},{14,10},{1,13},{3,15... | collective-permute-start | bytes 1179656 | tf_op jit(solution)/shard_map/ppermute | solution.py:115
  110.2 63.7 %collective-permute-start.5 = (f32[6,32,512]{2,1,0:T(8,128)}, f32[6,32,512]{2,1,0:T(8,128)S(1)}, u32[]{:S(2)}, u32[]{:S(2)}) collective-permute-start(f32[6,32,512]{2,1,0:T(8,128)} %get-tuple-element.14), channel_id=1, source_target_pairs={{0,10},{2,12},{4,14},{6,0},{8,2},{10,4},{12,6},{14,8},{1,11},{3,13... | collective-permute-start | bytes 1179656 | tf_op jit(solution)/shard_map/ppermute | solution.py:115
  116.2 49.7 %collective-permute-start.3 = (f32[6,32,512]{2,1,0:T(8,128)}, f32[6,32,512]{2,1,0:T(8,128)S(1)}, u32[]{:S(2)}, u32[]{:S(2)}) collective-permute-start(f32[6,32,512]{2,1,0:T(8,128)} %get-tuple-element.16), channel_id=1, source_target_pairs={{0,6},{2,8},{4,10},{6,12},{8,14},{10,0},{12,2},{14,4},{1,7},{3,9},... | collective-permute-start | bytes 1179656 | tf_op jit(solution)/shard_map/ppermute | solution.py:115
  117.2 56.7 %collective-permute-start.4 = (f32[6,32,512]{2,1,0:T(8,128)}, f32[6,32,512]{2,1,0:T(8,128)S(1)}, u32[]{:S(2)}, u32[]{:S(2)}) collective-permute-start(f32[6,32,512]{2,1,0:T(8,128)} %get-tuple-element.15), channel_id=1, source_target_pairs={{0,8},{2,10},{4,12},{6,14},{8,0},{10,2},{12,4},{14,6},{1,9},{3,11}... | collective-permute-start | bytes 1179656 | tf_op jit(solution)/shard_map/ppermute | solution.py:115
  190.4 3.2 %slice-start = ((f32[96,16384]{1,0:T(8,128)}), f32[12,16384]{1,0:T(8,128)S(1)}, s32[]{:S(2)}) async-start(f32[96,16384]{1,0:T(8,128)} %shard_map.47), calls=%async_computation.1 | async-start | bytes 2097152 | tf_op jit(solution)/shard_map/slice | solution.py:131
  190.6 15.1 %collective-permute-start.8 = (bf16[2,6,32,512]{3,2,1,0:T(8,128)(2,1)S(1)}, bf16[2,6,32,512]{3,2,1,0:T(8,128)(2,1)}, u32[]{:S(2)}, u32[]{:S(2)}) collective-permute-start(bf16[2,6,32,512]{3,2,1,0:T(8,128)(2,1)S(1)} %bitcast.90), channel_id=1, source_target_pairs={{0,2},{2,4},{4,6},{6,8},{8,10},{10,12},{12,14},{14,0},{1,3},{3,5},... | collective-permute-start | bytes 1179656 | tf_op jit(solution)/shard_map/ppermute | solution.py:134
  193.6 14.1 %collective-permute-start.9 = (bf16[2,6,32,512]{3,2,1,0:T(8,128)(2,1)}, bf16[2,6,32,512]{3,2,1,0:T(8,128)(2,1)}, u32[]{:S(2)}, u32[]{:S(2)}) collective-permute-start(bf16[2,6,32,512]{3,2,1,0:T(8,128)(2,1)} %bitcast.33), channel_id=1, source_target_pairs={{0,4},{2,6},{4,8},{6,10},{8,12},{10,14},{12,0},{14,2},{1,5},{3,7},... | collective-permute-start | bytes 1179656 | tf_op jit(solution)/shard_map/ppermute | solution.py:134
  193.6 1.0 copy-start.1
  195.0 69.4 %collective-permute-start.13 = (bf16[2,6,32,512]{3,2,1,0:T(8,128)(2,1)S(1)}, bf16[2,6,32,512]{3,2,1,0:T(8,128)(2,1)S(1)}, u32[]{:S(2)}, u32[]{:S(2)}) collective-permute-start(bf16[2,6,32,512]{3,2,1,0:T(8,128)(2,1)S(1)} %bitcast.92), channel_id=1, source_target_pairs={{0,12},{2,14},{4,0},{6,2},{8,4},{10,6},{12,8},{14,10},{1,13},{3,15... | collective-permute-start | bytes 1179656 | tf_op jit(solution)/shard_map/ppermute | solution.py:134
  198.9 65.6 %collective-permute-start.14 = (bf16[2,6,32,512]{3,2,1,0:T(8,128)(2,1)S(1)}, bf16[2,6,32,512]{3,2,1,0:T(8,128)(2,1)S(1)}, u32[]{:S(2)}, u32[]{:S(2)}) collective-permute-start(bf16[2,6,32,512]{3,2,1,0:T(8,128)(2,1)S(1)} %bitcast.91), channel_id=1, source_target_pairs={{0,14},{2,0},{4,2},{6,4},{8,6},{10,8},{12,10},{14,12},{1,15},{3,1}... | collective-permute-start | bytes 1179656 | tf_op jit(solution)/shard_map/ppermute | solution.py:134
  201.1 63.2 %collective-permute-start.12 = (bf16[2,6,32,512]{3,2,1,0:T(8,128)(2,1)S(1)}, bf16[2,6,32,512]{3,2,1,0:T(8,128)(2,1)S(1)}, u32[]{:S(2)}, u32[]{:S(2)}) collective-permute-start(bf16[2,6,32,512]{3,2,1,0:T(8,128)(2,1)S(1)} %bitcast.93), channel_id=1, source_target_pairs={{0,10},{2,12},{4,14},{6,0},{8,2},{10,4},{12,6},{14,8},{1,11},{3,13... | collective-permute-start | bytes 1179656 | tf_op jit(solution)/shard_map/ppermute | solution.py:134
  205.7 49.4 %collective-permute-start.10 = (bf16[2,6,32,512]{3,2,1,0:T(8,128)(2,1)S(1)}, bf16[2,6,32,512]{3,2,1,0:T(8,128)(2,1)S(1)}, u32[]{:S(2)}, u32[]{:S(2)}) collective-permute-start(bf16[2,6,32,512]{3,2,1,0:T(8,128)(2,1)S(1)} %bitcast.95), channel_id=1, source_target_pairs={{0,6},{2,8},{4,10},{6,12},{8,14},{10,0},{12,2},{14,4},{1,7},{3,9},... | collective-permute-start | bytes 1179656 | tf_op jit(solution)/shard_map/ppermute | solution.py:134
  207.7 56.5 %collective-permute-start.11 = (bf16[2,6,32,512]{3,2,1,0:T(8,128)(2,1)S(1)}, bf16[2,6,32,512]{3,2,1,0:T(8,128)(2,1)S(1)}, u32[]{:S(2)}, u32[]{:S(2)}) collective-permute-start(bf16[2,6,32,512]{3,2,1,0:T(8,128)(2,1)S(1)} %bitcast.94), channel_id=1, source_target_pairs={{0,8},{2,10},{4,12},{6,14},{8,0},{10,2},{12,4},{14,6},{1,9},{3,11}... | collective-permute-start | bytes 1179656 | tf_op jit(solution)/shard_map/ppermute | solution.py:134
  264.5 2.7 copy-start
Sparse Core Ops, SparseCore 0:
  9.5 53.2 all-gather.1

commit v13 on v12

--- a/solution.py
+++ b/solution.py
@@ -92,8 +92,16 @@
     modes = panel.shape[-1]
     nbd = lax.axis_size("blade")
     mine = jnp.swapaxes(panel.reshape(-1, bs, modes), 1, 2)
-    pt = lax.all_gather(mine, ("blade", "dof"), axis=0, tiled=True)
-    proj = _project(pt, stiffness, block_rows.reshape(-1), block_cols.reshape(-1))
+    nd = lax.axis_size("dof")
+    pt = lax.all_gather(mine, ("dof", "blade"), axis=0, tiled=True)
+    bpd = mine.shape[0]
+
+    def remap(j):
+        j = jnp.clip(j.reshape(-1), 0, pt.shape[0] - 1)
+        k = j // bpd
+        return ((k % nd) * nbd + k // nd) * bpd + j % bpd
+
+    proj = _project(pt, stiffness, remap(block_rows), remap(block_cols))
 
     if lax.axis_size("dof") == 2:
         rows_half = modes // 2

time: 276 us -> 276 us (level)
  no operation moved by 1% of the time
where the time goes in v13:
time: 276 us; the launch traced here: 275 us
  waiting for transfers between devices  155 us (56%)
  starting transfers between devices  37.5 us (14%)
  Pallas kernels  33.3 us (12%)
  local copies, waits for them, and re-layouts  22.1 us (8%)
  between operations  13.7 us (5%)
  other arithmetic  13.1 us (5%)
    ppermute x7, waiting for transfers between devices, body(): lax.ppermute(piece, 'blade', [(j, (j + t) % nbd) for j in range(nbd)])  59.5 us
    all_gather x1, waiting for transfers between devices, body(): pt = lax.all_gather(mine, ('dof', 'blade'), axis=0, tiled=True)  52.4 us
    ppermute x7, waiting for transfers between devices, body(): lax.ppermute(piece, 'blade', [(j, (j + s) % nbd) for j in range(nbd)])  38.1 us
    ppermute x7, starting transfers between devices, body(): lax.ppermute(piece, 'blade', [(j, (j + s) % nbd) for j in range(nbd)])  30.2 us
    pallas_call x1, Pallas kernels, _project(): pl.pallas_call(_project_kernel, grid_spec=grid_spec, out_shape=jax.ShapeD...  25.1 us
    unnamed x28, local copies, waits for them, and re-layouts  12.4 us
    pallas_call x1, Pallas kernels, _dft(): pl.pallas_call(_dft_kernel, grid=(n // tn,), in_specs=[pl.BlockSpec((rows...  8.2 us
    ppermute x7, starting transfers between devices, body(): lax.ppermute(piece, 'blade', [(j, (j + t) % nbd) for j in range(nbd)])  6.92 us
  transfers between devices with their start and end apart: 16, of which 9 were waited for; matrix products, arithmetic and copies ran while one was open for 5% of the time, Pallas kernels for 0%

profile of v13, /device:TPU:0, one launch (start us, length us, event | category | flops | bytes accessed | tf_op | source)
XLA Modules:
  0.0 275.0 jit_solution(6041935697156331198)
XLA Ops:
  6.5 1.8 copy.6
  8.3 0.0 all-gather.2.cloned.1.call-update
  8.4 0.7 broadcast_clamp_fusion
  9.1 0.1 min.20
  9.1 0.1 min.18
  9.2 0.6 fusion.11.cols_ref
  9.8 0.6 fusion.8.rows_ref
  10.4 52.4 %all-gather.2.cloned.1.call-done.pt_ref = bf16[32,512,128]{2,1,0:T(8,128)(2,1)} async-done(((bf16[2,512,128]{2,1,0:T(8,128)(2,1)}), bf16[32,512,128]{2,1,0:T(8,128)(2,1)}) %all-gather.2.cloned.1.call-update) | async-done | bytes 4194320 | tf_op jit(solution)/shard_map/all_gather | solution.py:96
  62.9 25.1 %shard_map.46 = f32[6,512,512]{2,1,0:T(8,128)} custom-call(s32[192]{0:T(256)} %fusion.8.rows_ref, s32[192]{0:T(256)} %fusion.11.cols_ref, bf16[32,512,128]{2,1,0:T(8,128)(2,1)} %all-gather.2.cloned.1.call-done.pt_ref, bf16[6,32,128,128]{3,2,1,0:T(8,128)(2,1)} %s_ref.1), custom_call_target="tpu_custom_call" | custom-call | tf_op jit(solution)/shard_map/pallas_call | solution.py:44
  88.0 2.2 constant_dynamic-slice_fusion
  90.2 0.3 collective-permute-start
  90.5 0.1 iota_add_fusion
  90.6 0.1 add.259
  90.6 0.1 iota_add_fusion.1
  90.7 5.3 %collective-permute-done = f32[6,256,512]{2,1,0:T(8,128)} collective-permute-done((f32[6,256,512]{2,1,0:T(8,128)S(1)}, f32[6,256,512]{2,1,0:T(8,128)}, u32[]{:S(2)}, u32[]{:S(2)}) %collective-permute-start) | collective-permute-done | bytes 3145760 | tf_op jit(solution)/shard_map/ppermute | solution.py:111
  96.0 3.6 %dynamic-slice_add_fusion = f32[6,256,512]{2,1,0:T(8,128)S(1)} fusion(f32[6,256,512]{2,1,0:T(8,128)} %collective-permute-done, f32[6,512,512]{2,1,0:T(8,128)} %shard_map.46, s32[]{:T(128)S(6)} %select_n.198), kind=kLoop, calls=%fused_computation | loop fusion | flops 786432 | bytes 9437188 | tf_op jit(solution)/shard_map/add | solution.py:111
  99.6 1.5 dynamic-slice_bitcast_fusion
  101.1 0.6 collective-permute-start.1
  101.6 0.2 fusion.4
  101.9 1.5 collective-permute-start.2
  103.4 0.6 pad_maximum_fusion
  104.0 1.5 reshape.164.w_ref
  105.5 4.2 %collective-permute-start.7 = (f32[6,32,512]{2,1,0:T(8,128)S(1)}, f32[6,32,512]{2,1,0:T(8,128)S(1)}, u32[]{:S(2)}, u32[]{:S(2)}) collective-permute-start(f32[6,32,512]{2,1,0:T(8,128)S(1)} %get-tuple-element.12), channel_id=1, source_target_pairs={{0,14},{2,0},{4,2},{6,4},{8,6},{10,8},{12,10},{14,12},{1,15},{3,1}... | collective-permute-start | bytes 1179656 | tf_op jit(solution)/shard_map/ppermute | solution.py:123
  109.7 0.5 collective-permute-start.6
  110.2 6.0 %collective-permute-done.1 = f32[6,32,512]{2,1,0:T(8,128)} collective-permute-done((f32[6,32,512]{2,1,0:T(8,128)}, f32[6,32,512]{2,1,0:T(8,128)}, u32[]{:S(2)}, u32[]{:S(2)}) %collective-permute-start.1) | collective-permute-done | bytes 393248 | tf_op jit(solution)/shard_map/ppermute | solution.py:123
  116.2 1.0 bitcast_dynamic-update-slice_fusion.6
  117.2 23.4 %collective-permute-start.4 = (f32[6,32,512]{2,1,0:T(8,128)}, f32[6,32,512]{2,1,0:T(8,128)S(1)}, u32[]{:S(2)}, u32[]{:S(2)}) collective-permute-start(f32[6,32,512]{2,1,0:T(8,128)} %get-tuple-element.15), channel_id=1, source_target_pairs={{0,8},{2,10},{4,12},{6,14},{8,0},{10,2},{12,4},{14,6},{1,9},{3,11}... | collective-permute-start | bytes 1179656 | tf_op jit(solution)/shard_map/ppermute | solution.py:123
  140.7 1.0 bitcast_dynamic-update-slice_fusion.5
  141.7 24.2 %collective-permute-done.3 = f32[6,32,512]{2,1,0:T(8,128)S(1)} collective-permute-done((f32[6,32,512]{2,1,0:T(8,128)}, f32[6,32,512]{2,1,0:T(8,128)S(1)}, u32[]{:S(2)}, u32[]{:S(2)}) %collective-permute-start.3) | collective-permute-done | bytes 393248 | tf_op jit(solution)/shard_map/ppermute | solution.py:123
  166.0 7.9 %collective-permute-done.4 = f32[6,32,512]{2,1,0:T(8,128)S(1)} collective-permute-done((f32[6,32,512]{2,1,0:T(8,128)}, f32[6,32,512]{2,1,0:T(8,128)S(1)}, u32[]{:S(2)}, u32[]{:S(2)}) %collective-permute-start.4) | collective-permute-done | bytes 393248 | tf_op jit(solution)/shard_map/ppermute | solution.py:123
  174.1 3.4 %copy.7 = f32[6,8,32,512]{3,1,2,0:T(8,128)} copy(f32[6,8,32,512]{3,2,1,0:T(8,128)S(1)} %bitcast.73) | data formatting | bytes 6291456
  177.5 8.2 %shard_map.47 = f32[96,16384]{1,0:T(8,128)} custom-call(f32[96,48]{1,0:T(8,128)} %reshape.164.w_ref, f32[48,16384]{1,0:T(8,128)} %bitcast.72), custom_call_target="tpu_custom_call" | custom-call | tf_op jit(solution)/shard_map/pallas_call | solution.py:72
  185.7 3.1 %convert.9 = bf16[96,16384]{1,0:T(8,128)(2,1)S(1)} convert(f32[96,16384]{1,0:T(8,128)} %shard_map.47) | non-fusion elementwise | flops 1572864 | bytes 9437184 | tf_op jit(solution)/shard_map/convert.6
  188.8 1.6 fusion.16
  190.5 0.2 copy.9
  190.7 1.0 collective-permute-start.8
  191.6 1.2 copy.10
  192.8 0.8 slice.57
  193.6 0.6 copy.8
  194.2 0.1 slice.55
  194.3 0.4 copy-done.1
  194.7 0.2 copy.15
  194.9 0.2 copy.14
  195.1 3.9 %collective-permute-start.13 = (bf16[2,6,32,512]{3,2,1,0:T(8,128)(2,1)S(1)}, bf16[2,6,32,512]{3,2,1,0:T(8,128)(2,1)S(1)}, u32[]{:S(2)}, u32[]{:S(2)}) collective-permute-start(bf16[2,6,32,512]{3,2,1,0:T(8,128)(2,1)S(1)} %bitcast.92), channel_id=1, source_target_pairs={{0,12},{2,14},{4,0},{6,2},{8,4},{10,6},{12,8},{14,10},{1,13},{3,15... | collective-permute-start | bytes 1179656 | tf_op jit(solution)/shard_map/ppermute | solution.py:142
  198.9 2.0 collective-permute-start.14
  200.9 0.2 copy.13
  201.1 0.1 collective-permute-start.12
  201.2 0.2 copy.12
  201.4 0.2 copy.11
  201.6 0.8 broadcast_in_dim.2
  202.4 0.1 constant_dynamic-update-slice_fusion
  202.5 3.2 %collective-permute-done.8 = bf16[2,6,32,512]{3,2,1,0:T(8,128)(2,1)} collective-permute-done((bf16[2,6,32,512]{3,2,1,0:T(8,128)(2,1)S(1)}, bf16[2,6,32,512]{3,2,1,0:T(8,128)(2,1)}, u32[]{:S(2)}, u32[]{:S(2)}) %collective-permute-start.8) | collective-permute-done | bytes 393248 | tf_op jit(solution)/shard_map/ppermute | solution.py:142
  205.7 1.1 convert_dynamic-update-slice_fusion.6
  206.8 1.0 collective-permute-done.9
  207.8 1.1 convert_dynamic-update-slice_fusion.5
  208.8 46.3 %collective-permute-done.10 = bf16[2,6,32,512]{3,2,1,0:T(8,128)(2,1)S(1)} collective-permute-done((bf16[2,6,32,512]{3,2,1,0:T(8,128)(2,1)S(1)}, bf16[2,6,32,512]{3,2,1,0:T(8,128)(2,1)S(1)}, u32[]{:S(2)}, u32[]{:S(2)}) %collective-permute-start.10) | collective-permute-done | bytes 393248 | tf_op jit(solution)/shard_map/ppermute | solution.py:142
  255.1 0.1 convert_dynamic-update-slice_fusion.4
  255.2 9.0 %collective-permute-done.11 = bf16[2,6,32,512]{3,2,1,0:T(8,128)(2,1)S(1)} collective-permute-done((bf16[2,6,32,512]{3,2,1,0:T(8,128)(2,1)S(1)}, bf16[2,6,32,512]{3,2,1,0:T(8,128)(2,1)S(1)}, u32[]{:S(2)}, u32[]{:S(2)}) %collective-permute-start.11) | collective-permute-done | bytes 393248 | tf_op jit(solution)/shard_map/ppermute | solution.py:142
  264.2 0.1 convert_dynamic-update-slice_fusion.3
  264.3 0.1 convert_dynamic-update-slice_fusion.2
  264.4 0.1 convert_dynamic-update-slice_fusion.1
  264.5 0.0 copy-start
  264.5 2.7 copy-done
  267.2 1.0 convert_dynamic-update-slice_fusion
  (29 shorter events, 0.4 us)
Async XLA Ops:
  6.5 56.3 %all-gather.2.cloned.1.call-start = ((), (), s32[]{:S(2)}) async-start(), calls=%async_computation | async-start | bytes 4456448 | tf_op jit(solution)/shard_map/all_gather | solution.py:96
  90.2 5.9 %collective-permute-start = (f32[6,256,512]{2,1,0:T(8,128)S(1)}, f32[6,256,512]{2,1,0:T(8,128)}, u32[]{:S(2)}, u32[]{:S(2)}) collective-permute-start(f32[6,256,512]{2,1,0:T(8,128)S(1)} %constant_dynamic-slice_fusion), channel_id=1, source_target_pairs={{0,1},{1,0},{2,3},{3,2},{4,5},{5,4},{6,7},{7,6},{8,9},{9,8},{10,11... | collective-permute-start | bytes 9437192 | tf_op jit(solution)/shard_map/ppermute | solution.py:111
  101.1 15.1 %collective-permute-start.1 = (f32[6,32,512]{2,1,0:T(8,128)}, f32[6,32,512]{2,1,0:T(8,128)}, u32[]{:S(2)}, u32[]{:S(2)}) collective-permute-start(f32[6,32,512]{2,1,0:T(8,128)} %get-tuple-element.18), channel_id=1, source_target_pairs={{0,2},{2,4},{4,6},{6,8},{8,10},{10,12},{12,14},{14,0},{1,3},{3,5},... | collective-permute-start | bytes 1179656 | tf_op jit(solution)/shard_map/ppermute | solution.py:123
  101.9 15.4 %collective-permute-start.2 = (f32[6,32,512]{2,1,0:T(8,128)}, f32[6,32,512]{2,1,0:T(8,128)}, u32[]{:S(2)}, u32[]{:S(2)}) collective-permute-start(f32[6,32,512]{2,1,0:T(8,128)} %get-tuple-element.17), channel_id=1, source_target_pairs={{0,4},{2,6},{4,8},{6,10},{8,12},{10,14},{12,0},{14,2},{1,5},{3,7},... | collective-permute-start | bytes 1179656 | tf_op jit(solution)/shard_map/ppermute | solution.py:123
  105.5 68.5 %collective-permute-start.7 = (f32[6,32,512]{2,1,0:T(8,128)S(1)}, f32[6,32,512]{2,1,0:T(8,128)S(1)}, u32[]{:S(2)}, u32[]{:S(2)}) collective-permute-start(f32[6,32,512]{2,1,0:T(8,128)S(1)} %get-tuple-element.12), channel_id=1, source_target_pairs={{0,14},{2,0},{4,2},{6,4},{8,6},{10,8},{12,10},{14,12},{1,15},{3,1}... | collective-permute-start | bytes 1179656 | tf_op jit(solution)/shard_map/ppermute | solution.py:123
  109.7 64.3 %collective-permute-start.6 = (f32[6,32,512]{2,1,0:T(8,128)}, f32[6,32,512]{2,1,0:T(8,128)S(1)}, u32[]{:S(2)}, u32[]{:S(2)}) collective-permute-start(f32[6,32,512]{2,1,0:T(8,128)} %get-tuple-element.13), channel_id=1, source_target_pairs={{0,12},{2,14},{4,0},{6,2},{8,4},{10,6},{12,8},{14,10},{1,13},{3,15... | collective-permute-start | bytes 1179656 | tf_op jit(solution)/shard_map/ppermute | solution.py:123
  110.2 63.7 %collective-permute-start.5 = (f32[6,32,512]{2,1,0:T(8,128)}, f32[6,32,512]{2,1,0:T(8,128)S(1)}, u32[]{:S(2)}, u32[]{:S(2)}) collective-permute-start(f32[6,32,512]{2,1,0:T(8,128)} %get-tuple-element.14), channel_id=1, source_target_pairs={{0,10},{2,12},{4,14},{6,0},{8,2},{10,4},{12,6},{14,8},{1,11},{3,13... | collective-permute-start | bytes 1179656 | tf_op jit(solution)/shard_map/ppermute | solution.py:123
  116.2 49.7 %collective-permute-start.3 = (f32[6,32,512]{2,1,0:T(8,128)}, f32[6,32,512]{2,1,0:T(8,128)S(1)}, u32[]{:S(2)}, u32[]{:S(2)}) collective-permute-start(f32[6,32,512]{2,1,0:T(8,128)} %get-tuple-element.16), channel_id=1, source_target_pairs={{0,6},{2,8},{4,10},{6,12},{8,14},{10,0},{12,2},{14,4},{1,7},{3,9},... | collective-permute-start | bytes 1179656 | tf_op jit(solution)/shard_map/ppermute | solution.py:123
  117.2 56.7 %collective-permute-start.4 = (f32[6,32,512]{2,1,0:T(8,128)}, f32[6,32,512]{2,1,0:T(8,128)S(1)}, u32[]{:S(2)}, u32[]{:S(2)}) collective-permute-start(f32[6,32,512]{2,1,0:T(8,128)} %get-tuple-element.15), channel_id=1, source_target_pairs={{0,8},{2,10},{4,12},{6,14},{8,0},{10,2},{12,4},{14,6},{1,9},{3,11}... | collective-permute-start | bytes 1179656 | tf_op jit(solution)/shard_map/ppermute | solution.py:123
  190.5 3.2 %slice-start = ((f32[96,16384]{1,0:T(8,128)}), f32[12,16384]{1,0:T(8,128)S(1)}, s32[]{:S(2)}) async-start(f32[96,16384]{1,0:T(8,128)} %shard_map.47), calls=%async_computation.1 | async-start | bytes 2097152 | tf_op jit(solution)/shard_map/slice | solution.py:139
  190.7 15.1 %collective-permute-start.8 = (bf16[2,6,32,512]{3,2,1,0:T(8,128)(2,1)S(1)}, bf16[2,6,32,512]{3,2,1,0:T(8,128)(2,1)}, u32[]{:S(2)}, u32[]{:S(2)}) collective-permute-start(bf16[2,6,32,512]{3,2,1,0:T(8,128)(2,1)S(1)} %bitcast.90), channel_id=1, source_target_pairs={{0,2},{2,4},{4,6},{6,8},{8,10},{10,12},{12,14},{14,0},{1,3},{3,5},... | collective-permute-start | bytes 1179656 | tf_op jit(solution)/shard_map/ppermute | solution.py:142
  193.6 14.1 %collective-permute-start.9 = (bf16[2,6,32,512]{3,2,1,0:T(8,128)(2,1)}, bf16[2,6,32,512]{3,2,1,0:T(8,128)(2,1)}, u32[]{:S(2)}, u32[]{:S(2)}) collective-permute-start(bf16[2,6,32,512]{3,2,1,0:T(8,128)(2,1)} %bitcast.33), channel_id=1, source_target_pairs={{0,4},{2,6},{4,8},{6,10},{8,12},{10,14},{12,0},{14,2},{1,5},{3,7},... | collective-permute-start | bytes 1179656 | tf_op jit(solution)/shard_map/ppermute | solution.py:142
  193.6 1.0 copy-start.1
  195.1 69.4 %collective-permute-start.13 = (bf16[2,6,32,512]{3,2,1,0:T(8,128)(2,1)S(1)}, bf16[2,6,32,512]{3,2,1,0:T(8,128)(2,1)S(1)}, u32[]{:S(2)}, u32[]{:S(2)}) collective-permute-start(bf16[2,6,32,512]{3,2,1,0:T(8,128)(2,1)S(1)} %bitcast.92), channel_id=1, source_target_pairs={{0,12},{2,14},{4,0},{6,2},{8,4},{10,6},{12,8},{14,10},{1,13},{3,15... | collective-permute-start | bytes 1179656 | tf_op jit(solution)/shard_map/ppermute | solution.py:142
  198.9 65.6 %collective-permute-start.14 = (bf16[2,6,32,512]{3,2,1,0:T(8,128)(2,1)S(1)}, bf16[2,6,32,512]{3,2,1,0:T(8,128)(2,1)S(1)}, u32[]{:S(2)}, u32[]{:S(2)}) collective-permute-start(bf16[2,6,32,512]{3,2,1,0:T(8,128)(2,1)S(1)} %bitcast.91), channel_id=1, source_target_pairs={{0,14},{2,0},{4,2},{6,4},{8,6},{10,8},{12,10},{14,12},{1,15},{3,1}... | collective-permute-start | bytes 1179656 | tf_op jit(solution)/shard_map/ppermute | solution.py:142
  201.1 63.2 %collective-permute-start.12 = (bf16[2,6,32,512]{3,2,1,0:T(8,128)(2,1)S(1)}, bf16[2,6,32,512]{3,2,1,0:T(8,128)(2,1)S(1)}, u32[]{:S(2)}, u32[]{:S(2)}) collective-permute-start(bf16[2,6,32,512]{3,2,1,0:T(8,128)(2,1)S(1)} %bitcast.93), channel_id=1, source_target_pairs={{0,10},{2,12},{4,14},{6,0},{8,2},{10,4},{12,6},{14,8},{1,11},{3,13... | collective-permute-start | bytes 1179656 | tf_op jit(solution)/shard_map/ppermute | solution.py:142
  205.7 49.4 %collective-permute-start.10 = (bf16[2,6,32,512]{3,2,1,0:T(8,128)(2,1)S(1)}, bf16[2,6,32,512]{3,2,1,0:T(8,128)(2,1)S(1)}, u32[]{:S(2)}, u32[]{:S(2)}) collective-permute-start(bf16[2,6,32,512]{3,2,1,0:T(8,128)(2,1)S(1)} %bitcast.95), channel_id=1, source_target_pairs={{0,6},{2,8},{4,10},{6,12},{8,14},{10,0},{12,2},{14,4},{1,7},{3,9},... | collective-permute-start | bytes 1179656 | tf_op jit(solution)/shard_map/ppermute | solution.py:142
  207.8 56.5 %collective-permute-start.11 = (bf16[2,6,32,512]{3,2,1,0:T(8,128)(2,1)S(1)}, bf16[2,6,32,512]{3,2,1,0:T(8,128)(2,1)S(1)}, u32[]{:S(2)}, u32[]{:S(2)}) collective-permute-start(bf16[2,6,32,512]{3,2,1,0:T(8,128)(2,1)S(1)} %bitcast.94), channel_id=1, source_target_pairs={{0,8},{2,10},{4,12},{6,14},{8,0},{10,2},{12,4},{14,6},{1,9},{3,11}... | collective-permute-start | bytes 1179656 | tf_op jit(solution)/shard_map/ppermute | solution.py:142
  264.5 2.7 copy-start
Sparse Core Ops, SparseCore 0:
  9.6 53.2 all-gather.1

commit v14 on v10

--- a/solution.py
+++ b/solution.py
@@ -95,15 +95,22 @@
     pt = lax.all_gather(mine, ("blade", "dof"), axis=0, tiled=True)
     proj = _project(pt, stiffness, block_rows.reshape(-1), block_cols.reshape(-1))
 
-    half = lax.psum_scatter(proj, "dof", scatter_dimension=1, tiled=True)
     me = lax.axis_index("blade")
-    rows_half = half.shape[1]
+    rows_half = modes // lax.axis_size("dof")
     r = rows_half // nbd
-    chunks = half.reshape(nbl, nbd, r, modes)
+    if lax.axis_size("dof") == 2:
+        d = lax.axis_index("dof")
+        mine = lax.dynamic_slice_in_dim(proj, d * rows_half, rows_half, axis=1)
+        other = lax.dynamic_slice_in_dim(proj, (1 - d) * rows_half, rows_half, axis=1)
+        halves = [mine, lax.ppermute(other, "dof", [(0, 1), (1, 0)])]
+    else:
+        halves = [lax.psum_scatter(proj, "dof", scatter_dimension=1, tiled=True)]
+    halves = [h.reshape(nbl, nbd, r, modes) for h in halves]
 
     got = []
     for s in range(nbd):
-        piece = lax.dynamic_index_in_dim(chunks, (me + s) % nbd, axis=1, keepdims=False)
+        cut = [lax.dynamic_index_in_dim(h, (me + s) % nbd, axis=1, keepdims=False) for h in halves]
+        piece = cut[0] + cut[1] if len(cut) > 1 else cut[0]
         if s:
             piece = lax.ppermute(piece, "blade", [(j, (j + s) % nbd) for j in range(nbd)])
         got.append(piece)

time: 278 us -> 280 us (level)
  other arithmetic: 7.6 us -> 14.1 us
  waiting for transfers between devices: 160 us -> 154 us
  local copies, waits for them, and re-layouts: 22 us -> 25.6 us
    reduce_scatter x1 -> x0, waiting for transfers between devices: 12.8 us -> none  [body(): half = lax.psum_scatter(proj, 'dof', scatter_dimension=1, tiled=True)]
    dynamic_slice x0 -> x1, local copies, waits for them, and re-layouts: none -> 5.57 us  [body(): mine = lax.dynamic_slice_in_dim(proj, d * rows_half, rows_half, axis=1)]
    ppermute x0 -> x1, waiting for transfers between devices: none -> 5.51 us  [body(): halves = [mine, lax.ppermute(other, 'dof', [(0, 1), (1, 0)])]]
    add x0 -> x2, other arithmetic: none -> 4.09 us  [body(): piece = cut[0] + cut[1] if len(cut) > 1 else cut[0]]
    unnamed x28 -> x29, local copies, waits for them, and re-layouts: 11.5 us -> 11.4 us
  transfers between devices with their start and end apart: 16 -> 16, of which waited for: 10 -> 10; matrix products, arithmetic and copies ran while one was open for 5% -> 6% of each run, Pallas kernels for 0% -> 0%
where the time goes in v14:
time: 280 us; the launch traced here: 279 us
  waiting for transfers between devices  154 us (55%)
  starting transfers between devices  39 us (14%)
  Pallas kernels  33.3 us (12%)
  local copies, waits for them, and re-layouts  25.6 us (9%)
  other arithmetic  14.1 us (5%)
  between operations  13.7 us (5%)
    ppermute x7, waiting for transfers between devices, body(): lax.ppermute(piece, 'blade', [(j, (j + t) % nbd) for j in range(nbd)])  58.8 us
    all_gather x1, waiting for transfers between devices, body(): pt = lax.all_gather(mine, ('blade', 'dof'), axis=0, tiled=True)  51.8 us
    ppermute x7, waiting for transfers between devices, body(): lax.ppermute(piece, 'blade', [(j, (j + s) % nbd) for j in range(nbd)])  37.4 us
    ppermute x7, starting transfers between devices, body(): lax.ppermute(piece, 'blade', [(j, (j + s) % nbd) for j in range(nbd)])  31.9 us
    pallas_call x1, Pallas kernels, _project(): pl.pallas_call(_project_kernel, grid_spec=grid_spec, out_shape=jax.ShapeD...  25.1 us
    unnamed x29, local copies, waits for them, and re-layouts  11.4 us
    pallas_call x1, Pallas kernels, _dft(): pl.pallas_call(_dft_kernel, grid=(n // tn,), in_specs=[pl.BlockSpec((rows...  8.2 us
    ppermute x7, starting transfers between devices, body(): lax.ppermute(piece, 'blade', [(j, (j + t) % nbd) for j in range(nbd)])  6.85 us
  transfers between devices with their start and end apart: 16, of which 10 were waited for; matrix products, arithmetic and copies ran while one was open for 6% of the time, Pallas kernels for 0%

profile of v14, /device:TPU:0, one launch (start us, length us, event | category | flops | bytes accessed | tf_op | source)
XLA Modules:
  0.0 279.3 jit_solution(10339601110208687324)
XLA Ops:
  6.5 1.8 copy.28
  8.3 0.0 all-gather.2.cloned.1.call-update
  8.4 1.3 reshape.190.rows_ref
  9.7 1.3 reshape.191.cols_ref
  11.0 51.8 %all-gather.2.cloned.1.call-done.pt_ref = bf16[32,512,128]{2,1,0:T(8,128)(2,1)} async-done(((bf16[2,512,128]{2,1,0:T(8,128)(2,1)}), bf16[32,512,128]{2,1,0:T(8,128)(2,1)}) %all-gather.2.cloned.1.call-update) | async-done | bytes 4194320 | tf_op jit(solution)/shard_map/all_gather | solution.py:95
  62.8 25.1 %shard_map.46 = f32[6,512,512]{2,1,0:T(8,128)} custom-call(s32[192]{0:T(256)} %reshape.190.rows_ref, s32[192]{0:T(256)} %reshape.191.cols_ref, bf16[32,512,128]{2,1,0:T(8,128)(2,1)} %all-gather.2.cloned.1.call-done.pt_ref, bf16[6,32,128,128]{3,2,1,0:T(8,128)(2,1)} %s_ref.1), custom_call_target="tpu_custom_call" | custom-call | tf_op jit(solution)/shard_map/pallas_call | solution.py:44
  87.9 5.6 %constant_dynamic-slice_fusion.1 = (f32[6,256,512]{2,1,0:T(8,128)S(1)}, f32[6,256,512]{2,1,0:T(8,128)}) fusion(f32[6,512,512]{2,1,0:T(8,128)} %shard_map.46, s32[]{:T(128)S(6)} %select_n.182, s32[]{:T(128)S(6)} %select_n.185), kind=kLoop, calls=%fused_computation.42 | loop fusion | bytes 12582920 | tf_op jit(solution)/shard_map/dynamic_slice | solution.py:103
  93.5 0.3 collective-permute-start
  93.8 0.1 iota_add_fusion
  93.8 0.1 add.300
  93.9 0.1 iota_add_fusion.1
  94.0 5.5 %collective-permute-done = f32[6,256,512]{2,1,0:T(8,128)} collective-permute-done((f32[6,256,512]{2,1,0:T(8,128)}, f32[6,256,512]{2,1,0:T(8,128)}, u32[]{:S(2)}, u32[]{:S(2)}) %collective-permute-start) | collective-permute-done | bytes 3145760 | tf_op jit(solution)/shard_map/ppermute | solution.py:105
  99.5 3.0 %fusion = (f32[6,32,512]{2,1,0:T(8,128)S(1)}, f32[6,32,512]{2,1,0:T(8,128)}, f32[6,32,512]{2,1,0:T(8,128)}, f32[6,32,512]{2,1,0:T(8,128)}, f32[6,32,512]{2,1,0:T(8,128)}, /*index=5*/f32[6,32,512]{2,1,0:T(8,128)}) fusion(f32[6,8,32,512]{3,2,1,0:T(8,128)} %bitcast.3, s32[]{:T(128)S(6)} %select_n.197, f32[6,8,32,512]{3,2,1,0:T(8,128)S(1)} %bitcast.118, ...), kind=kLoop, calls=%fused_computation.8 | loop fusion | flops 589824 | bytes 7077912 | tf_op jit(solution)/shard_map/add | solution.py:113
  102.5 0.6 collective-permute-start.1
  103.1 0.8 fusion.12
  103.9 1.4 pad_maximum_fusion
  105.3 1.5 reshape.189.w_ref
  106.8 1.5 collective-permute-start.2
  108.3 1.1 add_bitcast_fusion
  109.3 4.2 %collective-permute-start.7 = (f32[6,32,512]{2,1,0:T(8,128)S(1)}, f32[6,32,512]{2,1,0:T(8,128)S(1)}, u32[]{:S(2)}, u32[]{:S(2)}) collective-permute-start(f32[6,32,512]{2,1,0:T(8,128)S(1)} %add_bitcast_fusion), channel_id=1, source_target_pairs={{0,14},{2,0},{4,2},{6,4},{8,6},{10,8},{12,10},{14,12},{1,15},{3,1}... | collective-permute-start | bytes 1179656 | tf_op jit(solution)/shard_map/ppermute | solution.py:115
  113.6 0.5 collective-permute-start.6
  114.1 0.0 collective-permute-start.5
  114.1 1.1 fusion.7
  115.2 2.5 collective-permute-done.1
  117.6 0.5 collective-permute-start.3
  118.1 1.0 bitcast_dynamic-update-slice_fusion.6
  119.2 1.7 collective-permute-done.2
  120.8 24.6 %collective-permute-start.4 = (f32[6,32,512]{2,1,0:T(8,128)S(1)}, f32[6,32,512]{2,1,0:T(8,128)S(1)}, u32[]{:S(2)}, u32[]{:S(2)}) collective-permute-start(f32[6,32,512]{2,1,0:T(8,128)S(1)} %copy-done.2), channel_id=1, source_target_pairs={{0,8},{2,10},{4,12},{6,14},{8,0},{10,2},{12,4},{14,6},{1,9},{3,11}... | collective-permute-start | bytes 1179656 | tf_op jit(solution)/shard_map/ppermute | solution.py:115
  145.5 21.9 %collective-permute-done.3 = f32[6,32,512]{2,1,0:T(8,128)S(1)} collective-permute-done((f32[6,32,512]{2,1,0:T(8,128)}, f32[6,32,512]{2,1,0:T(8,128)S(1)}, u32[]{:S(2)}, u32[]{:S(2)}) %collective-permute-start.3) | collective-permute-done | bytes 393248 | tf_op jit(solution)/shard_map/ppermute | solution.py:115
  167.4 11.4 %collective-permute-done.4 = f32[6,32,512]{2,1,0:T(8,128)S(1)} collective-permute-done((f32[6,32,512]{2,1,0:T(8,128)S(1)}, f32[6,32,512]{2,1,0:T(8,128)S(1)}, u32[]{:S(2)}, u32[]{:S(2)}) %collective-permute-start.4) | collective-permute-done | bytes 393248 | tf_op jit(solution)/shard_map/ppermute | solution.py:115
  179.0 3.4 %copy.57 = f32[6,8,32,512]{3,1,2,0:T(8,128)} copy(f32[6,8,32,512]{3,2,1,0:T(8,128)S(1)} %bitcast.121) | data formatting | bytes 6291456
  182.4 8.2 %shard_map.47 = f32[96,16384]{1,0:T(8,128)} custom-call(f32[96,48]{1,0:T(8,128)} %reshape.189.w_ref, f32[48,16384]{1,0:T(8,128)} %bitcast.117), custom_call_target="tpu_custom_call" | custom-call | tf_op jit(solution)/shard_map/pallas_call | solution.py:72
  190.6 3.1 %convert.9 = bf16[96,16384]{1,0:T(8,128)(2,1)S(1)} convert(f32[96,16384]{1,0:T(8,128)} %shard_map.47) | non-fusion elementwise | flops 1572864 | bytes 9437184 | tf_op jit(solution)/shard_map/convert.6
  193.7 1.6 fusion.18
  195.4 0.2 copy.59
  195.6 0.1 collective-permute-start.8
  195.6 1.2 copy.60
  196.9 0.8 slice.57
  197.7 0.6 copy.58
  198.3 0.1 slice.55
  198.3 0.4 copy-done.1
  198.7 0.2 copy.65
  198.9 0.2 copy.64
  199.1 3.9 %collective-permute-start.13 = (bf16[2,6,32,512]{3,2,1,0:T(8,128)(2,1)S(1)}, bf16[2,6,32,512]{3,2,1,0:T(8,128)(2,1)S(1)}, u32[]{:S(2)}, u32[]{:S(2)}) collective-permute-start(bf16[2,6,32,512]{3,2,1,0:T(8,128)(2,1)S(1)} %bitcast.140), channel_id=1, source_target_pairs={{0,12},{2,14},{4,0},{6,2},{8,4},{10,6},{12,8},{14,10},{1,13},{3,15... | collective-permute-start | bytes 1179656 | tf_op jit(solution)/shard_map/ppermute | solution.py:134
  203.0 2.9 %collective-permute-start.14 = (bf16[2,6,32,512]{3,2,1,0:T(8,128)(2,1)S(1)}, bf16[2,6,32,512]{3,2,1,0:T(8,128)(2,1)S(1)}, u32[]{:S(2)}, u32[]{:S(2)}) collective-permute-start(bf16[2,6,32,512]{3,2,1,0:T(8,128)(2,1)S(1)} %bitcast.139), channel_id=1, source_target_pairs={{0,14},{2,0},{4,2},{6,4},{8,6},{10,8},{12,10},{14,12},{1,15},{3,1}... | collective-permute-start | bytes 1179656 | tf_op jit(solution)/shard_map/ppermute | solution.py:134
  205.8 0.2 copy.63
  206.0 0.1 collective-permute-start.12
  206.1 0.2 copy.62
  206.3 0.2 copy.61
  206.5 0.8 broadcast_in_dim.2
  207.3 0.1 constant_dynamic-update-slice_fusion
  207.4 3.2 %collective-permute-done.8 = bf16[2,6,32,512]{3,2,1,0:T(8,128)(2,1)} collective-permute-done((bf16[2,6,32,512]{3,2,1,0:T(8,128)(2,1)S(1)}, bf16[2,6,32,512]{3,2,1,0:T(8,128)(2,1)}, u32[]{:S(2)}, u32[]{:S(2)}) %collective-permute-start.8) | collective-permute-done | bytes 393248 | tf_op jit(solution)/shard_map/ppermute | solution.py:134
  210.6 1.1 convert_dynamic-update-slice_fusion.6
  211.7 0.1 collective-permute-done.9
  211.8 1.1 convert_dynamic-update-slice_fusion.5
  212.9 47.1 %collective-permute-done.10 = bf16[2,6,32,512]{3,2,1,0:T(8,128)(2,1)S(1)} collective-permute-done((bf16[2,6,32,512]{3,2,1,0:T(8,128)(2,1)S(1)}, bf16[2,6,32,512]{3,2,1,0:T(8,128)(2,1)S(1)}, u32[]{:S(2)}, u32[]{:S(2)}) %collective-permute-start.10) | collective-permute-done | bytes 393248 | tf_op jit(solution)/shard_map/ppermute | solution.py:134
  260.0 0.1 convert_dynamic-update-slice_fusion.4
  260.1 8.3 %collective-permute-done.11 = bf16[2,6,32,512]{3,2,1,0:T(8,128)(2,1)S(1)} collective-permute-done((bf16[2,6,32,512]{3,2,1,0:T(8,128)(2,1)S(1)}, bf16[2,6,32,512]{3,2,1,0:T(8,128)(2,1)S(1)}, u32[]{:S(2)}, u32[]{:S(2)}) %collective-permute-start.11) | collective-permute-done | bytes 393248 | tf_op jit(solution)/shard_map/ppermute | solution.py:134
  268.4 0.1 convert_dynamic-update-slice_fusion.3
  268.5 0.1 convert_dynamic-update-slice_fusion.2
  268.6 0.1 convert_dynamic-update-slice_fusion.1
  268.7 0.0 copy-start
  268.8 2.7 copy-done
  271.5 1.0 convert_dynamic-update-slice_fusion
  (28 shorter events, 0.4 us)
Async XLA Ops:
  6.5 56.3 %all-gather.2.cloned.1.call-start = ((), (), s32[]{:S(2)}) async-start(), calls=%async_computation | async-start | bytes 4456448 | tf_op jit(solution)/shard_map/all_gather | solution.py:95
  93.5 6.0 %collective-permute-start = (f32[6,256,512]{2,1,0:T(8,128)}, f32[6,256,512]{2,1,0:T(8,128)}, u32[]{:S(2)}, u32[]{:S(2)}) collective-permute-start(f32[6,256,512]{2,1,0:T(8,128)} %get-tuple-element.12), channel_id=1, source_target_pairs={{0,1},{1,0},{2,3},{3,2},{4,5},{5,4},{6,7},{7,6},{8,9},{9,8},{10,11... | collective-permute-start | bytes 9437192 | tf_op jit(solution)/shard_map/ppermute | solution.py:105
  102.5 15.1 %collective-permute-start.1 = (f32[6,32,512]{2,1,0:T(8,128)}, f32[6,32,512]{2,1,0:T(8,128)}, u32[]{:S(2)}, u32[]{:S(2)}) collective-permute-start(f32[6,32,512]{2,1,0:T(8,128)} %get-tuple-element.10), channel_id=1, source_target_pairs={{0,2},{2,4},{4,6},{6,8},{8,10},{10,12},{12,14},{14,0},{1,3},{3,5},... | collective-permute-start | bytes 1179656 | tf_op jit(solution)/shard_map/ppermute | solution.py:115
  106.8 14.0 %copy-start.2 = (f32[6,32,512]{2,1,0:T(8,128)S(1)}, f32[6,32,512]{2,1,0:T(8,128)}, u32[]{:S(2)}) copy-start(f32[6,32,512]{2,1,0:T(8,128)} %get-tuple-element.7) | copy-start | bytes 1179652
  106.8 14.0 %collective-permute-start.2 = (f32[6,32,512]{2,1,0:T(8,128)}, f32[6,32,512]{2,1,0:T(8,128)S(1)}, u32[]{:S(2)}, u32[]{:S(2)}) collective-permute-start(f32[6,32,512]{2,1,0:T(8,128)} %get-tuple-element.9), channel_id=1, source_target_pairs={{0,4},{2,6},{4,8},{6,10},{8,12},{10,14},{12,0},{14,2},{1,5},{3,7},... | collective-permute-start | bytes 1179656 | tf_op jit(solution)/shard_map/ppermute | solution.py:115
  109.3 69.6 %collective-permute-start.7 = (f32[6,32,512]{2,1,0:T(8,128)S(1)}, f32[6,32,512]{2,1,0:T(8,128)S(1)}, u32[]{:S(2)}, u32[]{:S(2)}) collective-permute-start(f32[6,32,512]{2,1,0:T(8,128)S(1)} %add_bitcast_fusion), channel_id=1, source_target_pairs={{0,14},{2,0},{4,2},{6,4},{8,6},{10,8},{12,10},{14,12},{1,15},{3,1}... | collective-permute-start | bytes 1179656 | tf_op jit(solution)/shard_map/ppermute | solution.py:115
  113.6 65.3 %collective-permute-start.6 = (f32[6,32,512]{2,1,0:T(8,128)S(1)}, f32[6,32,512]{2,1,0:T(8,128)S(1)}, u32[]{:S(2)}, u32[]{:S(2)}) collective-permute-start(f32[6,32,512]{2,1,0:T(8,128)S(1)} %get-tuple-element.5), channel_id=1, source_target_pairs={{0,12},{2,14},{4,0},{6,2},{8,4},{10,6},{12,8},{14,10},{1,13},{3,15... | collective-permute-start | bytes 1179656 | tf_op jit(solution)/shard_map/ppermute | solution.py:115
  114.1 64.7 %collective-permute-start.5 = (f32[6,32,512]{2,1,0:T(8,128)}, f32[6,32,512]{2,1,0:T(8,128)S(1)}, u32[]{:S(2)}, u32[]{:S(2)}) collective-permute-start(f32[6,32,512]{2,1,0:T(8,128)} %get-tuple-element.6), channel_id=1, source_target_pairs={{0,10},{2,12},{4,14},{6,0},{8,2},{10,4},{12,6},{14,8},{1,11},{3,13... | collective-permute-start | bytes 1179656 | tf_op jit(solution)/shard_map/ppermute | solution.py:115
  117.6 49.7 %collective-permute-start.3 = (f32[6,32,512]{2,1,0:T(8,128)}, f32[6,32,512]{2,1,0:T(8,128)S(1)}, u32[]{:S(2)}, u32[]{:S(2)}) collective-permute-start(f32[6,32,512]{2,1,0:T(8,128)} %get-tuple-element.8), channel_id=1, source_target_pairs={{0,6},{2,8},{4,10},{6,12},{8,14},{10,0},{12,2},{14,4},{1,7},{3,9},... | collective-permute-start | bytes 1179656 | tf_op jit(solution)/shard_map/ppermute | solution.py:115
  120.8 57.9 %collective-permute-start.4 = (f32[6,32,512]{2,1,0:T(8,128)S(1)}, f32[6,32,512]{2,1,0:T(8,128)S(1)}, u32[]{:S(2)}, u32[]{:S(2)}) collective-permute-start(f32[6,32,512]{2,1,0:T(8,128)S(1)} %copy-done.2), channel_id=1, source_target_pairs={{0,8},{2,10},{4,12},{6,14},{8,0},{10,2},{12,4},{14,6},{1,9},{3,11}... | collective-permute-start | bytes 1179656 | tf_op jit(solution)/shard_map/ppermute | solution.py:115
  195.4 2.3 slice-start
  195.6 15.0 %collective-permute-start.8 = (bf16[2,6,32,512]{3,2,1,0:T(8,128)(2,1)S(1)}, bf16[2,6,32,512]{3,2,1,0:T(8,128)(2,1)}, u32[]{:S(2)}, u32[]{:S(2)}) collective-permute-start(bf16[2,6,32,512]{3,2,1,0:T(8,128)(2,1)S(1)} %bitcast.138), channel_id=1, source_target_pairs={{0,2},{2,4},{4,6},{6,8},{8,10},{10,12},{12,14},{14,0},{1,3},{3,5},... | collective-permute-start | bytes 1179656 | tf_op jit(solution)/shard_map/ppermute | solution.py:134
  197.7 14.1 %collective-permute-start.9 = (bf16[2,6,32,512]{3,2,1,0:T(8,128)(2,1)}, bf16[2,6,32,512]{3,2,1,0:T(8,128)(2,1)}, u32[]{:S(2)}, u32[]{:S(2)}) collective-permute-start(bf16[2,6,32,512]{3,2,1,0:T(8,128)(2,1)} %bitcast.48), channel_id=1, source_target_pairs={{0,4},{2,6},{4,8},{6,10},{8,12},{10,14},{12,0},{14,2},{1,5},{3,7},... | collective-permute-start | bytes 1179656 | tf_op jit(solution)/shard_map/ppermute | solution.py:134
  197.7 1.0 copy-start.1
  199.1 69.5 %collective-permute-start.13 = (bf16[2,6,32,512]{3,2,1,0:T(8,128)(2,1)S(1)}, bf16[2,6,32,512]{3,2,1,0:T(8,128)(2,1)S(1)}, u32[]{:S(2)}, u32[]{:S(2)}) collective-permute-start(bf16[2,6,32,512]{3,2,1,0:T(8,128)(2,1)S(1)} %bitcast.140), channel_id=1, source_target_pairs={{0,12},{2,14},{4,0},{6,2},{8,4},{10,6},{12,8},{14,10},{1,13},{3,15... | collective-permute-start | bytes 1179656 | tf_op jit(solution)/shard_map/ppermute | solution.py:134
  203.0 65.8 %collective-permute-start.14 = (bf16[2,6,32,512]{3,2,1,0:T(8,128)(2,1)S(1)}, bf16[2,6,32,512]{3,2,1,0:T(8,128)(2,1)S(1)}, u32[]{:S(2)}, u32[]{:S(2)}) collective-permute-start(bf16[2,6,32,512]{3,2,1,0:T(8,128)(2,1)S(1)} %bitcast.139), channel_id=1, source_target_pairs={{0,14},{2,0},{4,2},{6,4},{8,6},{10,8},{12,10},{14,12},{1,15},{3,1}... | collective-permute-start | bytes 1179656 | tf_op jit(solution)/shard_map/ppermute | solution.py:134
  206.0 62.5 %collective-permute-start.12 = (bf16[2,6,32,512]{3,2,1,0:T(8,128)(2,1)S(1)}, bf16[2,6,32,512]{3,2,1,0:T(8,128)(2,1)S(1)}, u32[]{:S(2)}, u32[]{:S(2)}) collective-permute-start(bf16[2,6,32,512]{3,2,1,0:T(8,128)(2,1)S(1)} %bitcast.141), channel_id=1, source_target_pairs={{0,10},{2,12},{4,14},{6,0},{8,2},{10,4},{12,6},{14,8},{1,11},{3,13... | collective-permute-start | bytes 1179656 | tf_op jit(solution)/shard_map/ppermute | solution.py:134
  210.6 49.5 %collective-permute-start.10 = (bf16[2,6,32,512]{3,2,1,0:T(8,128)(2,1)S(1)}, bf16[2,6,32,512]{3,2,1,0:T(8,128)(2,1)S(1)}, u32[]{:S(2)}, u32[]{:S(2)}) collective-permute-start(bf16[2,6,32,512]{3,2,1,0:T(8,128)(2,1)S(1)} %bitcast.143), channel_id=1, source_target_pairs={{0,6},{2,8},{4,10},{6,12},{8,14},{10,0},{12,2},{14,4},{1,7},{3,9},... | collective-permute-start | bytes 1179656 | tf_op jit(solution)/shard_map/ppermute | solution.py:134
  211.8 56.6 %collective-permute-start.11 = (bf16[2,6,32,512]{3,2,1,0:T(8,128)(2,1)S(1)}, bf16[2,6,32,512]{3,2,1,0:T(8,128)(2,1)S(1)}, u32[]{:S(2)}, u32[]{:S(2)}) collective-permute-start(bf16[2,6,32,512]{3,2,1,0:T(8,128)(2,1)S(1)} %bitcast.142), channel_id=1, source_target_pairs={{0,8},{2,10},{4,12},{6,14},{8,0},{10,2},{12,4},{14,6},{1,9},{3,11}... | collective-permute-start | bytes 1179656 | tf_op jit(solution)/shard_map/ppermute | solution.py:134
  268.7 2.7 copy-start
Sparse Core Ops, SparseCore 0:
  9.5 53.2 all-gather.1

commit v15 on v5

--- a/solution.py
+++ b/solution.py
@@ -8,37 +8,39 @@
 from jax.sharding import PartitionSpec as P
 
 
-def _project_kernel(rows_ref, cols_ref, pb_ref, pt_ref, s_ref, o_ref, lt_ref, img_ref):
+_NT = (((1,), (1,)), ((), ()))
+
+
+def _project_kernel(rows_ref, cols_ref, pt_ref, s_ref, o_ref, lt_ref, it_ref):
     b = pl.program_id(0)
     nblk = s_ref.shape[1]
     bs = s_ref.shape[2]
-    last = pb_ref.shape[0] - 1
+    last = pt_ref.shape[0] - 1
     for n in range(nblk):
         c = jnp.minimum(jnp.maximum(cols_ref[b * nblk + n], 0), last)
         r = jnp.minimum(jnp.maximum(rows_ref[b * nblk + n], 0), last)
-        im = jnp.dot(s_ref[0, n], pb_ref[c], preferred_element_type=jnp.float32)
-        img_ref[n * bs:(n + 1) * bs, :] = im.astype(jnp.bfloat16)
+        im = lax.dot_general(pt_ref[c], s_ref[0, n], _NT, preferred_element_type=jnp.float32)
+        it_ref[:, n * bs:(n + 1) * bs] = im.astype(jnp.bfloat16)
         lt_ref[:, n * bs:(n + 1) * bs] = pt_ref[r]
-    o_ref[0] = jnp.dot(lt_ref[...], img_ref[...], preferred_element_type=jnp.float32)
+    o_ref[0] = lax.dot_general(lt_ref[...], it_ref[...], _NT, preferred_element_type=jnp.float32)
 
 
-def _project(pb, pt, stiffness, rows, cols, start, nbl):
+def _project(pt, stiffness, rows, cols, start, nbl):
     _, nblk, bs, _ = stiffness.shape
-    nrb, _, modes = pb.shape
+    nrb, modes, _ = pt.shape
     rows = rows[start * nblk:(start + nbl) * nblk]
     cols = cols[start * nblk:(start + nbl) * nblk]
     grid_spec = pltpu.PrefetchScalarGridSpec(
         num_scalar_prefetch=2,
         grid=(nbl,),
         in_specs=[
-            pl.BlockSpec((nrb, bs, modes), lambda b, rr, cc: (0, 0, 0)),
             pl.BlockSpec((nrb, modes, bs), lambda b, rr, cc: (0, 0, 0)),
             pl.BlockSpec((1, nblk, bs, bs), lambda b, rr, cc: (b + start, 0, 0, 0)),
         ],
         out_specs=pl.BlockSpec((1, modes, modes), lambda b, rr, cc: (b, 0, 0)),
         scratch_shapes=[
             pltpu.VMEM((modes, nblk * bs), jnp.bfloat16),
-            pltpu.VMEM((nblk * bs, modes), jnp.bfloat16),
+            pltpu.VMEM((modes, nblk * bs), jnp.bfloat16),
         ],
     )
     return pl.pallas_call(
@@ -49,7 +51,7 @@
             dimension_semantics=("arbitrary",),
             vmem_limit_bytes=56 * 1024 * 1024,
         ),
-    )(rows, cols, pb, pt, stiffness)
+    )(rows, cols, pt, stiffness)
 
 
 def _dft_kernel(w_ref, x_ref, o_ref):
@@ -91,9 +93,8 @@
     nbl, nblk, bs, _ = stiffness.shape
     modes = panel.shape[-1]
     nbd = lax.axis_size("blade")
-    whole = lax.all_gather(panel, ("blade", "dof"), axis=0, tiled=True)
-    pb = whole.reshape(-1, bs, modes)
-    pt = jnp.swapaxes(pb, 1, 2)
+    mine = jnp.swapaxes(panel.reshape(-1, bs, modes), 1, 2)
+    pt = lax.all_gather(mine, ("blade", "dof"), axis=0, tiled=True)
     rows_all = block_rows.reshape(-1)
     cols_all = block_cols.reshape(-1)
     me = lax.axis_index("blade")
@@ -104,8 +105,14 @@
     size = nbl // groups
     parts = [[] for _ in range(nbd)]
     for g in range(groups):
-        proj = _project(pb, pt, stiffness, rows_all, cols_all, g * size, size)
-        half = lax.psum_scatter(proj, "dof", scatter_dimension=1, tiled=True)
+        proj = _project(pt, stiffness, rows_all, cols_all, g * size, size)
+        if lax.axis_size("dof") == 2:
+            d = lax.axis_index("dof")
+            mine = lax.dynamic_slice_in_dim(proj, d * rows_half, rows_half, axis=1)
+            other = lax.dynamic_slice_in_dim(proj, (1 - d) * rows_half, rows_half, axis=1)
+            half = mine + lax.ppermute(other, "dof", [(0, 1), (1, 0)])
+        else:
+            half = lax.psum_scatter(proj, "dof", scatter_dimension=1, tiled=True)
         chunks = half.reshape(size, nbd, r, modes)
         for s in range(nbd):
             piece = lax.dynamic_index_in_dim(chunks, (me + s) % nbd, axis=1, keepdims=False)
@@ -129,7 +136,9 @@
     for t in range(nbd):
         piece = spec[t]
         if t:
+            piece = piece.astype(jnp.bfloat16)
             piece = lax.ppermute(piece, "blade", [(j, (j + t) % nbd) for j in range(nbd)])
+            piece = piece.astype(jnp.float32)
         at = ((me - t) % nbd) * r
         out = lax.dynamic_update_slice(out, piece, (0, 0, at, 0))
     return out

time: 356 us -> 280 us (0.79)
  the two profiles are of different devices: /device:TPU:28 before, /device:TPU:0 now
where the time goes in v15:
time: 280 us; the launch traced here: 279 us
  waiting for transfers between devices  147 us (52%)
  starting transfers between devices  43.5 us (16%)
  Pallas kernels  37.4 us (13%)
  local copies, waits for them, and re-layouts  25.2 us (9%)
  between operations  13.8 us (5%)
  other arithmetic  11.8 us (4%)
    ppermute x7, waiting for transfers between devices, body(): lax.ppermute(piece, 'blade', [(j, (j + t) % nbd) for j in range(nbd)])  59.6 us
    all_gather x1, waiting for transfers between devices, body(): pt = lax.all_gather(mine, ('blade', 'dof'), axis=0, tiled=True)  51.6 us
    ppermute x14, waiting for transfers between devices, body(): lax.ppermute(piece, 'blade', [(j, (j + s) % nbd) for j in range(nbd)])  35.6 us
    ppermute x14, starting transfers between devices, body(): lax.ppermute(piece, 'blade', [(j, (j + s) % nbd) for j in range(nbd)])  35.1 us
    pallas_call x2, Pallas kernels, _project(): pl.pallas_call(_project_kernel, grid_spec=grid_spec, out_shape=jax.ShapeD...  29.2 us
    unnamed x25, local copies, waits for them, and re-layouts  10.2 us
    pallas_call x1, Pallas kernels, _dft(): pl.pallas_call(_dft_kernel, grid=(n // tn,), in_specs=[pl.BlockSpec((rows...  8.2 us
    ppermute x7, starting transfers between devices, body(): lax.ppermute(piece, 'blade', [(j, (j + t) % nbd) for j in range(nbd)])  7.86 us
  transfers between devices with their start and end apart: 24, of which 12 were waited for; matrix products, arithmetic and copies ran while one was open for 7% of the time, Pallas kernels for 5%

profile of v15, /device:TPU:0, one launch (start us, length us, event | category | flops | bytes accessed | tf_op | source)
XLA Modules:
  0.0 278.9 jit_solution(13537552966324422263)
XLA Ops:
  6.5 1.8 copy.6
  8.4 0.8 fusion.20
  9.1 0.7 slice.68.rows_ref
  9.8 0.8 fusion.19
  10.5 0.7 slice.70.cols_ref
  11.2 51.6 %all-gather.2.cloned.1.call-done.pt_ref = bf16[32,512,128]{2,1,0:T(8,128)(2,1)} async-done(((bf16[2,512,128]{2,1,0:T(8,128)(2,1)}), bf16[32,512,128]{2,1,0:T(8,128)(2,1)}) %all-gather.2.cloned.1.call-update) | async-done | bytes 4194320 | tf_op jit(solution)/shard_map/all_gather | solution.py:97
  62.8 14.6 %shard_map.47 = f32[3,512,512]{2,1,0:T(8,128)} custom-call(s32[96]{0:T(128)} %slice.68.rows_ref, s32[96]{0:T(128)} %slice.70.cols_ref, bf16[32,512,128]{2,1,0:T(8,128)(2,1)} %all-gather.2.cloned.1.call-done.pt_ref, bf16[6,32,128,128]{3,2,1,0:T(8,128)(2,1)} %s_ref.3), custom_call_target="tpu_custom_call" | custom-call | tf_op jit(solution)/shard_map/pallas_call | solution.py:46
  77.4 2.8 constant_dynamic-slice_fusion
  80.2 0.3 collective-permute-start.1
  80.5 0.6 slice.64.rows_ref
  81.1 0.6 slice.66.cols_ref
  81.7 14.6 %shard_map.46 = f32[3,512,512]{2,1,0:T(8,128)} custom-call(s32[96]{0:T(128)} %slice.64.rows_ref, s32[96]{0:T(128)} %slice.66.cols_ref, bf16[32,512,128]{2,1,0:T(8,128)(2,1)} %all-gather.2.cloned.1.call-done.pt_ref, bf16[6,32,128,128]{3,2,1,0:T(8,128)(2,1)} %s_ref.3), custom_call_target="tpu_custom_call" | custom-call | tf_op jit(solution)/shard_map/pallas_call | solution.py:46
  96.3 2.8 %constant_dynamic-slice_fusion.1 = f32[3,256,512]{2,1,0:T(8,128)} fusion(f32[3,512,512]{2,1,0:T(8,128)} %shard_map.46, s32[]{:T(128)S(6)} %select_n.185), kind=kLoop, calls=%fused_computation.53 | loop fusion | bytes 3145732 | tf_op jit(solution)/shard_map/dynamic_slice | solution.py:112
  99.1 0.2 collective-permute-start
  99.6 0.2 fusion.12
  99.9 1.9 dynamic-slice_add_fusion
  101.8 0.2 dynamic-slice_bitcast_fusion
  102.0 0.6 collective-permute-start.3
  102.6 0.3 collective-permute-done
  102.9 1.8 dynamic-slice_add_fusion.1
  104.7 0.2 dynamic-slice_bitcast_fusion.1
  104.8 2.1 collective-permute-start.2
  107.0 0.6 reshape.164.w_ref
  107.6 2.6 collective-permute-start.15
  110.2 0.6 collective-permute-start.4
  110.8 1.7 collective-permute-done.3
  112.6 4.3 %collective-permute-done.2 = f32[3,32,512]{2,1,0:T(8,128)} collective-permute-done((f32[3,32,512]{2,1,0:T(8,128)S(1)}, f32[3,32,512]{2,1,0:T(8,128)}, u32[]{:S(2)}, u32[]{:S(2)}) %collective-permute-start.2) | collective-permute-done | bytes 196640 | tf_op jit(solution)/shard_map/ppermute | solution.py:120
  116.9 2.2 collective-permute-start.6
  119.1 1.0 fusion.1
  120.1 2.2 collective-permute-start.9
  122.3 2.0 collective-permute-done.4
  124.3 2.2 collective-permute-start.8
  126.5 19.1 %collective-permute-done.7 = f32[3,32,512]{2,1,0:T(8,128)S(1)} collective-permute-done((f32[3,32,512]{2,1,0:T(8,128)S(1)}, f32[3,32,512]{2,1,0:T(8,128)S(1)}, u32[]{:S(2)}, u32[]{:S(2)}) %collective-permute-start.7) | collective-permute-done | bytes 196640 | tf_op jit(solution)/shard_map/ppermute | solution.py:120
  145.6 4.3 %collective-permute-done.6 = f32[3,32,512]{2,1,0:T(8,128)S(1)} collective-permute-done((f32[3,32,512]{2,1,0:T(8,128)S(1)}, f32[3,32,512]{2,1,0:T(8,128)S(1)}, u32[]{:S(2)}, u32[]{:S(2)}) %collective-permute-start.6) | collective-permute-done | bytes 196640 | tf_op jit(solution)/shard_map/ppermute | solution.py:120
  149.9 7.8 %collective-permute-start.13 = (f32[3,32,512]{2,1,0:T(8,128)S(1)}, f32[3,32,512]{2,1,0:T(8,128)S(1)}, u32[]{:S(2)}, u32[]{:S(2)}) collective-permute-start(f32[3,32,512]{2,1,0:T(8,128)S(1)} %get-tuple-element.21), channel_id=1, source_target_pairs={{0,12},{2,14},{4,0},{6,2},{8,4},{10,6},{12,8},{14,10},{1,13},{3,15... | collective-permute-start | bytes 589832 | tf_op jit(solution)/shard_map/ppermute | solution.py:120
  157.8 9.6 %collective-permute-start.12 = (f32[3,32,512]{2,1,0:T(8,128)S(1)}, f32[3,32,512]{2,1,0:T(8,128)S(1)}, u32[]{:S(2)}, u32[]{:S(2)}) collective-permute-start(f32[3,32,512]{2,1,0:T(8,128)S(1)} %get-tuple-element.13), channel_id=1, source_target_pairs={{0,12},{2,14},{4,0},{6,2},{8,4},{10,6},{12,8},{14,10},{1,13},{3,15... | collective-permute-start | bytes 589832 | tf_op jit(solution)/shard_map/ppermute | solution.py:120
  167.4 5.1 %collective-permute-start.14 = (f32[3,32,512]{2,1,0:T(8,128)S(1)}, f32[3,32,512]{2,1,0:T(8,128)S(1)}, u32[]{:S(2)}, u32[]{:S(2)}) collective-permute-start(f32[3,32,512]{2,1,0:T(8,128)S(1)} %get-tuple-element.12), channel_id=1, source_target_pairs={{0,14},{2,0},{4,2},{6,4},{8,6},{10,8},{12,10},{14,12},{1,15},{3,1}... | collective-permute-start | bytes 589832 | tf_op jit(solution)/shard_map/ppermute | solution.py:120
  172.6 4.2 %collective-permute-done.14 = f32[3,32,512]{2,1,0:T(8,128)S(1)} collective-permute-done((f32[3,32,512]{2,1,0:T(8,128)S(1)}, f32[3,32,512]{2,1,0:T(8,128)S(1)}, u32[]{:S(2)}, u32[]{:S(2)}) %collective-permute-start.14) | collective-permute-done | bytes 196640 | tf_op jit(solution)/shard_map/ppermute | solution.py:120
  176.8 3.4 %copy.7 = f32[6,8,32,512]{3,1,2,0:T(8,128)} copy(f32[6,8,32,512]{3,2,1,0:T(8,128)S(1)} %bitcast.108) | data formatting | bytes 6291456
  180.3 8.2 %shard_map.48 = f32[96,16384]{1,0:T(8,128)} custom-call(f32[96,48]{1,0:T(8,128)} %reshape.164.w_ref, f32[48,16384]{1,0:T(8,128)} %bitcast.105), custom_call_target="tpu_custom_call" | custom-call | tf_op jit(solution)/shard_map/pallas_call | solution.py:74
  188.5 3.1 %convert.9 = bf16[96,16384]{1,0:T(8,128)(2,1)S(1)} convert(f32[96,16384]{1,0:T(8,128)} %shard_map.48) | non-fusion elementwise | flops 1572864 | bytes 9437184 | tf_op jit(solution)/shard_map/convert.6
  191.6 1.6 fusion.18
  193.2 0.2 copy.9
  193.4 2.7 collective-permute-start.16
  196.1 1.2 copy.10
  197.3 0.8 slice.89
  198.1 0.9 collective-permute-start.17
  199.0 0.6 copy.8
  199.7 0.4 copy-done.3
  200.1 0.2 copy.15
  200.2 0.2 copy.14
  200.4 2.9 %collective-permute-start.21 = (bf16[2,6,32,512]{3,2,1,0:T(8,128)(2,1)S(1)}, bf16[2,6,32,512]{3,2,1,0:T(8,128)(2,1)S(1)}, u32[]{:S(2)}, u32[]{:S(2)}) collective-permute-start(bf16[2,6,32,512]{3,2,1,0:T(8,128)(2,1)S(1)} %bitcast.127), channel_id=1, source_target_pairs={{0,12},{2,14},{4,0},{6,2},{8,4},{10,6},{12,8},{14,10},{1,13},{3,15... | collective-permute-start | bytes 1179656 | tf_op jit(solution)/shard_map/ppermute | solution.py:140
  203.4 0.7 collective-permute-start.22
  204.3 0.6 collective-permute-start.20
  205.1 0.2 copy.11
  205.3 0.8 broadcast_in_dim.2
  206.2 2.6 collective-permute-done.16
  208.8 1.1 convert_dynamic-update-slice_fusion.6
  209.9 2.4 collective-permute-done.17
  212.3 1.1 convert_dynamic-update-slice_fusion.5
  213.4 43.0 %collective-permute-done.18 = bf16[2,6,32,512]{3,2,1,0:T(8,128)(2,1)S(1)} collective-permute-done((bf16[2,6,32,512]{3,2,1,0:T(8,128)(2,1)S(1)}, bf16[2,6,32,512]{3,2,1,0:T(8,128)(2,1)S(1)}, u32[]{:S(2)}, u32[]{:S(2)}) %collective-permute-start.18) | collective-permute-done | bytes 393248 | tf_op jit(solution)/shard_map/ppermute | solution.py:140
  256.4 11.6 %collective-permute-done.19 = bf16[2,6,32,512]{3,2,1,0:T(8,128)(2,1)S(1)} collective-permute-done((bf16[2,6,32,512]{3,2,1,0:T(8,128)(2,1)S(1)}, bf16[2,6,32,512]{3,2,1,0:T(8,128)(2,1)S(1)}, u32[]{:S(2)}, u32[]{:S(2)}) %collective-permute-start.19) | collective-permute-done | bytes 393248 | tf_op jit(solution)/shard_map/ppermute | solution.py:140
  268.4 2.7 copy-done.2
  271.1 1.0 convert_dynamic-update-slice_fusion
  (54 shorter events, 1.5 us)
Async XLA Ops:
  6.5 56.3 %all-gather.2.cloned.1.call-start = ((), (), s32[]{:S(2)}) async-start(), calls=%async_computation | async-start | bytes 4456448 | tf_op jit(solution)/shard_map/all_gather | solution.py:97
  80.2 19.7 %collective-permute-start.1 = (f32[3,256,512]{2,1,0:T(8,128)}, f32[3,256,512]{2,1,0:T(8,128)}, u32[]{:S(2)}, u32[]{:S(2)}) collective-permute-start(f32[3,256,512]{2,1,0:T(8,128)} %constant_dynamic-slice_fusion), channel_id=1, source_target_pairs={{0,1},{1,0},{2,3},{3,2},{4,5},{5,4},{6,7},{7,6},{8,9},{9,8},{10,11... | collective-permute-start | bytes 4718600 | tf_op jit(solution)/shard_map/ppermute | solution.py:113
  96.3 3.6 %copy-start.1 = (f32[3,512,512]{2,1,0:T(8,128)S(1)}, f32[3,512,512]{2,1,0:T(8,128)}, u32[]{:S(2)}) copy-start(f32[3,512,512]{2,1,0:T(8,128)} %shard_map.47) | copy-start | bytes 9437188
  99.1 3.8 %collective-permute-start = (f32[3,256,512]{2,1,0:T(8,128)}, f32[3,256,512]{2,1,0:T(8,128)}, u32[]{:S(2)}, u32[]{:S(2)}) collective-permute-start(f32[3,256,512]{2,1,0:T(8,128)} %constant_dynamic-slice_fusion.1), channel_id=1, source_target_pairs={{0,1},{1,0},{2,3},{3,2},{4,5},{5,4},{6,7},{7,6},{8,9},{9,8},{10,11... | collective-permute-start | bytes 4718600 | tf_op jit(solution)/shard_map/ppermute | solution.py:113
  99.9 3.0 %copy-start = (f32[3,512,512]{2,1,0:T(8,128)S(1)}, f32[3,512,512]{2,1,0:T(8,128)}, u32[]{:S(2)}) copy-start(f32[3,512,512]{2,1,0:T(8,128)} %shard_map.46) | copy-start | bytes 9437188
  102.0 10.6 %collective-permute-start.3 = (f32[3,32,512]{2,1,0:T(8,128)S(1)}, f32[3,32,512]{2,1,0:T(8,128)S(1)}, u32[]{:S(2)}, u32[]{:S(2)}) collective-permute-start(f32[3,32,512]{2,1,0:T(8,128)S(1)} %get-tuple-element.26), channel_id=1, source_target_pairs={{0,2},{2,4},{4,6},{6,8},{8,10},{10,12},{12,14},{14,0},{1,3},{3,5},... | collective-permute-start | bytes 589832 | tf_op jit(solution)/shard_map/ppermute | solution.py:120
  104.8 12.1 %collective-permute-start.2 = (f32[3,32,512]{2,1,0:T(8,128)S(1)}, f32[3,32,512]{2,1,0:T(8,128)}, u32[]{:S(2)}, u32[]{:S(2)}) collective-permute-start(f32[3,32,512]{2,1,0:T(8,128)S(1)} %get-tuple-element.18), channel_id=1, source_target_pairs={{0,2},{2,4},{4,6},{6,8},{8,10},{10,12},{12,14},{14,0},{1,3},{3,5},... | collective-permute-start | bytes 589832 | tf_op jit(solution)/shard_map/ppermute | solution.py:120
  107.6 65.0 %collective-permute-start.15 = (f32[3,32,512]{2,1,0:T(8,128)S(1)}, f32[3,32,512]{2,1,0:T(8,128)S(1)}, u32[]{:S(2)}, u32[]{:S(2)}) collective-permute-start(f32[3,32,512]{2,1,0:T(8,128)S(1)} %get-tuple-element.20), channel_id=1, source_target_pairs={{0,14},{2,0},{4,2},{6,4},{8,6},{10,8},{12,10},{14,12},{1,15},{3,1}... | collective-permute-start | bytes 589832 | tf_op jit(solution)/shard_map/ppermute | solution.py:120
  110.2 9.8 %collective-permute-start.5 = (f32[3,32,512]{2,1,0:T(8,128)S(1)}, f32[3,32,512]{2,1,0:T(8,128)S(1)}, u32[]{:S(2)}, u32[]{:S(2)}) collective-permute-start(f32[3,32,512]{2,1,0:T(8,128)S(1)} %get-tuple-element.25), channel_id=1, source_target_pairs={{0,4},{2,6},{4,8},{6,10},{8,12},{10,14},{12,0},{14,2},{1,5},{3,7},... | collective-permute-start | bytes 589832 | tf_op jit(solution)/shard_map/ppermute | solution.py:120
  110.2 14.0 %collective-permute-start.4 = (f32[3,32,512]{2,1,0:T(8,128)S(1)}, f32[3,32,512]{2,1,0:T(8,128)S(1)}, u32[]{:S(2)}, u32[]{:S(2)}) collective-permute-start(f32[3,32,512]{2,1,0:T(8,128)S(1)} %get-tuple-element.17), channel_id=1, source_target_pairs={{0,4},{2,6},{4,8},{6,10},{8,12},{10,14},{12,0},{14,2},{1,5},{3,7},... | collective-permute-start | bytes 589832 | tf_op jit(solution)/shard_map/ppermute | solution.py:120
  112.6 33.0 %collective-permute-start.7 = (f32[3,32,512]{2,1,0:T(8,128)S(1)}, f32[3,32,512]{2,1,0:T(8,128)S(1)}, u32[]{:S(2)}, u32[]{:S(2)}) collective-permute-start(f32[3,32,512]{2,1,0:T(8,128)S(1)} %get-tuple-element.24), channel_id=1, source_target_pairs={{0,6},{2,8},{4,10},{6,12},{8,14},{10,0},{12,2},{14,4},{1,7},{3,9},... | collective-permute-start | bytes 589832 | tf_op jit(solution)/shard_map/ppermute | solution.py:120
  116.9 33.0 %collective-permute-start.6 = (f32[3,32,512]{2,1,0:T(8,128)S(1)}, f32[3,32,512]{2,1,0:T(8,128)S(1)}, u32[]{:S(2)}, u32[]{:S(2)}) collective-permute-start(f32[3,32,512]{2,1,0:T(8,128)S(1)} %get-tuple-element.16), channel_id=1, source_target_pairs={{0,6},{2,8},{4,10},{6,12},{8,14},{10,0},{12,2},{14,4},{1,7},{3,9},... | collective-permute-start | bytes 589832 | tf_op jit(solution)/shard_map/ppermute | solution.py:120
  120.1 29.8 %collective-permute-start.9 = (f32[3,32,512]{2,1,0:T(8,128)S(1)}, f32[3,32,512]{2,1,0:T(8,128)S(1)}, u32[]{:S(2)}, u32[]{:S(2)}) collective-permute-start(f32[3,32,512]{2,1,0:T(8,128)S(1)} %get-tuple-element.23), channel_id=1, source_target_pairs={{0,8},{2,10},{4,12},{6,14},{8,0},{10,2},{12,4},{14,6},{1,9},{3,11}... | collective-permute-start | bytes 589832 | tf_op jit(solution)/shard_map/ppermute | solution.py:120
  124.3 33.5 %collective-permute-start.8 = (f32[3,32,512]{2,1,0:T(8,128)S(1)}, f32[3,32,512]{2,1,0:T(8,128)S(1)}, u32[]{:S(2)}, u32[]{:S(2)}) collective-permute-start(f32[3,32,512]{2,1,0:T(8,128)S(1)} %get-tuple-element.15), channel_id=1, source_target_pairs={{0,8},{2,10},{4,12},{6,14},{8,0},{10,2},{12,4},{14,6},{1,9},{3,11}... | collective-permute-start | bytes 589832 | tf_op jit(solution)/shard_map/ppermute | solution.py:120
  145.6 21.8 %collective-permute-start.11 = (f32[3,32,512]{2,1,0:T(8,128)S(1)}, f32[3,32,512]{2,1,0:T(8,128)S(1)}, u32[]{:S(2)}, u32[]{:S(2)}) collective-permute-start(f32[3,32,512]{2,1,0:T(8,128)S(1)} %get-tuple-element.22), channel_id=1, source_target_pairs={{0,10},{2,12},{4,14},{6,0},{8,2},{10,4},{12,6},{14,8},{1,11},{3,13... | collective-permute-start | bytes 589832 | tf_op jit(solution)/shard_map/ppermute | solution.py:120
  149.9 22.6 %collective-permute-start.10 = (f32[3,32,512]{2,1,0:T(8,128)S(1)}, f32[3,32,512]{2,1,0:T(8,128)S(1)}, u32[]{:S(2)}, u32[]{:S(2)}) collective-permute-start(f32[3,32,512]{2,1,0:T(8,128)S(1)} %get-tuple-element.14), channel_id=1, source_target_pairs={{0,10},{2,12},{4,14},{6,0},{8,2},{10,4},{12,6},{14,8},{1,11},{3,13... | collective-permute-start | bytes 589832 | tf_op jit(solution)/shard_map/ppermute | solution.py:120
  149.9 22.6 %collective-permute-start.13 = (f32[3,32,512]{2,1,0:T(8,128)S(1)}, f32[3,32,512]{2,1,0:T(8,128)S(1)}, u32[]{:S(2)}, u32[]{:S(2)}) collective-permute-start(f32[3,32,512]{2,1,0:T(8,128)S(1)} %get-tuple-element.21), channel_id=1, source_target_pairs={{0,12},{2,14},{4,0},{6,2},{8,4},{10,6},{12,8},{14,10},{1,13},{3,15... | collective-permute-start | bytes 589832 | tf_op jit(solution)/shard_map/ppermute | solution.py:120
  157.8 14.8 %collective-permute-start.12 = (f32[3,32,512]{2,1,0:T(8,128)S(1)}, f32[3,32,512]{2,1,0:T(8,128)S(1)}, u32[]{:S(2)}, u32[]{:S(2)}) collective-permute-start(f32[3,32,512]{2,1,0:T(8,128)S(1)} %get-tuple-element.13), channel_id=1, source_target_pairs={{0,12},{2,14},{4,0},{6,2},{8,4},{10,6},{12,8},{14,10},{1,13},{3,15... | collective-permute-start | bytes 589832 | tf_op jit(solution)/shard_map/ppermute | solution.py:120
  167.4 9.4 %collective-permute-start.14 = (f32[3,32,512]{2,1,0:T(8,128)S(1)}, f32[3,32,512]{2,1,0:T(8,128)S(1)}, u32[]{:S(2)}, u32[]{:S(2)}) collective-permute-start(f32[3,32,512]{2,1,0:T(8,128)S(1)} %get-tuple-element.12), channel_id=1, source_target_pairs={{0,14},{2,0},{4,2},{6,4},{8,6},{10,8},{12,10},{14,12},{1,15},{3,1}... | collective-permute-start | bytes 589832 | tf_op jit(solution)/shard_map/ppermute | solution.py:120
  193.2 5.8 %slice-start = ((f32[96,16384]{1,0:T(8,128)}), f32[12,16384]{1,0:T(8,128)S(1)}, s32[]{:S(2)}) async-start(f32[96,16384]{1,0:T(8,128)} %shard_map.48), calls=%async_computation.1 | async-start | bytes 2097152 | tf_op jit(solution)/shard_map/slice | solution.py:137
  193.4 15.4 %collective-permute-start.16 = (bf16[2,6,32,512]{3,2,1,0:T(8,128)(2,1)S(1)}, bf16[2,6,32,512]{3,2,1,0:T(8,128)(2,1)}, u32[]{:S(2)}, u32[]{:S(2)}) collective-permute-start(bf16[2,6,32,512]{3,2,1,0:T(8,128)(2,1)S(1)} %bitcast.125), channel_id=1, source_target_pairs={{0,2},{2,4},{4,6},{6,8},{8,10},{10,12},{12,14},{14,0},{1,3},{3,5},... | collective-permute-start | bytes 1179656 | tf_op jit(solution)/shard_map/ppermute | solution.py:140
  198.1 14.2 %collective-permute-start.17 = (bf16[2,6,32,512]{3,2,1,0:T(8,128)(2,1)}, bf16[2,6,32,512]{3,2,1,0:T(8,128)(2,1)}, u32[]{:S(2)}, u32[]{:S(2)}) collective-permute-start(bf16[2,6,32,512]{3,2,1,0:T(8,128)(2,1)} %bitcast.43), channel_id=1, source_target_pairs={{0,4},{2,6},{4,8},{6,10},{8,12},{10,14},{12,0},{14,2},{1,5},{3,7},... | collective-permute-start | bytes 1179656 | tf_op jit(solution)/shard_map/ppermute | solution.py:140
  199.0 1.0 copy-start.3
  200.4 67.8 %collective-permute-start.21 = (bf16[2,6,32,512]{3,2,1,0:T(8,128)(2,1)S(1)}, bf16[2,6,32,512]{3,2,1,0:T(8,128)(2,1)S(1)}, u32[]{:S(2)}, u32[]{:S(2)}) collective-permute-start(bf16[2,6,32,512]{3,2,1,0:T(8,128)(2,1)S(1)} %bitcast.127), channel_id=1, source_target_pairs={{0,12},{2,14},{4,0},{6,2},{8,4},{10,6},{12,8},{14,10},{1,13},{3,15... | collective-permute-start | bytes 1179656 | tf_op jit(solution)/shard_map/ppermute | solution.py:140
  203.4 65.0 %collective-permute-start.22 = (bf16[2,6,32,512]{3,2,1,0:T(8,128)(2,1)S(1)}, bf16[2,6,32,512]{3,2,1,0:T(8,128)(2,1)S(1)}, u32[]{:S(2)}, u32[]{:S(2)}) collective-permute-start(bf16[2,6,32,512]{3,2,1,0:T(8,128)(2,1)S(1)} %bitcast.126), channel_id=1, source_target_pairs={{0,14},{2,0},{4,2},{6,4},{8,6},{10,8},{12,10},{14,12},{1,15},{3,1}... | collective-permute-start | bytes 1179656 | tf_op jit(solution)/shard_map/ppermute | solution.py:140
  204.3 63.9 %collective-permute-start.20 = (bf16[2,6,32,512]{3,2,1,0:T(8,128)(2,1)S(1)}, bf16[2,6,32,512]{3,2,1,0:T(8,128)(2,1)S(1)}, u32[]{:S(2)}, u32[]{:S(2)}) collective-permute-start(bf16[2,6,32,512]{3,2,1,0:T(8,128)(2,1)S(1)} %bitcast.128), channel_id=1, source_target_pairs={{0,10},{2,12},{4,14},{6,0},{8,2},{10,4},{12,6},{14,8},{1,11},{3,13... | collective-permute-start | bytes 1179656 | tf_op jit(solution)/shard_map/ppermute | solution.py:140
  208.8 47.6 %collective-permute-start.18 = (bf16[2,6,32,512]{3,2,1,0:T(8,128)(2,1)S(1)}, bf16[2,6,32,512]{3,2,1,0:T(8,128)(2,1)S(1)}, u32[]{:S(2)}, u32[]{:S(2)}) collective-permute-start(bf16[2,6,32,512]{3,2,1,0:T(8,128)(2,1)S(1)} %bitcast.130), channel_id=1, source_target_pairs={{0,6},{2,8},{4,10},{6,12},{8,14},{10,0},{12,2},{14,4},{1,7},{3,9},... | collective-permute-start | bytes 1179656 | tf_op jit(solution)/shard_map/ppermute | solution.py:140
  212.3 55.8 %collective-permute-start.19 = (bf16[2,6,32,512]{3,2,1,0:T(8,128)(2,1)S(1)}, bf16[2,6,32,512]{3,2,1,0:T(8,128)(2,1)S(1)}, u32[]{:S(2)}, u32[]{:S(2)}) collective-permute-start(bf16[2,6,32,512]{3,2,1,0:T(8,128)(2,1)S(1)} %bitcast.129), channel_id=1, source_target_pairs={{0,8},{2,10},{4,12},{6,14},{8,0},{10,2},{12,4},{14,6},{1,9},{3,11}... | collective-permute-start | bytes 1179656 | tf_op jit(solution)/shard_map/ppermute | solution.py:140
  268.4 2.7 copy-start.2
Sparse Core Ops, SparseCore 0:
  9.5 53.2 all-gather.1

commit v16 on v12

--- a/solution.py
+++ b/solution.py
@@ -108,14 +108,6 @@
     r = rows_half // nbd
     chunks = half.reshape(nbl, nbd, r, modes)
 
-    got = []
-    for s in range(nbd):
-        piece = lax.dynamic_index_in_dim(chunks, (me + s) % nbd, axis=1, keepdims=False)
-        if s:
-            piece = lax.ppermute(piece, "blade", [(j, (j + s) % nbd) for j in range(nbd)])
-        got.append(piece)
-    stacked = jnp.stack(got).reshape(nbd * nbl, r * modes)
-
     count = nbl * nbd
     src = (me - jnp.arange(nbd, dtype=jnp.int32)) % nbd
     blade = (nbl * src[:, None] + jnp.arange(nbl, dtype=jnp.int32)[None, :]).reshape(-1)
@@ -123,18 +115,29 @@
     harm = (nbl * dst[:, None] + jnp.arange(nbl, dtype=jnp.int32)[None, :]).reshape(-1)
     cosine, sine = _trig(harm[:, None], blade[None, :], count)
     weights = jnp.stack([cosine.reshape(nbd, nbl, -1), sine.reshape(nbd, nbl, -1)], axis=1)
-    spec = _dft(weights.reshape(2 * count, count), stacked)
-    spec = spec.reshape(nbd, 2, nbl, r, modes)
+    weights = weights.reshape(2 * count, count)
 
+    nh = 2 if r % 16 == 0 else 1
+    rh = r // nh
     out = jnp.zeros((2, nbl, rows_half, modes), jnp.float32)
-    for t in range(nbd):
-        piece = spec[t]
-        if t:
-            piece = piece.astype(jnp.bfloat16)
-            piece = lax.ppermute(piece, "blade", [(j, (j + t) % nbd) for j in range(nbd)])
-            piece = piece.astype(jnp.float32)
-        at = ((me - t) % nbd) * r
-        out = lax.dynamic_update_slice(out, piece, (0, 0, at, 0))
+    for hh in range(nh):
+        got = []
+        for s in range(nbd):
+            piece = lax.dynamic_index_in_dim(chunks, (me + s) % nbd, axis=1, keepdims=False)
+            piece = piece[:, hh * rh:(hh + 1) * rh]
+            if s:
+                piece = lax.ppermute(piece, "blade", [(j, (j + s) % nbd) for j in range(nbd)])
+            got.append(piece)
+        stacked = jnp.stack(got).reshape(nbd * nbl, rh * modes)
+        spec = _dft(weights, stacked).reshape(nbd, 2, nbl, rh, modes)
+        for t in range(nbd):
+            piece = spec[t]
+            if t:
+                piece = piece.astype(jnp.bfloat16)
+                piece = lax.ppermute(piece, "blade", [(j, (j + t) % nbd) for j in range(nbd)])
+                piece = piece.astype(jnp.float32)
+            at = ((me - t) % nbd) * r + hh * rh
+            out = lax.dynamic_update_slice(out, piece, (0, 0, at, 0))
     return out
 
 

time: 276 us -> 300 us (1.087)
  the two profiles are of different devices: /device:TPU:0 before, /device:TPU:26 now
where the time goes in v16:
time: 300 us; the launch traced here: 299 us
  waiting for transfers between devices  172 us (57%)
  starting transfers between devices  42.6 us (14%)
  Pallas kernels  34.5 us (12%)
  local copies, waits for them, and re-layouts  26.4 us (9%)
  between operations  14.1 us (5%)
  other arithmetic  9.4 us (3%)
    ppermute x14, waiting for transfers between devices, body(): lax.ppermute(piece, 'blade', [(j, (j + t) % nbd) for j in range(nbd)])  60.5 us
    ppermute x14, waiting for transfers between devices, body(): lax.ppermute(piece, 'blade', [(j, (j + s) % nbd) for j in range(nbd)])  59 us
    all_gather x1, waiting for transfers between devices, body(): pt = lax.all_gather(mine, ('blade', 'dof'), axis=0, tiled=True)  48.5 us
    pallas_call x1, Pallas kernels, _project(): pl.pallas_call(_project_kernel, grid_spec=grid_spec, out_shape=jax.ShapeD...  25.1 us
    ppermute x14, starting transfers between devices, body(): lax.ppermute(piece, 'blade', [(j, (j + s) % nbd) for j in range(nbd)])  24.9 us
    ppermute x14, starting transfers between devices, body(): lax.ppermute(piece, 'blade', [(j, (j + t) % nbd) for j in range(nbd)])  17.3 us
    unnamed x53, local copies, waits for them, and re-layouts  11.8 us
    pallas_call x2, Pallas kernels, _dft(): pl.pallas_call(_dft_kernel, grid=(n // tn,), in_specs=[pl.BlockSpec((rows...  9.44 us
  transfers between devices with their start and end apart: 30, of which 16 were waited for; matrix products, arithmetic and copies ran while one was open for 6% of the time, Pallas kernels for 2%

profile of v16, /device:TPU:26, one launch (start us, length us, event | category | flops | bytes accessed | tf_op | source)
XLA Modules:
  0.0 299.5 jit_solution(1769681574966675719)
XLA Ops:
  6.5 1.8 copy.6
  8.4 1.4 reshape.189.rows_ref
  9.7 1.3 reshape.190.cols_ref
  11.1 48.5 %all-gather.2.cloned.1.call-done.pt_ref = bf16[32,512,128]{2,1,0:T(8,128)(2,1)} async-done(((bf16[2,512,128]{2,1,0:T(8,128)(2,1)}), bf16[32,512,128]{2,1,0:T(8,128)(2,1)}) %all-gather.2.cloned.1.call-update) | async-done | bytes 4194320 | tf_op jit(solution)/shard_map/all_gather | solution.py:95
  59.6 25.1 %shard_map.46 = f32[6,512,512]{2,1,0:T(8,128)} custom-call(s32[192]{0:T(256)} %reshape.189.rows_ref, s32[192]{0:T(256)} %reshape.190.cols_ref, bf16[32,512,128]{2,1,0:T(8,128)(2,1)} %all-gather.2.cloned.1.call-done.pt_ref, bf16[6,32,128,128]{3,2,1,0:T(8,128)(2,1)} %s_ref.1), custom_call_target="tpu_custom_call" | custom-call | tf_op jit(solution)/shard_map/pallas_call | solution.py:44
  84.7 2.2 constant_dynamic-slice_fusion
  86.9 0.3 collective-permute-start
  87.7 0.6 reshape.188.w_ref
  88.4 4.4 %collective-permute-done = f32[6,256,512]{2,1,0:T(8,128)} collective-permute-done((f32[6,256,512]{2,1,0:T(8,128)S(1)}, f32[6,256,512]{2,1,0:T(8,128)}, u32[]{:S(2)}, u32[]{:S(2)}) %collective-permute-start) | collective-permute-done | bytes 3145760 | tf_op jit(solution)/shard_map/ppermute | solution.py:103
  92.7 3.6 %dynamic-slice_add_fusion = f32[6,256,512]{2,1,0:T(8,128)S(1)} fusion(f32[6,256,512]{2,1,0:T(8,128)} %collective-permute-done, f32[6,512,512]{2,1,0:T(8,128)} %shard_map.46, s32[]{:T(128)S(6)} %select_n.222), kind=kLoop, calls=%fused_computation | loop fusion | flops 786432 | bytes 9437188 | tf_op jit(solution)/shard_map/add | solution.py:103
  96.3 0.3 dynamic-slice_bitcast_fusion
  96.7 0.7 fusion.14
  97.4 1.4 collective-permute-start.21
  98.8 1.5 collective-permute-start.7
  100.3 0.7 fusion.15
  101.0 1.2 collective-permute-start.20
  102.1 0.5 collective-permute-start.6
  102.7 0.7 fusion.16
  103.4 0.7 fusion.17
  104.1 0.7 fusion.18
  104.8 0.7 fusion.19
  105.5 0.7 fusion.20
  106.2 0.6 collective-permute-start.15
  106.8 10.9 %collective-permute-done.15 = f32[6,16,512]{2,1,0:T(8,128)S(1)} collective-permute-done((f32[6,16,512]{2,1,0:T(8,128)S(1)}, f32[6,16,512]{2,1,0:T(8,128)S(1)}, u32[]{:S(2)}, u32[]{:S(2)}) %collective-permute-start.15) | collective-permute-done | bytes 196640 | tf_op jit(solution)/shard_map/ppermute | solution.py:129
  117.7 1.2 collective-permute-start.16
  118.9 5.7 %collective-permute-done.16 = f32[6,16,512]{2,1,0:T(8,128)S(1)} collective-permute-done((f32[6,16,512]{2,1,0:T(8,128)S(1)}, f32[6,16,512]{2,1,0:T(8,128)S(1)}, u32[]{:S(2)}, u32[]{:S(2)}) %collective-permute-start.16) | collective-permute-done | bytes 196640 | tf_op jit(solution)/shard_map/ppermute | solution.py:129
  124.8 11.7 %collective-permute-done.17 = f32[6,16,512]{2,1,0:T(8,128)S(1)} collective-permute-done((f32[6,16,512]{2,1,0:T(8,128)S(1)}, f32[6,16,512]{2,1,0:T(8,128)S(1)}, u32[]{:S(2)}, u32[]{:S(2)}) %collective-permute-start.17) | collective-permute-done | bytes 196640 | tf_op jit(solution)/shard_map/ppermute | solution.py:129
  136.5 9.7 %collective-permute-done.18 = f32[6,16,512]{2,1,0:T(8,128)S(1)} collective-permute-done((f32[6,16,512]{2,1,0:T(8,128)S(1)}, f32[6,16,512]{2,1,0:T(8,128)S(1)}, u32[]{:S(2)}, u32[]{:S(2)}) %collective-permute-start.18) | collective-permute-done | bytes 196640 | tf_op jit(solution)/shard_map/ppermute | solution.py:129
  146.3 9.5 %collective-permute-done.19 = f32[6,16,512]{2,1,0:T(8,128)S(1)} collective-permute-done((f32[6,16,512]{2,1,0:T(8,128)S(1)}, f32[6,16,512]{2,1,0:T(8,128)S(1)}, u32[]{:S(2)}, u32[]{:S(2)}) %collective-permute-start.19) | collective-permute-done | bytes 196640 | tf_op jit(solution)/shard_map/ppermute | solution.py:129
  155.8 14.0 %collective-permute-start.4 = (f32[6,16,512]{2,1,0:T(8,128)}, f32[6,16,512]{2,1,0:T(8,128)}, u32[]{:S(2)}, u32[]{:S(2)}) collective-permute-start(f32[6,16,512]{2,1,0:T(8,128)} %get-tuple-element.34), channel_id=1, source_target_pairs={{0,8},{2,10},{4,12},{6,14},{8,0},{10,2},{12,4},{14,6},{1,9},{3,11}... | collective-permute-start | bytes 589832 | tf_op jit(solution)/shard_map/ppermute | solution.py:129
  169.9 2.0 copy.16
  172.0 4.8 %shard_map.48 = f32[96,8192]{1,0:T(8,128)} custom-call(f32[96,48]{1,0:T(8,128)} %reshape.188.w_ref, f32[48,8192]{1,0:T(8,128)} %bitcast.130), custom_call_target="tpu_custom_call" | custom-call | tf_op jit(solution)/shard_map/pallas_call | solution.py:72
  176.7 2.1 convert.19
  178.9 0.7 collective-permute-done.1
  179.5 1.6 collective-permute-start.2
  181.1 0.9 bitcast_dynamic-update-slice_fusion.13
  182.0 4.0 %collective-permute-done.2 = f32[6,16,512]{2,1,0:T(8,128)S(1)} collective-permute-done((f32[6,16,512]{2,1,0:T(8,128)S(1)}, f32[6,16,512]{2,1,0:T(8,128)S(1)}, u32[]{:S(2)}, u32[]{:S(2)}) %collective-permute-start.2) | collective-permute-done | bytes 196640 | tf_op jit(solution)/shard_map/ppermute | solution.py:129
  186.1 2.8 collective-permute-start.3
  188.9 6.8 %collective-permute-done.3 = f32[6,16,512]{2,1,0:T(8,128)S(1)} collective-permute-done((f32[6,16,512]{2,1,0:T(8,128)S(1)}, f32[6,16,512]{2,1,0:T(8,128)S(1)}, u32[]{:S(2)}, u32[]{:S(2)}) %collective-permute-start.3) | collective-permute-done | bytes 196640 | tf_op jit(solution)/shard_map/ppermute | solution.py:129
  195.7 0.9 bitcast_dynamic-update-slice_fusion.10
  196.7 0.9 bitcast_dynamic-update-slice_fusion.9
  197.7 2.1 copy.7
  199.7 4.7 %shard_map.47 = f32[96,8192]{1,0:T(8,128)} custom-call(f32[96,48]{1,0:T(8,128)} %reshape.188.w_ref, f32[48,8192]{1,0:T(8,128)} %bitcast.129), custom_call_target="tpu_custom_call" | custom-call | tf_op jit(solution)/shard_map/pallas_call | solution.py:72
  204.4 2.1 convert.18
  206.5 0.3 fusion.13
  207.4 3.8 %collective-permute-start.12 = (bf16[2,6,16,512]{3,2,1,0:T(8,128)(2,1)S(1)}, bf16[2,6,16,512]{3,2,1,0:T(8,128)(2,1)S(1)}, u32[]{:S(2)}, u32[]{:S(2)}) collective-permute-start(bf16[2,6,16,512]{3,2,1,0:T(8,128)(2,1)S(1)} %bitcast.172), channel_id=1, source_target_pairs={{0,10},{2,12},{4,14},{6,0},{8,2},{10,4},{12,6},{14,8},{1,11},{3,13... | collective-permute-start | bytes 589832 | tf_op jit(solution)/shard_map/ppermute | solution.py:137
  211.3 0.6 collective-permute-start.11
  212.0 1.8 collective-permute-start.8
  214.1 0.3 copy.8
  214.7 0.4 slice-done.1
  215.1 0.3 copy.17
  216.2 0.8 broadcast_in_dim.2
  217.1 5.4 %collective-permute-done.8 = bf16[2,6,16,512]{3,2,1,0:T(8,128)(2,1)S(1)} collective-permute-done((bf16[2,6,16,512]{3,2,1,0:T(8,128)(2,1)S(1)}, bf16[2,6,16,512]{3,2,1,0:T(8,128)(2,1)S(1)}, u32[]{:S(2)}, u32[]{:S(2)}) %collective-permute-start.8) | collective-permute-done | bytes 196640 | tf_op jit(solution)/shard_map/ppermute | solution.py:137
  222.4 2.3 collective-permute-start.9
  224.8 6.6 %collective-permute-done.9 = bf16[2,6,16,512]{3,2,1,0:T(8,128)(2,1)S(1)} collective-permute-done((bf16[2,6,16,512]{3,2,1,0:T(8,128)(2,1)S(1)}, bf16[2,6,16,512]{3,2,1,0:T(8,128)(2,1)S(1)}, u32[]{:S(2)}, u32[]{:S(2)}) %collective-permute-start.9) | collective-permute-done | bytes 196640 | tf_op jit(solution)/shard_map/ppermute | solution.py:137
  231.5 15.6 %collective-permute-done.10 = bf16[2,6,16,512]{3,2,1,0:T(8,128)(2,1)S(1)} collective-permute-done((bf16[2,6,16,512]{3,2,1,0:T(8,128)(2,1)S(1)}, bf16[2,6,16,512]{3,2,1,0:T(8,128)(2,1)S(1)}, u32[]{:S(2)}, u32[]{:S(2)}) %collective-permute-start.10) | collective-permute-done | bytes 196640 | tf_op jit(solution)/shard_map/ppermute | solution.py:137
  247.4 4.4 %collective-permute-start.25 = (bf16[2,6,16,512]{3,2,1,0:T(8,128)(2,1)S(1)}, bf16[2,6,16,512]{3,2,1,0:T(8,128)(2,1)S(1)}, u32[]{:S(2)}, u32[]{:S(2)}) collective-permute-start(bf16[2,6,16,512]{3,2,1,0:T(8,128)(2,1)S(1)} %bitcast.171), channel_id=1, source_target_pairs={{0,8},{2,10},{4,12},{6,14},{8,0},{10,2},{12,4},{14,6},{1,9},{3,11}... | collective-permute-start | bytes 589832 | tf_op jit(solution)/shard_map/ppermute | solution.py:137
  251.9 1.5 collective-permute-start.22
  253.5 9.4 %collective-permute-done.22 = bf16[2,6,16,512]{3,2,1,0:T(8,128)(2,1)S(1)} collective-permute-done((bf16[2,6,16,512]{3,2,1,0:T(8,128)(2,1)S(1)}, bf16[2,6,16,512]{3,2,1,0:T(8,128)(2,1)S(1)}, u32[]{:S(2)}, u32[]{:S(2)}) %collective-permute-start.22) | collective-permute-done | bytes 196640 | tf_op jit(solution)/shard_map/ppermute | solution.py:137
  262.9 2.5 collective-permute-start.23
  265.4 11.2 %collective-permute-done.23 = bf16[2,6,16,512]{3,2,1,0:T(8,128)(2,1)S(1)} collective-permute-done((bf16[2,6,16,512]{3,2,1,0:T(8,128)(2,1)S(1)}, bf16[2,6,16,512]{3,2,1,0:T(8,128)(2,1)S(1)}, u32[]{:S(2)}, u32[]{:S(2)}) %collective-permute-start.23) | collective-permute-done | bytes 196640 | tf_op jit(solution)/shard_map/ppermute | solution.py:137
  276.6 12.3 %collective-permute-done.24 = bf16[2,6,16,512]{3,2,1,0:T(8,128)(2,1)S(1)} collective-permute-done((bf16[2,6,16,512]{3,2,1,0:T(8,128)(2,1)S(1)}, bf16[2,6,16,512]{3,2,1,0:T(8,128)(2,1)S(1)}, u32[]{:S(2)}, u32[]{:S(2)}) %collective-permute-start.24) | collective-permute-done | bytes 196640 | tf_op jit(solution)/shard_map/ppermute | solution.py:137
  289.2 2.7 copy-done
  291.9 0.8 convert_dynamic-update-slice_fusion
  (100 shorter events, 3.7 us)
Async XLA Ops:
  6.5 53.0 %all-gather.2.cloned.1.call-start = ((), (), s32[]{:S(2)}) async-start(), calls=%async_computation | async-start | bytes 4456448 | tf_op jit(solution)/shard_map/all_gather | solution.py:95
  86.9 5.9 %collective-permute-start = (f32[6,256,512]{2,1,0:T(8,128)S(1)}, f32[6,256,512]{2,1,0:T(8,128)}, u32[]{:S(2)}, u32[]{:S(2)}) collective-permute-start(f32[6,256,512]{2,1,0:T(8,128)S(1)} %constant_dynamic-slice_fusion), channel_id=1, source_target_pairs={{0,1},{1,0},{2,3},{3,2},{4,5},{5,4},{6,7},{7,6},{8,9},{9,8},{10,11... | collective-permute-start | bytes 9437192 | tf_op jit(solution)/shard_map/ppermute | solution.py:103
  97.4 72.5 %collective-permute-start.21 = (f32[6,16,512]{2,1,0:T(8,128)S(1)}, f32[6,16,512]{2,1,0:T(8,128)S(1)}, u32[]{:S(2)}, u32[]{:S(2)}) collective-permute-start(f32[6,16,512]{2,1,0:T(8,128)S(1)} %get-tuple-element.27), channel_id=1, source_target_pairs={{0,14},{2,0},{4,2},{6,4},{8,6},{10,8},{12,10},{14,12},{1,15},{3,1}... | collective-permute-start | bytes 589832 | tf_op jit(solution)/shard_map/ppermute | solution.py:129
  98.8 98.8 %collective-permute-start.7 = (f32[6,16,512]{2,1,0:T(8,128)}, f32[6,16,512]{2,1,0:T(8,128)S(1)}, u32[]{:S(2)}, u32[]{:S(2)}) collective-permute-start(f32[6,16,512]{2,1,0:T(8,128)} %get-tuple-element.28), channel_id=1, source_target_pairs={{0,14},{2,0},{4,2},{6,4},{8,6},{10,8},{12,10},{14,12},{1,15},{3,1}... | collective-permute-start | bytes 589832 | tf_op jit(solution)/shard_map/ppermute | solution.py:129
  101.0 54.8 %collective-permute-start.20 = (f32[6,16,512]{2,1,0:T(8,128)S(1)}, f32[6,16,512]{2,1,0:T(8,128)S(1)}, u32[]{:S(2)}, u32[]{:S(2)}) collective-permute-start(f32[6,16,512]{2,1,0:T(8,128)S(1)} %get-tuple-element.29), channel_id=1, source_target_pairs={{0,12},{2,14},{4,0},{6,2},{8,4},{10,6},{12,8},{14,10},{1,13},{3,15... | collective-permute-start | bytes 589832 | tf_op jit(solution)/shard_map/ppermute | solution.py:129
  102.1 95.5 %collective-permute-start.6 = (f32[6,16,512]{2,1,0:T(8,128)}, f32[6,16,512]{2,1,0:T(8,128)S(1)}, u32[]{:S(2)}, u32[]{:S(2)}) collective-permute-start(f32[6,16,512]{2,1,0:T(8,128)} %get-tuple-element.30), channel_id=1, source_target_pairs={{0,12},{2,14},{4,0},{6,2},{8,4},{10,6},{12,8},{14,10},{1,13},{3,15... | collective-permute-start | bytes 589832 | tf_op jit(solution)/shard_map/ppermute | solution.py:129
  106.2 11.5 %collective-permute-start.15 = (f32[6,16,512]{2,1,0:T(8,128)S(1)}, f32[6,16,512]{2,1,0:T(8,128)S(1)}, u32[]{:S(2)}, u32[]{:S(2)}) collective-permute-start(f32[6,16,512]{2,1,0:T(8,128)S(1)} %get-tuple-element.39), channel_id=1, source_target_pairs={{0,2},{2,4},{4,6},{6,8},{8,10},{10,12},{12,14},{14,0},{1,3},{3,5},... | collective-permute-start | bytes 589832 | tf_op jit(solution)/shard_map/ppermute | solution.py:129
  117.7 6.8 %collective-permute-start.16 = (f32[6,16,512]{2,1,0:T(8,128)S(1)}, f32[6,16,512]{2,1,0:T(8,128)S(1)}, u32[]{:S(2)}, u32[]{:S(2)}) collective-permute-start(f32[6,16,512]{2,1,0:T(8,128)S(1)} %get-tuple-element.37), channel_id=1, source_target_pairs={{0,4},{2,6},{4,8},{6,10},{8,12},{10,14},{12,0},{14,2},{1,5},{3,7},... | collective-permute-start | bytes 589832 | tf_op jit(solution)/shard_map/ppermute | solution.py:129
  124.5 12.0 %collective-permute-start.17 = (f32[6,16,512]{2,1,0:T(8,128)S(1)}, f32[6,16,512]{2,1,0:T(8,128)S(1)}, u32[]{:S(2)}, u32[]{:S(2)}) collective-permute-start(f32[6,16,512]{2,1,0:T(8,128)S(1)} %get-tuple-element.35), channel_id=1, source_target_pairs={{0,6},{2,8},{4,10},{6,12},{8,14},{10,0},{12,2},{14,4},{1,7},{3,9},... | collective-permute-start | bytes 589832 | tf_op jit(solution)/shard_map/ppermute | solution.py:129
  136.5 9.7 %collective-permute-start.18 = (f32[6,16,512]{2,1,0:T(8,128)S(1)}, f32[6,16,512]{2,1,0:T(8,128)S(1)}, u32[]{:S(2)}, u32[]{:S(2)}) collective-permute-start(f32[6,16,512]{2,1,0:T(8,128)S(1)} %get-tuple-element.33), channel_id=1, source_target_pairs={{0,8},{2,10},{4,12},{6,14},{8,0},{10,2},{12,4},{14,6},{1,9},{3,11}... | collective-permute-start | bytes 589832 | tf_op jit(solution)/shard_map/ppermute | solution.py:129
  146.3 9.5 %collective-permute-start.19 = (f32[6,16,512]{2,1,0:T(8,128)S(1)}, f32[6,16,512]{2,1,0:T(8,128)S(1)}, u32[]{:S(2)}, u32[]{:S(2)}) collective-permute-start(f32[6,16,512]{2,1,0:T(8,128)S(1)} %get-tuple-element.31), channel_id=1, source_target_pairs={{0,10},{2,12},{4,14},{6,0},{8,2},{10,4},{12,6},{14,8},{1,11},{3,13... | collective-permute-start | bytes 589832 | tf_op jit(solution)/shard_map/ppermute | solution.py:129
  155.8 40.9 %collective-permute-start.5 = (f32[6,16,512]{2,1,0:T(8,128)}, f32[6,16,512]{2,1,0:T(8,128)}, u32[]{:S(2)}, u32[]{:S(2)}) collective-permute-start(f32[6,16,512]{2,1,0:T(8,128)} %get-tuple-element.32), channel_id=1, source_target_pairs={{0,10},{2,12},{4,14},{6,0},{8,2},{10,4},{12,6},{14,8},{1,11},{3,13... | collective-permute-start | bytes 589832 | tf_op jit(solution)/shard_map/ppermute | solution.py:129
  155.8 39.9 %collective-permute-start.4 = (f32[6,16,512]{2,1,0:T(8,128)}, f32[6,16,512]{2,1,0:T(8,128)}, u32[]{:S(2)}, u32[]{:S(2)}) collective-permute-start(f32[6,16,512]{2,1,0:T(8,128)} %get-tuple-element.34), channel_id=1, source_target_pairs={{0,8},{2,10},{4,12},{6,14},{8,0},{10,2},{12,4},{14,6},{1,9},{3,11}... | collective-permute-start | bytes 589832 | tf_op jit(solution)/shard_map/ppermute | solution.py:129
  169.8 9.7 %collective-permute-start.1 = (f32[6,16,512]{2,1,0:T(8,128)}, f32[6,16,512]{2,1,0:T(8,128)}, u32[]{:S(2)}, u32[]{:S(2)}) collective-permute-start(f32[6,16,512]{2,1,0:T(8,128)} %get-tuple-element.40), channel_id=1, source_target_pairs={{0,2},{2,4},{4,6},{6,8},{8,10},{10,12},{12,14},{14,0},{1,3},{3,5},... | collective-permute-start | bytes 589832 | tf_op jit(solution)/shard_map/ppermute | solution.py:129
  176.7 2.8 copy-start.2
  176.7 9.4 %copy-start.1 = (f32[6,16,512]{2,1,0:T(8,128)S(1)}, f32[6,16,512]{2,1,0:T(8,128)}, u32[]{:S(2)}) copy-start(f32[6,16,512]{2,1,0:T(8,128)} %get-tuple-element.36) | copy-start | bytes 589828
  179.5 6.5 %collective-permute-start.2 = (f32[6,16,512]{2,1,0:T(8,128)S(1)}, f32[6,16,512]{2,1,0:T(8,128)S(1)}, u32[]{:S(2)}, u32[]{:S(2)}) collective-permute-start(f32[6,16,512]{2,1,0:T(8,128)S(1)} %copy-done.2), channel_id=1, source_target_pairs={{0,4},{2,6},{4,8},{6,10},{8,12},{10,14},{12,0},{14,2},{1,5},{3,7},... | collective-permute-start | bytes 589832 | tf_op jit(solution)/shard_map/ppermute | solution.py:129
  186.1 9.6 %collective-permute-start.3 = (f32[6,16,512]{2,1,0:T(8,128)S(1)}, f32[6,16,512]{2,1,0:T(8,128)S(1)}, u32[]{:S(2)}, u32[]{:S(2)}) collective-permute-start(f32[6,16,512]{2,1,0:T(8,128)S(1)} %copy-done.1), channel_id=1, source_target_pairs={{0,6},{2,8},{4,10},{6,12},{8,14},{10,0},{12,2},{14,4},{1,7},{3,9},... | collective-permute-start | bytes 589832 | tf_op jit(solution)/shard_map/ppermute | solution.py:129
  207.0 40.4 %collective-permute-start.13 = (bf16[2,6,16,512]{3,2,1,0:T(8,128)(2,1)S(1)}, bf16[2,6,16,512]{3,2,1,0:T(8,128)(2,1)S(1)}, u32[]{:S(2)}, u32[]{:S(2)}) collective-permute-start(bf16[2,6,16,512]{3,2,1,0:T(8,128)(2,1)S(1)} %bitcast.169), channel_id=1, source_target_pairs={{0,12},{2,14},{4,0},{6,2},{8,4},{10,6},{12,8},{14,10},{1,13},{3,15... | collective-permute-start | bytes 589832 | tf_op jit(solution)/shard_map/ppermute | solution.py:137
  207.1 44.8 %collective-permute-start.14 = (bf16[2,6,16,512]{3,2,1,0:T(8,128)(2,1)S(1)}, bf16[2,6,16,512]{3,2,1,0:T(8,128)(2,1)S(1)}, u32[]{:S(2)}, u32[]{:S(2)}) collective-permute-start(bf16[2,6,16,512]{3,2,1,0:T(8,128)(2,1)S(1)} %bitcast.167), channel_id=1, source_target_pairs={{0,14},{2,0},{4,2},{6,4},{8,6},{10,8},{12,10},{14,12},{1,15},{3,1}... | collective-permute-start | bytes 589832 | tf_op jit(solution)/shard_map/ppermute | solution.py:137
  207.4 39.9 %collective-permute-start.12 = (bf16[2,6,16,512]{3,2,1,0:T(8,128)(2,1)S(1)}, bf16[2,6,16,512]{3,2,1,0:T(8,128)(2,1)S(1)}, u32[]{:S(2)}, u32[]{:S(2)}) collective-permute-start(bf16[2,6,16,512]{3,2,1,0:T(8,128)(2,1)S(1)} %bitcast.172), channel_id=1, source_target_pairs={{0,10},{2,12},{4,14},{6,0},{8,2},{10,4},{12,6},{14,8},{1,11},{3,13... | collective-permute-start | bytes 589832 | tf_op jit(solution)/shard_map/ppermute | solution.py:137
  211.3 2.8 slice-start
  211.3 35.9 %collective-permute-start.11 = (bf16[2,6,16,512]{3,2,1,0:T(8,128)(2,1)S(1)}, bf16[2,6,16,512]{3,2,1,0:T(8,128)(2,1)S(1)}, u32[]{:S(2)}, u32[]{:S(2)}) collective-permute-start(bf16[2,6,16,512]{3,2,1,0:T(8,128)(2,1)S(1)} %bitcast.174), channel_id=1, source_target_pairs={{0,8},{2,10},{4,12},{6,14},{8,0},{10,2},{12,4},{14,6},{1,9},{3,11}... | collective-permute-start | bytes 589832 | tf_op jit(solution)/shard_map/ppermute | solution.py:137
  212.0 10.5 %collective-permute-start.8 = (bf16[2,6,16,512]{3,2,1,0:T(8,128)(2,1)S(1)}, bf16[2,6,16,512]{3,2,1,0:T(8,128)(2,1)S(1)}, u32[]{:S(2)}, u32[]{:S(2)}) collective-permute-start(bf16[2,6,16,512]{3,2,1,0:T(8,128)(2,1)S(1)} %bitcast.178), channel_id=1, source_target_pairs={{0,2},{2,4},{4,6},{6,8},{8,10},{10,12},{12,14},{14,0},{1,3},{3,5},... | collective-permute-start | bytes 589832 | tf_op jit(solution)/shard_map/ppermute | solution.py:137
  214.1 1.0 slice-start.1
  222.4 9.0 %collective-permute-start.9 = (bf16[2,6,16,512]{3,2,1,0:T(8,128)(2,1)S(1)}, bf16[2,6,16,512]{3,2,1,0:T(8,128)(2,1)S(1)}, u32[]{:S(2)}, u32[]{:S(2)}) collective-permute-start(bf16[2,6,16,512]{3,2,1,0:T(8,128)(2,1)S(1)} %bitcast.179), channel_id=1, source_target_pairs={{0,4},{2,6},{4,8},{6,10},{8,12},{10,14},{12,0},{14,2},{1,5},{3,7},... | collective-permute-start | bytes 589832 | tf_op jit(solution)/shard_map/ppermute | solution.py:137
  231.4 15.7 %collective-permute-start.10 = (bf16[2,6,16,512]{3,2,1,0:T(8,128)(2,1)S(1)}, bf16[2,6,16,512]{3,2,1,0:T(8,128)(2,1)S(1)}, u32[]{:S(2)}, u32[]{:S(2)}) collective-permute-start(bf16[2,6,16,512]{3,2,1,0:T(8,128)(2,1)S(1)} %bitcast.177), channel_id=1, source_target_pairs={{0,6},{2,8},{4,10},{6,12},{8,14},{10,0},{12,2},{14,4},{1,7},{3,9},... | collective-permute-start | bytes 589832 | tf_op jit(solution)/shard_map/ppermute | solution.py:137
  247.1 42.0 %collective-permute-start.27 = (bf16[2,6,16,512]{3,2,1,0:T(8,128)(2,1)S(1)}, bf16[2,6,16,512]{3,2,1,0:T(8,128)(2,1)S(1)}, u32[]{:S(2)}, u32[]{:S(2)}) collective-permute-start(bf16[2,6,16,512]{3,2,1,0:T(8,128)(2,1)S(1)} %bitcast.168), channel_id=1, source_target_pairs={{0,12},{2,14},{4,0},{6,2},{8,4},{10,6},{12,8},{14,10},{1,13},{3,15... | collective-permute-start | bytes 589832 | tf_op jit(solution)/shard_map/ppermute | solution.py:137
  247.2 42.0 %collective-permute-start.28 = (bf16[2,6,16,512]{3,2,1,0:T(8,128)(2,1)S(1)}, bf16[2,6,16,512]{3,2,1,0:T(8,128)(2,1)S(1)}, u32[]{:S(2)}, u32[]{:S(2)}) collective-permute-start(bf16[2,6,16,512]{3,2,1,0:T(8,128)(2,1)S(1)} %bitcast.166), channel_id=1, source_target_pairs={{0,14},{2,0},{4,2},{6,4},{8,6},{10,8},{12,10},{14,12},{1,15},{3,1}... | collective-permute-start | bytes 589832 | tf_op jit(solution)/shard_map/ppermute | solution.py:137
  247.3 41.7 %collective-permute-start.26 = (bf16[2,6,16,512]{3,2,1,0:T(8,128)(2,1)S(1)}, bf16[2,6,16,512]{3,2,1,0:T(8,128)(2,1)S(1)}, u32[]{:S(2)}, u32[]{:S(2)}) collective-permute-start(bf16[2,6,16,512]{3,2,1,0:T(8,128)(2,1)S(1)} %bitcast.170), channel_id=1, source_target_pairs={{0,10},{2,12},{4,14},{6,0},{8,2},{10,4},{12,6},{14,8},{1,11},{3,13... | collective-permute-start | bytes 589832 | tf_op jit(solution)/shard_map/ppermute | solution.py:137
  247.4 41.6 %collective-permute-start.25 = (bf16[2,6,16,512]{3,2,1,0:T(8,128)(2,1)S(1)}, bf16[2,6,16,512]{3,2,1,0:T(8,128)(2,1)S(1)}, u32[]{:S(2)}, u32[]{:S(2)}) collective-permute-start(bf16[2,6,16,512]{3,2,1,0:T(8,128)(2,1)S(1)} %bitcast.171), channel_id=1, source_target_pairs={{0,8},{2,10},{4,12},{6,14},{8,0},{10,2},{12,4},{14,6},{1,9},{3,11}... | collective-permute-start | bytes 589832 | tf_op jit(solution)/shard_map/ppermute | solution.py:137
  251.9 11.0 %collective-permute-start.22 = (bf16[2,6,16,512]{3,2,1,0:T(8,128)(2,1)S(1)}, bf16[2,6,16,512]{3,2,1,0:T(8,128)(2,1)S(1)}, u32[]{:S(2)}, u32[]{:S(2)}) collective-permute-start(bf16[2,6,16,512]{3,2,1,0:T(8,128)(2,1)S(1)} %bitcast.176), channel_id=1, source_target_pairs={{0,2},{2,4},{4,6},{6,8},{8,10},{10,12},{12,14},{14,0},{1,3},{3,5},... | collective-permute-start | bytes 589832 | tf_op jit(solution)/shard_map/ppermute | solution.py:137
  262.9 13.7 %collective-permute-start.23 = (bf16[2,6,16,512]{3,2,1,0:T(8,128)(2,1)S(1)}, bf16[2,6,16,512]{3,2,1,0:T(8,128)(2,1)S(1)}, u32[]{:S(2)}, u32[]{:S(2)}) collective-permute-start(bf16[2,6,16,512]{3,2,1,0:T(8,128)(2,1)S(1)} %bitcast.175), channel_id=1, source_target_pairs={{0,4},{2,6},{4,8},{6,10},{8,12},{10,14},{12,0},{14,2},{1,5},{3,7},... | collective-permute-start | bytes 589832 | tf_op jit(solution)/shard_map/ppermute | solution.py:137
  276.6 12.3 %collective-permute-start.24 = (bf16[2,6,16,512]{3,2,1,0:T(8,128)(2,1)S(1)}, bf16[2,6,16,512]{3,2,1,0:T(8,128)(2,1)S(1)}, u32[]{:S(2)}, u32[]{:S(2)}) collective-permute-start(bf16[2,6,16,512]{3,2,1,0:T(8,128)(2,1)S(1)} %bitcast.173), channel_id=1, source_target_pairs={{0,6},{2,8},{4,10},{6,12},{8,14},{10,0},{12,2},{14,4},{1,7},{3,9},... | collective-permute-start | bytes 589832 | tf_op jit(solution)/shard_map/ppermute | solution.py:137
  289.1 2.7 copy-start
Sparse Core Ops, SparseCore 0:
  9.5 49.9 all-gather.1

commit v17 on v10

--- a/solution.py
+++ b/solution.py
@@ -11,7 +11,7 @@
 _NT = (((1,), (1,)), ((), ()))
 
 
-def _project_kernel(rows_ref, cols_ref, pt_ref, s_ref, o_ref, lt_ref, it_ref):
+def _project_kernel(rows_ref, cols_ref, side_ref, pt_ref, s_ref, mine_ref, other_ref, lt_ref, it_ref):
     b = pl.program_id(0)
     nblk = s_ref.shape[1]
     bs = s_ref.shape[2]
@@ -22,20 +22,28 @@
         im = lax.dot_general(pt_ref[c], s_ref[0, n], _NT, preferred_element_type=jnp.float32)
         it_ref[:, n * bs:(n + 1) * bs] = im.astype(jnp.bfloat16)
         lt_ref[:, n * bs:(n + 1) * bs] = pt_ref[r]
-    o_ref[0] = lax.dot_general(lt_ref[...], it_ref[...], _NT, preferred_element_type=jnp.float32)
+    acc = lax.dot_general(lt_ref[...], it_ref[...], _NT, preferred_element_type=jnp.float32)
+    h = mine_ref.shape[1]
+    first = side_ref[0] == 0
+    mine_ref[0] = jnp.where(first, acc[:h], acc[h:])
+    other_ref[0] = jnp.where(first, acc[h:], acc[:h])
 
 
-def _project(pt, stiffness, rows, cols):
+def _project(pt, stiffness, rows, cols, side):
     nbl, nblk, bs, _ = stiffness.shape
     nrb, modes, _ = pt.shape
+    h = modes // 2
     grid_spec = pltpu.PrefetchScalarGridSpec(
-        num_scalar_prefetch=2,
+        num_scalar_prefetch=3,
         grid=(nbl,),
         in_specs=[
-            pl.BlockSpec((nrb, modes, bs), lambda b, rr, cc: (0, 0, 0)),
-            pl.BlockSpec((1, nblk, bs, bs), lambda b, rr, cc: (b, 0, 0, 0)),
+            pl.BlockSpec((nrb, modes, bs), lambda b, rr, cc, sd: (0, 0, 0)),
+            pl.BlockSpec((1, nblk, bs, bs), lambda b, rr, cc, sd: (b, 0, 0, 0)),
         ],
-        out_specs=pl.BlockSpec((1, modes, modes), lambda b, rr, cc: (b, 0, 0)),
+        out_specs=[
+            pl.BlockSpec((1, h, modes), lambda b, rr, cc, sd: (b, 0, 0)),
+            pl.BlockSpec((1, h, modes), lambda b, rr, cc, sd: (b, 0, 0)),
+        ],
         scratch_shapes=[
             pltpu.VMEM((modes, nblk * bs), jnp.bfloat16),
             pltpu.VMEM((modes, nblk * bs), jnp.bfloat16),
@@ -44,12 +52,12 @@
     return pl.pallas_call(
         _project_kernel,
         grid_spec=grid_spec,
-        out_shape=jax.ShapeDtypeStruct((nbl, modes, modes), jnp.float32),
+        out_shape=[jax.ShapeDtypeStruct((nbl, h, modes), jnp.float32)] * 2,
         compiler_params=pltpu.CompilerParams(
             dimension_semantics=("arbitrary",),
             vmem_limit_bytes=56 * 1024 * 1024,
         ),
-    )(rows, cols, pt, stiffness)
+    )(rows, cols, side, pt, stiffness)
 
 
 def _dft_kernel(w_ref, x_ref, o_ref):
@@ -93,9 +101,15 @@
     nbd = lax.axis_size("blade")
     mine = jnp.swapaxes(panel.reshape(-1, bs, modes), 1, 2)
     pt = lax.all_gather(mine, ("blade", "dof"), axis=0, tiled=True)
-    proj = _project(pt, stiffness, block_rows.reshape(-1), block_cols.reshape(-1))
+    nd = lax.axis_size("dof")
+    side = (lax.axis_index("dof") % 2).reshape(1).astype(jnp.int32)
+    mine, other = _project(pt, stiffness, block_rows.reshape(-1), block_cols.reshape(-1), side)
 
-    half = lax.psum_scatter(proj, "dof", scatter_dimension=1, tiled=True)
+    if nd == 2:
+        half = mine + lax.ppermute(other, "dof", [(0, 1), (1, 0)])
+    else:
+        proj = jnp.concatenate([mine, other], axis=1)
+        half = lax.psum_scatter(proj, "dof", scatter_dimension=1, tiled=True)
     me = lax.axis_index("blade")
     rows_half = half.shape[1]
     r = rows_half // nbd

time: 278 us -> 275 us (0.989)
  waiting for transfers between devices: 160 us -> 155 us
  other arithmetic: 7.6 us -> 11.2 us
  starting transfers between devices: 40.4 us -> 37.4 us
    reduce_scatter x1 -> x0, waiting for transfers between devices: 12.8 us -> none  [body(): half = lax.psum_scatter(proj, 'dof', scatter_dimension=1, tiled=True)]
    ppermute x0 -> x1, waiting for transfers between devices: none -> 5.38 us  [body(): half = mine + lax.ppermute(other, 'dof', [(0, 1), (1, 0)])]
    add x0 -> x1, other arithmetic: none -> 3.59 us  [body(): half = mine + lax.ppermute(other, 'dof', [(0, 1), (1, 0)])]
    ppermute x7, starting transfers between devices: 33.5 us -> 30.2 us  [body(): lax.ppermute(piece, 'blade', [(j, (j + s) % nbd) for j in range(nbd)])]
    unnamed x28 -> x30, local copies, waits for them, and re-layouts: 11.5 us -> 14 us
  transfers between devices with their start and end apart: 16 -> 16, of which waited for: 10 -> 9; matrix products, arithmetic and copies ran while one was open for 5% -> 5% of each run, Pallas kernels for 0% -> 0%
where the time goes in v17:
time: 275 us
  waiting for transfers between devices  155 us (56%)
  starting transfers between devices  37.4 us (14%)
  Pallas kernels  33.3 us (12%)
  local copies, waits for them, and re-layouts  24.1 us (9%)
  between operations  13.7 us (5%)
  other arithmetic  11.2 us (4%)
    ppermute x7, waiting for transfers between devices, body(): lax.ppermute(piece, 'blade', [(j, (j + t) % nbd) for j in range(nbd)])  59.5 us
    all_gather x1, waiting for transfers between devices, body(): pt = lax.all_gather(mine, ('blade', 'dof'), axis=0, tiled=True)  51.8 us
    ppermute x7, waiting for transfers between devices, body(): lax.ppermute(piece, 'blade', [(j, (j + s) % nbd) for j in range(nbd)])  38.1 us
    ppermute x7, starting transfers between devices, body(): lax.ppermute(piece, 'blade', [(j, (j + s) % nbd) for j in range(nbd)])  30.2 us
    pallas_call x1, Pallas kernels, _project(): pl.pallas_call(_project_kernel, grid_spec=grid_spec, out_shape=[jax.Shape...  25.1 us
    unnamed x30, local copies, waits for them, and re-layouts  14 us
    pallas_call x1, Pallas kernels, _dft(): pl.pallas_call(_dft_kernel, grid=(n // tn,), in_specs=[pl.BlockSpec((rows...  8.2 us
    ppermute x7, starting transfers between devices, body(): lax.ppermute(piece, 'blade', [(j, (j + t) % nbd) for j in range(nbd)])  6.92 us
  transfers between devices with their start and end apart: 16, of which 9 were waited for; matrix products, arithmetic and copies ran while one was open for 5% of the time, Pallas kernels for 0%

profile of v17, /device:TPU:0, one launch (start us, length us, event | category | flops | bytes accessed | tf_op | source)
XLA Modules:
  0.0 274.5 jit_solution(16320443701373974069)
XLA Ops:
  6.5 1.8 copy.6
  8.3 0.0 all-gather.2.cloned.1.call-update
  8.4 1.3 reshape.166.rows_ref
  9.7 1.4 reshape.167.cols_ref
  11.1 51.8 %all-gather.2.cloned.1.call-done.pt_ref = bf16[32,512,128]{2,1,0:T(8,128)(2,1)} async-done(((bf16[2,512,128]{2,1,0:T(8,128)(2,1)}), bf16[32,512,128]{2,1,0:T(8,128)(2,1)}) %all-gather.2.cloned.1.call-update) | async-done | bytes 4194320 | tf_op jit(solution)/shard_map/all_gather | solution.py:103
  62.8 25.1 %shard_map.46 = (f32[6,256,512]{2,1,0:T(8,128)}, f32[6,256,512]{2,1,0:T(8,128)}) custom-call(s32[192]{0:T(256)} %reshape.166.rows_ref, s32[192]{0:T(256)} %reshape.167.cols_ref, s32[1]{0:T(128)} %bitcast.side_ref, bf16[32,512,128]{2,1,0:T(8,128)(2,1)} %all-gather.2.cloned.1.call-done.pt_ref, bf16[6,32,128,128]{3,2,1,0:T(8,128)(2,1)} %s_ref.1), custom_call_target="tpu_custom_call" | custom-call | tf_op jit(solution)/shard_map/pallas_call | solution.py:52
  88.0 0.3 collective-permute-start
  88.2 0.1 iota_add_fusion
  88.3 0.1 add.222
  88.4 0.1 iota_add_fusion.1
  88.4 5.4 %collective-permute-done = f32[6,256,512]{2,1,0:T(8,128)S(1)} collective-permute-done((f32[6,256,512]{2,1,0:T(8,128)}, f32[6,256,512]{2,1,0:T(8,128)S(1)}, u32[]{:S(2)}, u32[]{:S(2)}) %collective-permute-start) | collective-permute-done | bytes 3145760 | tf_op jit(solution)/shard_map/ppermute | solution.py:109
  93.8 1.6 copy-done.1
  95.5 3.6 %add.225 = f32[6,256,512]{2,1,0:T(8,128)S(1)} add(f32[6,256,512]{2,1,0:T(8,128)} %get-tuple-element.7, f32[6,256,512]{2,1,0:T(8,128)} %copy-done.1) | non-fusion elementwise | flops 786432 | bytes 9437184 | tf_op jit(solution)/shard_map/add | solution.py:109
  99.1 1.5 dynamic-slice_bitcast_fusion
  100.5 0.6 collective-permute-start.1
  101.1 0.2 fusion.4
  101.3 1.5 collective-permute-start.2
  102.9 0.6 pad_maximum_fusion
  103.5 1.5 reshape.165.w_ref
  104.9 4.2 %collective-permute-start.7 = (f32[6,32,512]{2,1,0:T(8,128)S(1)}, f32[6,32,512]{2,1,0:T(8,128)S(1)}, u32[]{:S(2)}, u32[]{:S(2)}) collective-permute-start(f32[6,32,512]{2,1,0:T(8,128)S(1)} %get-tuple-element.16), channel_id=1, source_target_pairs={{0,14},{2,0},{4,2},{6,4},{8,6},{10,8},{12,10},{14,12},{1,15},{3,1}... | collective-permute-start | bytes 1179656 | tf_op jit(solution)/shard_map/ppermute | solution.py:122
  109.1 0.5 collective-permute-start.6
  109.7 6.0 %collective-permute-done.1 = f32[6,32,512]{2,1,0:T(8,128)} collective-permute-done((f32[6,32,512]{2,1,0:T(8,128)}, f32[6,32,512]{2,1,0:T(8,128)}, u32[]{:S(2)}, u32[]{:S(2)}) %collective-permute-start.1) | collective-permute-done | bytes 393248 | tf_op jit(solution)/shard_map/ppermute | solution.py:122
  115.6 1.0 bitcast_dynamic-update-slice_fusion.6
  116.7 0.0 collective-permute-done.2
  116.7 23.4 %collective-permute-start.4 = (f32[6,32,512]{2,1,0:T(8,128)}, f32[6,32,512]{2,1,0:T(8,128)S(1)}, u32[]{:S(2)}, u32[]{:S(2)}) collective-permute-start(f32[6,32,512]{2,1,0:T(8,128)} %get-tuple-element.19), channel_id=1, source_target_pairs={{0,8},{2,10},{4,12},{6,14},{8,0},{10,2},{12,4},{14,6},{1,9},{3,11}... | collective-permute-start | bytes 1179656 | tf_op jit(solution)/shard_map/ppermute | solution.py:122
  140.1 1.0 bitcast_dynamic-update-slice_fusion.5
  141.1 24.2 %collective-permute-done.3 = f32[6,32,512]{2,1,0:T(8,128)S(1)} collective-permute-done((f32[6,32,512]{2,1,0:T(8,128)}, f32[6,32,512]{2,1,0:T(8,128)S(1)}, u32[]{:S(2)}, u32[]{:S(2)}) %collective-permute-start.3) | collective-permute-done | bytes 393248 | tf_op jit(solution)/shard_map/ppermute | solution.py:122
  165.4 7.9 %collective-permute-done.4 = f32[6,32,512]{2,1,0:T(8,128)S(1)} collective-permute-done((f32[6,32,512]{2,1,0:T(8,128)}, f32[6,32,512]{2,1,0:T(8,128)S(1)}, u32[]{:S(2)}, u32[]{:S(2)}) %collective-permute-start.4) | collective-permute-done | bytes 393248 | tf_op jit(solution)/shard_map/ppermute | solution.py:122
  173.4 0.0 collective-permute-done.6
  173.5 3.4 %copy.7 = f32[6,8,32,512]{3,1,2,0:T(8,128)} copy(f32[6,8,32,512]{3,2,1,0:T(8,128)S(1)} %bitcast.74) | data formatting | bytes 6291456
  177.0 8.2 %shard_map.47 = f32[96,16384]{1,0:T(8,128)} custom-call(f32[96,48]{1,0:T(8,128)} %reshape.165.w_ref, f32[48,16384]{1,0:T(8,128)} %bitcast.73), custom_call_target="tpu_custom_call" | custom-call | tf_op jit(solution)/shard_map/pallas_call | solution.py:80
  185.2 3.1 %convert.9 = bf16[96,16384]{1,0:T(8,128)(2,1)S(1)} convert(f32[96,16384]{1,0:T(8,128)} %shard_map.47) | non-fusion elementwise | flops 1572864 | bytes 9437184 | tf_op jit(solution)/shard_map/convert.6
  188.3 1.6 fusion.10
  189.9 0.2 copy.9
  190.1 1.0 collective-permute-start.8
  191.1 1.2 copy.10
  192.3 0.8 slice.57
  193.1 0.0 collective-permute-start.9
  193.1 0.6 copy.8
  193.7 0.1 slice.55
  193.8 0.4 copy-done.2
  194.1 0.2 copy.15
  194.3 0.2 copy.14
  194.5 3.9 %collective-permute-start.13 = (bf16[2,6,32,512]{3,2,1,0:T(8,128)(2,1)S(1)}, bf16[2,6,32,512]{3,2,1,0:T(8,128)(2,1)S(1)}, u32[]{:S(2)}, u32[]{:S(2)}) collective-permute-start(bf16[2,6,32,512]{3,2,1,0:T(8,128)(2,1)S(1)} %bitcast.93), channel_id=1, source_target_pairs={{0,12},{2,14},{4,0},{6,2},{8,4},{10,6},{12,8},{14,10},{1,13},{3,15... | collective-permute-start | bytes 1179656 | tf_op jit(solution)/shard_map/ppermute | solution.py:141
  198.4 2.0 collective-permute-start.14
  200.4 0.2 copy.13
  200.6 0.1 collective-permute-start.12
  200.7 0.2 copy.12
  200.9 0.2 copy.11
  201.1 0.8 broadcast_in_dim.2
  201.9 0.1 constant_dynamic-update-slice_fusion
  201.9 3.2 %collective-permute-done.8 = bf16[2,6,32,512]{3,2,1,0:T(8,128)(2,1)} collective-permute-done((bf16[2,6,32,512]{3,2,1,0:T(8,128)(2,1)S(1)}, bf16[2,6,32,512]{3,2,1,0:T(8,128)(2,1)}, u32[]{:S(2)}, u32[]{:S(2)}) %collective-permute-start.8) | collective-permute-done | bytes 393248 | tf_op jit(solution)/shard_map/ppermute | solution.py:141
  205.2 1.1 convert_dynamic-update-slice_fusion.6
  206.3 1.0 collective-permute-done.9
  207.2 1.1 convert_dynamic-update-slice_fusion.5
  208.3 46.3 %collective-permute-done.10 = bf16[2,6,32,512]{3,2,1,0:T(8,128)(2,1)S(1)} collective-permute-done((bf16[2,6,32,512]{3,2,1,0:T(8,128)(2,1)S(1)}, bf16[2,6,32,512]{3,2,1,0:T(8,128)(2,1)S(1)}, u32[]{:S(2)}, u32[]{:S(2)}) %collective-permute-start.10) | collective-permute-done | bytes 393248 | tf_op jit(solution)/shard_map/ppermute | solution.py:141
  254.6 0.1 convert_dynamic-update-slice_fusion.4
  254.7 9.0 %collective-permute-done.11 = bf16[2,6,32,512]{3,2,1,0:T(8,128)(2,1)S(1)} collective-permute-done((bf16[2,6,32,512]{3,2,1,0:T(8,128)(2,1)S(1)}, bf16[2,6,32,512]{3,2,1,0:T(8,128)(2,1)S(1)}, u32[]{:S(2)}, u32[]{:S(2)}) %collective-permute-start.11) | collective-permute-done | bytes 393248 | tf_op jit(solution)/shard_map/ppermute | solution.py:141
  263.7 0.1 convert_dynamic-update-slice_fusion.3
  263.8 0.1 convert_dynamic-update-slice_fusion.2
  263.9 0.1 convert_dynamic-update-slice_fusion.1
  264.0 0.0 copy-start
  264.0 2.7 copy-done
  266.7 1.0 convert_dynamic-update-slice_fusion
  (27 shorter events, 0.4 us)
Async XLA Ops:
  6.5 56.3 %all-gather.2.cloned.1.call-start = ((), (), s32[]{:S(2)}) async-start(), calls=%async_computation | async-start | bytes 4456448 | tf_op jit(solution)/shard_map/all_gather | solution.py:103
  88.0 5.9 %collective-permute-start = (f32[6,256,512]{2,1,0:T(8,128)}, f32[6,256,512]{2,1,0:T(8,128)S(1)}, u32[]{:S(2)}, u32[]{:S(2)}) collective-permute-start(f32[6,256,512]{2,1,0:T(8,128)} %get-tuple-element.8), channel_id=1, source_target_pairs={{0,1},{1,0},{2,3},{3,2},{4,5},{5,4},{6,7},{7,6},{8,9},{9,8},{10,11... | collective-permute-start | bytes 9437192 | tf_op jit(solution)/shard_map/ppermute | solution.py:109
  93.8 1.6 copy-start.1
  100.5 15.1 %collective-permute-start.1 = (f32[6,32,512]{2,1,0:T(8,128)}, f32[6,32,512]{2,1,0:T(8,128)}, u32[]{:S(2)}, u32[]{:S(2)}) collective-permute-start(f32[6,32,512]{2,1,0:T(8,128)} %get-tuple-element.22), channel_id=1, source_target_pairs={{0,2},{2,4},{4,6},{6,8},{8,10},{10,12},{12,14},{14,0},{1,3},{3,5},... | collective-permute-start | bytes 1179656 | tf_op jit(solution)/shard_map/ppermute | solution.py:122
  101.3 15.4 %collective-permute-start.2 = (f32[6,32,512]{2,1,0:T(8,128)}, f32[6,32,512]{2,1,0:T(8,128)}, u32[]{:S(2)}, u32[]{:S(2)}) collective-permute-start(f32[6,32,512]{2,1,0:T(8,128)} %get-tuple-element.21), channel_id=1, source_target_pairs={{0,4},{2,6},{4,8},{6,10},{8,12},{10,14},{12,0},{14,2},{1,5},{3,7},... | collective-permute-start | bytes 1179656 | tf_op jit(solution)/shard_map/ppermute | solution.py:122
  104.9 68.5 %collective-permute-start.7 = (f32[6,32,512]{2,1,0:T(8,128)S(1)}, f32[6,32,512]{2,1,0:T(8,128)S(1)}, u32[]{:S(2)}, u32[]{:S(2)}) collective-permute-start(f32[6,32,512]{2,1,0:T(8,128)S(1)} %get-tuple-element.16), channel_id=1, source_target_pairs={{0,14},{2,0},{4,2},{6,4},{8,6},{10,8},{12,10},{14,12},{1,15},{3,1}... | collective-permute-start | bytes 1179656 | tf_op jit(solution)/shard_map/ppermute | solution.py:122
  109.1 64.3 %collective-permute-start.6 = (f32[6,32,512]{2,1,0:T(8,128)}, f32[6,32,512]{2,1,0:T(8,128)S(1)}, u32[]{:S(2)}, u32[]{:S(2)}) collective-permute-start(f32[6,32,512]{2,1,0:T(8,128)} %get-tuple-element.17), channel_id=1, source_target_pairs={{0,12},{2,14},{4,0},{6,2},{8,4},{10,6},{12,8},{14,10},{1,13},{3,15... | collective-permute-start | bytes 1179656 | tf_op jit(solution)/shard_map/ppermute | solution.py:122
  109.6 63.7 %collective-permute-start.5 = (f32[6,32,512]{2,1,0:T(8,128)}, f32[6,32,512]{2,1,0:T(8,128)S(1)}, u32[]{:S(2)}, u32[]{:S(2)}) collective-permute-start(f32[6,32,512]{2,1,0:T(8,128)} %get-tuple-element.18), channel_id=1, source_target_pairs={{0,10},{2,12},{4,14},{6,0},{8,2},{10,4},{12,6},{14,8},{1,11},{3,13... | collective-permute-start | bytes 1179656 | tf_op jit(solution)/shard_map/ppermute | solution.py:122
  115.6 49.7 %collective-permute-start.3 = (f32[6,32,512]{2,1,0:T(8,128)}, f32[6,32,512]{2,1,0:T(8,128)S(1)}, u32[]{:S(2)}, u32[]{:S(2)}) collective-permute-start(f32[6,32,512]{2,1,0:T(8,128)} %get-tuple-element.20), channel_id=1, source_target_pairs={{0,6},{2,8},{4,10},{6,12},{8,14},{10,0},{12,2},{14,4},{1,7},{3,9},... | collective-permute-start | bytes 1179656 | tf_op jit(solution)/shard_map/ppermute | solution.py:122
  116.7 56.7 %collective-permute-start.4 = (f32[6,32,512]{2,1,0:T(8,128)}, f32[6,32,512]{2,1,0:T(8,128)S(1)}, u32[]{:S(2)}, u32[]{:S(2)}) collective-permute-start(f32[6,32,512]{2,1,0:T(8,128)} %get-tuple-element.19), channel_id=1, source_target_pairs={{0,8},{2,10},{4,12},{6,14},{8,0},{10,2},{12,4},{14,6},{1,9},{3,11}... | collective-permute-start | bytes 1179656 | tf_op jit(solution)/shard_map/ppermute | solution.py:122
  189.9 3.2 %slice-start = ((f32[96,16384]{1,0:T(8,128)}), f32[12,16384]{1,0:T(8,128)S(1)}, s32[]{:S(2)}) async-start(f32[96,16384]{1,0:T(8,128)} %shard_map.47), calls=%async_computation.1 | async-start | bytes 2097152 | tf_op jit(solution)/shard_map/slice | solution.py:138
  190.1 15.1 %collective-permute-start.8 = (bf16[2,6,32,512]{3,2,1,0:T(8,128)(2,1)S(1)}, bf16[2,6,32,512]{3,2,1,0:T(8,128)(2,1)}, u32[]{:S(2)}, u32[]{:S(2)}) collective-permute-start(bf16[2,6,32,512]{3,2,1,0:T(8,128)(2,1)S(1)} %bitcast.91), channel_id=1, source_target_pairs={{0,2},{2,4},{4,6},{6,8},{8,10},{10,12},{12,14},{14,0},{1,3},{3,5},... | collective-permute-start | bytes 1179656 | tf_op jit(solution)/shard_map/ppermute | solution.py:141
  193.1 14.1 %collective-permute-start.9 = (bf16[2,6,32,512]{3,2,1,0:T(8,128)(2,1)}, bf16[2,6,32,512]{3,2,1,0:T(8,128)(2,1)}, u32[]{:S(2)}, u32[]{:S(2)}) collective-permute-start(bf16[2,6,32,512]{3,2,1,0:T(8,128)(2,1)} %bitcast.34), channel_id=1, source_target_pairs={{0,4},{2,6},{4,8},{6,10},{8,12},{10,14},{12,0},{14,2},{1,5},{3,7},... | collective-permute-start | bytes 1179656 | tf_op jit(solution)/shard_map/ppermute | solution.py:141
  193.1 1.0 copy-start.2
  194.5 69.4 %collective-permute-start.13 = (bf16[2,6,32,512]{3,2,1,0:T(8,128)(2,1)S(1)}, bf16[2,6,32,512]{3,2,1,0:T(8,128)(2,1)S(1)}, u32[]{:S(2)}, u32[]{:S(2)}) collective-permute-start(bf16[2,6,32,512]{3,2,1,0:T(8,128)(2,1)S(1)} %bitcast.93), channel_id=1, source_target_pairs={{0,12},{2,14},{4,0},{6,2},{8,4},{10,6},{12,8},{14,10},{1,13},{3,15... | collective-permute-start | bytes 1179656 | tf_op jit(solution)/shard_map/ppermute | solution.py:141
  198.4 65.6 %collective-permute-start.14 = (bf16[2,6,32,512]{3,2,1,0:T(8,128)(2,1)S(1)}, bf16[2,6,32,512]{3,2,1,0:T(8,128)(2,1)S(1)}, u32[]{:S(2)}, u32[]{:S(2)}) collective-permute-start(bf16[2,6,32,512]{3,2,1,0:T(8,128)(2,1)S(1)} %bitcast.92), channel_id=1, source_target_pairs={{0,14},{2,0},{4,2},{6,4},{8,6},{10,8},{12,10},{14,12},{1,15},{3,1}... | collective-permute-start | bytes 1179656 | tf_op jit(solution)/shard_map/ppermute | solution.py:141
  200.6 63.2 %collective-permute-start.12 = (bf16[2,6,32,512]{3,2,1,0:T(8,128)(2,1)S(1)}, bf16[2,6,32,512]{3,2,1,0:T(8,128)(2,1)S(1)}, u32[]{:S(2)}, u32[]{:S(2)}) collective-permute-start(bf16[2,6,32,512]{3,2,1,0:T(8,128)(2,1)S(1)} %bitcast.94), channel_id=1, source_target_pairs={{0,10},{2,12},{4,14},{6,0},{8,2},{10,4},{12,6},{14,8},{1,11},{3,13... | collective-permute-start | bytes 1179656 | tf_op jit(solution)/shard_map/ppermute | solution.py:141
  205.2 49.4 %collective-permute-start.10 = (bf16[2,6,32,512]{3,2,1,0:T(8,128)(2,1)S(1)}, bf16[2,6,32,512]{3,2,1,0:T(8,128)(2,1)S(1)}, u32[]{:S(2)}, u32[]{:S(2)}) collective-permute-start(bf16[2,6,32,512]{3,2,1,0:T(8,128)(2,1)S(1)} %bitcast.96), channel_id=1, source_target_pairs={{0,6},{2,8},{4,10},{6,12},{8,14},{10,0},{12,2},{14,4},{1,7},{3,9},... | collective-permute-start | bytes 1179656 | tf_op jit(solution)/shard_map/ppermute | solution.py:141
  207.2 56.5 %collective-permute-start.11 = (bf16[2,6,32,512]{3,2,1,0:T(8,128)(2,1)S(1)}, bf16[2,6,32,512]{3,2,1,0:T(8,128)(2,1)S(1)}, u32[]{:S(2)}, u32[]{:S(2)}) collective-permute-start(bf16[2,6,32,512]{3,2,1,0:T(8,128)(2,1)S(1)} %bitcast.95), channel_id=1, source_target_pairs={{0,8},{2,10},{4,12},{6,14},{8,0},{10,2},{12,4},{14,6},{1,9},{3,11}... | collective-permute-start | bytes 1179656 | tf_op jit(solution)/shard_map/ppermute | solution.py:141
  264.0 2.7 copy-start
Sparse Core Ops, SparseCore 0:
  9.5 53.2 all-gather.1

commit v18 on v17

--- a/solution.py
+++ b/solution.py
@@ -95,6 +95,16 @@
     return jnp.cos(angle), -jnp.sin(angle)
 
 
+def _shift_order(n):
+    rest = sorted(range(1, n), key=lambda s: -min(s, n - s))
+    out = [0]
+    while rest:
+        out.append(rest.pop(0))
+        if rest:
+            out.append(rest.pop())
+    return out
+
+
 def body(panel, stiffness, block_rows, block_cols):
     nbl, nblk, bs, _ = stiffness.shape
     modes = panel.shape[-1]
@@ -115,12 +125,13 @@
     r = rows_half // nbd
     chunks = half.reshape(nbl, nbd, r, modes)
 
-    got = []
-    for s in range(nbd):
+    order = _shift_order(nbd)
+    got = [None] * nbd
+    for s in order:
         piece = lax.dynamic_index_in_dim(chunks, (me + s) % nbd, axis=1, keepdims=False)
         if s:
             piece = lax.ppermute(piece, "blade", [(j, (j + s) % nbd) for j in range(nbd)])
-        got.append(piece)
+        got[s] = piece
     stacked = jnp.stack(got).reshape(nbd * nbl, r * modes)
 
     count = nbl * nbd
@@ -134,7 +145,7 @@
     spec = spec.reshape(nbd, 2, nbl, r, modes)
 
     out = jnp.zeros((2, nbl, rows_half, modes), jnp.float32)
-    for t in range(nbd):
+    for t in order:
         piece = spec[t]
         if t:
             piece = piece.astype(jnp.bfloat16)

time: 275 us -> 275 us (level)
  waiting for transfers between devices: 155 us -> 145 us
  starting transfers between devices: 37.4 us -> 47.1 us
    ppermute x7, starting transfers between devices: 6.92 us -> 16.6 us  [body(): lax.ppermute(piece, 'blade', [(j, (j + t) % nbd) for j in range(nbd)])]
    ppermute x7, waiting for transfers between devices: 59.5 us -> 50 us  [body(): lax.ppermute(piece, 'blade', [(j, (j + t) % nbd) for j in range(nbd)])]
  transfers between devices with their start and end apart: 16 -> 16, of which waited for: 9 -> 7; matrix products, arithmetic and copies ran while one was open for 5% -> 5% of each run, Pallas kernels for 0% -> 0%
where the time goes in v18:
time: 275 us
  waiting for transfers between devices  145 us (53%)
  starting transfers between devices  47.1 us (17%)
  Pallas kernels  33.3 us (12%)
  local copies, waits for them, and re-layouts  24.1 us (9%)
  between operations  13.8 us (5%)
  other arithmetic  11.2 us (4%)
    all_gather x1, waiting for transfers between devices, body(): pt = lax.all_gather(mine, ('blade', 'dof'), axis=0, tiled=True)  51.8 us
    ppermute x7, waiting for transfers between devices, body(): lax.ppermute(piece, 'blade', [(j, (j + t) % nbd) for j in range(nbd)])  50 us
    ppermute x7, waiting for transfers between devices, body(): lax.ppermute(piece, 'blade', [(j, (j + s) % nbd) for j in range(nbd)])  38.1 us
    ppermute x7, starting transfers between devices, body(): lax.ppermute(piece, 'blade', [(j, (j + s) % nbd) for j in range(nbd)])  30.2 us
    pallas_call x1, Pallas kernels, _project(): pl.pallas_call(_project_kernel, grid_spec=grid_spec, out_shape=[jax.Shape...  25.1 us
    ppermute x7, starting transfers between devices, body(): lax.ppermute(piece, 'blade', [(j, (j + t) % nbd) for j in range(nbd)])  16.6 us
    unnamed x30, local copies, waits for them, and re-layouts  14.1 us
    pallas_call x1, Pallas kernels, _dft(): pl.pallas_call(_dft_kernel, grid=(n // tn,), in_specs=[pl.BlockSpec((rows...  8.2 us
  transfers between devices with their start and end apart: 16, of which 7 were waited for; matrix products, arithmetic and copies ran while one was open for 5% of the time, Pallas kernels for 0%

profile of v18, /device:TPU:0, one launch (start us, length us, event | category | flops | bytes accessed | tf_op | source)
XLA Modules:
  0.0 274.7 jit_solution(7117183647611579508)
XLA Ops:
  6.5 1.8 copy.6
  8.3 0.0 all-gather.2.cloned.1.call-update
  8.4 1.3 reshape.166.rows_ref
  9.7 1.4 reshape.167.cols_ref
  11.1 51.8 %all-gather.2.cloned.1.call-done.pt_ref = bf16[32,512,128]{2,1,0:T(8,128)(2,1)} async-done(((bf16[2,512,128]{2,1,0:T(8,128)(2,1)}), bf16[32,512,128]{2,1,0:T(8,128)(2,1)}) %all-gather.2.cloned.1.call-update) | async-done | bytes 4194320 | tf_op jit(solution)/shard_map/all_gather | solution.py:113
  62.8 25.1 %shard_map.46 = (f32[6,256,512]{2,1,0:T(8,128)}, f32[6,256,512]{2,1,0:T(8,128)}) custom-call(s32[192]{0:T(256)} %reshape.166.rows_ref, s32[192]{0:T(256)} %reshape.167.cols_ref, s32[1]{0:T(128)} %bitcast.side_ref, bf16[32,512,128]{2,1,0:T(8,128)(2,1)} %all-gather.2.cloned.1.call-done.pt_ref, bf16[6,32,128,128]{3,2,1,0:T(8,128)(2,1)} %s_ref.1), custom_call_target="tpu_custom_call" | custom-call | tf_op jit(solution)/shard_map/pallas_call | solution.py:52
  88.0 0.3 collective-permute-start
  88.2 0.1 iota_add_fusion
  88.3 0.1 add.222
  88.4 0.1 iota_add_fusion.1
  88.4 5.4 %collective-permute-done = f32[6,256,512]{2,1,0:T(8,128)S(1)} collective-permute-done((f32[6,256,512]{2,1,0:T(8,128)}, f32[6,256,512]{2,1,0:T(8,128)S(1)}, u32[]{:S(2)}, u32[]{:S(2)}) %collective-permute-start) | collective-permute-done | bytes 3145760 | tf_op jit(solution)/shard_map/ppermute | solution.py:119
  93.8 1.6 copy-done.1
  95.5 3.6 %add.225 = f32[6,256,512]{2,1,0:T(8,128)S(1)} add(f32[6,256,512]{2,1,0:T(8,128)} %get-tuple-element.7, f32[6,256,512]{2,1,0:T(8,128)} %copy-done.1) | non-fusion elementwise | flops 786432 | bytes 9437184 | tf_op jit(solution)/shard_map/add | solution.py:119
  99.1 1.5 dynamic-slice_bitcast_fusion
  100.5 0.6 collective-permute-start.1
  101.1 0.2 fusion.4
  101.3 1.5 collective-permute-start.2
  102.9 0.6 pad_maximum_fusion
  103.5 1.5 reshape.165.w_ref
  104.9 4.2 %collective-permute-start.7 = (f32[6,32,512]{2,1,0:T(8,128)S(1)}, f32[6,32,512]{2,1,0:T(8,128)S(1)}, u32[]{:S(2)}, u32[]{:S(2)}) collective-permute-start(f32[6,32,512]{2,1,0:T(8,128)S(1)} %get-tuple-element.16), channel_id=1, source_target_pairs={{0,14},{2,0},{4,2},{6,4},{8,6},{10,8},{12,10},{14,12},{1,15},{3,1}... | collective-permute-start | bytes 1179656 | tf_op jit(solution)/shard_map/ppermute | solution.py:133
  109.1 0.5 collective-permute-start.6
  109.6 0.0 collective-permute-start.5
  109.7 6.0 %collective-permute-done.1 = f32[6,32,512]{2,1,0:T(8,128)} collective-permute-done((f32[6,32,512]{2,1,0:T(8,128)}, f32[6,32,512]{2,1,0:T(8,128)}, u32[]{:S(2)}, u32[]{:S(2)}) %collective-permute-start.1) | collective-permute-done | bytes 393248 | tf_op jit(solution)/shard_map/ppermute | solution.py:133
  115.6 0.0 collective-permute-start.3
  115.6 1.0 bitcast_dynamic-update-slice_fusion.6
  116.7 0.0 collective-permute-done.2
  116.7 23.4 %collective-permute-start.4 = (f32[6,32,512]{2,1,0:T(8,128)}, f32[6,32,512]{2,1,0:T(8,128)S(1)}, u32[]{:S(2)}, u32[]{:S(2)}) collective-permute-start(f32[6,32,512]{2,1,0:T(8,128)} %get-tuple-element.19), channel_id=1, source_target_pairs={{0,8},{2,10},{4,12},{6,14},{8,0},{10,2},{12,4},{14,6},{1,9},{3,11}... | collective-permute-start | bytes 1179656 | tf_op jit(solution)/shard_map/ppermute | solution.py:133
  140.1 1.0 bitcast_dynamic-update-slice_fusion.5
  141.1 24.2 %collective-permute-done.3 = f32[6,32,512]{2,1,0:T(8,128)S(1)} collective-permute-done((f32[6,32,512]{2,1,0:T(8,128)}, f32[6,32,512]{2,1,0:T(8,128)S(1)}, u32[]{:S(2)}, u32[]{:S(2)}) %collective-permute-start.3) | collective-permute-done | bytes 393248 | tf_op jit(solution)/shard_map/ppermute | solution.py:133
  165.4 7.9 %collective-permute-done.4 = f32[6,32,512]{2,1,0:T(8,128)S(1)} collective-permute-done((f32[6,32,512]{2,1,0:T(8,128)}, f32[6,32,512]{2,1,0:T(8,128)S(1)}, u32[]{:S(2)}, u32[]{:S(2)}) %collective-permute-start.4) | collective-permute-done | bytes 393248 | tf_op jit(solution)/shard_map/ppermute | solution.py:133
  173.5 3.4 %copy.7 = f32[6,8,32,512]{3,1,2,0:T(8,128)} copy(f32[6,8,32,512]{3,2,1,0:T(8,128)S(1)} %bitcast.74) | data formatting | bytes 6291456
  177.0 8.2 %shard_map.47 = f32[96,16384]{1,0:T(8,128)} custom-call(f32[96,48]{1,0:T(8,128)} %reshape.165.w_ref, f32[48,16384]{1,0:T(8,128)} %bitcast.73), custom_call_target="tpu_custom_call" | custom-call | tf_op jit(solution)/shard_map/pallas_call | solution.py:80
  185.2 3.1 %convert.9 = bf16[96,16384]{1,0:T(8,128)(2,1)S(1)} convert(f32[96,16384]{1,0:T(8,128)} %shard_map.47) | non-fusion elementwise | flops 1572864 | bytes 9437184 | tf_op jit(solution)/shard_map/convert.6
  188.3 1.6 fusion.10
  189.9 0.2 copy.9
  190.1 0.1 collective-permute-start.8
  190.2 1.2 copy.10
  191.4 0.8 slice.57
  192.2 1.3 collective-permute-start.9
  193.5 0.6 copy.8
  194.1 0.1 slice.55
  194.2 0.4 copy-done.2
  194.6 0.2 copy.15
  194.8 0.2 copy.14
  195.0 3.4 %collective-permute-start.13 = (bf16[2,6,32,512]{3,2,1,0:T(8,128)(2,1)S(1)}, bf16[2,6,32,512]{3,2,1,0:T(8,128)(2,1)S(1)}, u32[]{:S(2)}, u32[]{:S(2)}) collective-permute-start(bf16[2,6,32,512]{3,2,1,0:T(8,128)(2,1)S(1)} %bitcast.93), channel_id=1, source_target_pairs={{0,12},{2,14},{4,0},{6,2},{8,4},{10,6},{12,8},{14,10},{1,13},{3,15... | collective-permute-start | bytes 1179656 | tf_op jit(solution)/shard_map/ppermute | solution.py:152
  198.4 0.2 copy.13
  198.6 1.7 collective-permute-start.12
  200.3 0.2 copy.12
  200.5 0.2 copy.11
  200.7 0.8 broadcast_in_dim.2
  201.5 0.1 constant_dynamic-update-slice_fusion
  201.6 6.6 %collective-permute-done.8 = bf16[2,6,32,512]{3,2,1,0:T(8,128)(2,1)} collective-permute-done((bf16[2,6,32,512]{3,2,1,0:T(8,128)(2,1)S(1)}, bf16[2,6,32,512]{3,2,1,0:T(8,128)(2,1)}, u32[]{:S(2)}, u32[]{:S(2)}) %collective-permute-start.8) | collective-permute-done | bytes 393248 | tf_op jit(solution)/shard_map/ppermute | solution.py:152
  208.1 10.0 %collective-permute-start.10 = (bf16[2,6,32,512]{3,2,1,0:T(8,128)(2,1)S(1)}, bf16[2,6,32,512]{3,2,1,0:T(8,128)(2,1)S(1)}, u32[]{:S(2)}, u32[]{:S(2)}) collective-permute-start(bf16[2,6,32,512]{3,2,1,0:T(8,128)(2,1)S(1)} %bitcast.96), channel_id=1, source_target_pairs={{0,6},{2,8},{4,10},{6,12},{8,14},{10,0},{12,2},{14,4},{1,7},{3,9},... | collective-permute-start | bytes 1179656 | tf_op jit(solution)/shard_map/ppermute | solution.py:152
  218.1 1.1 convert_dynamic-update-slice_fusion.6
  219.2 0.1 collective-permute-start.11
  219.3 1.1 convert_dynamic-update-slice_fusion.5
  220.4 43.4 %collective-permute-done.10 = bf16[2,6,32,512]{3,2,1,0:T(8,128)(2,1)S(1)} collective-permute-done((bf16[2,6,32,512]{3,2,1,0:T(8,128)(2,1)S(1)}, bf16[2,6,32,512]{3,2,1,0:T(8,128)(2,1)S(1)}, u32[]{:S(2)}, u32[]{:S(2)}) %collective-permute-start.10) | collective-permute-done | bytes 393248 | tf_op jit(solution)/shard_map/ppermute | solution.py:152
  263.8 0.1 convert_dynamic-update-slice_fusion.4
  263.9 0.1 convert_dynamic-update-slice_fusion.3
  264.0 0.1 convert_dynamic-update-slice_fusion.2
  264.1 0.1 convert_dynamic-update-slice_fusion.1
  264.2 0.0 copy-start
  264.2 2.7 copy-done
  266.9 1.0 convert_dynamic-update-slice_fusion
  (27 shorter events, 0.4 us)
Async XLA Ops:
  6.5 56.3 %all-gather.2.cloned.1.call-start = ((), (), s32[]{:S(2)}) async-start(), calls=%async_computation | async-start | bytes 4456448 | tf_op jit(solution)/shard_map/all_gather | solution.py:113
  88.0 5.9 %collective-permute-start = (f32[6,256,512]{2,1,0:T(8,128)}, f32[6,256,512]{2,1,0:T(8,128)S(1)}, u32[]{:S(2)}, u32[]{:S(2)}) collective-permute-start(f32[6,256,512]{2,1,0:T(8,128)} %get-tuple-element.8), channel_id=1, source_target_pairs={{0,1},{1,0},{2,3},{3,2},{4,5},{5,4},{6,7},{7,6},{8,9},{9,8},{10,11... | collective-permute-start | bytes 9437192 | tf_op jit(solution)/shard_map/ppermute | solution.py:119
  93.8 1.6 copy-start.1
  100.5 15.1 %collective-permute-start.1 = (f32[6,32,512]{2,1,0:T(8,128)}, f32[6,32,512]{2,1,0:T(8,128)}, u32[]{:S(2)}, u32[]{:S(2)}) collective-permute-start(f32[6,32,512]{2,1,0:T(8,128)} %get-tuple-element.22), channel_id=1, source_target_pairs={{0,2},{2,4},{4,6},{6,8},{8,10},{10,12},{12,14},{14,0},{1,3},{3,5},... | collective-permute-start | bytes 1179656 | tf_op jit(solution)/shard_map/ppermute | solution.py:133
  101.3 15.4 %collective-permute-start.2 = (f32[6,32,512]{2,1,0:T(8,128)}, f32[6,32,512]{2,1,0:T(8,128)}, u32[]{:S(2)}, u32[]{:S(2)}) collective-permute-start(f32[6,32,512]{2,1,0:T(8,128)} %get-tuple-element.21), channel_id=1, source_target_pairs={{0,4},{2,6},{4,8},{6,10},{8,12},{10,14},{12,0},{14,2},{1,5},{3,7},... | collective-permute-start | bytes 1179656 | tf_op jit(solution)/shard_map/ppermute | solution.py:133
  104.9 68.5 %collective-permute-start.7 = (f32[6,32,512]{2,1,0:T(8,128)S(1)}, f32[6,32,512]{2,1,0:T(8,128)S(1)}, u32[]{:S(2)}, u32[]{:S(2)}) collective-permute-start(f32[6,32,512]{2,1,0:T(8,128)S(1)} %get-tuple-element.16), channel_id=1, source_target_pairs={{0,14},{2,0},{4,2},{6,4},{8,6},{10,8},{12,10},{14,12},{1,15},{3,1}... | collective-permute-start | bytes 1179656 | tf_op jit(solution)/shard_map/ppermute | solution.py:133
  109.1 64.3 %collective-permute-start.6 = (f32[6,32,512]{2,1,0:T(8,128)}, f32[6,32,512]{2,1,0:T(8,128)S(1)}, u32[]{:S(2)}, u32[]{:S(2)}) collective-permute-start(f32[6,32,512]{2,1,0:T(8,128)} %get-tuple-element.17), channel_id=1, source_target_pairs={{0,12},{2,14},{4,0},{6,2},{8,4},{10,6},{12,8},{14,10},{1,13},{3,15... | collective-permute-start | bytes 1179656 | tf_op jit(solution)/shard_map/ppermute | solution.py:133
  109.6 63.7 %collective-permute-start.5 = (f32[6,32,512]{2,1,0:T(8,128)}, f32[6,32,512]{2,1,0:T(8,128)S(1)}, u32[]{:S(2)}, u32[]{:S(2)}) collective-permute-start(f32[6,32,512]{2,1,0:T(8,128)} %get-tuple-element.18), channel_id=1, source_target_pairs={{0,10},{2,12},{4,14},{6,0},{8,2},{10,4},{12,6},{14,8},{1,11},{3,13... | collective-permute-start | bytes 1179656 | tf_op jit(solution)/shard_map/ppermute | solution.py:133
  115.6 49.7 %collective-permute-start.3 = (f32[6,32,512]{2,1,0:T(8,128)}, f32[6,32,512]{2,1,0:T(8,128)S(1)}, u32[]{:S(2)}, u32[]{:S(2)}) collective-permute-start(f32[6,32,512]{2,1,0:T(8,128)} %get-tuple-element.20), channel_id=1, source_target_pairs={{0,6},{2,8},{4,10},{6,12},{8,14},{10,0},{12,2},{14,4},{1,7},{3,9},... | collective-permute-start | bytes 1179656 | tf_op jit(solution)/shard_map/ppermute | solution.py:133
  116.7 56.7 %collective-permute-start.4 = (f32[6,32,512]{2,1,0:T(8,128)}, f32[6,32,512]{2,1,0:T(8,128)S(1)}, u32[]{:S(2)}, u32[]{:S(2)}) collective-permute-start(f32[6,32,512]{2,1,0:T(8,128)} %get-tuple-element.19), channel_id=1, source_target_pairs={{0,8},{2,10},{4,12},{6,14},{8,0},{10,2},{12,4},{14,6},{1,9},{3,11}... | collective-permute-start | bytes 1179656 | tf_op jit(solution)/shard_map/ppermute | solution.py:133
  189.9 3.6 %slice-start = ((f32[96,16384]{1,0:T(8,128)}), f32[12,16384]{1,0:T(8,128)S(1)}, s32[]{:S(2)}) async-start(f32[96,16384]{1,0:T(8,128)} %shard_map.47), calls=%async_computation.1 | async-start | bytes 2097152 | tf_op jit(solution)/shard_map/slice | solution.py:149
  190.1 18.0 %collective-permute-start.8 = (bf16[2,6,32,512]{3,2,1,0:T(8,128)(2,1)S(1)}, bf16[2,6,32,512]{3,2,1,0:T(8,128)(2,1)}, u32[]{:S(2)}, u32[]{:S(2)}) collective-permute-start(bf16[2,6,32,512]{3,2,1,0:T(8,128)(2,1)S(1)} %bitcast.91), channel_id=1, source_target_pairs={{0,8},{2,10},{4,12},{6,14},{8,0},{10,2},{12,4},{14,6},{1,9},{3,11}... | collective-permute-start | bytes 1179656 | tf_op jit(solution)/shard_map/ppermute | solution.py:152
  192.2 27.0 %collective-permute-start.9 = (bf16[2,6,32,512]{3,2,1,0:T(8,128)(2,1)}, bf16[2,6,32,512]{3,2,1,0:T(8,128)(2,1)}, u32[]{:S(2)}, u32[]{:S(2)}) collective-permute-start(bf16[2,6,32,512]{3,2,1,0:T(8,128)(2,1)} %bitcast.34), channel_id=1, source_target_pairs={{0,14},{2,0},{4,2},{6,4},{8,6},{10,8},{12,10},{14,12},{1,15},{3,1}... | collective-permute-start | bytes 1179656 | tf_op jit(solution)/shard_map/ppermute | solution.py:152
  193.5 1.0 copy-start.2
  195.0 69.1 %collective-permute-start.13 = (bf16[2,6,32,512]{3,2,1,0:T(8,128)(2,1)S(1)}, bf16[2,6,32,512]{3,2,1,0:T(8,128)(2,1)S(1)}, u32[]{:S(2)}, u32[]{:S(2)}) collective-permute-start(bf16[2,6,32,512]{3,2,1,0:T(8,128)(2,1)S(1)} %bitcast.93), channel_id=1, source_target_pairs={{0,12},{2,14},{4,0},{6,2},{8,4},{10,6},{12,8},{14,10},{1,13},{3,15... | collective-permute-start | bytes 1179656 | tf_op jit(solution)/shard_map/ppermute | solution.py:152
  198.4 65.8 %collective-permute-start.14 = (bf16[2,6,32,512]{3,2,1,0:T(8,128)(2,1)S(1)}, bf16[2,6,32,512]{3,2,1,0:T(8,128)(2,1)S(1)}, u32[]{:S(2)}, u32[]{:S(2)}) collective-permute-start(bf16[2,6,32,512]{3,2,1,0:T(8,128)(2,1)S(1)} %bitcast.92), channel_id=1, source_target_pairs={{0,4},{2,6},{4,8},{6,10},{8,12},{10,14},{12,0},{14,2},{1,5},{3,7},... | collective-permute-start | bytes 1179656 | tf_op jit(solution)/shard_map/ppermute | solution.py:152
  198.6 65.4 %collective-permute-start.12 = (bf16[2,6,32,512]{3,2,1,0:T(8,128)(2,1)S(1)}, bf16[2,6,32,512]{3,2,1,0:T(8,128)(2,1)S(1)}, u32[]{:S(2)}, u32[]{:S(2)}) collective-permute-start(bf16[2,6,32,512]{3,2,1,0:T(8,128)(2,1)S(1)} %bitcast.94), channel_id=1, source_target_pairs={{0,10},{2,12},{4,14},{6,0},{8,2},{10,4},{12,6},{14,8},{1,11},{3,13... | collective-permute-start | bytes 1179656 | tf_op jit(solution)/shard_map/ppermute | solution.py:152
  208.1 55.6 %collective-permute-start.10 = (bf16[2,6,32,512]{3,2,1,0:T(8,128)(2,1)S(1)}, bf16[2,6,32,512]{3,2,1,0:T(8,128)(2,1)S(1)}, u32[]{:S(2)}, u32[]{:S(2)}) collective-permute-start(bf16[2,6,32,512]{3,2,1,0:T(8,128)(2,1)S(1)} %bitcast.96), channel_id=1, source_target_pairs={{0,6},{2,8},{4,10},{6,12},{8,14},{10,0},{12,2},{14,4},{1,7},{3,9},... | collective-permute-start | bytes 1179656 | tf_op jit(solution)/shard_map/ppermute | solution.py:152
  219.2 44.6 %collective-permute-start.11 = (bf16[2,6,32,512]{3,2,1,0:T(8,128)(2,1)S(1)}, bf16[2,6,32,512]{3,2,1,0:T(8,128)(2,1)S(1)}, u32[]{:S(2)}, u32[]{:S(2)}) collective-permute-start(bf16[2,6,32,512]{3,2,1,0:T(8,128)(2,1)S(1)} %bitcast.95), channel_id=1, source_target_pairs={{0,2},{2,4},{4,6},{6,8},{8,10},{10,12},{12,14},{14,0},{1,3},{3,5},... | collective-permute-start | bytes 1179656 | tf_op jit(solution)/shard_map/ppermute | solution.py:152
  264.2 2.7 copy-start
Sparse Core Ops, SparseCore 0:
  9.5 53.2 all-gather.1

commit v19 on v17

--- a/solution.py
+++ b/solution.py
@@ -60,7 +60,7 @@
     )(rows, cols, side, pt, stiffness)
 
 
-def _dft_kernel(w_ref, x_ref, o_ref):
+def _dft_kernel(w_ref, x_ref, own_ref, far_ref):
     x = x_ref[...]
     xh = x.astype(jnp.bfloat16)
     xl = (x - xh.astype(jnp.float32)).astype(jnp.bfloat16)
@@ -70,10 +70,12 @@
     acc = jnp.dot(wh, xh, preferred_element_type=jnp.float32)
     acc += jnp.dot(wh, xl, preferred_element_type=jnp.float32)
     acc += jnp.dot(wl, xh, preferred_element_type=jnp.float32)
-    o_ref[...] = acc
+    k = own_ref.shape[0]
+    own_ref[...] = acc[:k]
+    far_ref[...] = acc[k:].astype(far_ref.dtype)
 
 
-def _dft(weights, x):
+def _dft(weights, x, own):
     rows, k = weights.shape
     n = x.shape[1]
     tn = 2048 if n % 2048 == 0 else n
@@ -84,8 +86,14 @@
             pl.BlockSpec((rows, k), lambda i: (0, 0)),
             pl.BlockSpec((k, tn), lambda i: (0, i)),
         ],
-        out_specs=pl.BlockSpec((rows, tn), lambda i: (0, i)),
-        out_shape=jax.ShapeDtypeStruct((rows, n), jnp.float32),
+        out_specs=[
+            pl.BlockSpec((own, tn), lambda i: (0, i)),
+            pl.BlockSpec((rows - own, tn), lambda i: (0, i)),
+        ],
+        out_shape=[
+            jax.ShapeDtypeStruct((own, n), jnp.float32),
+            jax.ShapeDtypeStruct((rows - own, n), jnp.bfloat16),
+        ],
         compiler_params=pltpu.CompilerParams(dimension_semantics=("arbitrary",)),
     )(weights, x)
 
@@ -130,16 +138,17 @@
     harm = (nbl * dst[:, None] + jnp.arange(nbl, dtype=jnp.int32)[None, :]).reshape(-1)
     cosine, sine = _trig(harm[:, None], blade[None, :], count)
     weights = jnp.stack([cosine.reshape(nbd, nbl, -1), sine.reshape(nbd, nbl, -1)], axis=1)
-    spec = _dft(weights.reshape(2 * count, count), stacked)
-    spec = spec.reshape(nbd, 2, nbl, r, modes)
+    own, far = _dft(weights.reshape(2 * count, count), stacked, 2 * nbl)
+    far = far.reshape(nbd - 1, 2, nbl, r, modes)
 
     out = jnp.zeros((2, nbl, rows_half, modes), jnp.float32)
     for t in range(nbd):
-        piece = spec[t]
         if t:
-            piece = piece.astype(jnp.bfloat16)
+            piece = far[t - 1]
             piece = lax.ppermute(piece, "blade", [(j, (j + t) % nbd) for j in range(nbd)])
             piece = piece.astype(jnp.float32)
+        else:
+            piece = own.reshape(2, nbl, r, modes)
         at = ((me - t) % nbd) * r
         out = lax.dynamic_update_slice(out, piece, (0, 0, at, 0))
     return out

time: 275 us -> 272 us (0.989)
  other arithmetic: 11.2 us -> 8.06 us
    another operation x1 -> x0, other arithmetic: 3.13 us -> none
    unnamed x30 -> x28, local copies, waits for them, and re-layouts: 14 us -> 13.1 us
  transfers between devices with their start and end apart: 16 -> 16, of which waited for: 9 -> 8; matrix products, arithmetic and copies ran while one was open for 5% -> 5% of each run, Pallas kernels for 0% -> 0%
where the time goes in v19:
time: 272 us; the launch traced here: 271 us
  waiting for transfers between devices  155 us (57%)
  starting transfers between devices  37.4 us (14%)
  Pallas kernels  32.9 us (12%)
  local copies, waits for them, and re-layouts  24.2 us (9%)
  between operations  13.9 us (5%)
  other arithmetic  8.06 us (3%)
    ppermute x7, waiting for transfers between devices, body(): lax.ppermute(piece, 'blade', [(j, (j + t) % nbd) for j in range(nbd)])  59.4 us
    all_gather x1, waiting for transfers between devices, body(): pt = lax.all_gather(mine, ('blade', 'dof'), axis=0, tiled=True)  51.8 us
    ppermute x7, waiting for transfers between devices, body(): lax.ppermute(piece, 'blade', [(j, (j + s) % nbd) for j in range(nbd)])  38.2 us
    ppermute x7, starting transfers between devices, body(): lax.ppermute(piece, 'blade', [(j, (j + s) % nbd) for j in range(nbd)])  30.2 us
    pallas_call x1, Pallas kernels, _project(): pl.pallas_call(_project_kernel, grid_spec=grid_spec, out_shape=[jax.Shape...  25.2 us
    unnamed x28, local copies, waits for them, and re-layouts  13.1 us
    pallas_call x1, Pallas kernels, _dft(): pl.pallas_call(_dft_kernel, grid=(n // tn,), in_specs=[pl.BlockSpec((rows...  7.73 us
    ppermute x7, starting transfers between devices, body(): lax.ppermute(piece, 'blade', [(j, (j + t) % nbd) for j in range(nbd)])  6.88 us
  transfers between devices with their start and end apart: 16, of which 8 were waited for; matrix products, arithmetic and copies ran while one was open for 5% of the time, Pallas kernels for 0%

profile of v19, /device:TPU:0, one launch (start us, length us, event | category | flops | bytes accessed | tf_op | source)
XLA Modules:
  0.0 271.1 jit_solution(2644871552818932760)
XLA Ops:
  6.5 1.8 copy.6
  8.3 0.0 all-gather.2.cloned.1.call-update
  8.4 1.3 reshape.160.rows_ref
  9.7 1.3 reshape.161.cols_ref
  11.0 51.8 %all-gather.2.cloned.1.call-done.pt_ref = bf16[32,512,128]{2,1,0:T(8,128)(2,1)} async-done(((bf16[2,512,128]{2,1,0:T(8,128)(2,1)}), bf16[32,512,128]{2,1,0:T(8,128)(2,1)}) %all-gather.2.cloned.1.call-update) | async-done | bytes 4194320 | tf_op jit(solution)/shard_map/all_gather | solution.py:111
  62.8 25.2 %shard_map.46 = (f32[6,256,512]{2,1,0:T(8,128)}, f32[6,256,512]{2,1,0:T(8,128)}) custom-call(s32[192]{0:T(256)} %reshape.160.rows_ref, s32[192]{0:T(256)} %reshape.161.cols_ref, s32[1]{0:T(128)} %bitcast.side_ref, bf16[32,512,128]{2,1,0:T(8,128)(2,1)} %all-gather.2.cloned.1.call-done.pt_ref, bf16[6,32,128,128]{3,2,1,0:T(8,128)(2,1)} %s_ref.1), custom_call_target="tpu_custom_call" | custom-call | tf_op jit(solution)/shard_map/pallas_call | solution.py:52
  88.0 0.3 collective-permute-start
  88.2 0.1 iota_add_fusion
  88.3 0.1 add.222
  88.4 0.1 iota_add_fusion.1
  88.5 5.4 %collective-permute-done = f32[6,256,512]{2,1,0:T(8,128)S(1)} collective-permute-done((f32[6,256,512]{2,1,0:T(8,128)}, f32[6,256,512]{2,1,0:T(8,128)S(1)}, u32[]{:S(2)}, u32[]{:S(2)}) %collective-permute-start) | collective-permute-done | bytes 3145760 | tf_op jit(solution)/shard_map/ppermute | solution.py:117
  93.8 1.6 copy-done.1
  95.5 3.6 %add.225 = f32[6,256,512]{2,1,0:T(8,128)S(1)} add(f32[6,256,512]{2,1,0:T(8,128)} %get-tuple-element.9, f32[6,256,512]{2,1,0:T(8,128)} %copy-done.1) | non-fusion elementwise | flops 786432 | bytes 9437184 | tf_op jit(solution)/shard_map/add | solution.py:117
  99.1 1.5 dynamic-slice_bitcast_fusion
  100.5 0.6 collective-permute-start.1
  101.1 0.2 fusion.4
  101.3 1.5 collective-permute-start.2
  102.9 0.6 pad_maximum_fusion
  103.5 1.5 reshape.159.w_ref
  104.9 4.2 %collective-permute-start.7 = (f32[6,32,512]{2,1,0:T(8,128)S(1)}, f32[6,32,512]{2,1,0:T(8,128)S(1)}, u32[]{:S(2)}, u32[]{:S(2)}) collective-permute-start(f32[6,32,512]{2,1,0:T(8,128)S(1)} %get-tuple-element.13), channel_id=1, source_target_pairs={{0,14},{2,0},{4,2},{6,4},{8,6},{10,8},{12,10},{14,12},{1,15},{3,1}... | collective-permute-start | bytes 1179656 | tf_op jit(solution)/shard_map/ppermute | solution.py:130
  109.1 0.5 collective-permute-start.6
  109.7 6.0 %collective-permute-done.1 = f32[6,32,512]{2,1,0:T(8,128)} collective-permute-done((f32[6,32,512]{2,1,0:T(8,128)}, f32[6,32,512]{2,1,0:T(8,128)}, u32[]{:S(2)}, u32[]{:S(2)}) %collective-permute-start.1) | collective-permute-done | bytes 393248 | tf_op jit(solution)/shard_map/ppermute | solution.py:130
  115.6 1.0 bitcast_dynamic-update-slice_fusion.6
  116.7 0.0 collective-permute-done.2
  116.7 23.4 %collective-permute-start.4 = (f32[6,32,512]{2,1,0:T(8,128)}, f32[6,32,512]{2,1,0:T(8,128)S(1)}, u32[]{:S(2)}, u32[]{:S(2)}) collective-permute-start(f32[6,32,512]{2,1,0:T(8,128)} %get-tuple-element.16), channel_id=1, source_target_pairs={{0,8},{2,10},{4,12},{6,14},{8,0},{10,2},{12,4},{14,6},{1,9},{3,11}... | collective-permute-start | bytes 1179656 | tf_op jit(solution)/shard_map/ppermute | solution.py:130
  140.1 1.0 bitcast_dynamic-update-slice_fusion.5
  141.1 24.2 %collective-permute-done.3 = f32[6,32,512]{2,1,0:T(8,128)S(1)} collective-permute-done((f32[6,32,512]{2,1,0:T(8,128)}, f32[6,32,512]{2,1,0:T(8,128)S(1)}, u32[]{:S(2)}, u32[]{:S(2)}) %collective-permute-start.3) | collective-permute-done | bytes 393248 | tf_op jit(solution)/shard_map/ppermute | solution.py:130
  165.4 7.9 %collective-permute-done.4 = f32[6,32,512]{2,1,0:T(8,128)S(1)} collective-permute-done((f32[6,32,512]{2,1,0:T(8,128)}, f32[6,32,512]{2,1,0:T(8,128)S(1)}, u32[]{:S(2)}, u32[]{:S(2)}) %collective-permute-start.4) | collective-permute-done | bytes 393248 | tf_op jit(solution)/shard_map/ppermute | solution.py:130
  173.4 0.0 collective-permute-done.6
  173.5 3.5 %copy.7 = f32[6,8,32,512]{3,1,2,0:T(8,128)} copy(f32[6,8,32,512]{3,2,1,0:T(8,128)S(1)} %bitcast.73) | data formatting | bytes 6291456
  177.0 7.7 %shard_map.47 = (f32[12,16384]{1,0:T(8,128)}, bf16[84,16384]{1,0:T(8,128)(2,1)}) custom-call(f32[96,48]{1,0:T(8,128)} %reshape.159.w_ref, f32[48,16384]{1,0:T(8,128)} %bitcast.70), custom_call_target="tpu_custom_call" | custom-call | tf_op jit(solution)/shard_map/pallas_call | solution.py:82
  184.7 2.6 fusion.10
  187.4 0.2 copy.9
  187.6 1.0 collective-permute-start.8
  188.5 0.2 copy.10
  188.7 0.1 collective-permute-start.9
  188.9 1.8 copy.8
  190.8 0.1 slice.35
  190.8 0.2 copy.15
  191.0 0.2 copy.14
  191.2 3.7 %collective-permute-start.13 = (bf16[2,6,32,512]{3,2,1,0:T(8,128)(2,1)S(1)}, bf16[2,6,32,512]{3,2,1,0:T(8,128)(2,1)S(1)}, u32[]{:S(2)}, u32[]{:S(2)}) collective-permute-start(bf16[2,6,32,512]{3,2,1,0:T(8,128)(2,1)S(1)} %bitcast.94), channel_id=1, source_target_pairs={{0,12},{2,14},{4,0},{6,2},{8,4},{10,6},{12,8},{14,10},{1,13},{3,15... | collective-permute-start | bytes 1179656 | tf_op jit(solution)/shard_map/ppermute | solution.py:148
  194.9 2.0 collective-permute-start.14
  197.0 0.2 copy.13
  197.1 0.1 collective-permute-start.12
  197.2 0.2 copy.12
  197.4 0.2 copy.11
  197.6 0.8 broadcast_in_dim.2
  198.4 0.1 constant_dynamic-update-slice_fusion
  198.5 4.1 %collective-permute-done.8 = bf16[2,6,32,512]{3,2,1,0:T(8,128)(2,1)} collective-permute-done((bf16[2,6,32,512]{3,2,1,0:T(8,128)(2,1)S(1)}, bf16[2,6,32,512]{3,2,1,0:T(8,128)(2,1)}, u32[]{:S(2)}, u32[]{:S(2)}) %collective-permute-start.8) | collective-permute-done | bytes 393248 | tf_op jit(solution)/shard_map/ppermute | solution.py:148
  202.6 0.0 collective-permute-start.10
  202.6 1.1 convert_dynamic-update-slice_fusion.6
  203.7 0.1 collective-permute-start.11
  203.8 1.1 convert_dynamic-update-slice_fusion.5
  204.9 47.2 %collective-permute-done.10 = bf16[2,6,32,512]{3,2,1,0:T(8,128)(2,1)S(1)} collective-permute-done((bf16[2,6,32,512]{3,2,1,0:T(8,128)(2,1)S(1)}, bf16[2,6,32,512]{3,2,1,0:T(8,128)(2,1)S(1)}, u32[]{:S(2)}, u32[]{:S(2)}) %collective-permute-start.10) | collective-permute-done | bytes 393248 | tf_op jit(solution)/shard_map/ppermute | solution.py:148
  252.0 0.1 convert_dynamic-update-slice_fusion.4
  252.1 8.1 %collective-permute-done.11 = bf16[2,6,32,512]{3,2,1,0:T(8,128)(2,1)S(1)} collective-permute-done((bf16[2,6,32,512]{3,2,1,0:T(8,128)(2,1)S(1)}, bf16[2,6,32,512]{3,2,1,0:T(8,128)(2,1)S(1)}, u32[]{:S(2)}, u32[]{:S(2)}) %collective-permute-start.11) | collective-permute-done | bytes 393248 | tf_op jit(solution)/shard_map/ppermute | solution.py:148
  260.2 0.1 convert_dynamic-update-slice_fusion.3
  260.3 0.0 collective-permute-done.12
  260.3 0.1 convert_dynamic-update-slice_fusion.2
  260.4 0.0 collective-permute-done.13
  260.4 0.1 convert_dynamic-update-slice_fusion.1
  260.5 0.0 copy-start
  260.6 2.7 copy-done
  263.2 1.0 convert_dynamic-update-slice_fusion
  (22 shorter events, 0.4 us)
Async XLA Ops:
  6.5 56.3 %all-gather.2.cloned.1.call-start = ((), (), s32[]{:S(2)}) async-start(), calls=%async_computation | async-start | bytes 4456448 | tf_op jit(solution)/shard_map/all_gather | solution.py:111
  88.0 5.9 %collective-permute-start = (f32[6,256,512]{2,1,0:T(8,128)}, f32[6,256,512]{2,1,0:T(8,128)S(1)}, u32[]{:S(2)}, u32[]{:S(2)}) collective-permute-start(f32[6,256,512]{2,1,0:T(8,128)} %get-tuple-element.10), channel_id=1, source_target_pairs={{0,1},{1,0},{2,3},{3,2},{4,5},{5,4},{6,7},{7,6},{8,9},{9,8},{10,11... | collective-permute-start | bytes 9437192 | tf_op jit(solution)/shard_map/ppermute | solution.py:117
  93.8 1.6 copy-start.1
  100.5 15.1 %collective-permute-start.1 = (f32[6,32,512]{2,1,0:T(8,128)}, f32[6,32,512]{2,1,0:T(8,128)}, u32[]{:S(2)}, u32[]{:S(2)}) collective-permute-start(f32[6,32,512]{2,1,0:T(8,128)} %get-tuple-element.19), channel_id=1, source_target_pairs={{0,2},{2,4},{4,6},{6,8},{8,10},{10,12},{12,14},{14,0},{1,3},{3,5},... | collective-permute-start | bytes 1179656 | tf_op jit(solution)/shard_map/ppermute | solution.py:130
  101.3 15.4 %collective-permute-start.2 = (f32[6,32,512]{2,1,0:T(8,128)}, f32[6,32,512]{2,1,0:T(8,128)}, u32[]{:S(2)}, u32[]{:S(2)}) collective-permute-start(f32[6,32,512]{2,1,0:T(8,128)} %get-tuple-element.18), channel_id=1, source_target_pairs={{0,4},{2,6},{4,8},{6,10},{8,12},{10,14},{12,0},{14,2},{1,5},{3,7},... | collective-permute-start | bytes 1179656 | tf_op jit(solution)/shard_map/ppermute | solution.py:130
  104.9 68.5 %collective-permute-start.7 = (f32[6,32,512]{2,1,0:T(8,128)S(1)}, f32[6,32,512]{2,1,0:T(8,128)S(1)}, u32[]{:S(2)}, u32[]{:S(2)}) collective-permute-start(f32[6,32,512]{2,1,0:T(8,128)S(1)} %get-tuple-element.13), channel_id=1, source_target_pairs={{0,14},{2,0},{4,2},{6,4},{8,6},{10,8},{12,10},{14,12},{1,15},{3,1}... | collective-permute-start | bytes 1179656 | tf_op jit(solution)/shard_map/ppermute | solution.py:130
  109.1 64.3 %collective-permute-start.6 = (f32[6,32,512]{2,1,0:T(8,128)}, f32[6,32,512]{2,1,0:T(8,128)S(1)}, u32[]{:S(2)}, u32[]{:S(2)}) collective-permute-start(f32[6,32,512]{2,1,0:T(8,128)} %get-tuple-element.14), channel_id=1, source_target_pairs={{0,12},{2,14},{4,0},{6,2},{8,4},{10,6},{12,8},{14,10},{1,13},{3,15... | collective-permute-start | bytes 1179656 | tf_op jit(solution)/shard_map/ppermute | solution.py:130
  109.6 63.7 %collective-permute-start.5 = (f32[6,32,512]{2,1,0:T(8,128)}, f32[6,32,512]{2,1,0:T(8,128)S(1)}, u32[]{:S(2)}, u32[]{:S(2)}) collective-permute-start(f32[6,32,512]{2,1,0:T(8,128)} %get-tuple-element.15), channel_id=1, source_target_pairs={{0,10},{2,12},{4,14},{6,0},{8,2},{10,4},{12,6},{14,8},{1,11},{3,13... | collective-permute-start | bytes 1179656 | tf_op jit(solution)/shard_map/ppermute | solution.py:130
  115.6 49.7 %collective-permute-start.3 = (f32[6,32,512]{2,1,0:T(8,128)}, f32[6,32,512]{2,1,0:T(8,128)S(1)}, u32[]{:S(2)}, u32[]{:S(2)}) collective-permute-start(f32[6,32,512]{2,1,0:T(8,128)} %get-tuple-element.17), channel_id=1, source_target_pairs={{0,6},{2,8},{4,10},{6,12},{8,14},{10,0},{12,2},{14,4},{1,7},{3,9},... | collective-permute-start | bytes 1179656 | tf_op jit(solution)/shard_map/ppermute | solution.py:130
  116.7 56.7 %collective-permute-start.4 = (f32[6,32,512]{2,1,0:T(8,128)}, f32[6,32,512]{2,1,0:T(8,128)S(1)}, u32[]{:S(2)}, u32[]{:S(2)}) collective-permute-start(f32[6,32,512]{2,1,0:T(8,128)} %get-tuple-element.16), channel_id=1, source_target_pairs={{0,8},{2,10},{4,12},{6,14},{8,0},{10,2},{12,4},{14,6},{1,9},{3,11}... | collective-permute-start | bytes 1179656 | tf_op jit(solution)/shard_map/ppermute | solution.py:130
  187.6 15.1 %collective-permute-start.8 = (bf16[2,6,32,512]{3,2,1,0:T(8,128)(2,1)S(1)}, bf16[2,6,32,512]{3,2,1,0:T(8,128)(2,1)}, u32[]{:S(2)}, u32[]{:S(2)}) collective-permute-start(bf16[2,6,32,512]{3,2,1,0:T(8,128)(2,1)S(1)} %bitcast.91), channel_id=1, source_target_pairs={{0,2},{2,4},{4,6},{6,8},{8,10},{10,12},{12,14},{14,0},{1,3},{3,5},... | collective-permute-start | bytes 1179656 | tf_op jit(solution)/shard_map/ppermute | solution.py:148
  188.7 15.0 %collective-permute-start.9 = (bf16[2,6,32,512]{3,2,1,0:T(8,128)(2,1)S(1)}, bf16[2,6,32,512]{3,2,1,0:T(8,128)(2,1)}, u32[]{:S(2)}, u32[]{:S(2)}) collective-permute-start(bf16[2,6,32,512]{3,2,1,0:T(8,128)(2,1)S(1)} %bitcast.92), channel_id=1, source_target_pairs={{0,4},{2,6},{4,8},{6,10},{8,12},{10,14},{12,0},{14,2},{1,5},{3,7},... | collective-permute-start | bytes 1179656 | tf_op jit(solution)/shard_map/ppermute | solution.py:148
  191.2 69.2 %collective-permute-start.13 = (bf16[2,6,32,512]{3,2,1,0:T(8,128)(2,1)S(1)}, bf16[2,6,32,512]{3,2,1,0:T(8,128)(2,1)S(1)}, u32[]{:S(2)}, u32[]{:S(2)}) collective-permute-start(bf16[2,6,32,512]{3,2,1,0:T(8,128)(2,1)S(1)} %bitcast.94), channel_id=1, source_target_pairs={{0,12},{2,14},{4,0},{6,2},{8,4},{10,6},{12,8},{14,10},{1,13},{3,15... | collective-permute-start | bytes 1179656 | tf_op jit(solution)/shard_map/ppermute | solution.py:148
  194.9 65.6 %collective-permute-start.14 = (bf16[2,6,32,512]{3,2,1,0:T(8,128)(2,1)S(1)}, bf16[2,6,32,512]{3,2,1,0:T(8,128)(2,1)S(1)}, u32[]{:S(2)}, u32[]{:S(2)}) collective-permute-start(bf16[2,6,32,512]{3,2,1,0:T(8,128)(2,1)S(1)} %bitcast.93), channel_id=1, source_target_pairs={{0,14},{2,0},{4,2},{6,4},{8,6},{10,8},{12,10},{14,12},{1,15},{3,1}... | collective-permute-start | bytes 1179656 | tf_op jit(solution)/shard_map/ppermute | solution.py:148
  197.1 63.2 %collective-permute-start.12 = (bf16[2,6,32,512]{3,2,1,0:T(8,128)(2,1)S(1)}, bf16[2,6,32,512]{3,2,1,0:T(8,128)(2,1)S(1)}, u32[]{:S(2)}, u32[]{:S(2)}) collective-permute-start(bf16[2,6,32,512]{3,2,1,0:T(8,128)(2,1)S(1)} %bitcast.95), channel_id=1, source_target_pairs={{0,10},{2,12},{4,14},{6,0},{8,2},{10,4},{12,6},{14,8},{1,11},{3,13... | collective-permute-start | bytes 1179656 | tf_op jit(solution)/shard_map/ppermute | solution.py:148
  202.6 49.4 %collective-permute-start.10 = (bf16[2,6,32,512]{3,2,1,0:T(8,128)(2,1)S(1)}, bf16[2,6,32,512]{3,2,1,0:T(8,128)(2,1)S(1)}, u32[]{:S(2)}, u32[]{:S(2)}) collective-permute-start(bf16[2,6,32,512]{3,2,1,0:T(8,128)(2,1)S(1)} %bitcast.97), channel_id=1, source_target_pairs={{0,6},{2,8},{4,10},{6,12},{8,14},{10,0},{12,2},{14,4},{1,7},{3,9},... | collective-permute-start | bytes 1179656 | tf_op jit(solution)/shard_map/ppermute | solution.py:148
  203.7 56.5 %collective-permute-start.11 = (bf16[2,6,32,512]{3,2,1,0:T(8,128)(2,1)S(1)}, bf16[2,6,32,512]{3,2,1,0:T(8,128)(2,1)S(1)}, u32[]{:S(2)}, u32[]{:S(2)}) collective-permute-start(bf16[2,6,32,512]{3,2,1,0:T(8,128)(2,1)S(1)} %bitcast.96), channel_id=1, source_target_pairs={{0,8},{2,10},{4,12},{6,14},{8,0},{10,2},{12,4},{14,6},{1,9},{3,11}... | collective-permute-start | bytes 1179656 | tf_op jit(solution)/shard_map/ppermute | solution.py:148
  260.5 2.7 copy-start
Sparse Core Ops, SparseCore 0:
  9.5 53.2 all-gather.1

commit v20 on v19

--- a/solution.py
+++ b/solution.py
@@ -78,7 +78,7 @@
 def _dft(weights, x, own):
     rows, k = weights.shape
     n = x.shape[1]
-    tn = 2048 if n % 2048 == 0 else n
+    tn = 4096 if n % 4096 == 0 else n
     return pl.pallas_call(
         _dft_kernel,
         grid=(n // tn,),

time: 272 us -> 270 us (level)
  no operation moved by 1% of the time
where the time goes in v20:
time: 270 us; the launch traced here: 269 us
  waiting for transfers between devices  155 us (57%)
  starting transfers between devices  37.4 us (14%)
  Pallas kernels  31.1 us (12%)
  local copies, waits for them, and re-layouts  24.1 us (9%)
  between operations  13.9 us (5%)
  other arithmetic  8.06 us (3%)
    ppermute x7, waiting for transfers between devices, body(): lax.ppermute(piece, 'blade', [(j, (j + t) % nbd) for j in range(nbd)])  59.4 us
    all_gather x1, waiting for transfers between devices, body(): pt = lax.all_gather(mine, ('blade', 'dof'), axis=0, tiled=True)  51.8 us
    ppermute x7, waiting for transfers between devices, body(): lax.ppermute(piece, 'blade', [(j, (j + s) % nbd) for j in range(nbd)])  38.2 us
    ppermute x7, starting transfers between devices, body(): lax.ppermute(piece, 'blade', [(j, (j + s) % nbd) for j in range(nbd)])  30.2 us
    pallas_call x1, Pallas kernels, _project(): pl.pallas_call(_project_kernel, grid_spec=grid_spec, out_shape=[jax.Shape...  25.2 us
    unnamed x28, local copies, waits for them, and re-layouts  13.1 us
    ppermute x7, starting transfers between devices, body(): lax.ppermute(piece, 'blade', [(j, (j + t) % nbd) for j in range(nbd)])  6.88 us
    pallas_call x1, Pallas kernels, _dft(): pl.pallas_call(_dft_kernel, grid=(n // tn,), in_specs=[pl.BlockSpec((rows...  5.91 us
  transfers between devices with their start and end apart: 16, of which 8 were waited for; matrix products, arithmetic and copies ran while one was open for 5% of the time, Pallas kernels for 0%

profile of v20, /device:TPU:0, one launch (start us, length us, event | category | flops | bytes accessed | tf_op | source)
XLA Modules:
  0.0 269.2 jit_solution(4998188470844078159)
XLA Ops:
  6.5 1.8 copy.6
  8.3 0.0 all-gather.2.cloned.1.call-update
  8.4 1.3 reshape.160.rows_ref
  9.7 1.3 reshape.161.cols_ref
  11.0 51.8 %all-gather.2.cloned.1.call-done.pt_ref = bf16[32,512,128]{2,1,0:T(8,128)(2,1)} async-done(((bf16[2,512,128]{2,1,0:T(8,128)(2,1)}), bf16[32,512,128]{2,1,0:T(8,128)(2,1)}) %all-gather.2.cloned.1.call-update) | async-done | bytes 4194320 | tf_op jit(solution)/shard_map/all_gather | solution.py:111
  62.8 25.2 %shard_map.46 = (f32[6,256,512]{2,1,0:T(8,128)}, f32[6,256,512]{2,1,0:T(8,128)}) custom-call(s32[192]{0:T(256)} %reshape.160.rows_ref, s32[192]{0:T(256)} %reshape.161.cols_ref, s32[1]{0:T(128)} %bitcast.side_ref, bf16[32,512,128]{2,1,0:T(8,128)(2,1)} %all-gather.2.cloned.1.call-done.pt_ref, bf16[6,32,128,128]{3,2,1,0:T(8,128)(2,1)} %s_ref.1), custom_call_target="tpu_custom_call" | custom-call | tf_op jit(solution)/shard_map/pallas_call | solution.py:52
  88.0 0.3 collective-permute-start
  88.2 0.1 iota_add_fusion
  88.3 0.1 add.222
  88.4 0.1 iota_add_fusion.1
  88.5 5.4 %collective-permute-done = f32[6,256,512]{2,1,0:T(8,128)S(1)} collective-permute-done((f32[6,256,512]{2,1,0:T(8,128)}, f32[6,256,512]{2,1,0:T(8,128)S(1)}, u32[]{:S(2)}, u32[]{:S(2)}) %collective-permute-start) | collective-permute-done | bytes 3145760 | tf_op jit(solution)/shard_map/ppermute | solution.py:117
  93.8 1.6 copy-done.1
  95.5 3.6 %add.225 = f32[6,256,512]{2,1,0:T(8,128)S(1)} add(f32[6,256,512]{2,1,0:T(8,128)} %get-tuple-element.9, f32[6,256,512]{2,1,0:T(8,128)} %copy-done.1) | non-fusion elementwise | flops 786432 | bytes 9437184 | tf_op jit(solution)/shard_map/add | solution.py:117
  99.1 1.5 dynamic-slice_bitcast_fusion
  100.5 0.6 collective-permute-start.1
  101.1 0.2 fusion.4
  101.3 1.5 collective-permute-start.2
  102.9 0.6 pad_maximum_fusion
  103.5 1.5 reshape.159.w_ref
  104.9 4.2 %collective-permute-start.7 = (f32[6,32,512]{2,1,0:T(8,128)S(1)}, f32[6,32,512]{2,1,0:T(8,128)S(1)}, u32[]{:S(2)}, u32[]{:S(2)}) collective-permute-start(f32[6,32,512]{2,1,0:T(8,128)S(1)} %get-tuple-element.13), channel_id=1, source_target_pairs={{0,14},{2,0},{4,2},{6,4},{8,6},{10,8},{12,10},{14,12},{1,15},{3,1}... | collective-permute-start | bytes 1179656 | tf_op jit(solution)/shard_map/ppermute | solution.py:130
  109.1 0.5 collective-permute-start.6
  109.6 0.0 collective-permute-start.5
  109.7 6.0 %collective-permute-done.1 = f32[6,32,512]{2,1,0:T(8,128)} collective-permute-done((f32[6,32,512]{2,1,0:T(8,128)}, f32[6,32,512]{2,1,0:T(8,128)}, u32[]{:S(2)}, u32[]{:S(2)}) %collective-permute-start.1) | collective-permute-done | bytes 393248 | tf_op jit(solution)/shard_map/ppermute | solution.py:130
  115.6 0.0 collective-permute-start.3
  115.6 1.0 bitcast_dynamic-update-slice_fusion.6
  116.7 23.4 %collective-permute-start.4 = (f32[6,32,512]{2,1,0:T(8,128)}, f32[6,32,512]{2,1,0:T(8,128)S(1)}, u32[]{:S(2)}, u32[]{:S(2)}) collective-permute-start(f32[6,32,512]{2,1,0:T(8,128)} %get-tuple-element.16), channel_id=1, source_target_pairs={{0,8},{2,10},{4,12},{6,14},{8,0},{10,2},{12,4},{14,6},{1,9},{3,11}... | collective-permute-start | bytes 1179656 | tf_op jit(solution)/shard_map/ppermute | solution.py:130
  140.1 1.0 bitcast_dynamic-update-slice_fusion.5
  141.1 24.2 %collective-permute-done.3 = f32[6,32,512]{2,1,0:T(8,128)S(1)} collective-permute-done((f32[6,32,512]{2,1,0:T(8,128)}, f32[6,32,512]{2,1,0:T(8,128)S(1)}, u32[]{:S(2)}, u32[]{:S(2)}) %collective-permute-start.3) | collective-permute-done | bytes 393248 | tf_op jit(solution)/shard_map/ppermute | solution.py:130
  165.4 7.9 %collective-permute-done.4 = f32[6,32,512]{2,1,0:T(8,128)S(1)} collective-permute-done((f32[6,32,512]{2,1,0:T(8,128)}, f32[6,32,512]{2,1,0:T(8,128)S(1)}, u32[]{:S(2)}, u32[]{:S(2)}) %collective-permute-start.4) | collective-permute-done | bytes 393248 | tf_op jit(solution)/shard_map/ppermute | solution.py:130
  173.4 0.0 collective-permute-done.5
  173.5 0.0 collective-permute-done.7
  173.5 3.5 %copy.7 = f32[6,8,32,512]{3,1,2,0:T(8,128)} copy(f32[6,8,32,512]{3,2,1,0:T(8,128)S(1)} %bitcast.73) | data formatting | bytes 6291456
  177.0 5.9 %shard_map.47 = (f32[12,16384]{1,0:T(8,128)}, bf16[84,16384]{1,0:T(8,128)(2,1)}) custom-call(f32[96,48]{1,0:T(8,128)} %reshape.159.w_ref, f32[48,16384]{1,0:T(8,128)} %bitcast.70), custom_call_target="tpu_custom_call" | custom-call | tf_op jit(solution)/shard_map/pallas_call | solution.py:82
  182.9 2.6 fusion.10
  185.5 0.2 copy.9
  185.7 1.0 collective-permute-start.8
  186.7 0.2 copy.10
  186.9 0.1 collective-permute-start.9
  187.1 1.8 copy.8
  189.0 0.1 slice.35
  189.0 0.2 copy.15
  189.2 0.2 copy.14
  189.4 3.7 %collective-permute-start.13 = (bf16[2,6,32,512]{3,2,1,0:T(8,128)(2,1)S(1)}, bf16[2,6,32,512]{3,2,1,0:T(8,128)(2,1)S(1)}, u32[]{:S(2)}, u32[]{:S(2)}) collective-permute-start(bf16[2,6,32,512]{3,2,1,0:T(8,128)(2,1)S(1)} %bitcast.94), channel_id=1, source_target_pairs={{0,12},{2,14},{4,0},{6,2},{8,4},{10,6},{12,8},{14,10},{1,13},{3,15... | collective-permute-start | bytes 1179656 | tf_op jit(solution)/shard_map/ppermute | solution.py:148
  193.1 2.0 collective-permute-start.14
  195.1 0.2 copy.13
  195.3 0.1 collective-permute-start.12
  195.4 0.2 copy.12
  195.6 0.2 copy.11
  195.8 0.8 broadcast_in_dim.2
  196.6 0.1 constant_dynamic-update-slice_fusion
  196.7 4.1 %collective-permute-done.8 = bf16[2,6,32,512]{3,2,1,0:T(8,128)(2,1)} collective-permute-done((bf16[2,6,32,512]{3,2,1,0:T(8,128)(2,1)S(1)}, bf16[2,6,32,512]{3,2,1,0:T(8,128)(2,1)}, u32[]{:S(2)}, u32[]{:S(2)}) %collective-permute-start.8) | collective-permute-done | bytes 393248 | tf_op jit(solution)/shard_map/ppermute | solution.py:148
  200.8 1.1 convert_dynamic-update-slice_fusion.6
  201.9 0.0 collective-permute-done.9
  201.9 0.1 collective-permute-start.11
  202.0 1.1 convert_dynamic-update-slice_fusion.5
  203.1 47.1 %collective-permute-done.10 = bf16[2,6,32,512]{3,2,1,0:T(8,128)(2,1)S(1)} collective-permute-done((bf16[2,6,32,512]{3,2,1,0:T(8,128)(2,1)S(1)}, bf16[2,6,32,512]{3,2,1,0:T(8,128)(2,1)S(1)}, u32[]{:S(2)}, u32[]{:S(2)}) %collective-permute-start.10) | collective-permute-done | bytes 393248 | tf_op jit(solution)/shard_map/ppermute | solution.py:148
  250.2 0.1 convert_dynamic-update-slice_fusion.4
  250.3 8.1 %collective-permute-done.11 = bf16[2,6,32,512]{3,2,1,0:T(8,128)(2,1)S(1)} collective-permute-done((bf16[2,6,32,512]{3,2,1,0:T(8,128)(2,1)S(1)}, bf16[2,6,32,512]{3,2,1,0:T(8,128)(2,1)S(1)}, u32[]{:S(2)}, u32[]{:S(2)}) %collective-permute-start.11) | collective-permute-done | bytes 393248 | tf_op jit(solution)/shard_map/ppermute | solution.py:148
  258.4 0.1 convert_dynamic-update-slice_fusion.3
  258.5 0.1 convert_dynamic-update-slice_fusion.2
  258.6 0.1 convert_dynamic-update-slice_fusion.1
  258.7 0.0 copy-start
  258.7 2.7 copy-done
  261.4 1.0 convert_dynamic-update-slice_fusion
  (22 shorter events, 0.4 us)
Async XLA Ops:
  6.5 56.3 %all-gather.2.cloned.1.call-start = ((), (), s32[]{:S(2)}) async-start(), calls=%async_computation | async-start | bytes 4456448 | tf_op jit(solution)/shard_map/all_gather | solution.py:111
  88.0 5.9 %collective-permute-start = (f32[6,256,512]{2,1,0:T(8,128)}, f32[6,256,512]{2,1,0:T(8,128)S(1)}, u32[]{:S(2)}, u32[]{:S(2)}) collective-permute-start(f32[6,256,512]{2,1,0:T(8,128)} %get-tuple-element.10), channel_id=1, source_target_pairs={{0,1},{1,0},{2,3},{3,2},{4,5},{5,4},{6,7},{7,6},{8,9},{9,8},{10,11... | collective-permute-start | bytes 9437192 | tf_op jit(solution)/shard_map/ppermute | solution.py:117
  93.8 1.6 copy-start.1
  100.5 15.1 %collective-permute-start.1 = (f32[6,32,512]{2,1,0:T(8,128)}, f32[6,32,512]{2,1,0:T(8,128)}, u32[]{:S(2)}, u32[]{:S(2)}) collective-permute-start(f32[6,32,512]{2,1,0:T(8,128)} %get-tuple-element.19), channel_id=1, source_target_pairs={{0,2},{2,4},{4,6},{6,8},{8,10},{10,12},{12,14},{14,0},{1,3},{3,5},... | collective-permute-start | bytes 1179656 | tf_op jit(solution)/shard_map/ppermute | solution.py:130
  101.3 15.4 %collective-permute-start.2 = (f32[6,32,512]{2,1,0:T(8,128)}, f32[6,32,512]{2,1,0:T(8,128)}, u32[]{:S(2)}, u32[]{:S(2)}) collective-permute-start(f32[6,32,512]{2,1,0:T(8,128)} %get-tuple-element.18), channel_id=1, source_target_pairs={{0,4},{2,6},{4,8},{6,10},{8,12},{10,14},{12,0},{14,2},{1,5},{3,7},... | collective-permute-start | bytes 1179656 | tf_op jit(solution)/shard_map/ppermute | solution.py:130
  104.9 68.5 %collective-permute-start.7 = (f32[6,32,512]{2,1,0:T(8,128)S(1)}, f32[6,32,512]{2,1,0:T(8,128)S(1)}, u32[]{:S(2)}, u32[]{:S(2)}) collective-permute-start(f32[6,32,512]{2,1,0:T(8,128)S(1)} %get-tuple-element.13), channel_id=1, source_target_pairs={{0,14},{2,0},{4,2},{6,4},{8,6},{10,8},{12,10},{14,12},{1,15},{3,1}... | collective-permute-start | bytes 1179656 | tf_op jit(solution)/shard_map/ppermute | solution.py:130
  109.1 64.3 %collective-permute-start.6 = (f32[6,32,512]{2,1,0:T(8,128)}, f32[6,32,512]{2,1,0:T(8,128)S(1)}, u32[]{:S(2)}, u32[]{:S(2)}) collective-permute-start(f32[6,32,512]{2,1,0:T(8,128)} %get-tuple-element.14), channel_id=1, source_target_pairs={{0,12},{2,14},{4,0},{6,2},{8,4},{10,6},{12,8},{14,10},{1,13},{3,15... | collective-permute-start | bytes 1179656 | tf_op jit(solution)/shard_map/ppermute | solution.py:130
  109.6 63.7 %collective-permute-start.5 = (f32[6,32,512]{2,1,0:T(8,128)}, f32[6,32,512]{2,1,0:T(8,128)S(1)}, u32[]{:S(2)}, u32[]{:S(2)}) collective-permute-start(f32[6,32,512]{2,1,0:T(8,128)} %get-tuple-element.15), channel_id=1, source_target_pairs={{0,10},{2,12},{4,14},{6,0},{8,2},{10,4},{12,6},{14,8},{1,11},{3,13... | collective-permute-start | bytes 1179656 | tf_op jit(solution)/shard_map/ppermute | solution.py:130
  115.6 49.7 %collective-permute-start.3 = (f32[6,32,512]{2,1,0:T(8,128)}, f32[6,32,512]{2,1,0:T(8,128)S(1)}, u32[]{:S(2)}, u32[]{:S(2)}) collective-permute-start(f32[6,32,512]{2,1,0:T(8,128)} %get-tuple-element.17), channel_id=1, source_target_pairs={{0,6},{2,8},{4,10},{6,12},{8,14},{10,0},{12,2},{14,4},{1,7},{3,9},... | collective-permute-start | bytes 1179656 | tf_op jit(solution)/shard_map/ppermute | solution.py:130
  116.7 56.7 %collective-permute-start.4 = (f32[6,32,512]{2,1,0:T(8,128)}, f32[6,32,512]{2,1,0:T(8,128)S(1)}, u32[]{:S(2)}, u32[]{:S(2)}) collective-permute-start(f32[6,32,512]{2,1,0:T(8,128)} %get-tuple-element.16), channel_id=1, source_target_pairs={{0,8},{2,10},{4,12},{6,14},{8,0},{10,2},{12,4},{14,6},{1,9},{3,11}... | collective-permute-start | bytes 1179656 | tf_op jit(solution)/shard_map/ppermute | solution.py:130
  185.7 15.1 %collective-permute-start.8 = (bf16[2,6,32,512]{3,2,1,0:T(8,128)(2,1)S(1)}, bf16[2,6,32,512]{3,2,1,0:T(8,128)(2,1)}, u32[]{:S(2)}, u32[]{:S(2)}) collective-permute-start(bf16[2,6,32,512]{3,2,1,0:T(8,128)(2,1)S(1)} %bitcast.91), channel_id=1, source_target_pairs={{0,2},{2,4},{4,6},{6,8},{8,10},{10,12},{12,14},{14,0},{1,3},{3,5},... | collective-permute-start | bytes 1179656 | tf_op jit(solution)/shard_map/ppermute | solution.py:148
  186.9 15.0 %collective-permute-start.9 = (bf16[2,6,32,512]{3,2,1,0:T(8,128)(2,1)S(1)}, bf16[2,6,32,512]{3,2,1,0:T(8,128)(2,1)}, u32[]{:S(2)}, u32[]{:S(2)}) collective-permute-start(bf16[2,6,32,512]{3,2,1,0:T(8,128)(2,1)S(1)} %bitcast.92), channel_id=1, source_target_pairs={{0,4},{2,6},{4,8},{6,10},{8,12},{10,14},{12,0},{14,2},{1,5},{3,7},... | collective-permute-start | bytes 1179656 | tf_op jit(solution)/shard_map/ppermute | solution.py:148
  189.4 69.2 %collective-permute-start.13 = (bf16[2,6,32,512]{3,2,1,0:T(8,128)(2,1)S(1)}, bf16[2,6,32,512]{3,2,1,0:T(8,128)(2,1)S(1)}, u32[]{:S(2)}, u32[]{:S(2)}) collective-permute-start(bf16[2,6,32,512]{3,2,1,0:T(8,128)(2,1)S(1)} %bitcast.94), channel_id=1, source_target_pairs={{0,12},{2,14},{4,0},{6,2},{8,4},{10,6},{12,8},{14,10},{1,13},{3,15... | collective-permute-start | bytes 1179656 | tf_op jit(solution)/shard_map/ppermute | solution.py:148
  193.1 65.6 %collective-permute-start.14 = (bf16[2,6,32,512]{3,2,1,0:T(8,128)(2,1)S(1)}, bf16[2,6,32,512]{3,2,1,0:T(8,128)(2,1)S(1)}, u32[]{:S(2)}, u32[]{:S(2)}) collective-permute-start(bf16[2,6,32,512]{3,2,1,0:T(8,128)(2,1)S(1)} %bitcast.93), channel_id=1, source_target_pairs={{0,14},{2,0},{4,2},{6,4},{8,6},{10,8},{12,10},{14,12},{1,15},{3,1}... | collective-permute-start | bytes 1179656 | tf_op jit(solution)/shard_map/ppermute | solution.py:148
  195.3 63.2 %collective-permute-start.12 = (bf16[2,6,32,512]{3,2,1,0:T(8,128)(2,1)S(1)}, bf16[2,6,32,512]{3,2,1,0:T(8,128)(2,1)S(1)}, u32[]{:S(2)}, u32[]{:S(2)}) collective-permute-start(bf16[2,6,32,512]{3,2,1,0:T(8,128)(2,1)S(1)} %bitcast.95), channel_id=1, source_target_pairs={{0,10},{2,12},{4,14},{6,0},{8,2},{10,4},{12,6},{14,8},{1,11},{3,13... | collective-permute-start | bytes 1179656 | tf_op jit(solution)/shard_map/ppermute | solution.py:148
  200.8 49.4 %collective-permute-start.10 = (bf16[2,6,32,512]{3,2,1,0:T(8,128)(2,1)S(1)}, bf16[2,6,32,512]{3,2,1,0:T(8,128)(2,1)S(1)}, u32[]{:S(2)}, u32[]{:S(2)}) collective-permute-start(bf16[2,6,32,512]{3,2,1,0:T(8,128)(2,1)S(1)} %bitcast.97), channel_id=1, source_target_pairs={{0,6},{2,8},{4,10},{6,12},{8,14},{10,0},{12,2},{14,4},{1,7},{3,9},... | collective-permute-start | bytes 1179656 | tf_op jit(solution)/shard_map/ppermute | solution.py:148
  201.9 56.5 %collective-permute-start.11 = (bf16[2,6,32,512]{3,2,1,0:T(8,128)(2,1)S(1)}, bf16[2,6,32,512]{3,2,1,0:T(8,128)(2,1)S(1)}, u32[]{:S(2)}, u32[]{:S(2)}) collective-permute-start(bf16[2,6,32,512]{3,2,1,0:T(8,128)(2,1)S(1)} %bitcast.96), channel_id=1, source_target_pairs={{0,8},{2,10},{4,12},{6,14},{8,0},{10,2},{12,4},{14,6},{1,9},{3,11}... | collective-permute-start | bytes 1179656 | tf_op jit(solution)/shard_map/ppermute | solution.py:148
  258.7 2.7 %copy-start = (f32[2,6,256,512]{3,2,1,0:T(8,128)}, f32[2,6,256,512]{3,2,1,0:T(8,128)S(1)}, u32[]{:S(2)}) copy-start(f32[2,6,256,512]{3,2,1,0:T(8,128)S(1)} %convert_dynamic-update-slice_fusion.1) | copy-start | bytes 18874372
Sparse Core Ops, SparseCore 0:
  9.5 53.2 all-gather.1

commit v21 on v20

--- a/solution.py
+++ b/solution.py
@@ -78,7 +78,7 @@
 def _dft(weights, x, own):
     rows, k = weights.shape
     n = x.shape[1]
-    tn = 4096 if n % 4096 == 0 else n
+    tn = 8192 if n % 8192 == 0 else n
     return pl.pallas_call(
         _dft_kernel,
         grid=(n // tn,),

time: 270 us -> 269 us (level)
  no operation moved by 1% of the time
where the time goes in v21:
time: 269 us
  waiting for transfers between devices  155 us (58%)
  starting transfers between devices  37.4 us (14%)
  Pallas kernels  30.6 us (11%)
  local copies, waits for them, and re-layouts  24.1 us (9%)
  between operations  13.9 us (5%)
  other arithmetic  8.06 us (3%)
    ppermute x7, waiting for transfers between devices, body(): lax.ppermute(piece, 'blade', [(j, (j + t) % nbd) for j in range(nbd)])  59.4 us
    all_gather x1, waiting for transfers between devices, body(): pt = lax.all_gather(mine, ('blade', 'dof'), axis=0, tiled=True)  51.8 us
    ppermute x7, waiting for transfers between devices, body(): lax.ppermute(piece, 'blade', [(j, (j + s) % nbd) for j in range(nbd)])  38.2 us
    ppermute x7, starting transfers between devices, body(): lax.ppermute(piece, 'blade', [(j, (j + s) % nbd) for j in range(nbd)])  30.2 us
    pallas_call x1, Pallas kernels, _project(): pl.pallas_call(_project_kernel, grid_spec=grid_spec, out_shape=[jax.Shape...  25.2 us
    unnamed x28, local copies, waits for them, and re-layouts  13.1 us
    ppermute x7, starting transfers between devices, body(): lax.ppermute(piece, 'blade', [(j, (j + t) % nbd) for j in range(nbd)])  6.88 us
    pallas_call x1, Pallas kernels, _dft(): pl.pallas_call(_dft_kernel, grid=(n // tn,), in_specs=[pl.BlockSpec((rows...  5.44 us
  transfers between devices with their start and end apart: 16, of which 8 were waited for; matrix products, arithmetic and copies ran while one was open for 5% of the time, Pallas kernels for 0%

profile of v21, /device:TPU:0, one launch (start us, length us, event | category | flops | bytes accessed | tf_op | source)
XLA Modules:
  0.0 268.8 jit_solution(4335882571729819424)
XLA Ops:
  6.5 1.8 copy.6
  8.3 0.0 all-gather.2.cloned.1.call-update
  8.4 1.3 reshape.160.rows_ref
  9.7 1.3 reshape.161.cols_ref
  11.0 51.8 %all-gather.2.cloned.1.call-done.pt_ref = bf16[32,512,128]{2,1,0:T(8,128)(2,1)} async-done(((bf16[2,512,128]{2,1,0:T(8,128)(2,1)}), bf16[32,512,128]{2,1,0:T(8,128)(2,1)}) %all-gather.2.cloned.1.call-update) | async-done | bytes 4194320 | tf_op jit(solution)/shard_map/all_gather | solution.py:111
  62.8 25.2 %shard_map.46 = (f32[6,256,512]{2,1,0:T(8,128)}, f32[6,256,512]{2,1,0:T(8,128)}) custom-call(s32[192]{0:T(256)} %reshape.160.rows_ref, s32[192]{0:T(256)} %reshape.161.cols_ref, s32[1]{0:T(128)} %bitcast.side_ref, bf16[32,512,128]{2,1,0:T(8,128)(2,1)} %all-gather.2.cloned.1.call-done.pt_ref, bf16[6,32,128,128]{3,2,1,0:T(8,128)(2,1)} %s_ref.1), custom_call_target="tpu_custom_call" | custom-call | tf_op jit(solution)/shard_map/pallas_call | solution.py:52
  88.0 0.3 collective-permute-start
  88.2 0.1 iota_add_fusion
  88.3 0.1 add.222
  88.4 0.1 iota_add_fusion.1
  88.5 5.4 %collective-permute-done = f32[6,256,512]{2,1,0:T(8,128)S(1)} collective-permute-done((f32[6,256,512]{2,1,0:T(8,128)}, f32[6,256,512]{2,1,0:T(8,128)S(1)}, u32[]{:S(2)}, u32[]{:S(2)}) %collective-permute-start) | collective-permute-done | bytes 3145760 | tf_op jit(solution)/shard_map/ppermute | solution.py:117
  93.8 1.6 copy-done.1
  95.5 3.6 %add.225 = f32[6,256,512]{2,1,0:T(8,128)S(1)} add(f32[6,256,512]{2,1,0:T(8,128)} %get-tuple-element.9, f32[6,256,512]{2,1,0:T(8,128)} %copy-done.1) | non-fusion elementwise | flops 786432 | bytes 9437184 | tf_op jit(solution)/shard_map/add | solution.py:117
  99.1 1.5 dynamic-slice_bitcast_fusion
  100.5 0.6 collective-permute-start.1
  101.1 0.2 fusion.4
  101.3 1.5 collective-permute-start.2
  102.9 0.6 pad_maximum_fusion
  103.5 1.5 reshape.159.w_ref
  104.9 4.2 %collective-permute-start.7 = (f32[6,32,512]{2,1,0:T(8,128)S(1)}, f32[6,32,512]{2,1,0:T(8,128)S(1)}, u32[]{:S(2)}, u32[]{:S(2)}) collective-permute-start(f32[6,32,512]{2,1,0:T(8,128)S(1)} %get-tuple-element.13), channel_id=1, source_target_pairs={{0,14},{2,0},{4,2},{6,4},{8,6},{10,8},{12,10},{14,12},{1,15},{3,1}... | collective-permute-start | bytes 1179656 | tf_op jit(solution)/shard_map/ppermute | solution.py:130
  109.1 0.5 collective-permute-start.6
  109.6 0.0 collective-permute-start.5
  109.7 6.0 %collective-permute-done.1 = f32[6,32,512]{2,1,0:T(8,128)} collective-permute-done((f32[6,32,512]{2,1,0:T(8,128)}, f32[6,32,512]{2,1,0:T(8,128)}, u32[]{:S(2)}, u32[]{:S(2)}) %collective-permute-start.1) | collective-permute-done | bytes 393248 | tf_op jit(solution)/shard_map/ppermute | solution.py:130
  115.6 0.0 collective-permute-start.3
  115.6 1.0 bitcast_dynamic-update-slice_fusion.6
  116.7 23.4 %collective-permute-start.4 = (f32[6,32,512]{2,1,0:T(8,128)}, f32[6,32,512]{2,1,0:T(8,128)S(1)}, u32[]{:S(2)}, u32[]{:S(2)}) collective-permute-start(f32[6,32,512]{2,1,0:T(8,128)} %get-tuple-element.16), channel_id=1, source_target_pairs={{0,8},{2,10},{4,12},{6,14},{8,0},{10,2},{12,4},{14,6},{1,9},{3,11}... | collective-permute-start | bytes 1179656 | tf_op jit(solution)/shard_map/ppermute | solution.py:130
  140.1 1.0 bitcast_dynamic-update-slice_fusion.5
  141.1 24.2 %collective-permute-done.3 = f32[6,32,512]{2,1,0:T(8,128)S(1)} collective-permute-done((f32[6,32,512]{2,1,0:T(8,128)}, f32[6,32,512]{2,1,0:T(8,128)S(1)}, u32[]{:S(2)}, u32[]{:S(2)}) %collective-permute-start.3) | collective-permute-done | bytes 393248 | tf_op jit(solution)/shard_map/ppermute | solution.py:130
  165.4 7.9 %collective-permute-done.4 = f32[6,32,512]{2,1,0:T(8,128)S(1)} collective-permute-done((f32[6,32,512]{2,1,0:T(8,128)}, f32[6,32,512]{2,1,0:T(8,128)S(1)}, u32[]{:S(2)}, u32[]{:S(2)}) %collective-permute-start.4) | collective-permute-done | bytes 393248 | tf_op jit(solution)/shard_map/ppermute | solution.py:130
  173.4 0.0 collective-permute-done.6
  173.5 0.0 collective-permute-done.7
  173.5 3.5 %copy.7 = f32[6,8,32,512]{3,1,2,0:T(8,128)} copy(f32[6,8,32,512]{3,2,1,0:T(8,128)S(1)} %bitcast.73) | data formatting | bytes 6291456
  177.0 5.4 %shard_map.47 = (f32[12,16384]{1,0:T(8,128)}, bf16[84,16384]{1,0:T(8,128)(2,1)}) custom-call(f32[96,48]{1,0:T(8,128)} %reshape.159.w_ref, f32[48,16384]{1,0:T(8,128)} %bitcast.70), custom_call_target="tpu_custom_call" | custom-call | tf_op jit(solution)/shard_map/pallas_call | solution.py:82
  182.4 2.6 fusion.10
  185.1 0.2 copy.9
  185.3 1.0 collective-permute-start.8
  186.2 0.2 copy.10
  186.4 0.1 collective-permute-start.9
  186.6 1.8 copy.8
  188.5 0.1 slice.35
  188.5 0.2 copy.15
  188.7 0.2 copy.14
  188.9 3.7 %collective-permute-start.13 = (bf16[2,6,32,512]{3,2,1,0:T(8,128)(2,1)S(1)}, bf16[2,6,32,512]{3,2,1,0:T(8,128)(2,1)S(1)}, u32[]{:S(2)}, u32[]{:S(2)}) collective-permute-start(bf16[2,6,32,512]{3,2,1,0:T(8,128)(2,1)S(1)} %bitcast.94), channel_id=1, source_target_pairs={{0,12},{2,14},{4,0},{6,2},{8,4},{10,6},{12,8},{14,10},{1,13},{3,15... | collective-permute-start | bytes 1179656 | tf_op jit(solution)/shard_map/ppermute | solution.py:148
  192.7 2.0 collective-permute-start.14
  194.7 0.2 copy.13
  194.9 0.1 collective-permute-start.12
  194.9 0.2 copy.12
  195.1 0.2 copy.11
  195.3 0.8 broadcast_in_dim.2
  196.1 0.1 constant_dynamic-update-slice_fusion
  196.2 4.1 %collective-permute-done.8 = bf16[2,6,32,512]{3,2,1,0:T(8,128)(2,1)} collective-permute-done((bf16[2,6,32,512]{3,2,1,0:T(8,128)(2,1)S(1)}, bf16[2,6,32,512]{3,2,1,0:T(8,128)(2,1)}, u32[]{:S(2)}, u32[]{:S(2)}) %collective-permute-start.8) | collective-permute-done | bytes 393248 | tf_op jit(solution)/shard_map/ppermute | solution.py:148
  200.3 0.0 collective-permute-start.10
  200.3 1.1 convert_dynamic-update-slice_fusion.6
  201.4 0.1 collective-permute-start.11
  201.5 1.1 convert_dynamic-update-slice_fusion.5
  202.6 47.2 %collective-permute-done.10 = bf16[2,6,32,512]{3,2,1,0:T(8,128)(2,1)S(1)} collective-permute-done((bf16[2,6,32,512]{3,2,1,0:T(8,128)(2,1)S(1)}, bf16[2,6,32,512]{3,2,1,0:T(8,128)(2,1)S(1)}, u32[]{:S(2)}, u32[]{:S(2)}) %collective-permute-start.10) | collective-permute-done | bytes 393248 | tf_op jit(solution)/shard_map/ppermute | solution.py:148
  249.8 0.1 convert_dynamic-update-slice_fusion.4
  249.8 8.1 %collective-permute-done.11 = bf16[2,6,32,512]{3,2,1,0:T(8,128)(2,1)S(1)} collective-permute-done((bf16[2,6,32,512]{3,2,1,0:T(8,128)(2,1)S(1)}, bf16[2,6,32,512]{3,2,1,0:T(8,128)(2,1)S(1)}, u32[]{:S(2)}, u32[]{:S(2)}) %collective-permute-start.11) | collective-permute-done | bytes 393248 | tf_op jit(solution)/shard_map/ppermute | solution.py:148
  257.9 0.1 convert_dynamic-update-slice_fusion.3
  258.0 0.1 convert_dynamic-update-slice_fusion.2
  258.2 0.1 convert_dynamic-update-slice_fusion.1
  258.2 0.0 copy-start
  258.3 2.7 copy-done
  261.0 1.0 convert_dynamic-update-slice_fusion
  (22 shorter events, 0.4 us)
Async XLA Ops:
  6.5 56.3 %all-gather.2.cloned.1.call-start = ((), (), s32[]{:S(2)}) async-start(), calls=%async_computation | async-start | bytes 4456448 | tf_op jit(solution)/shard_map/all_gather | solution.py:111
  88.0 5.9 %collective-permute-start = (f32[6,256,512]{2,1,0:T(8,128)}, f32[6,256,512]{2,1,0:T(8,128)S(1)}, u32[]{:S(2)}, u32[]{:S(2)}) collective-permute-start(f32[6,256,512]{2,1,0:T(8,128)} %get-tuple-element.10), channel_id=1, source_target_pairs={{0,1},{1,0},{2,3},{3,2},{4,5},{5,4},{6,7},{7,6},{8,9},{9,8},{10,11... | collective-permute-start | bytes 9437192 | tf_op jit(solution)/shard_map/ppermute | solution.py:117
  93.8 1.6 copy-start.1
  100.5 15.1 %collective-permute-start.1 = (f32[6,32,512]{2,1,0:T(8,128)}, f32[6,32,512]{2,1,0:T(8,128)}, u32[]{:S(2)}, u32[]{:S(2)}) collective-permute-start(f32[6,32,512]{2,1,0:T(8,128)} %get-tuple-element.19), channel_id=1, source_target_pairs={{0,2},{2,4},{4,6},{6,8},{8,10},{10,12},{12,14},{14,0},{1,3},{3,5},... | collective-permute-start | bytes 1179656 | tf_op jit(solution)/shard_map/ppermute | solution.py:130
  101.3 15.4 %collective-permute-start.2 = (f32[6,32,512]{2,1,0:T(8,128)}, f32[6,32,512]{2,1,0:T(8,128)}, u32[]{:S(2)}, u32[]{:S(2)}) collective-permute-start(f32[6,32,512]{2,1,0:T(8,128)} %get-tuple-element.18), channel_id=1, source_target_pairs={{0,4},{2,6},{4,8},{6,10},{8,12},{10,14},{12,0},{14,2},{1,5},{3,7},... | collective-permute-start | bytes 1179656 | tf_op jit(solution)/shard_map/ppermute | solution.py:130
  104.9 68.5 %collective-permute-start.7 = (f32[6,32,512]{2,1,0:T(8,128)S(1)}, f32[6,32,512]{2,1,0:T(8,128)S(1)}, u32[]{:S(2)}, u32[]{:S(2)}) collective-permute-start(f32[6,32,512]{2,1,0:T(8,128)S(1)} %get-tuple-element.13), channel_id=1, source_target_pairs={{0,14},{2,0},{4,2},{6,4},{8,6},{10,8},{12,10},{14,12},{1,15},{3,1}... | collective-permute-start | bytes 1179656 | tf_op jit(solution)/shard_map/ppermute | solution.py:130
  109.1 64.3 %collective-permute-start.6 = (f32[6,32,512]{2,1,0:T(8,128)}, f32[6,32,512]{2,1,0:T(8,128)S(1)}, u32[]{:S(2)}, u32[]{:S(2)}) collective-permute-start(f32[6,32,512]{2,1,0:T(8,128)} %get-tuple-element.14), channel_id=1, source_target_pairs={{0,12},{2,14},{4,0},{6,2},{8,4},{10,6},{12,8},{14,10},{1,13},{3,15... | collective-permute-start | bytes 1179656 | tf_op jit(solution)/shard_map/ppermute | solution.py:130
  109.6 63.7 %collective-permute-start.5 = (f32[6,32,512]{2,1,0:T(8,128)}, f32[6,32,512]{2,1,0:T(8,128)S(1)}, u32[]{:S(2)}, u32[]{:S(2)}) collective-permute-start(f32[6,32,512]{2,1,0:T(8,128)} %get-tuple-element.15), channel_id=1, source_target_pairs={{0,10},{2,12},{4,14},{6,0},{8,2},{10,4},{12,6},{14,8},{1,11},{3,13... | collective-permute-start | bytes 1179656 | tf_op jit(solution)/shard_map/ppermute | solution.py:130
  115.6 49.7 %collective-permute-start.3 = (f32[6,32,512]{2,1,0:T(8,128)}, f32[6,32,512]{2,1,0:T(8,128)S(1)}, u32[]{:S(2)}, u32[]{:S(2)}) collective-permute-start(f32[6,32,512]{2,1,0:T(8,128)} %get-tuple-element.17), channel_id=1, source_target_pairs={{0,6},{2,8},{4,10},{6,12},{8,14},{10,0},{12,2},{14,4},{1,7},{3,9},... | collective-permute-start | bytes 1179656 | tf_op jit(solution)/shard_map/ppermute | solution.py:130
  116.7 56.7 %collective-permute-start.4 = (f32[6,32,512]{2,1,0:T(8,128)}, f32[6,32,512]{2,1,0:T(8,128)S(1)}, u32[]{:S(2)}, u32[]{:S(2)}) collective-permute-start(f32[6,32,512]{2,1,0:T(8,128)} %get-tuple-element.16), channel_id=1, source_target_pairs={{0,8},{2,10},{4,12},{6,14},{8,0},{10,2},{12,4},{14,6},{1,9},{3,11}... | collective-permute-start | bytes 1179656 | tf_op jit(solution)/shard_map/ppermute | solution.py:130
  185.3 15.1 %collective-permute-start.8 = (bf16[2,6,32,512]{3,2,1,0:T(8,128)(2,1)S(1)}, bf16[2,6,32,512]{3,2,1,0:T(8,128)(2,1)}, u32[]{:S(2)}, u32[]{:S(2)}) collective-permute-start(bf16[2,6,32,512]{3,2,1,0:T(8,128)(2,1)S(1)} %bitcast.91), channel_id=1, source_target_pairs={{0,2},{2,4},{4,6},{6,8},{8,10},{10,12},{12,14},{14,0},{1,3},{3,5},... | collective-permute-start | bytes 1179656 | tf_op jit(solution)/shard_map/ppermute | solution.py:148
  186.4 15.0 %collective-permute-start.9 = (bf16[2,6,32,512]{3,2,1,0:T(8,128)(2,1)S(1)}, bf16[2,6,32,512]{3,2,1,0:T(8,128)(2,1)}, u32[]{:S(2)}, u32[]{:S(2)}) collective-permute-start(bf16[2,6,32,512]{3,2,1,0:T(8,128)(2,1)S(1)} %bitcast.92), channel_id=1, source_target_pairs={{0,4},{2,6},{4,8},{6,10},{8,12},{10,14},{12,0},{14,2},{1,5},{3,7},... | collective-permute-start | bytes 1179656 | tf_op jit(solution)/shard_map/ppermute | solution.py:148
  188.9 69.2 %collective-permute-start.13 = (bf16[2,6,32,512]{3,2,1,0:T(8,128)(2,1)S(1)}, bf16[2,6,32,512]{3,2,1,0:T(8,128)(2,1)S(1)}, u32[]{:S(2)}, u32[]{:S(2)}) collective-permute-start(bf16[2,6,32,512]{3,2,1,0:T(8,128)(2,1)S(1)} %bitcast.94), channel_id=1, source_target_pairs={{0,12},{2,14},{4,0},{6,2},{8,4},{10,6},{12,8},{14,10},{1,13},{3,15... | collective-permute-start | bytes 1179656 | tf_op jit(solution)/shard_map/ppermute | solution.py:148
  192.7 65.6 %collective-permute-start.14 = (bf16[2,6,32,512]{3,2,1,0:T(8,128)(2,1)S(1)}, bf16[2,6,32,512]{3,2,1,0:T(8,128)(2,1)S(1)}, u32[]{:S(2)}, u32[]{:S(2)}) collective-permute-start(bf16[2,6,32,512]{3,2,1,0:T(8,128)(2,1)S(1)} %bitcast.93), channel_id=1, source_target_pairs={{0,14},{2,0},{4,2},{6,4},{8,6},{10,8},{12,10},{14,12},{1,15},{3,1}... | collective-permute-start | bytes 1179656 | tf_op jit(solution)/shard_map/ppermute | solution.py:148
  194.9 63.2 %collective-permute-start.12 = (bf16[2,6,32,512]{3,2,1,0:T(8,128)(2,1)S(1)}, bf16[2,6,32,512]{3,2,1,0:T(8,128)(2,1)S(1)}, u32[]{:S(2)}, u32[]{:S(2)}) collective-permute-start(bf16[2,6,32,512]{3,2,1,0:T(8,128)(2,1)S(1)} %bitcast.95), channel_id=1, source_target_pairs={{0,10},{2,12},{4,14},{6,0},{8,2},{10,4},{12,6},{14,8},{1,11},{3,13... | collective-permute-start | bytes 1179656 | tf_op jit(solution)/shard_map/ppermute | solution.py:148
  200.3 49.4 %collective-permute-start.10 = (bf16[2,6,32,512]{3,2,1,0:T(8,128)(2,1)S(1)}, bf16[2,6,32,512]{3,2,1,0:T(8,128)(2,1)S(1)}, u32[]{:S(2)}, u32[]{:S(2)}) collective-permute-start(bf16[2,6,32,512]{3,2,1,0:T(8,128)(2,1)S(1)} %bitcast.97), channel_id=1, source_target_pairs={{0,6},{2,8},{4,10},{6,12},{8,14},{10,0},{12,2},{14,4},{1,7},{3,9},... | collective-permute-start | bytes 1179656 | tf_op jit(solution)/shard_map/ppermute | solution.py:148
  201.4 56.5 %collective-permute-start.11 = (bf16[2,6,32,512]{3,2,1,0:T(8,128)(2,1)S(1)}, bf16[2,6,32,512]{3,2,1,0:T(8,128)(2,1)S(1)}, u32[]{:S(2)}, u32[]{:S(2)}) collective-permute-start(bf16[2,6,32,512]{3,2,1,0:T(8,128)(2,1)S(1)} %bitcast.96), channel_id=1, source_target_pairs={{0,8},{2,10},{4,12},{6,14},{8,0},{10,2},{12,4},{14,6},{1,9},{3,11}... | collective-permute-start | bytes 1179656 | tf_op jit(solution)/shard_map/ppermute | solution.py:148
  258.2 2.7 %copy-start = (f32[2,6,256,512]{3,2,1,0:T(8,128)}, f32[2,6,256,512]{3,2,1,0:T(8,128)S(1)}, u32[]{:S(2)}) copy-start(f32[2,6,256,512]{3,2,1,0:T(8,128)S(1)} %convert_dynamic-update-slice_fusion.1) | copy-start | bytes 18874372
Sparse Core Ops, SparseCore 0:
  9.5 53.2 all-gather.1
